TPU v7x, 32 devices: a whole 2x2x4 slice. The times are simulated.
32 devices in a mesh: parts: 2 (over y), user: 16 (over z, x, core).
Axes of the slice: x: 2, y: 2, z: 4, core: 2. Of those that a mesh axis runs over, the one named last changes fastest.
Arguments:
- counts: int32 [1024, 16384], P(None, ('parts', 'user')), parts along dimension 1, may hold values from 0 to 3
- first_bin: int32 [16384], P(('parts', 'user')), parts along dimension 0, may hold values from 0 to 511
- time_factor: float32 [2048, 128], P('parts'), parts along dimension 0, may hold values from -6 to 6
- user_factor: float32 [16384, 128], P(('parts', 'user')), parts along dimension 0, may hold values from -0.5 to 0.5
- user_base: float32 [16384], P(('parts', 'user')), parts along dimension 0, may hold values from -4 to 4
Outputs:
- new_time_factor: float32 [2048, 128], P(('parts', 'user')), parts along dimension 0
- new_user_factor: float32 [16384, 128], P(('parts', 'user')), parts along dimension 0
There are 2 independent parts, one for each index of `parts`. A program takes and returns all parts, laid end to end along the dimension named above; each array names one. Nothing has to cross between parts.
All inputs are finite; a program needn't handle non-finite values.
Results may differ from a plain program's by a relative error of at most 0.0003.
Values sent between devices are 32-bit elements; how exact they have to be, the bound alone decides.
No kernel may reach another device: no remote copies, remote signals or barrier semaphores. Data moves between devices by JAX's collectives and lax.ppermute only.
A program may use at most 64 MiB of HBM per device.

v0:
```python
import jax
import jax.numpy as jnp
from jax import lax
from jax.sharding import PartitionSpec as P

SWEEPS = 2


damping = 0.5
background = 0.5


def product(left, right):
    return jnp.dot(left, right, precision=lax.Precision.HIGHEST, preferred_element_type=jnp.float32)


def local_terms(time_factor, user_block, base_block, count_block, start_block):
    linear = product(time_factor, user_block.T) + base_block[None, :]
    time_bins = jnp.arange(time_factor.shape[0], dtype=jnp.int32)[:, None]
    observed = (time_bins >= start_block[None, :]).astype(jnp.float32)
    intensity = jax.nn.softplus(linear) + background
    gate_value = jax.nn.sigmoid(linear)
    residual = observed * gate_value * (1.0 - count_block.astype(jnp.float32) / intensity)
    curvature = observed * gate_value * gate_value / intensity
    return (residual, curvature)


def body(counts, first_bin, time_factor, user_factor, user_base):
    shard_rows = time_factor.shape[0] // lax.axis_size("user")
    offset = lax.axis_index("user") * shard_rows
    sweeps = SWEEPS
    mine_rows = time_factor
    for sweep in range(sweeps):
        residual, curvature = local_terms(time_factor, user_factor, user_base, counts, first_bin)
        grad_user = product(residual.T, time_factor)
        grad_time = lax.psum_scatter(
            product(residual, user_factor), "user", scatter_dimension=0, tiled=True
        )
        own_norm = jnp.sum(grad_time * grad_time) + jnp.sum(grad_user * grad_user)
        norm_total = lax.psum(own_norm, "user")
        grad_whole = lax.all_gather(grad_time, "user", axis=0, tiled=True)
        tangent_image = product(grad_whole, user_factor.T) + product(time_factor, grad_user.T)
        bending = jnp.sum(curvature * tangent_image * tangent_image)
        bend_total = lax.psum(bending, "user")
        relax_step = norm_total / (bend_total + damping * norm_total)
        user_factor = user_factor - relax_step * grad_user
        mine_rows = (
            lax.dynamic_slice_in_dim(time_factor, offset, shard_rows, 0) - relax_step * grad_time
        )
        if sweep + 1 < sweeps:
            time_factor = time_factor - relax_step * grad_whole
    return (mine_rows, user_factor)


def solution(mesh):
    return jax.shard_map(
        body,
        mesh=mesh,
        in_specs=(
            P(None, ("parts", "user")),
            P(("parts", "user")),
            P("parts", None),
            P(("parts", "user"), None),
            P(("parts", "user")),
        ),
        out_specs=(P(("parts", "user"), None), P(("parts", "user"), None)),
        check_vma=False,
    )
```

profile of v0, /device:TPU:0, one launch (start us, length us, event | category | flops | bytes accessed | tf_op | source)
XLA Modules:
  0.0 272.2 jit_solution(15472752577354228033)
XLA Ops:
  7.2 0.0 copy-start
  7.2 0.0 reduce-scatter.3.cloned.1.call-start
  7.2 6.9 %select_multiply_fusion.3 = (f32[1024,512]{1,0:T(8,128)S(1)}, f32[1024,512]{1,0:T(8,128)}) fusion(s32[1024,512]{1,0:T(8,128)} %param.5, s32[512]{0:T(512)} %param.6, f32[512]{0:T(512)} %param.9, f32[1024,128]{1,0:T(8,128)} %param.7, f32[512,128]{1,0:T(8,128)} %param.8), kind=kOutput, calls=%fused_computation.7 | convolution fusion | flops 814219264 | bytes 7081984 | tf_op jit(solution)/shard_map/dot_general | solution.py:14
  14.1 0.0 copy-start.1
  14.1 0.0 copy-done
  14.1 2.6 fusion.6
  16.7 0.0 reduce-scatter.3.cloned.1.call-update
  16.8 0.0 reduce-scatter.5.cloned.1.call-start
  16.8 0.0 copy-done.1
  16.8 4.0 %multiply_reduce_fusion.1 = (f32[]{:T(128)}, f32[512,128]{1,0:T(8,128)S(1)}) fusion(f32[1024,512]{1,0:T(8,128)S(1)} %get-tuple-element.6, f32[1024,128]{1,0:T(8,128)S(1)} %copy-done.1), kind=kOutput, calls=%fused_computation.22 | convolution fusion | flops 805437440 | bytes 2883588 | tf_op jit(solution)/shard_map/dot_general | solution.py:14
  20.8 0.0 copy-start.5
  20.8 0.0 copy-start.6
  20.8 54.6 %reduce-scatter.3.cloned.1.call-done = f32[64,128]{1,0:T(8,128)} async-done(((f32[1024,128]{1,0:T(8,128)}), f32[64,128]{1,0:T(8,128)}) %reduce-scatter.3.cloned.1.call-update) | async-done | bytes 32784 | tf_op jit(solution)/shard_map/reduce_scatter | solution.py:36
  75.4 0.0 copy-start.7
  75.4 21.4 %all_gather.6 = f32[1024,128]{1,0:T(8,128)S(1)} all-gather(f32[64,128]{1,0:T(8,128)} %reduce-scatter.3.cloned.1.call-done), channel_id=1, replica_groups=mesh['parts'=2,'user'=16] {'user'}, dimensions={0}, use_global_device_ids=true | all-gather | bytes 557056 | tf_op jit(solution)/shard_map/all_gather | solution.py:41
  96.8 1.8 fusion.7
  98.6 0.0 copy-done.5
  98.6 0.0 copy-done.6
  98.6 0.0 copy-done.7
  98.6 0.0 copy-start.3
  98.6 4.7 %fusion.4 = f32[]{:T(128)} fusion(f32[1024,512]{1,0:T(8,128)S(1)} %fusion.7, f32[512,128]{1,0:T(8,128)S(1)} %get-tuple-element.9, f32[1024,128]{1,0:T(8,128)S(1)} %copy-done.1, s32[512]{0:T(512)S(1)} %copy-done.5, f32[1024,512]{1,0:T(8,128)S(1)} %copy-done.7, f32[512]{0:T(512)S(1)} %copy-done.6), kind=kOutput, calls=%fused_computation.16 | convolution fusion | flops 815267840 | bytes 4984836 | tf_op jit(solution)/shard_map/dot_general | solution.py:14
  103.4 0.0 copy-done.3
  103.4 0.6 multiply_reduce_fusion.3
  105.3 30.6 %all-reduce.1 = (f32[]{:T(128)}, f32[]{:T(128)}) all-reduce(f32[]{:T(128)S(6)} %add.71, f32[]{:T(128)} %fusion.4), channel_id=1, replica_groups=mesh['parts'=2,'user'=16] {'user'}, use_global_device_ids=true, to_apply=%region_3.4 | all-reduce | flops 2 | bytes 16 | tf_op jit(solution)/shard_map/psum | solution.py:40
  137.8 0.0 copy-start.4
  137.8 0.1 multiply_subtract_fusion
  137.9 1.5 copy-done.4
  139.4 5.0 %select_multiply_fusion.1 = (f32[1024,512]{1,0:T(8,128)S(1)}, f32[1024,512]{1,0:T(8,128)}) fusion(s32[1024,512]{1,0:T(8,128)S(1)} %copy-done.4, s32[512]{0:T(512)S(1)} %copy-done.5, f32[512]{0:T(512)S(1)} %copy-done.6, f32[1024,128]{1,0:T(8,128)S(1)} %multiply_subtract_fusion, f32[512,128]{1,0:T(8,128)S(1)} %multiply_subtract_fusion.2), kind=kOutput, calls=%fused_computation.5 | convolution fusion | flops 814219264 | bytes 7081984 | tf_op jit(solution)/shard_map/dot_general | solution.py:14
  144.4 2.6 fusion.8
  147.0 0.0 reduce-scatter.5.cloned.1.call-update
  147.0 4.0 %multiply_reduce_fusion = (f32[]{:T(128)}, f32[512,128]{1,0:T(8,128)S(1)}) fusion(f32[1024,512]{1,0:T(8,128)S(1)} %get-tuple-element.10, f32[1024,128]{1,0:T(8,128)S(1)} %multiply_subtract_fusion), kind=kOutput, calls=%fused_computation.20 | convolution fusion | flops 805437440 | bytes 2883588 | tf_op jit(solution)/shard_map/dot_general | solution.py:14
  151.1 49.1 %reduce-scatter.5.cloned.1.call-done = f32[64,128]{1,0:T(8,128)} async-done(((f32[1024,128]{1,0:T(8,128)}), f32[64,128]{1,0:T(8,128)}) %reduce-scatter.5.cloned.1.call-update) | async-done | bytes 32784 | tf_op jit(solution)/shard_map/reduce_scatter | solution.py:36
  200.2 0.0 copy-start.2
  200.2 21.5 %all_gather.7 = f32[1024,128]{1,0:T(8,128)S(1)} all-gather(f32[64,128]{1,0:T(8,128)} %reduce-scatter.5.cloned.1.call-done), channel_id=1, replica_groups=mesh['parts'=2,'user'=16] {'user'}, dimensions={0}, use_global_device_ids=true | all-gather | bytes 557056 | tf_op jit(solution)/shard_map/all_gather | solution.py:41
  221.7 1.8 fusion.9
  223.5 0.0 copy-done.2
  223.5 0.6 multiply_reduce_fusion.2
  225.4 6.2 %fusion.5 = f32[]{:T(128)} fusion(f32[1024,512]{1,0:T(8,128)S(1)} %fusion.9, f32[1024,128]{1,0:T(8,128)S(1)} %multiply_subtract_fusion, f32[512,128]{1,0:T(8,128)S(1)} %get-tuple-element.13, s32[512]{0:T(512)S(1)} %copy-done.5, f32[1024,512]{1,0:T(8,128)} %get-tuple-element.11, f32[512]{0:T(512)S(1)} %copy-done.6), kind=kOutput, calls=%fused_computation.17 | convolution fusion | flops 815267840 | bytes 4984836 | tf_op jit(solution)/shard_map/dot_general | solution.py:14
  231.6 30.5 %all-reduce = (f32[]{:T(128)}, f32[]{:T(128)}) all-reduce(f32[]{:T(128)S(6)} %add.79, f32[]{:T(128)} %fusion.5), channel_id=1, replica_groups=mesh['parts'=2,'user'=16] {'user'}, use_global_device_ids=true, to_apply=%region_9.10 | all-reduce | flops 2 | bytes 16 | tf_op jit(solution)/shard_map/psum | solution.py:40
  264.0 0.7 multiply_subtract_fusion.1
  264.7 0.6 multiply_subtract_fusion.3
  (1 shorter events, 0.0 us)
Async XLA Ops:
  7.2 7.0 %copy-start = (f32[512,128]{1,0:T(8,128)S(1)}, f32[512,128]{1,0:T(8,128)}, u32[]{:S(2)}) copy-start(f32[512,128]{1,0:T(8,128)} %param.8) | copy-start | bytes 786436
  7.2 68.2 %reduce-scatter.3.cloned.1.call-start = ((), (), s32[]{:S(2)}) async-start(), calls=%async_computation.2 | async-start | bytes 557056 | tf_op jit(solution)/shard_map/reduce_scatter | solution.py:36
  14.1 2.7 copy-start.1
  16.8 183.4 %reduce-scatter.5.cloned.1.call-start = ((), (), s32[]{:S(2)}) async-start(), calls=%async_computation.3 | async-start | bytes 557056 | tf_op jit(solution)/shard_map/reduce_scatter | solution.py:36
  20.8 77.8 %copy-start.5 = (s32[512]{0:T(512)S(1)}, s32[512]{0:T(512)}, u32[]{:S(2)}) copy-start(s32[512]{0:T(512)} %param.6) | copy-start | bytes 6148
  20.8 77.8 %copy-start.6 = (f32[512]{0:T(512)S(1)}, f32[512]{0:T(512)}, u32[]{:S(2)}) copy-start(f32[512]{0:T(512)} %param.9) | copy-start | bytes 6148
  75.4 23.2 %copy-start.7 = (f32[1024,512]{1,0:T(8,128)S(1)}, f32[1024,512]{1,0:T(8,128)}, u32[]{:S(2)}) copy-start(f32[1024,512]{1,0:T(8,128)} %get-tuple-element.7) | copy-start | bytes 6291460
  98.6 4.7 %copy-start.3 = (f32[64,128]{1,0:T(8,128)S(1)}, f32[64,128]{1,0:T(8,128)}, u32[]{:S(2)}) copy-start(f32[64,128]{1,0:T(8,128)} %reduce-scatter.3.cloned.1.call-done) | copy-start | bytes 98308
  137.8 1.6 copy-start.4
  200.2 23.3 %copy-start.2 = (f32[64,128]{1,0:T(8,128)S(1)}, f32[64,128]{1,0:T(8,128)}, u32[]{:S(2)}) copy-start(f32[64,128]{1,0:T(8,128)} %reduce-scatter.5.cloned.1.call-done) | copy-start | bytes 98308
Sparse Core Ops, SparseCore 0:
  16.9 58.4 reduce-scatter.2
  147.2 52.9 reduce-scatter.4
where the time goes:
time: 273 us; the launch traced here: 272 us
  waiting for transfers between devices  104 us (38%)
  blocking collectives  104 us (38%)
  matrix products  39.7 us (15%)
  between operations  20.6 us (8%)
    reduce_scatter x2, waiting for transfers between devices, body(): lax.psum_scatter(product(residual, user_factor), 'user', scatter_dimensio...  104 us
    psum x2, blocking collectives, body(): norm_total = lax.psum(own_norm, 'user')  61 us
    all_gather x2, blocking collectives, body(): grad_whole = lax.all_gather(grad_time, 'user', axis=0, tiled=True)  42.9 us
    dot_general x10, matrix products, product(): jnp.dot(left, right, precision=lax.Precision.HIGHEST, preferred_element_t...  39.7 us
  transfers between devices with their start and end apart: 2, of which 2 were waited for; matrix products, arithmetic and copies ran while one was open for 3% of the time, Pallas kernels for 0%

commit v1 on v0

--- a/solution.py
+++ b/solution.py
@@ -25,36 +25,77 @@
     return (residual, curvature)
 
 
-def body(counts, first_bin, time_factor, user_factor, user_base):
-    shard_rows = time_factor.shape[0] // lax.axis_size("user")
+def exchange(value, n, distance):
+    return lax.ppermute(value, "user", [(i, i ^ distance) for i in range(n)])
+
+
+def sum_over_users(partial, n):
+    if n == 1:
+        return partial
+    if n & (n - 1) or partial.shape[0] % n:
+        return lax.psum(partial, "user")
+    me = lax.axis_index("user")
+    distances = []
+    d = 1
+    while d < n:
+        distances.append(d)
+        d *= 2
+    block = partial
+    for d in distances:
+        half = block.shape[0] // 2
+        upper = (me // d) % 2
+        keep = lax.dynamic_slice_in_dim(block, upper * half, half, 0)
+        send = lax.dynamic_slice_in_dim(block, (1 - upper) * half, half, 0)
+        block = keep + exchange(send, n, d)
+    for d in reversed(distances):
+        other = exchange(block, n, d)
+        upper = (me // d) % 2
+        both = jnp.concatenate([block, other], axis=0)
+        swapped = jnp.concatenate([other, block], axis=0)
+        block = jnp.where(upper == 0, both, swapped)
+    return block
+
+
+def sum_scalars(values, n):
+    lanes = jnp.zeros((1, 128), jnp.float32)
+    for k, v in enumerate(values):
+        lanes = lanes.at[0, k].set(v)
+    if n == 1:
+        total = lanes[0]
+    else:
+        spread = jnp.broadcast_to(lanes[None], (n, 1, 128))
+        total = jnp.sum(lax.all_to_all(spread, "user", 0, 0, tiled=False), axis=(0, 1))
+    return [total[k] for k in range(len(values))]
+
+
+def body(n, counts, first_bin, time_factor, user_factor, user_base):
+    shard_rows = time_factor.shape[0] // n
     offset = lax.axis_index("user") * shard_rows
-    sweeps = SWEEPS
     mine_rows = time_factor
-    for sweep in range(sweeps):
+    for sweep in range(SWEEPS):
         residual, curvature = local_terms(time_factor, user_factor, user_base, counts, first_bin)
         grad_user = product(residual.T, time_factor)
-        grad_time = lax.psum_scatter(
-            product(residual, user_factor), "user", scatter_dimension=0, tiled=True
-        )
-        own_norm = jnp.sum(grad_time * grad_time) + jnp.sum(grad_user * grad_user)
-        norm_total = lax.psum(own_norm, "user")
-        grad_whole = lax.all_gather(grad_time, "user", axis=0, tiled=True)
+        grad_whole = sum_over_users(product(residual, user_factor), n)
+        user_norm = jnp.sum(grad_user * grad_user)
         tangent_image = product(grad_whole, user_factor.T) + product(time_factor, grad_user.T)
         bending = jnp.sum(curvature * tangent_image * tangent_image)
-        bend_total = lax.psum(bending, "user")
+        user_norm_total, bend_total = sum_scalars([user_norm, bending], n)
+        norm_total = jnp.sum(grad_whole * grad_whole) + user_norm_total
         relax_step = norm_total / (bend_total + damping * norm_total)
         user_factor = user_factor - relax_step * grad_user
-        mine_rows = (
-            lax.dynamic_slice_in_dim(time_factor, offset, shard_rows, 0) - relax_step * grad_time
-        )
-        if sweep + 1 < sweeps:
+        if sweep + 1 < SWEEPS:
             time_factor = time_factor - relax_step * grad_whole
+        else:
+            mine_rows = lax.dynamic_slice_in_dim(
+                time_factor - relax_step * grad_whole, offset, shard_rows, 0
+            )
     return (mine_rows, user_factor)
 
 
 def solution(mesh):
+    n = mesh.shape["user"]
     return jax.shard_map(
-        body,
+        lambda *args: body(n, *args),
         mesh=mesh,
         in_specs=(
             P(None, ("parts", "user")),

time: 273 us -> 140 us (0.51)
  blocking collectives: 104 us -> 0 us
  waiting for transfers between devices: 104 us -> 49 us
  starting transfers between devices: 0.08 us -> 27.2 us
  between operations: 20.6 us -> 7.54 us
  other arithmetic: 2.65 us -> 10.3 us
  local copies, waits for them, and re-layouts: 1.51 us -> 7.18 us
    reduce_scatter x2 -> x0, waiting for transfers between devices: 104 us -> none  [body(): lax.psum_scatter(product(residual, user_factor), 'user', scatter_dimensio...]
    psum x2 -> x0, blocking collectives: 61 us -> none  [body(): norm_total = lax.psum(own_norm, 'user')]
    all_gather x2 -> x0, blocking collectives: 42.9 us -> none  [body(): grad_whole = lax.all_gather(grad_time, 'user', axis=0, tiled=True)]
    ppermute x0 -> x16, waiting for transfers between devices: none -> 37.3 us  [exchange(): return lax.ppermute(value, 'user', [(i, i ^ distance) for i in range(n)])]
    ppermute x0 -> x16, starting transfers between devices: none -> 18.2 us  [exchange(): return lax.ppermute(value, 'user', [(i, i ^ distance) for i in range(n)])]
    all_to_all x0 -> x2, waiting for transfers between devices: none -> 11.7 us  [sum_scalars(): lax.all_to_all(spread, 'user', 0, 0, tiled=False)]
    all_to_all x0 -> x2, starting transfers between devices: none -> 9.03 us  [sum_scalars(): lax.all_to_all(spread, 'user', 0, 0, tiled=False)]
    another operation x0 -> x4, other arithmetic: none -> 6.09 us
  transfers between devices with their start and end apart: 2 -> 18, of which waited for: 2 -> 14; matrix products, arithmetic and copies ran while one was open for 3% -> 10% of each run, Pallas kernels for 0% -> 0%
where the time goes in v1:
time: 140 us; the launch traced here: 139 us
  waiting for transfers between devices  49 us (35%)
  matrix products  38.3 us (27%)
  starting transfers between devices  27.2 us (19%)
  other arithmetic  10.3 us (7%)
  between operations  7.54 us (5%)
  local copies, waits for them, and re-layouts  7.18 us (5%)
    dot_general x10, matrix products, product(): jnp.dot(left, right, precision=lax.Precision.HIGHEST, preferred_element_t...  38.3 us
    ppermute x16, waiting for transfers between devices, exchange(): return lax.ppermute(value, 'user', [(i, i ^ distance) for i in range(n)])  37.3 us
    ppermute x16, starting transfers between devices, exchange(): return lax.ppermute(value, 'user', [(i, i ^ distance) for i in range(n)])  18.2 us
    all_to_all x2, waiting for transfers between devices, sum_scalars(): lax.all_to_all(spread, 'user', 0, 0, tiled=False)  11.7 us
    all_to_all x2, starting transfers between devices, sum_scalars(): lax.all_to_all(spread, 'user', 0, 0, tiled=False)  9.03 us
    another operation x4, other arithmetic  6.09 us
  transfers between devices with their start and end apart: 18, of which 14 were waited for; matrix products, arithmetic and copies ran while one was open for 10% of the time, Pallas kernels for 0%

profile of v1, /device:TPU:0, one launch (start us, length us, event | category | flops | bytes accessed | tf_op | source)
XLA Modules:
  0.0 139.5 jit_solution(6255286143477615936)
XLA Ops:
  0.6 0.0 copy-start.1
  0.7 6.9 %select_multiply_fusion.3 = (f32[1024,512]{1,0:T(8,128)S(1)}, f32[1024,512]{1,0:T(8,128)}) fusion(s32[1024,512]{1,0:T(8,128)} %param.13, s32[512]{0:T(512)} %param.14, f32[512]{0:T(512)} %param.17, f32[1024,128]{1,0:T(8,128)} %param.15, f32[512,128]{1,0:T(8,128)} %param.16), kind=kOutput, calls=%fused_computation.7 | convolution fusion | flops 814219264 | bytes 7081984 | tf_op jit(solution)/shard_map/dot_general | solution.py:14
  7.6 1.8 %fusion.11 = f32[1024,128]{1,0:T(8,128)S(1)} fusion(f32[1024,512]{1,0:T(8,128)S(1)} %get-tuple-element.56, f32[512,128]{1,0:T(8,128)S(1)} %copy-done.1), kind=kOutput, calls=%fused_computation.65 | convolution fusion | flops 805306368 | bytes 2883584 | tf_op jit(solution)/shard_map/dot_general | solution.py:14
  9.4 0.0 copy-start
  9.4 0.5 collective-permute-start
  9.9 1.3 collective-permute-done
  11.2 1.0 dynamic-slice_add_fusion.1
  12.2 2.9 %collective-permute-start.1 = (f32[256,128]{1,0:T(8,128)S(1)}, f32[256,128]{1,0:T(8,128)S(1)}, u32[]{:S(2)}, u32[]{:S(2)}) collective-permute-start(f32[256,128]{1,0:T(8,128)S(1)} %constant_dynamic-slice_fusion.8), channel_id=1, source_target_pairs={{0,2},{1,3},{2,0},{3,1},{4,6},{5,7},{6,4},{7,5},{8,10},{9,11},{10,... | collective-permute-start | bytes 393224 | tf_op jit(solution)/shard_map/ppermute | solution.py:29
  15.2 3.8 %collective-permute-done.1 = f32[256,128]{1,0:T(8,128)S(1)} collective-permute-done((f32[256,128]{1,0:T(8,128)S(1)}, f32[256,128]{1,0:T(8,128)S(1)}, u32[]{:S(2)}, u32[]{:S(2)}) %collective-permute-start.1) | collective-permute-done | bytes 131104 | tf_op jit(solution)/shard_map/ppermute | solution.py:29
  19.0 1.9 %collective-permute-start.2 = (f32[128,128]{1,0:T(8,128)S(1)}, f32[128,128]{1,0:T(8,128)S(1)}, u32[]{:S(2)}, u32[]{:S(2)}) collective-permute-start(f32[128,128]{1,0:T(8,128)S(1)} %constant_dynamic-slice_fusion.7), channel_id=1, source_target_pairs={{0,4},{1,5},{2,6},{3,7},{4,0},{5,1},{6,2},{7,3},{8,12},{9,13},{10,... | collective-permute-start | bytes 196616 | tf_op jit(solution)/shard_map/ppermute | solution.py:29
  20.9 2.4 %collective-permute-done.2 = f32[128,128]{1,0:T(8,128)S(1)} collective-permute-done((f32[128,128]{1,0:T(8,128)S(1)}, f32[128,128]{1,0:T(8,128)S(1)}, u32[]{:S(2)}, u32[]{:S(2)}) %collective-permute-start.2) | collective-permute-done | bytes 65568 | tf_op jit(solution)/shard_map/ppermute | solution.py:29
  23.4 2.9 %collective-permute-start.3 = (f32[64,128]{1,0:T(8,128)S(1)}, f32[64,128]{1,0:T(8,128)S(1)}, u32[]{:S(2)}, u32[]{:S(2)}) collective-permute-start(f32[64,128]{1,0:T(8,128)S(1)} %constant_dynamic-slice_fusion.6), channel_id=1, source_target_pairs={{0,8},{1,9},{2,10},{3,11},{4,12},{5,13},{6,14},{7,15},{8,0},{9,1},... | collective-permute-start | bytes 98312 | tf_op jit(solution)/shard_map/ppermute | solution.py:29
  26.3 2.0 %collective-permute-done.3 = f32[64,128]{1,0:T(8,128)S(1)} collective-permute-done((f32[64,128]{1,0:T(8,128)S(1)}, f32[64,128]{1,0:T(8,128)S(1)}, u32[]{:S(2)}, u32[]{:S(2)}) %collective-permute-start.3) | collective-permute-done | bytes 32800 | tf_op jit(solution)/shard_map/ppermute | solution.py:29
  28.2 2.9 %collective-permute-start.4 = (f32[64,128]{1,0:T(8,128)S(1)}, f32[64,128]{1,0:T(8,128)S(1)}, u32[]{:S(2)}, u32[]{:S(2)}) collective-permute-start(f32[64,128]{1,0:T(8,128)S(1)} %dynamic-slice_add_fusion.7), channel_id=1, source_target_pairs={{0,8},{1,9},{2,10},{3,11},{4,12},{5,13},{6,14},{7,15},{8,0},{9,1},... | collective-permute-start | bytes 98312 | tf_op jit(solution)/shard_map/ppermute | solution.py:29
  31.1 2.1 %collective-permute-done.4 = f32[64,128]{1,0:T(8,128)S(1)} collective-permute-done((f32[64,128]{1,0:T(8,128)S(1)}, f32[64,128]{1,0:T(8,128)S(1)}, u32[]{:S(2)}, u32[]{:S(2)}) %collective-permute-start.4) | collective-permute-done | bytes 32800 | tf_op jit(solution)/shard_map/ppermute | solution.py:29
  33.2 2.2 %collective-permute-start.5 = (f32[128,128]{1,0:T(8,128)S(1)}, f32[128,128]{1,0:T(8,128)S(1)}, u32[]{:S(2)}, u32[]{:S(2)}) collective-permute-start(f32[128,128]{1,0:T(8,128)S(1)} %maximum_select_fusion.7), channel_id=1, source_target_pairs={{0,4},{1,5},{2,6},{3,7},{4,0},{5,1},{6,2},{7,3},{8,12},{9,13},{10,... | collective-permute-start | bytes 196616 | tf_op jit(solution)/shard_map/ppermute | solution.py:29
  35.4 2.2 %collective-permute-done.5 = f32[128,128]{1,0:T(8,128)S(1)} collective-permute-done((f32[128,128]{1,0:T(8,128)S(1)}, f32[128,128]{1,0:T(8,128)S(1)}, u32[]{:S(2)}, u32[]{:S(2)}) %collective-permute-start.5) | collective-permute-done | bytes 65568 | tf_op jit(solution)/shard_map/ppermute | solution.py:29
  37.7 1.6 %collective-permute-start.6 = (f32[256,128]{1,0:T(8,128)S(1)}, f32[256,128]{1,0:T(8,128)S(1)}, u32[]{:S(2)}, u32[]{:S(2)}) collective-permute-start(f32[256,128]{1,0:T(8,128)S(1)} %maximum_select_fusion.4), channel_id=1, source_target_pairs={{0,2},{1,3},{2,0},{3,1},{4,6},{5,7},{6,4},{7,5},{8,10},{9,11},{10,... | collective-permute-start | bytes 393224 | tf_op jit(solution)/shard_map/ppermute | solution.py:29
  39.2 4.0 %multiply_reduce_fusion.3 = (f32[]{:T(128)}, f32[512,128]{1,0:T(8,128)S(1)}) fusion(f32[1024,512]{1,0:T(8,128)S(1)} %get-tuple-element.56, f32[1024,128]{1,0:T(8,128)S(1)} %copy-done), kind=kOutput, calls=%fused_computation.29 | convolution fusion | flops 805437440 | bytes 2883588 | tf_op jit(solution)/shard_map/dot_general | solution.py:14
  43.3 0.6 slice.79
  43.9 0.7 compare_reduce_fusion.1
  45.9 0.6 compare_reduce_fusion
  46.5 0.0 collective-permute-done.6
  46.6 0.1 collective-permute-start.7
  46.6 1.8 %fusion.12 = f32[512,1024]{0,1:T(8,128)S(1)} fusion(f32[512,128]{1,0:T(8,128)S(1)} %get-tuple-element.59, f32[1024,128]{1,0:T(8,128)S(1)} %copy-done), kind=kOutput, calls=%fused_computation.66 | convolution fusion | flops 805306368 | bytes 2883584 | tf_op jit(solution)/shard_map/dot_general | solution.py:14
  48.5 6.2 %fusion.4 = f32[]{:T(128)} fusion(f32[512,1024]{0,1:T(8,128)S(1)} %fusion.12, f32[512,128]{1,0:T(8,128)S(1)} %copy-done.2, s32[512]{0:T(512)S(1)} %copy-done.4, f32[1024,512]{1,0:T(8,128)} %get-tuple-element.57, f32[512]{0:T(512)S(1)} %copy-done.5, f32[512,128]{1,0:T(8,128)S(1)} %collective-permute-done.7, f32[512,128]{1,0:T(8,128)S(1)} %maximum_select_fusion.2, ...), kind=kOutput, calls=%fused_computation.16 | convolution fusion | flops 815661056 | bytes 4984837 | tf_op jit(solution)/shard_map/dot_general | solution.py:14
  54.7 2.4 %fusion.9 = f32[1,1]{1,0:T(1,128)} fusion(pred[1,1]{1,0:T(4,128)(4,1)} %bitcast.2, f32[1,1]{1,0:T(1,128)} %bitcast.4, s32[]{:T(128)} %bitcast.5, f32[1,1]{1,0:T(1,128)} %bitcast), kind=kLoop, calls=%fused_computation.63 | loop fusion | flops 1 | bytes 17 | tf_op jit(solution)/shard_map/select.5
  57.1 1.3 bitcast_dynamic-update-slice_fusion.1
  58.4 0.6 broadcast_in_dim.28
  59.0 5.6 %all-to-all-start = ((f32[16,1,128]{2,1,0:T(1,128)}), f32[16,1,128]{2,1,0:T(1,128)S(1)}, u32[]{:S(2)}, u32[]{:S(2)}) async-start(f32[16,1,128]{2,1,0:T(1,128)} %broadcast_in_dim.28), calls=%async_computation | async-start | bytes 16384 | tf_op jit(solution)/shard_map/all_to_all | solution.py:67
  64.6 0.7 multiply_reduce_fusion.1
  65.4 5.4 %all-to-all-done = f32[16,1,128]{2,1,0:T(1,128)S(1)} async-done(((f32[16,1,128]{2,1,0:T(1,128)}), f32[16,1,128]{2,1,0:T(1,128)S(1)}, u32[]{:S(2)}, u32[]{:S(2)}) %all-to-all-start) | async-done | bytes 8224 | tf_op jit(solution)/shard_map/all_to_all | solution.py:67
  70.7 0.6 fusion.8
  73.3 0.0 copy-start.3
  73.3 0.1 multiply_subtract_fusion
  73.4 1.5 %copy-done.3 = s32[1024,512]{1,0:T(8,128)S(1)} copy-done((s32[1024,512]{1,0:T(8,128)S(1)}, s32[1024,512]{1,0:T(8,128)}, u32[]{:S(2)}) %copy-start.3) | copy-done | bytes 2097176
  74.9 5.0 %select_multiply_fusion.1 = (f32[1024,512]{1,0:T(8,128)S(1)}, f32[1024,512]{1,0:T(8,128)}) fusion(s32[1024,512]{1,0:T(8,128)S(1)} %copy-done.3, s32[512]{0:T(512)S(1)} %copy-done.4, f32[512]{0:T(512)S(1)} %copy-done.5, f32[1024,128]{1,0:T(8,128)S(1)} %multiply_subtract_fusion, f32[512,128]{1,0:T(8,128)S(1)} %multiply_subtract_fusion.2), kind=kOutput, calls=%fused_computation.5 | convolution fusion | flops 814219264 | bytes 7081984 | tf_op jit(solution)/shard_map/dot_general | solution.py:14
  79.9 1.8 %fusion.13 = f32[1024,128]{1,0:T(8,128)S(1)} fusion(f32[1024,512]{1,0:T(8,128)S(1)} %get-tuple-element.60, f32[512,128]{1,0:T(8,128)S(1)} %multiply_subtract_fusion.2), kind=kOutput, calls=%fused_computation.67 | convolution fusion | flops 805306368 | bytes 2883584 | tf_op jit(solution)/shard_map/dot_general | solution.py:14
  81.7 0.1 collective-permute-start.8
  81.8 1.5 %collective-permute-done.8 = f32[512,128]{1,0:T(8,128)S(1)} collective-permute-done((f32[512,128]{1,0:T(8,128)S(1)}, f32[512,128]{1,0:T(8,128)S(1)}, u32[]{:S(2)}, u32[]{:S(2)}) %collective-permute-start.8) | collective-permute-done | bytes 262176 | tf_op jit(solution)/shard_map/ppermute | solution.py:29
  83.4 0.6 collective-permute-start.9
  84.0 5.0 %collective-permute-done.9 = f32[256,128]{1,0:T(8,128)S(1)} collective-permute-done((f32[256,128]{1,0:T(8,128)S(1)}, f32[256,128]{1,0:T(8,128)S(1)}, u32[]{:S(2)}, u32[]{:S(2)}) %collective-permute-start.9) | collective-permute-done | bytes 131104 | tf_op jit(solution)/shard_map/ppermute | solution.py:29
  89.0 0.6 collective-permute-start.10
  89.6 3.8 %collective-permute-done.10 = f32[128,128]{1,0:T(8,128)S(1)} collective-permute-done((f32[128,128]{1,0:T(8,128)S(1)}, f32[128,128]{1,0:T(8,128)S(1)}, u32[]{:S(2)}, u32[]{:S(2)}) %collective-permute-start.10) | collective-permute-done | bytes 65568 | tf_op jit(solution)/shard_map/ppermute | solution.py:29
  93.4 0.6 collective-permute-start.11
  94.0 4.6 %collective-permute-done.11 = f32[64,128]{1,0:T(8,128)S(1)} collective-permute-done((f32[64,128]{1,0:T(8,128)S(1)}, f32[64,128]{1,0:T(8,128)S(1)}, u32[]{:S(2)}, u32[]{:S(2)}) %collective-permute-start.11) | collective-permute-done | bytes 32800 | tf_op jit(solution)/shard_map/ppermute | solution.py:29
  98.6 0.3 collective-permute-start.12
  98.9 4.5 %collective-permute-done.12 = f32[64,128]{1,0:T(8,128)S(1)} collective-permute-done((f32[64,128]{1,0:T(8,128)S(1)}, f32[64,128]{1,0:T(8,128)S(1)}, u32[]{:S(2)}, u32[]{:S(2)}) %collective-permute-start.12) | collective-permute-done | bytes 32800 | tf_op jit(solution)/shard_map/ppermute | solution.py:29
  103.4 0.3 collective-permute-start.13
  103.7 4.1 %collective-permute-done.13 = f32[128,128]{1,0:T(8,128)S(1)} collective-permute-done((f32[128,128]{1,0:T(8,128)S(1)}, f32[128,128]{1,0:T(8,128)S(1)}, u32[]{:S(2)}, u32[]{:S(2)}) %collective-permute-start.13) | collective-permute-done | bytes 65568 | tf_op jit(solution)/shard_map/ppermute | solution.py:29
  107.8 0.7 collective-permute-start.14
  108.5 4.1 %multiply_reduce_fusion.2 = (f32[]{:T(128)}, f32[512,128]{1,0:T(8,128)S(1)}) fusion(f32[1024,512]{1,0:T(8,128)S(1)} %get-tuple-element.60, f32[1024,128]{1,0:T(8,128)S(1)} %multiply_subtract_fusion), kind=kOutput, calls=%fused_computation.26 | convolution fusion | flops 805437440 | bytes 2883588 | tf_op jit(solution)/shard_map/dot_general | solution.py:14
  114.0 0.1 collective-permute-start.15
  114.1 1.8 %fusion.14 = f32[1024,512]{1,0:T(8,128)S(1)} fusion(f32[1024,128]{1,0:T(8,128)S(1)} %multiply_subtract_fusion, f32[512,128]{1,0:T(8,128)S(1)} %get-tuple-element.63), kind=kOutput, calls=%fused_computation.68 | convolution fusion | flops 805306368 | bytes 2883584 | tf_op jit(solution)/shard_map/dot_general | solution.py:14
  115.9 0.7 multiply_reduce_fusion
  116.6 4.9 %fusion.5 = f32[]{:T(128)} fusion(f32[1024,512]{1,0:T(8,128)S(1)} %fusion.14, f32[1024,128]{1,0:T(8,128)S(1)} %get-tuple-element.51, f32[512,128]{1,0:T(8,128)S(1)} %multiply_subtract_fusion.2, s32[512]{0:T(512)S(1)} %copy-done.4, f32[1024,512]{1,0:T(8,128)S(1)} %copy-done.6, f32[512]{0:T(512)S(1)} %copy-done.5), kind=kOutput, calls=%fused_computation.17 | convolution fusion | flops 815267840 | bytes 4984836 | tf_op jit(solution)/shard_map/dot_general | solution.py:14
  121.5 2.3 %fusion.10 = f32[1,1]{1,0:T(1,128)} fusion(pred[1,1]{1,0:T(4,128)(4,1)} %bitcast.2, f32[1,1]{1,0:T(1,128)} %bitcast.12, s32[]{:T(128)} %bitcast.5, f32[1,1]{1,0:T(1,128)} %bitcast.10), kind=kLoop, calls=%fused_computation.64 | loop fusion | flops 1 | bytes 17 | tf_op jit(solution)/shard_map/select.7
  123.9 1.3 bitcast_dynamic-update-slice_fusion
  125.1 0.6 broadcast_in_dim.31
  125.8 3.5 %all-to-all-start.1 = ((f32[16,1,128]{2,1,0:T(1,128)}), f32[16,1,128]{2,1,0:T(1,128)S(1)}, u32[]{:S(2)}, u32[]{:S(2)}) async-start(f32[16,1,128]{2,1,0:T(1,128)} %broadcast_in_dim.31), calls=%async_computation.1 | async-start | bytes 16384 | tf_op jit(solution)/shard_map/all_to_all | solution.py:67
  129.2 6.3 %all-to-all-done.1 = f32[16,1,128]{2,1,0:T(1,128)S(1)} async-done(((f32[16,1,128]{2,1,0:T(1,128)}), f32[16,1,128]{2,1,0:T(1,128)S(1)}, u32[]{:S(2)}, u32[]{:S(2)}) %all-to-all-start.1) | async-done | bytes 8224 | tf_op jit(solution)/shard_map/all_to_all | solution.py:67
  135.5 0.6 fusion.7
  138.1 0.7 multiply_subtract_fusion.1
  138.8 0.6 dynamic-slice_subtract_fusion
  (40 shorter events, 0.4 us)
Async XLA Ops:
  0.6 6.9 %copy-start.1 = (f32[512,128]{1,0:T(8,128)S(1)}, f32[512,128]{1,0:T(8,128)}, u32[]{:S(2)}) copy-start(f32[512,128]{1,0:T(8,128)} %param.16) | copy-start | bytes 786436
  9.4 29.9 %copy-start = (f32[1024,128]{1,0:T(8,128)S(1)}, f32[1024,128]{1,0:T(8,128)}, u32[]{:S(2)}) copy-start(f32[1024,128]{1,0:T(8,128)} %param.15) | copy-start | bytes 1572868
  9.4 1.8 %collective-permute-start = (f32[512,128]{1,0:T(8,128)S(1)}, f32[512,128]{1,0:T(8,128)}, u32[]{:S(2)}, u32[]{:S(2)}) collective-permute-start(f32[512,128]{1,0:T(8,128)S(1)} %constant_dynamic-slice_fusion.9), channel_id=1, source_target_pairs={{0,1},{1,0},{2,3},{3,2},{4,5},{5,4},{6,7},{7,6},{8,9},{9,8},{10,11... | collective-permute-start | bytes 786440 | tf_op jit(solution)/shard_map/ppermute | solution.py:29
  12.2 6.7 %collective-permute-start.1 = (f32[256,128]{1,0:T(8,128)S(1)}, f32[256,128]{1,0:T(8,128)S(1)}, u32[]{:S(2)}, u32[]{:S(2)}) collective-permute-start(f32[256,128]{1,0:T(8,128)S(1)} %constant_dynamic-slice_fusion.8), channel_id=1, source_target_pairs={{0,2},{1,3},{2,0},{3,1},{4,6},{5,7},{6,4},{7,5},{8,10},{9,11},{10,... | collective-permute-start | bytes 393224 | tf_op jit(solution)/shard_map/ppermute | solution.py:29
  19.0 4.3 %collective-permute-start.2 = (f32[128,128]{1,0:T(8,128)S(1)}, f32[128,128]{1,0:T(8,128)S(1)}, u32[]{:S(2)}, u32[]{:S(2)}) collective-permute-start(f32[128,128]{1,0:T(8,128)S(1)} %constant_dynamic-slice_fusion.7), channel_id=1, source_target_pairs={{0,4},{1,5},{2,6},{3,7},{4,0},{5,1},{6,2},{7,3},{8,12},{9,13},{10,... | collective-permute-start | bytes 196616 | tf_op jit(solution)/shard_map/ppermute | solution.py:29
  23.4 4.9 %collective-permute-start.3 = (f32[64,128]{1,0:T(8,128)S(1)}, f32[64,128]{1,0:T(8,128)S(1)}, u32[]{:S(2)}, u32[]{:S(2)}) collective-permute-start(f32[64,128]{1,0:T(8,128)S(1)} %constant_dynamic-slice_fusion.6), channel_id=1, source_target_pairs={{0,8},{1,9},{2,10},{3,11},{4,12},{5,13},{6,14},{7,15},{8,0},{9,1},... | collective-permute-start | bytes 98312 | tf_op jit(solution)/shard_map/ppermute | solution.py:29
  28.2 4.9 %collective-permute-start.4 = (f32[64,128]{1,0:T(8,128)S(1)}, f32[64,128]{1,0:T(8,128)S(1)}, u32[]{:S(2)}, u32[]{:S(2)}) collective-permute-start(f32[64,128]{1,0:T(8,128)S(1)} %dynamic-slice_add_fusion.7), channel_id=1, source_target_pairs={{0,8},{1,9},{2,10},{3,11},{4,12},{5,13},{6,14},{7,15},{8,0},{9,1},... | collective-permute-start | bytes 98312 | tf_op jit(solution)/shard_map/ppermute | solution.py:29
  33.2 4.5 %collective-permute-start.5 = (f32[128,128]{1,0:T(8,128)S(1)}, f32[128,128]{1,0:T(8,128)S(1)}, u32[]{:S(2)}, u32[]{:S(2)}) collective-permute-start(f32[128,128]{1,0:T(8,128)S(1)} %maximum_select_fusion.7), channel_id=1, source_target_pairs={{0,4},{1,5},{2,6},{3,7},{4,0},{5,1},{6,2},{7,3},{8,12},{9,13},{10,... | collective-permute-start | bytes 196616 | tf_op jit(solution)/shard_map/ppermute | solution.py:29
  37.7 8.9 %collective-permute-start.6 = (f32[256,128]{1,0:T(8,128)S(1)}, f32[256,128]{1,0:T(8,128)S(1)}, u32[]{:S(2)}, u32[]{:S(2)}) collective-permute-start(f32[256,128]{1,0:T(8,128)S(1)} %maximum_select_fusion.4), channel_id=1, source_target_pairs={{0,2},{1,3},{2,0},{3,1},{4,6},{5,7},{6,4},{7,5},{8,10},{9,11},{10,... | collective-permute-start | bytes 393224 | tf_op jit(solution)/shard_map/ppermute | solution.py:29
  43.2 5.2 %copy-start.2 = (f32[512,128]{1,0:T(8,128)S(1)}, f32[512,128]{1,0:T(8,128)}, u32[]{:S(2)}) copy-start(f32[512,128]{1,0:T(8,128)} %param.16) | copy-start | bytes 786436
  43.2 5.2 %copy-start.4 = (s32[512]{0:T(512)S(1)}, s32[512]{0:T(512)}, u32[]{:S(2)}) copy-start(s32[512]{0:T(512)} %param.14) | copy-start | bytes 6148
  43.3 5.2 %copy-start.5 = (f32[512]{0:T(512)S(1)}, f32[512]{0:T(512)}, u32[]{:S(2)}) copy-start(f32[512]{0:T(512)} %param.17) | copy-start | bytes 6148
  46.6 1.9 %collective-permute-start.7 = (f32[512,128]{1,0:T(8,128)S(1)}, f32[512,128]{1,0:T(8,128)S(1)}, u32[]{:S(2)}, u32[]{:S(2)}) collective-permute-start(f32[512,128]{1,0:T(8,128)S(1)} %maximum_select_fusion.2), channel_id=1, source_target_pairs={{0,1},{1,0},{2,3},{3,2},{4,5},{5,4},{6,7},{7,6},{8,9},{9,8},{10,11... | collective-permute-start | bytes 786440 | tf_op jit(solution)/shard_map/ppermute | solution.py:29
  59.0 11.7 %all-to-all-start = ((f32[16,1,128]{2,1,0:T(1,128)}), f32[16,1,128]{2,1,0:T(1,128)S(1)}, u32[]{:S(2)}, u32[]{:S(2)}) async-start(f32[16,1,128]{2,1,0:T(1,128)} %broadcast_in_dim.28), calls=%async_computation | async-start | bytes 16384 | tf_op jit(solution)/shard_map/all_to_all | solution.py:67
  73.3 1.6 %copy-start.3 = (s32[1024,512]{1,0:T(8,128)S(1)}, s32[1024,512]{1,0:T(8,128)}, u32[]{:S(2)}) copy-start(s32[1024,512]{1,0:T(8,128)} %param.13) | copy-start | bytes 6291460
  81.7 1.6 %collective-permute-start.8 = (f32[512,128]{1,0:T(8,128)S(1)}, f32[512,128]{1,0:T(8,128)S(1)}, u32[]{:S(2)}, u32[]{:S(2)}) collective-permute-start(f32[512,128]{1,0:T(8,128)S(1)} %constant_dynamic-slice_fusion.4), channel_id=1, source_target_pairs={{0,1},{1,0},{2,3},{3,2},{4,5},{5,4},{6,7},{7,6},{8,9},{9,8},{10,11... | collective-permute-start | bytes 786440 | tf_op jit(solution)/shard_map/ppermute | solution.py:29
  83.4 5.6 %collective-permute-start.9 = (f32[256,128]{1,0:T(8,128)S(1)}, f32[256,128]{1,0:T(8,128)S(1)}, u32[]{:S(2)}, u32[]{:S(2)}) collective-permute-start(f32[256,128]{1,0:T(8,128)S(1)} %constant_dynamic-slice_fusion.3), channel_id=1, source_target_pairs={{0,2},{1,3},{2,0},{3,1},{4,6},{5,7},{6,4},{7,5},{8,10},{9,11},{10,... | collective-permute-start | bytes 393224 | tf_op jit(solution)/shard_map/ppermute | solution.py:29
  89.0 4.3 %collective-permute-start.10 = (f32[128,128]{1,0:T(8,128)S(1)}, f32[128,128]{1,0:T(8,128)S(1)}, u32[]{:S(2)}, u32[]{:S(2)}) collective-permute-start(f32[128,128]{1,0:T(8,128)S(1)} %constant_dynamic-slice_fusion.2), channel_id=1, source_target_pairs={{0,4},{1,5},{2,6},{3,7},{4,0},{5,1},{6,2},{7,3},{8,12},{9,13},{10,... | collective-permute-start | bytes 196616 | tf_op jit(solution)/shard_map/ppermute | solution.py:29
  93.4 5.2 %collective-permute-start.11 = (f32[64,128]{1,0:T(8,128)S(1)}, f32[64,128]{1,0:T(8,128)S(1)}, u32[]{:S(2)}, u32[]{:S(2)}) collective-permute-start(f32[64,128]{1,0:T(8,128)S(1)} %constant_dynamic-slice_fusion.1), channel_id=1, source_target_pairs={{0,8},{1,9},{2,10},{3,11},{4,12},{5,13},{6,14},{7,15},{8,0},{9,1},... | collective-permute-start | bytes 98312 | tf_op jit(solution)/shard_map/ppermute | solution.py:29
  98.6 4.8 %collective-permute-start.12 = (f32[64,128]{1,0:T(8,128)S(1)}, f32[64,128]{1,0:T(8,128)S(1)}, u32[]{:S(2)}, u32[]{:S(2)}) collective-permute-start(f32[64,128]{1,0:T(8,128)S(1)} %dynamic-slice_add_fusion.6), channel_id=1, source_target_pairs={{0,8},{1,9},{2,10},{3,11},{4,12},{5,13},{6,14},{7,15},{8,0},{9,1},... | collective-permute-start | bytes 98312 | tf_op jit(solution)/shard_map/ppermute | solution.py:29
  103.4 4.3 %collective-permute-start.13 = (f32[128,128]{1,0:T(8,128)S(1)}, f32[128,128]{1,0:T(8,128)S(1)}, u32[]{:S(2)}, u32[]{:S(2)}) collective-permute-start(f32[128,128]{1,0:T(8,128)S(1)} %maximum_select_fusion.8), channel_id=1, source_target_pairs={{0,4},{1,5},{2,6},{3,7},{4,0},{5,1},{6,2},{7,3},{8,12},{9,13},{10,... | collective-permute-start | bytes 196616 | tf_op jit(solution)/shard_map/ppermute | solution.py:29
  107.8 6.1 %collective-permute-start.14 = (f32[256,128]{1,0:T(8,128)S(1)}, f32[256,128]{1,0:T(8,128)S(1)}, u32[]{:S(2)}, u32[]{:S(2)}) collective-permute-start(f32[256,128]{1,0:T(8,128)S(1)} %maximum_select_fusion.5), channel_id=1, source_target_pairs={{0,2},{1,3},{2,0},{3,1},{4,6},{5,7},{6,4},{7,5},{8,10},{9,11},{10,... | collective-permute-start | bytes 393224 | tf_op jit(solution)/shard_map/ppermute | solution.py:29
  114.0 2.6 %copy-start.6 = (f32[1024,512]{1,0:T(8,128)S(1)}, f32[1024,512]{1,0:T(8,128)}, u32[]{:S(2)}) copy-start(f32[1024,512]{1,0:T(8,128)} %get-tuple-element.61) | copy-start | bytes 6291460
  114.0 1.9 %collective-permute-start.15 = (f32[512,128]{1,0:T(8,128)S(1)}, f32[512,128]{1,0:T(8,128)S(1)}, u32[]{:S(2)}, u32[]{:S(2)}) collective-permute-start(f32[512,128]{1,0:T(8,128)S(1)} %maximum_select_fusion.3), channel_id=1, source_target_pairs={{0,1},{1,0},{2,3},{3,2},{4,5},{5,4},{6,7},{7,6},{8,9},{9,8},{10,11... | collective-permute-start | bytes 786440 | tf_op jit(solution)/shard_map/ppermute | solution.py:29
  125.8 9.8 %all-to-all-start.1 = ((f32[16,1,128]{2,1,0:T(1,128)}), f32[16,1,128]{2,1,0:T(1,128)S(1)}, u32[]{:S(2)}, u32[]{:S(2)}) async-start(f32[16,1,128]{2,1,0:T(1,128)} %broadcast_in_dim.31), calls=%async_computation.1 | async-start | bytes 16384 | tf_op jit(solution)/shard_map/all_to_all | solution.py:67

commit v2 on v1

--- a/solution.py
+++ b/solution.py
@@ -17,11 +17,13 @@
 def local_terms(time_factor, user_block, base_block, count_block, start_block):
     linear = product(time_factor, user_block.T) + base_block[None, :]
     time_bins = jnp.arange(time_factor.shape[0], dtype=jnp.int32)[:, None]
-    observed = (time_bins >= start_block[None, :]).astype(jnp.float32)
-    intensity = jax.nn.softplus(linear) + background
-    gate_value = jax.nn.sigmoid(linear)
-    residual = observed * gate_value * (1.0 - count_block.astype(jnp.float32) / intensity)
-    curvature = observed * gate_value * gate_value / intensity
+    observed = time_bins >= start_block[None, :]
+    decay = jnp.exp(-jnp.abs(linear))
+    intensity = jnp.maximum(linear, 0.0) + jnp.log1p(decay) + background
+    gate_value = jnp.where(linear >= 0, 1.0, decay) / (1.0 + decay)
+    inverse = 1.0 / intensity
+    residual = jnp.where(observed, gate_value * (1.0 - count_block.astype(jnp.float32) * inverse), 0.0)
+    curvature = jnp.where(observed, gate_value * gate_value * inverse, 0.0)
     return (residual, curvature)
 
 
@@ -57,14 +59,13 @@
 
 
 def sum_scalars(values, n):
-    lanes = jnp.zeros((1, 128), jnp.float32)
+    lane = lax.broadcasted_iota(jnp.int32, (n, 1, 128), 2)
+    spread = jnp.zeros((n, 1, 128), jnp.float32)
     for k, v in enumerate(values):
-        lanes = lanes.at[0, k].set(v)
-    if n == 1:
-        total = lanes[0]
-    else:
-        spread = jnp.broadcast_to(lanes[None], (n, 1, 128))
-        total = jnp.sum(lax.all_to_all(spread, "user", 0, 0, tiled=False), axis=(0, 1))
+        spread = jnp.where(lane == k, v, spread)
+    if n > 1:
+        spread = lax.all_to_all(spread, "user", 0, 0, tiled=False)
+    total = jnp.sum(spread, axis=(0, 1))
     return [total[k] for k in range(len(values))]
 
 

time: 140 us -> 129 us (0.921)
  local copies, waits for them, and re-layouts: 7.18 us -> 2.78 us
  between operations: 7.54 us -> 4.9 us
  other arithmetic: 10.3 us -> 7.93 us
  matrix products: 38.3 us -> 36.7 us
    another operation x4 -> x0, other arithmetic: 6.09 us -> none
    select_n x0 -> x4, other arithmetic: none -> 3.77 us  [sum_scalars(): spread = jnp.where(lane == k, v, spread)]
    scatter x2 -> x0, local copies, waits for them, and re-layouts: 2.57 us -> none  [sum_scalars(): lanes = lanes.at[0, k].set(v)]
    dot_general x10, matrix products: 38.3 us -> 36.7 us  [product(): jnp.dot(left, right, precision=lax.Precision.HIGHEST, preferred_element_t...]
  transfers between devices with their start and end apart: 18 -> 18, of which waited for: 14 -> 14; matrix products, arithmetic and copies ran while one was open for 10% -> 11% of each run, Pallas kernels for 0% -> 0%
where the time goes in v2:
time: 129 us
  waiting for transfers between devices  49.7 us (39%)
  matrix products  36.7 us (28%)
  starting transfers between devices  26.4 us (20%)
  other arithmetic  7.93 us (6%)
  between operations  4.9 us (4%)
  local copies, waits for them, and re-layouts  2.78 us (2%)
    ppermute x16, waiting for transfers between devices, exchange(): return lax.ppermute(value, 'user', [(i, i ^ distance) for i in range(n)])  37.9 us
    dot_general x10, matrix products, product(): jnp.dot(left, right, precision=lax.Precision.HIGHEST, preferred_element_t...  36.7 us
    ppermute x16, starting transfers between devices, exchange(): return lax.ppermute(value, 'user', [(i, i ^ distance) for i in range(n)])  18.1 us
    all_to_all x2, waiting for transfers between devices, sum_scalars(): spread = lax.all_to_all(spread, 'user', 0, 0, tiled=False)  11.9 us
    all_to_all x2, starting transfers between devices, sum_scalars(): spread = lax.all_to_all(spread, 'user', 0, 0, tiled=False)  8.29 us
    select_n x4, other arithmetic, sum_scalars(): spread = jnp.where(lane == k, v, spread)  3.77 us
  transfers between devices with their start and end apart: 18, of which 14 were waited for; matrix products, arithmetic and copies ran while one was open for 11% of the time, Pallas kernels for 0%

profile of v2, /device:TPU:0, one launch (start us, length us, event | category | flops | bytes accessed | tf_op | source)
XLA Modules:
  0.0 128.5 jit_solution(9073957709105356860)
XLA Ops:
  0.6 0.0 copy-start.1
  0.7 6.8 %multiply_select_fusion.1 = (f32[1024,512]{1,0:T(8,128)S(1)}, f32[1024,512]{1,0:T(8,128)}) fusion(s32[1024,512]{1,0:T(8,128)} %param.5, s32[512]{0:T(512)} %param.6, f32[512]{0:T(512)} %param.9, f32[1024,128]{1,0:T(8,128)} %param.7, f32[512,128]{1,0:T(8,128)} %param.8), kind=kOutput, calls=%fused_computation.9 | convolution fusion | flops 814219264 | bytes 7081984 | tf_op jit(solution)/shard_map/dot_general | solution.py:14
  7.4 0.0 copy-done.1
  7.4 1.8 %fusion.5 = f32[1024,128]{1,0:T(8,128)S(1)} fusion(f32[1024,512]{1,0:T(8,128)S(1)} %get-tuple-element.8, f32[512,128]{1,0:T(8,128)S(1)} %copy-done.1), kind=kOutput, calls=%fused_computation.55 | convolution fusion | flops 805306368 | bytes 2883584 | tf_op jit(solution)/shard_map/dot_general | solution.py:14
  9.2 0.0 copy-start
  9.3 0.5 collective-permute-start
  9.8 1.3 %collective-permute-done = f32[512,128]{1,0:T(8,128)} collective-permute-done((f32[512,128]{1,0:T(8,128)S(1)}, f32[512,128]{1,0:T(8,128)}, u32[]{:S(2)}, u32[]{:S(2)}) %collective-permute-start) | collective-permute-done | bytes 262176 | tf_op jit(solution)/shard_map/ppermute | solution.py:31
  11.1 1.0 dynamic-slice_add_fusion.1
  12.1 2.9 %collective-permute-start.1 = (f32[256,128]{1,0:T(8,128)S(1)}, f32[256,128]{1,0:T(8,128)S(1)}, u32[]{:S(2)}, u32[]{:S(2)}) collective-permute-start(f32[256,128]{1,0:T(8,128)S(1)} %constant_dynamic-slice_fusion.6), channel_id=1, source_target_pairs={{0,2},{1,3},{2,0},{3,1},{4,6},{5,7},{6,4},{7,5},{8,10},{9,11},{10,... | collective-permute-start | bytes 393224 | tf_op jit(solution)/shard_map/ppermute | solution.py:31
  15.0 3.8 %collective-permute-done.1 = f32[256,128]{1,0:T(8,128)S(1)} collective-permute-done((f32[256,128]{1,0:T(8,128)S(1)}, f32[256,128]{1,0:T(8,128)S(1)}, u32[]{:S(2)}, u32[]{:S(2)}) %collective-permute-start.1) | collective-permute-done | bytes 131104 | tf_op jit(solution)/shard_map/ppermute | solution.py:31
  18.9 1.9 %collective-permute-start.2 = (f32[128,128]{1,0:T(8,128)S(1)}, f32[128,128]{1,0:T(8,128)S(1)}, u32[]{:S(2)}, u32[]{:S(2)}) collective-permute-start(f32[128,128]{1,0:T(8,128)S(1)} %constant_dynamic-slice_fusion.5), channel_id=1, source_target_pairs={{0,4},{1,5},{2,6},{3,7},{4,0},{5,1},{6,2},{7,3},{8,12},{9,13},{10,... | collective-permute-start | bytes 196616 | tf_op jit(solution)/shard_map/ppermute | solution.py:31
  20.8 2.4 %collective-permute-done.2 = f32[128,128]{1,0:T(8,128)S(1)} collective-permute-done((f32[128,128]{1,0:T(8,128)S(1)}, f32[128,128]{1,0:T(8,128)S(1)}, u32[]{:S(2)}, u32[]{:S(2)}) %collective-permute-start.2) | collective-permute-done | bytes 65568 | tf_op jit(solution)/shard_map/ppermute | solution.py:31
  23.2 2.9 %collective-permute-start.3 = (f32[64,128]{1,0:T(8,128)S(1)}, f32[64,128]{1,0:T(8,128)S(1)}, u32[]{:S(2)}, u32[]{:S(2)}) collective-permute-start(f32[64,128]{1,0:T(8,128)S(1)} %constant_dynamic-slice_fusion.4), channel_id=1, source_target_pairs={{0,8},{1,9},{2,10},{3,11},{4,12},{5,13},{6,14},{7,15},{8,0},{9,1},... | collective-permute-start | bytes 98312 | tf_op jit(solution)/shard_map/ppermute | solution.py:31
  26.1 2.0 %collective-permute-done.3 = f32[64,128]{1,0:T(8,128)S(1)} collective-permute-done((f32[64,128]{1,0:T(8,128)S(1)}, f32[64,128]{1,0:T(8,128)S(1)}, u32[]{:S(2)}, u32[]{:S(2)}) %collective-permute-start.3) | collective-permute-done | bytes 32800 | tf_op jit(solution)/shard_map/ppermute | solution.py:31
  28.1 2.9 %collective-permute-start.4 = (f32[64,128]{1,0:T(8,128)S(1)}, f32[64,128]{1,0:T(8,128)S(1)}, u32[]{:S(2)}, u32[]{:S(2)}) collective-permute-start(f32[64,128]{1,0:T(8,128)S(1)} %dynamic-slice_add_fusion.7), channel_id=1, source_target_pairs={{0,8},{1,9},{2,10},{3,11},{4,12},{5,13},{6,14},{7,15},{8,0},{9,1},... | collective-permute-start | bytes 98312 | tf_op jit(solution)/shard_map/ppermute | solution.py:31
  31.0 2.1 %collective-permute-done.4 = f32[64,128]{1,0:T(8,128)S(1)} collective-permute-done((f32[64,128]{1,0:T(8,128)S(1)}, f32[64,128]{1,0:T(8,128)S(1)}, u32[]{:S(2)}, u32[]{:S(2)}) %collective-permute-start.4) | collective-permute-done | bytes 32800 | tf_op jit(solution)/shard_map/ppermute | solution.py:31
  33.1 2.2 %collective-permute-start.5 = (f32[128,128]{1,0:T(8,128)S(1)}, f32[128,128]{1,0:T(8,128)S(1)}, u32[]{:S(2)}, u32[]{:S(2)}) collective-permute-start(f32[128,128]{1,0:T(8,128)S(1)} %maximum_select_fusion.7), channel_id=1, source_target_pairs={{0,4},{1,5},{2,6},{3,7},{4,0},{5,1},{6,2},{7,3},{8,12},{9,13},{10,... | collective-permute-start | bytes 196616 | tf_op jit(solution)/shard_map/ppermute | solution.py:31
  35.3 0.0 copy-done
  35.3 4.0 %multiply_reduce_fusion.3 = (f32[]{:T(128)}, f32[512,128]{1,0:T(8,128)S(1)}) fusion(f32[1024,512]{1,0:T(8,128)S(1)} %get-tuple-element.8, f32[1024,128]{1,0:T(8,128)S(1)} %copy-done), kind=kOutput, calls=%fused_computation.25 | convolution fusion | flops 805437440 | bytes 2883588 | tf_op jit(solution)/shard_map/dot_general | solution.py:14
  39.3 0.0 collective-permute-done.5
  39.4 1.6 %collective-permute-start.6 = (f32[256,128]{1,0:T(8,128)S(1)}, f32[256,128]{1,0:T(8,128)S(1)}, u32[]{:S(2)}, u32[]{:S(2)}) collective-permute-start(f32[256,128]{1,0:T(8,128)S(1)} %maximum_select_fusion.4), channel_id=1, source_target_pairs={{0,2},{1,3},{2,0},{3,1},{4,6},{5,7},{6,4},{7,5},{8,10},{9,11},{10,... | collective-permute-start | bytes 393224 | tf_op jit(solution)/shard_map/ppermute | solution.py:31
  40.9 0.6 compare_select_fusion.1
  41.6 2.8 %collective-permute-done.6 = f32[256,128]{1,0:T(8,128)S(1)} collective-permute-done((f32[256,128]{1,0:T(8,128)S(1)}, f32[256,128]{1,0:T(8,128)S(1)}, u32[]{:S(2)}, u32[]{:S(2)}) %collective-permute-start.6) | collective-permute-done | bytes 131104 | tf_op jit(solution)/shard_map/ppermute | solution.py:31
  44.4 0.1 collective-permute-start.7
  44.5 1.8 %fusion.6 = f32[512,1024]{0,1:T(8,128)S(1)} fusion(f32[512,128]{1,0:T(8,128)S(1)} %get-tuple-element.11, f32[1024,128]{1,0:T(8,128)S(1)} %copy-done), kind=kOutput, calls=%fused_computation.56 | convolution fusion | flops 805306368 | bytes 2883584 | tf_op jit(solution)/shard_map/dot_general | solution.py:14
  46.3 0.0 collective-permute-done.7
  46.3 6.3 %fusion = f32[]{:T(128)} fusion(f32[512,1024]{0,1:T(8,128)S(1)} %fusion.6, f32[512,128]{1,0:T(8,128)S(1)} %copy-done.2, s32[512]{0:T(512)S(1)} %copy-done.4, f32[512,128]{1,0:T(8,128)S(1)} %collective-permute-done.7, f32[512,128]{1,0:T(8,128)S(1)} %maximum_select_fusion.2, pred[]{:T(512)S(6)} %eq.47, f32[1024,512]{1,0:T(8,128)} %get-tuple-element.9, ...), kind=kOutput, calls=%fused_computation.2 | convolution fusion | flops 815661056 | bytes 4984837 | tf_op jit(solution)/shard_map/dot_general | solution.py:14
  52.6 1.2 broadcast_select_fusion.1
  53.9 4.8 %all-to-all-start = ((f32[16,1,128]{2,1,0:T(1,128)}), f32[16,1,128]{2,1,0:T(1,128)S(1)}, u32[]{:S(2)}, u32[]{:S(2)}) async-start(f32[16,1,128]{2,1,0:T(1,128)} %broadcast_select_fusion.1), calls=%async_computation | async-start | bytes 16384 | tf_op jit(solution)/shard_map/all_to_all | solution.py:67
  58.7 0.7 multiply_reduce_fusion.1
  59.5 5.6 %all-to-all-done = f32[16,1,128]{2,1,0:T(1,128)S(1)} async-done(((f32[16,1,128]{2,1,0:T(1,128)}), f32[16,1,128]{2,1,0:T(1,128)S(1)}, u32[]{:S(2)}, u32[]{:S(2)}) %all-to-all-start) | async-done | bytes 8224 | tf_op jit(solution)/shard_map/all_to_all | solution.py:67
  65.1 0.6 fusion.4
  67.6 0.0 copy-start.3
  67.7 0.1 multiply_subtract_fusion
  67.8 1.4 %copy-done.3 = s32[1024,512]{1,0:T(8,128)S(1)} copy-done((s32[1024,512]{1,0:T(8,128)S(1)}, s32[1024,512]{1,0:T(8,128)}, u32[]{:S(2)}) %copy-start.3) | copy-done | bytes 2097176
  69.2 3.6 %multiply_select_fusion = (f32[1024,512]{1,0:T(8,128)S(1)}, f32[1024,512]{1,0:T(8,128)S(1)}) fusion(s32[1024,512]{1,0:T(8,128)S(1)} %copy-done.3, s32[512]{0:T(512)S(1)} %copy-done.4, f32[512]{0:T(512)S(1)} %copy-done.5, f32[1024,128]{1,0:T(8,128)S(1)} %multiply_subtract_fusion, f32[512,128]{1,0:T(8,128)S(1)} %multiply_subtract_fusion.2), kind=kOutput, calls=%fused_computation.5 | convolution fusion | flops 814219264 | bytes 7081984 | tf_op jit(solution)/shard_map/dot_general | solution.py:14
  72.8 1.8 %fusion.7 = f32[1024,128]{1,0:T(8,128)S(1)} fusion(f32[1024,512]{1,0:T(8,128)S(1)} %get-tuple-element.12, f32[512,128]{1,0:T(8,128)S(1)} %multiply_subtract_fusion.2), kind=kOutput, calls=%fused_computation.57 | convolution fusion | flops 805306368 | bytes 2883584 | tf_op jit(solution)/shard_map/dot_general | solution.py:14
  74.6 0.1 collective-permute-start.8
  74.7 1.5 %collective-permute-done.8 = f32[512,128]{1,0:T(8,128)S(1)} collective-permute-done((f32[512,128]{1,0:T(8,128)S(1)}, f32[512,128]{1,0:T(8,128)S(1)}, u32[]{:S(2)}, u32[]{:S(2)}) %collective-permute-start.8) | collective-permute-done | bytes 262176 | tf_op jit(solution)/shard_map/ppermute | solution.py:31
  76.3 0.6 collective-permute-start.9
  76.9 5.0 %collective-permute-done.9 = f32[256,128]{1,0:T(8,128)S(1)} collective-permute-done((f32[256,128]{1,0:T(8,128)S(1)}, f32[256,128]{1,0:T(8,128)S(1)}, u32[]{:S(2)}, u32[]{:S(2)}) %collective-permute-start.9) | collective-permute-done | bytes 131104 | tf_op jit(solution)/shard_map/ppermute | solution.py:31
  81.9 0.6 collective-permute-start.10
  82.5 3.8 %collective-permute-done.10 = f32[128,128]{1,0:T(8,128)S(1)} collective-permute-done((f32[128,128]{1,0:T(8,128)S(1)}, f32[128,128]{1,0:T(8,128)S(1)}, u32[]{:S(2)}, u32[]{:S(2)}) %collective-permute-start.10) | collective-permute-done | bytes 65568 | tf_op jit(solution)/shard_map/ppermute | solution.py:31
  86.3 0.6 collective-permute-start.11
  86.9 4.6 %collective-permute-done.11 = f32[64,128]{1,0:T(8,128)S(1)} collective-permute-done((f32[64,128]{1,0:T(8,128)S(1)}, f32[64,128]{1,0:T(8,128)S(1)}, u32[]{:S(2)}, u32[]{:S(2)}) %collective-permute-start.11) | collective-permute-done | bytes 32800 | tf_op jit(solution)/shard_map/ppermute | solution.py:31
  91.5 0.3 collective-permute-start.12
  91.8 4.5 %collective-permute-done.12 = f32[64,128]{1,0:T(8,128)S(1)} collective-permute-done((f32[64,128]{1,0:T(8,128)S(1)}, f32[64,128]{1,0:T(8,128)S(1)}, u32[]{:S(2)}, u32[]{:S(2)}) %collective-permute-start.12) | collective-permute-done | bytes 32800 | tf_op jit(solution)/shard_map/ppermute | solution.py:31
  96.3 0.3 collective-permute-start.13
  96.6 4.1 %collective-permute-done.13 = f32[128,128]{1,0:T(8,128)S(1)} collective-permute-done((f32[128,128]{1,0:T(8,128)S(1)}, f32[128,128]{1,0:T(8,128)S(1)}, u32[]{:S(2)}, u32[]{:S(2)}) %collective-permute-start.13) | collective-permute-done | bytes 65568 | tf_op jit(solution)/shard_map/ppermute | solution.py:31
  100.7 0.7 collective-permute-start.14
  101.4 4.1 %multiply_reduce_fusion.2 = (f32[]{:T(128)}, f32[512,128]{1,0:T(8,128)S(1)}) fusion(f32[1024,512]{1,0:T(8,128)S(1)} %get-tuple-element.12, f32[1024,128]{1,0:T(8,128)S(1)} %multiply_subtract_fusion), kind=kOutput, calls=%fused_computation.22 | convolution fusion | flops 805437440 | bytes 2883588 | tf_op jit(solution)/shard_map/dot_general | solution.py:14
  105.5 0.6 compare_select_fusion
  106.1 0.0 collective-permute-done.14
  106.2 0.1 collective-permute-start.15
  106.2 1.8 %fusion.8 = f32[1024,512]{1,0:T(8,128)S(1)} fusion(f32[1024,128]{1,0:T(8,128)S(1)} %multiply_subtract_fusion, f32[512,128]{1,0:T(8,128)S(1)} %get-tuple-element.15), kind=kOutput, calls=%fused_computation.58 | convolution fusion | flops 805306368 | bytes 2883584 | tf_op jit(solution)/shard_map/dot_general | solution.py:14
  108.1 0.0 collective-permute-done.15
  108.1 0.7 multiply_reduce_fusion
  108.8 4.8 %fusion.1 = f32[]{:T(128)} fusion(f32[1024,512]{1,0:T(8,128)S(1)} %fusion.8, f32[1024,128]{1,0:T(8,128)S(1)} %get-tuple-element.3, f32[512,128]{1,0:T(8,128)S(1)} %multiply_subtract_fusion.2, s32[512]{0:T(512)S(1)} %copy-done.4, f32[1024,512]{1,0:T(8,128)S(1)} %get-tuple-element.13, f32[512]{0:T(512)S(1)} %copy-done.5), kind=kOutput, calls=%fused_computation.3 | convolution fusion | flops 815267840 | bytes 4984836 | tf_op jit(solution)/shard_map/dot_general | solution.py:14
  113.6 1.2 broadcast_select_fusion
  114.8 3.5 %all-to-all-start.1 = ((f32[16,1,128]{2,1,0:T(1,128)}), f32[16,1,128]{2,1,0:T(1,128)S(1)}, u32[]{:S(2)}, u32[]{:S(2)}) async-start(f32[16,1,128]{2,1,0:T(1,128)} %broadcast_select_fusion), calls=%async_computation.1 | async-start | bytes 16384 | tf_op jit(solution)/shard_map/all_to_all | solution.py:67
  118.3 6.3 %all-to-all-done.1 = f32[16,1,128]{2,1,0:T(1,128)S(1)} async-done(((f32[16,1,128]{2,1,0:T(1,128)}), f32[16,1,128]{2,1,0:T(1,128)S(1)}, u32[]{:S(2)}, u32[]{:S(2)}) %all-to-all-start.1) | async-done | bytes 8224 | tf_op jit(solution)/shard_map/all_to_all | solution.py:67
  124.6 0.6 fusion.3
  127.2 0.7 multiply_subtract_fusion.1
  127.9 0.6 dynamic-slice_subtract_fusion
  (31 shorter events, 0.4 us)
Async XLA Ops:
  0.6 6.8 %copy-start.1 = (f32[512,128]{1,0:T(8,128)S(1)}, f32[512,128]{1,0:T(8,128)}, u32[]{:S(2)}) copy-start(f32[512,128]{1,0:T(8,128)} %param.8) | copy-start | bytes 786436
  9.2 26.1 %copy-start = (f32[1024,128]{1,0:T(8,128)S(1)}, f32[1024,128]{1,0:T(8,128)}, u32[]{:S(2)}) copy-start(f32[1024,128]{1,0:T(8,128)} %param.7) | copy-start | bytes 1572868
  9.3 1.8 %collective-permute-start = (f32[512,128]{1,0:T(8,128)S(1)}, f32[512,128]{1,0:T(8,128)}, u32[]{:S(2)}, u32[]{:S(2)}) collective-permute-start(f32[512,128]{1,0:T(8,128)S(1)} %constant_dynamic-slice_fusion.7), channel_id=1, source_target_pairs={{0,1},{1,0},{2,3},{3,2},{4,5},{5,4},{6,7},{7,6},{8,9},{9,8},{10,11... | collective-permute-start | bytes 786440 | tf_op jit(solution)/shard_map/ppermute | solution.py:31
  12.1 6.7 %collective-permute-start.1 = (f32[256,128]{1,0:T(8,128)S(1)}, f32[256,128]{1,0:T(8,128)S(1)}, u32[]{:S(2)}, u32[]{:S(2)}) collective-permute-start(f32[256,128]{1,0:T(8,128)S(1)} %constant_dynamic-slice_fusion.6), channel_id=1, source_target_pairs={{0,2},{1,3},{2,0},{3,1},{4,6},{5,7},{6,4},{7,5},{8,10},{9,11},{10,... | collective-permute-start | bytes 393224 | tf_op jit(solution)/shard_map/ppermute | solution.py:31
  18.9 4.3 %collective-permute-start.2 = (f32[128,128]{1,0:T(8,128)S(1)}, f32[128,128]{1,0:T(8,128)S(1)}, u32[]{:S(2)}, u32[]{:S(2)}) collective-permute-start(f32[128,128]{1,0:T(8,128)S(1)} %constant_dynamic-slice_fusion.5), channel_id=1, source_target_pairs={{0,4},{1,5},{2,6},{3,7},{4,0},{5,1},{6,2},{7,3},{8,12},{9,13},{10,... | collective-permute-start | bytes 196616 | tf_op jit(solution)/shard_map/ppermute | solution.py:31
  23.2 4.9 %collective-permute-start.3 = (f32[64,128]{1,0:T(8,128)S(1)}, f32[64,128]{1,0:T(8,128)S(1)}, u32[]{:S(2)}, u32[]{:S(2)}) collective-permute-start(f32[64,128]{1,0:T(8,128)S(1)} %constant_dynamic-slice_fusion.4), channel_id=1, source_target_pairs={{0,8},{1,9},{2,10},{3,11},{4,12},{5,13},{6,14},{7,15},{8,0},{9,1},... | collective-permute-start | bytes 98312 | tf_op jit(solution)/shard_map/ppermute | solution.py:31
  28.1 4.9 %collective-permute-start.4 = (f32[64,128]{1,0:T(8,128)S(1)}, f32[64,128]{1,0:T(8,128)S(1)}, u32[]{:S(2)}, u32[]{:S(2)}) collective-permute-start(f32[64,128]{1,0:T(8,128)S(1)} %dynamic-slice_add_fusion.7), channel_id=1, source_target_pairs={{0,8},{1,9},{2,10},{3,11},{4,12},{5,13},{6,14},{7,15},{8,0},{9,1},... | collective-permute-start | bytes 98312 | tf_op jit(solution)/shard_map/ppermute | solution.py:31
  33.1 6.3 %collective-permute-start.5 = (f32[128,128]{1,0:T(8,128)S(1)}, f32[128,128]{1,0:T(8,128)S(1)}, u32[]{:S(2)}, u32[]{:S(2)}) collective-permute-start(f32[128,128]{1,0:T(8,128)S(1)} %maximum_select_fusion.7), channel_id=1, source_target_pairs={{0,4},{1,5},{2,6},{3,7},{4,0},{5,1},{6,2},{7,3},{8,12},{9,13},{10,... | collective-permute-start | bytes 196616 | tf_op jit(solution)/shard_map/ppermute | solution.py:31
  39.3 7.0 %copy-start.2 = (f32[512,128]{1,0:T(8,128)S(1)}, f32[512,128]{1,0:T(8,128)}, u32[]{:S(2)}) copy-start(f32[512,128]{1,0:T(8,128)} %param.8) | copy-start | bytes 786436
  39.3 7.0 %copy-start.4 = (s32[512]{0:T(512)S(1)}, s32[512]{0:T(512)}, u32[]{:S(2)}) copy-start(s32[512]{0:T(512)} %param.6) | copy-start | bytes 6148
  39.3 7.0 %copy-start.5 = (f32[512]{0:T(512)S(1)}, f32[512]{0:T(512)}, u32[]{:S(2)}) copy-start(f32[512]{0:T(512)} %param.9) | copy-start | bytes 6148
  39.4 5.0 %collective-permute-start.6 = (f32[256,128]{1,0:T(8,128)S(1)}, f32[256,128]{1,0:T(8,128)S(1)}, u32[]{:S(2)}, u32[]{:S(2)}) collective-permute-start(f32[256,128]{1,0:T(8,128)S(1)} %maximum_select_fusion.4), channel_id=1, source_target_pairs={{0,2},{1,3},{2,0},{3,1},{4,6},{5,7},{6,4},{7,5},{8,10},{9,11},{10,... | collective-permute-start | bytes 393224 | tf_op jit(solution)/shard_map/ppermute | solution.py:31
  44.4 1.9 %collective-permute-start.7 = (f32[512,128]{1,0:T(8,128)S(1)}, f32[512,128]{1,0:T(8,128)S(1)}, u32[]{:S(2)}, u32[]{:S(2)}) collective-permute-start(f32[512,128]{1,0:T(8,128)S(1)} %maximum_select_fusion.2), channel_id=1, source_target_pairs={{0,1},{1,0},{2,3},{3,2},{4,5},{5,4},{6,7},{7,6},{8,9},{9,8},{10,11... | collective-permute-start | bytes 786440 | tf_op jit(solution)/shard_map/ppermute | solution.py:31
  53.9 11.2 %all-to-all-start = ((f32[16,1,128]{2,1,0:T(1,128)}), f32[16,1,128]{2,1,0:T(1,128)S(1)}, u32[]{:S(2)}, u32[]{:S(2)}) async-start(f32[16,1,128]{2,1,0:T(1,128)} %broadcast_select_fusion.1), calls=%async_computation | async-start | bytes 16384 | tf_op jit(solution)/shard_map/all_to_all | solution.py:67
  67.6 1.6 %copy-start.3 = (s32[1024,512]{1,0:T(8,128)S(1)}, s32[1024,512]{1,0:T(8,128)}, u32[]{:S(2)}) copy-start(s32[1024,512]{1,0:T(8,128)} %param.5) | copy-start | bytes 6291460
  74.6 1.6 %collective-permute-start.8 = (f32[512,128]{1,0:T(8,128)S(1)}, f32[512,128]{1,0:T(8,128)S(1)}, u32[]{:S(2)}, u32[]{:S(2)}) collective-permute-start(f32[512,128]{1,0:T(8,128)S(1)} %constant_dynamic-slice_fusion.3), channel_id=1, source_target_pairs={{0,1},{1,0},{2,3},{3,2},{4,5},{5,4},{6,7},{7,6},{8,9},{9,8},{10,11... | collective-permute-start | bytes 786440 | tf_op jit(solution)/shard_map/ppermute | solution.py:31
  76.3 5.6 %collective-permute-start.9 = (f32[256,128]{1,0:T(8,128)S(1)}, f32[256,128]{1,0:T(8,128)S(1)}, u32[]{:S(2)}, u32[]{:S(2)}) collective-permute-start(f32[256,128]{1,0:T(8,128)S(1)} %constant_dynamic-slice_fusion.2), channel_id=1, source_target_pairs={{0,2},{1,3},{2,0},{3,1},{4,6},{5,7},{6,4},{7,5},{8,10},{9,11},{10,... | collective-permute-start | bytes 393224 | tf_op jit(solution)/shard_map/ppermute | solution.py:31
  81.9 4.3 %collective-permute-start.10 = (f32[128,128]{1,0:T(8,128)S(1)}, f32[128,128]{1,0:T(8,128)S(1)}, u32[]{:S(2)}, u32[]{:S(2)}) collective-permute-start(f32[128,128]{1,0:T(8,128)S(1)} %constant_dynamic-slice_fusion.1), channel_id=1, source_target_pairs={{0,4},{1,5},{2,6},{3,7},{4,0},{5,1},{6,2},{7,3},{8,12},{9,13},{10,... | collective-permute-start | bytes 196616 | tf_op jit(solution)/shard_map/ppermute | solution.py:31
  86.3 5.2 %collective-permute-start.11 = (f32[64,128]{1,0:T(8,128)S(1)}, f32[64,128]{1,0:T(8,128)S(1)}, u32[]{:S(2)}, u32[]{:S(2)}) collective-permute-start(f32[64,128]{1,0:T(8,128)S(1)} %constant_dynamic-slice_fusion), channel_id=1, source_target_pairs={{0,8},{1,9},{2,10},{3,11},{4,12},{5,13},{6,14},{7,15},{8,0},{9,1},... | collective-permute-start | bytes 98312 | tf_op jit(solution)/shard_map/ppermute | solution.py:31
  91.5 4.8 %collective-permute-start.12 = (f32[64,128]{1,0:T(8,128)S(1)}, f32[64,128]{1,0:T(8,128)S(1)}, u32[]{:S(2)}, u32[]{:S(2)}) collective-permute-start(f32[64,128]{1,0:T(8,128)S(1)} %dynamic-slice_add_fusion.6), channel_id=1, source_target_pairs={{0,8},{1,9},{2,10},{3,11},{4,12},{5,13},{6,14},{7,15},{8,0},{9,1},... | collective-permute-start | bytes 98312 | tf_op jit(solution)/shard_map/ppermute | solution.py:31
  96.3 4.3 %collective-permute-start.13 = (f32[128,128]{1,0:T(8,128)S(1)}, f32[128,128]{1,0:T(8,128)S(1)}, u32[]{:S(2)}, u32[]{:S(2)}) collective-permute-start(f32[128,128]{1,0:T(8,128)S(1)} %maximum_select_fusion.8), channel_id=1, source_target_pairs={{0,4},{1,5},{2,6},{3,7},{4,0},{5,1},{6,2},{7,3},{8,12},{9,13},{10,... | collective-permute-start | bytes 196616 | tf_op jit(solution)/shard_map/ppermute | solution.py:31
  100.7 5.4 %collective-permute-start.14 = (f32[256,128]{1,0:T(8,128)S(1)}, f32[256,128]{1,0:T(8,128)S(1)}, u32[]{:S(2)}, u32[]{:S(2)}) collective-permute-start(f32[256,128]{1,0:T(8,128)S(1)} %maximum_select_fusion.5), channel_id=1, source_target_pairs={{0,2},{1,3},{2,0},{3,1},{4,6},{5,7},{6,4},{7,5},{8,10},{9,11},{10,... | collective-permute-start | bytes 393224 | tf_op jit(solution)/shard_map/ppermute | solution.py:31
  106.2 1.9 %collective-permute-start.15 = (f32[512,128]{1,0:T(8,128)S(1)}, f32[512,128]{1,0:T(8,128)S(1)}, u32[]{:S(2)}, u32[]{:S(2)}) collective-permute-start(f32[512,128]{1,0:T(8,128)S(1)} %maximum_select_fusion.3), channel_id=1, source_target_pairs={{0,1},{1,0},{2,3},{3,2},{4,5},{5,4},{6,7},{7,6},{8,9},{9,8},{10,11... | collective-permute-start | bytes 786440 | tf_op jit(solution)/shard_map/ppermute | solution.py:31
  114.8 9.8 %all-to-all-start.1 = ((f32[16,1,128]{2,1,0:T(1,128)}), f32[16,1,128]{2,1,0:T(1,128)S(1)}, u32[]{:S(2)}, u32[]{:S(2)}) async-start(f32[16,1,128]{2,1,0:T(1,128)} %broadcast_select_fusion), calls=%async_computation.1 | async-start | bytes 16384 | tf_op jit(solution)/shard_map/all_to_all | solution.py:67

commit v3 on v2

--- a/solution.py
+++ b/solution.py
@@ -33,29 +33,38 @@
 
 def sum_over_users(partial, n):
     if n == 1:
-        return partial
+        return partial, [(partial, 0)]
     if n & (n - 1) or partial.shape[0] % n:
-        return lax.psum(partial, "user")
+        total = lax.psum(partial, "user")
+        return total, [(total, 0)]
     me = lax.axis_index("user")
     distances = []
     d = 1
     while d < n:
         distances.append(d)
         d *= 2
-    block = partial
-    for d in distances:
+    halving, butterfly = distances[:2], distances[2:]
+    block, offset = partial, 0
+    for d in halving:
         half = block.shape[0] // 2
         upper = (me // d) % 2
         keep = lax.dynamic_slice_in_dim(block, upper * half, half, 0)
         send = lax.dynamic_slice_in_dim(block, (1 - upper) * half, half, 0)
+        offset = offset + upper * half
         block = keep + exchange(send, n, d)
-    for d in reversed(distances):
+    for d in butterfly:
+        block = block + exchange(block, n, d)
+    pieces = [(block, offset)]
+    for d in reversed(halving):
+        rows = block.shape[0]
         other = exchange(block, n, d)
         upper = (me // d) % 2
+        pieces.append((other, offset + (1 - 2 * upper) * rows))
         both = jnp.concatenate([block, other], axis=0)
         swapped = jnp.concatenate([other, block], axis=0)
         block = jnp.where(upper == 0, both, swapped)
-    return block
+        offset = offset - upper * rows
+    return block, pieces
 
 
 def sum_scalars(values, n):
@@ -76,10 +85,16 @@
     for sweep in range(SWEEPS):
         residual, curvature = local_terms(time_factor, user_factor, user_base, counts, first_bin)
         grad_user = product(residual.T, time_factor)
-        grad_whole = sum_over_users(product(residual, user_factor), n)
+        grad_whole, pieces = sum_over_users(product(residual, user_factor), n)
         user_norm = jnp.sum(grad_user * grad_user)
-        tangent_image = product(grad_whole, user_factor.T) + product(time_factor, grad_user.T)
-        bending = jnp.sum(curvature * tangent_image * tangent_image)
+        bending = 0.0
+        for piece, first in pieces:
+            rows = piece.shape[0]
+            tangent_image = product(piece, user_factor.T) + product(
+                lax.dynamic_slice_in_dim(time_factor, first, rows, 0), grad_user.T
+            )
+            weight = lax.dynamic_slice_in_dim(curvature, first, rows, 0)
+            bending = bending + jnp.sum(weight * tangent_image * tangent_image)
         user_norm_total, bend_total = sum_scalars([user_norm, bending], n)
         norm_total = jnp.sum(grad_whole * grad_whole) + user_norm_total
         relax_step = norm_total / (bend_total + damping * norm_total)

time: 129 us -> 126 us (0.977)
  waiting for transfers between devices: 49.7 us -> 37.2 us
  matrix products: 36.7 us -> 43 us
  starting transfers between devices: 26.4 us -> 22 us
  between operations: 4.9 us -> 8.92 us
  local copies, waits for them, and re-layouts: 2.78 us -> 4.46 us
  other arithmetic: 7.93 us -> 9.39 us
    ppermute x16 -> x12, waiting for transfers between devices: 37.9 us -> 27.1 us  [exchange(): return lax.ppermute(value, 'user', [(i, i ^ distance) for i in range(n)])]
    dot_general x10 -> x18, matrix products: 36.7 us -> 43 us  [product(): jnp.dot(left, right, precision=lax.Precision.HIGHEST, preferred_element_t...]
    ppermute x16 -> x12, starting transfers between devices: 18.1 us -> 12.7 us  [exchange(): return lax.ppermute(value, 'user', [(i, i ^ distance) for i in range(n)])]
    all_to_all x2, waiting for transfers between devices: 11.9 us -> 10 us  [sum_scalars(): spread = lax.all_to_all(spread, 'user', 0, 0, tiled=False)]
  transfers between devices with their start and end apart: 18 -> 14, of which waited for: 14 -> 11; matrix products, arithmetic and copies ran while one was open for 11% -> 20% of each run, Pallas kernels for 0% -> 0%
where the time goes in v3:
time: 126 us; the launch traced here: 125 us
  matrix products  43 us (34%)
  waiting for transfers between devices  37.2 us (30%)
  starting transfers between devices  22 us (17%)
  other arithmetic  9.39 us (7%)
  between operations  8.92 us (7%)
  local copies, waits for them, and re-layouts  4.46 us (4%)
    dot_general x18, matrix products, product(): jnp.dot(left, right, precision=lax.Precision.HIGHEST, preferred_element_t...  43 us
    ppermute x12, waiting for transfers between devices, exchange(): return lax.ppermute(value, 'user', [(i, i ^ distance) for i in range(n)])  27.1 us
    ppermute x12, starting transfers between devices, exchange(): return lax.ppermute(value, 'user', [(i, i ^ distance) for i in range(n)])  12.7 us
    all_to_all x2, waiting for transfers between devices, sum_scalars(): spread = lax.all_to_all(spread, 'user', 0, 0, tiled=False)  10 us
    all_to_all x2, starting transfers between devices, sum_scalars(): spread = lax.all_to_all(spread, 'user', 0, 0, tiled=False)  9.23 us
    reduce_sum x2, other arithmetic, body(): norm_total = jnp.sum(grad_whole * grad_whole) + user_norm_total  2.6 us
  transfers between devices with their start and end apart: 14, of which 11 were waited for; matrix products, arithmetic and copies ran while one was open for 20% of the time, Pallas kernels for 0%

profile of v3, /device:TPU:0, one launch (start us, length us, event | category | flops | bytes accessed | tf_op | source)
XLA Modules:
  0.0 124.9 jit_solution(579600969004224620)
XLA Ops:
  0.7 7.0 %multiply_select_fusion.2 = (f32[1024,512]{1,0:T(8,128)}, f32[1024,512]{1,0:T(8,128)S(1)}) fusion(s32[512]{0:T(512)} %param.6, f32[512]{0:T(512)} %param.9, s32[1024,512]{1,0:T(8,128)} %param.5, f32[1024,128]{1,0:T(8,128)} %param.7, f32[512,128]{1,0:T(8,128)} %param.8), kind=kOutput, calls=%fused_computation.5 | convolution fusion | flops 815792128 | bytes 7081984 | tf_op jit(solution)/shard_map/dot_general | solution.py:14
  7.7 2.6 %fusion.26 = f32[1024,128]{1,0:T(8,128)} fusion(f32[1024,512]{1,0:T(8,128)S(1)} %get-tuple-element.7, f32[512,128]{1,0:T(8,128)S(1)} %copy-done), kind=kOutput, calls=%fused_computation.75 | convolution fusion | flops 805306368 | bytes 2883584 | tf_op jit(solution)/shard_map/dot_general | solution.py:14
  10.3 1.0 constant_dynamic-slice_fusion.3
  11.3 0.5 collective-permute-start
  11.8 4.0 %multiply_reduce_fusion.3 = (f32[]{:T(128)}, f32[512,128]{1,0:T(8,128)S(1)}) fusion(f32[1024,512]{1,0:T(8,128)S(1)} %get-tuple-element.7, f32[1024,128]{1,0:T(8,128)S(1)} %copy-done.1), kind=kOutput, calls=%fused_computation.42 | convolution fusion | flops 805437440 | bytes 2883588 | tf_op jit(solution)/shard_map/dot_general | solution.py:14
  15.8 0.0 collective-permute-done
  15.8 1.0 dynamic-slice_add_fusion.1
  16.8 2.7 %collective-permute-start.1 = (f32[256,128]{1,0:T(8,128)S(1)}, f32[256,128]{1,0:T(8,128)S(1)}, u32[]{:S(2)}, u32[]{:S(2)}) collective-permute-start(f32[256,128]{1,0:T(8,128)S(1)} %constant_dynamic-slice_fusion.2), channel_id=1, source_target_pairs={{0,2},{1,3},{2,0},{3,1},{4,6},{5,7},{6,4},{7,5},{8,10},{9,11},{10,... | collective-permute-start | bytes 393224 | tf_op jit(solution)/shard_map/ppermute | solution.py:31
  19.5 1.0 fusion.8
  20.5 3.1 %collective-permute-done.1 = f32[256,128]{1,0:T(8,128)S(1)} collective-permute-done((f32[256,128]{1,0:T(8,128)S(1)}, f32[256,128]{1,0:T(8,128)S(1)}, u32[]{:S(2)}, u32[]{:S(2)}) %collective-permute-start.1) | collective-permute-done | bytes 131104 | tf_op jit(solution)/shard_map/ppermute | solution.py:31
  23.6 1.9 %collective-permute-start.2 = (f32[256,128]{1,0:T(8,128)S(1)}, f32[256,128]{1,0:T(8,128)S(1)}, u32[]{:S(2)}, u32[]{:S(2)}) collective-permute-start(f32[256,128]{1,0:T(8,128)S(1)} %dynamic-slice_add_fusion.3), channel_id=1, source_target_pairs={{0,4},{1,5},{2,6},{3,7},{4,0},{5,1},{6,2},{7,3},{8,12},{9,13},{10,... | collective-permute-start | bytes 393224 | tf_op jit(solution)/shard_map/ppermute | solution.py:31
  25.5 0.6 fusion.14
  26.1 2.8 %collective-permute-done.2 = f32[256,128]{1,0:T(8,128)S(1)} collective-permute-done((f32[256,128]{1,0:T(8,128)S(1)}, f32[256,128]{1,0:T(8,128)S(1)}, u32[]{:S(2)}, u32[]{:S(2)}) %collective-permute-start.2) | collective-permute-done | bytes 131104 | tf_op jit(solution)/shard_map/ppermute | solution.py:31
  28.9 2.7 %collective-permute-start.3 = (f32[256,128]{1,0:T(8,128)S(1)}, f32[256,128]{1,0:T(8,128)S(1)}, u32[]{:S(2)}, u32[]{:S(2)}) collective-permute-start(f32[256,128]{1,0:T(8,128)S(1)} %add.175), channel_id=1, source_target_pairs={{0,8},{1,9},{2,10},{3,11},{4,12},{5,13},{6,14},{7,15},{8,0},{9,1},... | collective-permute-start | bytes 393224 | tf_op jit(solution)/shard_map/ppermute | solution.py:31
  31.6 1.4 %fusion.16 = f32[256,512]{1,0:T(8,128)} fusion(f32[512,128]{1,0:T(8,128)S(1)} %get-tuple-element.13, f32[1024,128]{1,0:T(8,128)S(1)} %copy-done.1, s32[]{:T(128)S(6)} %select_n.160), kind=kOutput, calls=%fused_computation.53 | convolution fusion | flops 201326592 | bytes 917508 | tf_op jit(solution)/shard_map/dot_general | solution.py:14
  33.0 4.0 %collective-permute-done.3 = f32[256,128]{1,0:T(8,128)S(1)} collective-permute-done((f32[256,128]{1,0:T(8,128)S(1)}, f32[256,128]{1,0:T(8,128)S(1)}, u32[]{:S(2)}, u32[]{:S(2)}) %collective-permute-start.3) | collective-permute-done | bytes 131104 | tf_op jit(solution)/shard_map/ppermute | solution.py:31
  37.0 1.4 %collective-permute-start.4 = (f32[256,128]{1,0:T(8,128)S(1)}, f32[256,128]{1,0:T(8,128)S(1)}, u32[]{:S(2)}, u32[]{:S(2)}) collective-permute-start(f32[256,128]{1,0:T(8,128)S(1)} %add.176), channel_id=1, source_target_pairs={{0,2},{1,3},{2,0},{3,1},{4,6},{5,7},{6,4},{7,5},{8,10},{9,11},{10,... | collective-permute-start | bytes 393224 | tf_op jit(solution)/shard_map/ppermute | solution.py:31
  38.5 0.6 compare_select_fusion.1
  39.1 3.0 %collective-permute-done.4 = f32[256,128]{1,0:T(8,128)S(1)} collective-permute-done((f32[256,128]{1,0:T(8,128)S(1)}, f32[256,128]{1,0:T(8,128)S(1)}, u32[]{:S(2)}, u32[]{:S(2)}) %collective-permute-start.4) | collective-permute-done | bytes 131104 | tf_op jit(solution)/shard_map/ppermute | solution.py:31
  42.1 0.1 collective-permute-start.5
  42.2 2.5 %fusion.2 = f32[]{:T(128)} fusion(f32[256,512]{1,0:T(8,128)} %fusion.16, f32[256,128]{1,0:T(8,128)S(1)} %add.176, f32[512,128]{1,0:T(8,128)S(1)} %copy-done, f32[1024,512]{1,0:T(8,128)} %get-tuple-element.6, s32[]{:T(128)S(6)} %select_n.160), kind=kOutput, calls=%fused_computation.25 | convolution fusion | flops 201850880 | bytes 1441800 | tf_op jit(solution)/shard_map/dot_general | solution.py:14
  44.6 2.3 %fusion.3 = f32[]{:T(128)} fusion(f32[256,512]{1,0:T(8,128)S(1)} %fusion.14, f32[256,128]{1,0:T(8,128)S(1)} %collective-permute-done.4, f32[512,128]{1,0:T(8,128)S(1)} %copy-done, f32[1024,512]{1,0:T(8,128)} %get-tuple-element.6, s32[]{:T(128)S(6)} %select_n.161), kind=kOutput, calls=%fused_computation.26 | convolution fusion | flops 201850880 | bytes 1441800 | tf_op jit(solution)/shard_map/dot_general | solution.py:14
  48.3 0.0 collective-permute-done.5
  48.3 3.0 %fusion = f32[]{:T(128)} fusion(f32[512,512]{1,0:T(8,128)S(1)} %fusion.8, f32[512,128]{1,0:T(8,128)S(1)} %collective-permute-done.5, f32[512,128]{1,0:T(8,128)S(1)} %copy-done, f32[1024,512]{1,0:T(8,128)} %get-tuple-element.6, s32[]{:T(128)S(6)} %select_n.162), kind=kOutput, calls=%fused_computation.23 | convolution fusion | flops 403701760 | bytes 2621448 | tf_op jit(solution)/shard_map/dot_general | solution.py:14
  52.0 0.6 broadcast_select_fusion.1
  52.6 5.8 %all-to-all-start = ((f32[16,1,128]{2,1,0:T(1,128)}), f32[16,1,128]{2,1,0:T(1,128)S(1)}, u32[]{:S(2)}, u32[]{:S(2)}) async-start(f32[16,1,128]{2,1,0:T(1,128)} %broadcast_select_fusion.1), calls=%async_computation | async-start | bytes 16384 | tf_op jit(solution)/shard_map/all_to_all | solution.py:76
  58.4 0.7 multiply_reduce_fusion.1
  59.1 5.6 %all-to-all-done = f32[16,1,128]{2,1,0:T(1,128)S(1)} async-done(((f32[16,1,128]{2,1,0:T(1,128)}), f32[16,1,128]{2,1,0:T(1,128)S(1)}, u32[]{:S(2)}, u32[]{:S(2)}) %all-to-all-start) | async-done | bytes 8224 | tf_op jit(solution)/shard_map/all_to_all | solution.py:76
  64.7 0.6 fusion.25
  67.3 0.0 copy-start.6
  67.4 0.1 multiply_subtract_fusion
  67.5 1.4 %copy-done.6 = s32[1024,512]{1,0:T(8,128)S(1)} copy-done((s32[1024,512]{1,0:T(8,128)S(1)}, s32[1024,512]{1,0:T(8,128)}, u32[]{:S(2)}) %copy-start.6) | copy-done | bytes 2097176
  68.9 5.1 %multiply_select_fusion = (f32[1024,512]{1,0:T(8,128)}, f32[1024,512]{1,0:T(8,128)S(1)}) fusion(s32[512]{0:T(512)S(1)} %copy-done.7, f32[512]{0:T(512)S(1)} %copy-done.8, s32[1024,512]{1,0:T(8,128)S(1)} %copy-done.6, f32[1024,128]{1,0:T(8,128)S(1)} %multiply_subtract_fusion, f32[512,128]{1,0:T(8,128)S(1)} %multiply_subtract_fusion.2), kind=kOutput, calls=%fused_computation | convolution fusion | flops 815792128 | bytes 7081984 | tf_op jit(solution)/shard_map/dot_general | solution.py:14
  74.1 1.8 %fusion.27 = f32[1024,128]{1,0:T(8,128)S(1)} fusion(f32[1024,512]{1,0:T(8,128)S(1)} %get-tuple-element.5, f32[512,128]{1,0:T(8,128)S(1)} %multiply_subtract_fusion.2), kind=kOutput, calls=%fused_computation.76 | convolution fusion | flops 805306368 | bytes 2883584 | tf_op jit(solution)/shard_map/dot_general | solution.py:14
  75.9 0.8 copy-done.5
  76.7 0.1 collective-permute-start.6
  76.8 1.5 %collective-permute-done.6 = f32[512,128]{1,0:T(8,128)S(1)} collective-permute-done((f32[512,128]{1,0:T(8,128)S(1)}, f32[512,128]{1,0:T(8,128)S(1)}, u32[]{:S(2)}, u32[]{:S(2)}) %collective-permute-start.6) | collective-permute-done | bytes 262176 | tf_op jit(solution)/shard_map/ppermute | solution.py:31
  78.3 1.0 dynamic-slice_add_fusion
  79.3 0.6 collective-permute-start.7
  79.9 4.0 %multiply_reduce_fusion.2 = (f32[]{:T(128)}, f32[512,128]{1,0:T(8,128)S(1)}) fusion(f32[1024,512]{1,0:T(8,128)S(1)} %get-tuple-element.5, f32[1024,128]{1,0:T(8,128)S(1)} %multiply_subtract_fusion), kind=kOutput, calls=%fused_computation.37 | convolution fusion | flops 805437440 | bytes 2883588 | tf_op jit(solution)/shard_map/dot_general | solution.py:14
  83.9 1.0 collective-permute-done.7
  84.9 0.6 collective-permute-start.8
  85.5 1.0 fusion.6
  86.5 3.5 %collective-permute-done.8 = f32[256,128]{1,0:T(8,128)S(1)} collective-permute-done((f32[256,128]{1,0:T(8,128)S(1)}, f32[256,128]{1,0:T(8,128)S(1)}, u32[]{:S(2)}, u32[]{:S(2)}) %collective-permute-start.8) | collective-permute-done | bytes 131104 | tf_op jit(solution)/shard_map/ppermute | solution.py:31
  90.0 0.6 collective-permute-start.9
  90.6 0.6 fusion.10
  91.2 6.1 %collective-permute-done.9 = f32[256,128]{1,0:T(8,128)S(1)} collective-permute-done((f32[256,128]{1,0:T(8,128)S(1)}, f32[256,128]{1,0:T(8,128)S(1)}, u32[]{:S(2)}, u32[]{:S(2)}) %collective-permute-start.9) | collective-permute-done | bytes 131104 | tf_op jit(solution)/shard_map/ppermute | solution.py:31
  97.3 1.6 %collective-permute-start.10 = (f32[256,128]{1,0:T(8,128)S(1)}, f32[256,128]{1,0:T(8,128)S(1)}, u32[]{:S(2)}, u32[]{:S(2)}) collective-permute-start(f32[256,128]{1,0:T(8,128)S(1)} %add.197), channel_id=1, source_target_pairs={{0,2},{1,3},{2,0},{3,1},{4,6},{5,7},{6,4},{7,5},{8,10},{9,11},{10,... | collective-permute-start | bytes 393224 | tf_op jit(solution)/shard_map/ppermute | solution.py:31
  98.9 0.6 fusion.12
  99.5 0.7 compare_select_fusion
  100.2 2.2 %collective-permute-done.10 = f32[256,128]{1,0:T(8,128)S(1)} collective-permute-done((f32[256,128]{1,0:T(8,128)S(1)}, f32[256,128]{1,0:T(8,128)S(1)}, u32[]{:S(2)}, u32[]{:S(2)}) %collective-permute-start.10) | collective-permute-done | bytes 131104 | tf_op jit(solution)/shard_map/ppermute | solution.py:31
  102.3 0.7 maximum_select_fusion.3
  103.0 0.0 collective-permute-start.11
  103.0 1.3 %fusion.4 = f32[]{:T(128)} fusion(f32[256,512]{1,0:T(8,128)S(1)} %fusion.12, f32[256,128]{1,0:T(8,128)S(1)} %add.197, f32[512,128]{1,0:T(8,128)S(1)} %multiply_subtract_fusion.2, f32[1024,512]{1,0:T(8,128)S(1)} %copy-done.3, s32[]{:T(128)S(6)} %select_n.160), kind=kOutput, calls=%fused_computation.27 | convolution fusion | flops 201850880 | bytes 1441800 | tf_op jit(solution)/shard_map/dot_general | solution.py:14
  104.3 1.3 %fusion.5 = f32[]{:T(128)} fusion(f32[256,512]{1,0:T(8,128)S(1)} %fusion.10, f32[256,128]{1,0:T(8,128)S(1)} %collective-permute-done.10, f32[512,128]{1,0:T(8,128)S(1)} %multiply_subtract_fusion.2, f32[1024,512]{1,0:T(8,128)S(1)} %copy-done.3, s32[]{:T(128)S(6)} %select_n.161), kind=kOutput, calls=%fused_computation.28 | convolution fusion | flops 201850880 | bytes 1441800 | tf_op jit(solution)/shard_map/dot_general | solution.py:14
  106.9 0.0 collective-permute-done.11
  106.9 3.0 %fusion.1 = f32[]{:T(128)} fusion(f32[512,512]{1,0:T(8,128)S(1)} %fusion.6, f32[512,128]{1,0:T(8,128)S(1)} %collective-permute-done.11, f32[512,128]{1,0:T(8,128)S(1)} %multiply_subtract_fusion.2, f32[1024,512]{1,0:T(8,128)} %get-tuple-element.4, s32[]{:T(128)S(6)} %select_n.162), kind=kOutput, calls=%fused_computation.24 | convolution fusion | flops 403701760 | bytes 2621448 | tf_op jit(solution)/shard_map/dot_general | solution.py:14
  110.5 0.6 broadcast_select_fusion
  111.1 3.5 %all-to-all-start.1 = ((f32[16,1,128]{2,1,0:T(1,128)}), f32[16,1,128]{2,1,0:T(1,128)S(1)}, u32[]{:S(2)}, u32[]{:S(2)}) async-start(f32[16,1,128]{2,1,0:T(1,128)} %broadcast_select_fusion), calls=%async_computation.1 | async-start | bytes 16384 | tf_op jit(solution)/shard_map/all_to_all | solution.py:76
  114.6 1.9 %multiply_reduce_fusion = (f32[]{:T(128)}, f32[1024,128]{1,0:T(8,128)S(1)}) fusion(f32[512,128]{1,0:T(8,128)} %maximum_select_fusion.3, f32[512,128]{1,0:T(8,128)S(1)} %collective-permute-done.11, pred[]{:T(512)S(6)} %eq.31), kind=kLoop, calls=%fused_computation.31 | loop fusion | flops 655359 | bytes 1048581 | tf_op jit(solution)/shard_map/reduce_sum | solution.py:99
  116.5 4.4 %all-to-all-done.1 = f32[16,1,128]{2,1,0:T(1,128)S(1)} async-done(((f32[16,1,128]{2,1,0:T(1,128)}), f32[16,1,128]{2,1,0:T(1,128)S(1)}, u32[]{:S(2)}, u32[]{:S(2)}) %all-to-all-start.1) | async-done | bytes 8224 | tf_op jit(solution)/shard_map/all_to_all | solution.py:76
  120.9 0.6 fusion.24
  123.5 0.7 multiply_subtract_fusion.1
  124.3 0.6 dynamic-slice_subtract_fusion
  (29 shorter events, 0.3 us)
Async XLA Ops:
  0.6 7.1 %copy-start = (f32[512,128]{1,0:T(8,128)S(1)}, f32[512,128]{1,0:T(8,128)}, u32[]{:S(2)}) copy-start(f32[512,128]{1,0:T(8,128)} %param.8) | copy-start | bytes 786436
  7.7 4.1 %copy-start.1 = (f32[1024,128]{1,0:T(8,128)S(1)}, f32[1024,128]{1,0:T(8,128)}, u32[]{:S(2)}) copy-start(f32[1024,128]{1,0:T(8,128)} %param.7) | copy-start | bytes 1572868
  11.3 4.5 %collective-permute-start = (f32[512,128]{1,0:T(8,128)S(1)}, f32[512,128]{1,0:T(8,128)}, u32[]{:S(2)}, u32[]{:S(2)}) collective-permute-start(f32[512,128]{1,0:T(8,128)S(1)} %constant_dynamic-slice_fusion.3), channel_id=1, source_target_pairs={{0,1},{1,0},{2,3},{3,2},{4,5},{5,4},{6,7},{7,6},{8,9},{9,8},{10,11... | collective-permute-start | bytes 786440 | tf_op jit(solution)/shard_map/ppermute | solution.py:31
  11.8 4.0 %copy-start.4 = (f32[1024,128]{1,0:T(8,128)S(1)}, f32[1024,128]{1,0:T(8,128)}, u32[]{:S(2)}) copy-start(f32[1024,128]{1,0:T(8,128)} %fusion.26) | copy-start | bytes 1572868
  16.8 6.7 %collective-permute-start.1 = (f32[256,128]{1,0:T(8,128)S(1)}, f32[256,128]{1,0:T(8,128)S(1)}, u32[]{:S(2)}, u32[]{:S(2)}) collective-permute-start(f32[256,128]{1,0:T(8,128)S(1)} %constant_dynamic-slice_fusion.2), channel_id=1, source_target_pairs={{0,2},{1,3},{2,0},{3,1},{4,6},{5,7},{6,4},{7,5},{8,10},{9,11},{10,... | collective-permute-start | bytes 393224 | tf_op jit(solution)/shard_map/ppermute | solution.py:31
  23.6 5.3 %collective-permute-start.2 = (f32[256,128]{1,0:T(8,128)S(1)}, f32[256,128]{1,0:T(8,128)S(1)}, u32[]{:S(2)}, u32[]{:S(2)}) collective-permute-start(f32[256,128]{1,0:T(8,128)S(1)} %dynamic-slice_add_fusion.3), channel_id=1, source_target_pairs={{0,4},{1,5},{2,6},{3,7},{4,0},{5,1},{6,2},{7,3},{8,12},{9,13},{10,... | collective-permute-start | bytes 393224 | tf_op jit(solution)/shard_map/ppermute | solution.py:31
  28.9 8.1 %collective-permute-start.3 = (f32[256,128]{1,0:T(8,128)S(1)}, f32[256,128]{1,0:T(8,128)S(1)}, u32[]{:S(2)}, u32[]{:S(2)}) collective-permute-start(f32[256,128]{1,0:T(8,128)S(1)} %add.175), channel_id=1, source_target_pairs={{0,8},{1,9},{2,10},{3,11},{4,12},{5,13},{6,14},{7,15},{8,0},{9,1},... | collective-permute-start | bytes 393224 | tf_op jit(solution)/shard_map/ppermute | solution.py:31
  37.0 5.0 %collective-permute-start.4 = (f32[256,128]{1,0:T(8,128)S(1)}, f32[256,128]{1,0:T(8,128)S(1)}, u32[]{:S(2)}, u32[]{:S(2)}) collective-permute-start(f32[256,128]{1,0:T(8,128)S(1)} %add.176), channel_id=1, source_target_pairs={{0,2},{1,3},{2,0},{3,1},{4,6},{5,7},{6,4},{7,5},{8,10},{9,11},{10,... | collective-permute-start | bytes 393224 | tf_op jit(solution)/shard_map/ppermute | solution.py:31
  42.1 6.2 %collective-permute-start.5 = (f32[512,128]{1,0:T(8,128)S(1)}, f32[512,128]{1,0:T(8,128)S(1)}, u32[]{:S(2)}, u32[]{:S(2)}) collective-permute-start(f32[512,128]{1,0:T(8,128)S(1)} %maximum_select_fusion.2), channel_id=1, source_target_pairs={{0,1},{1,0},{2,3},{3,2},{4,5},{5,4},{6,7},{7,6},{8,9},{9,8},{10,11... | collective-permute-start | bytes 786440 | tf_op jit(solution)/shard_map/ppermute | solution.py:31
  47.0 20.4 %copy-start.2 = (f32[1024,128]{1,0:T(8,128)S(1)}, f32[1024,128]{1,0:T(8,128)}, u32[]{:S(2)}) copy-start(f32[1024,128]{1,0:T(8,128)} %param.7) | copy-start | bytes 1572868
  51.3 16.2 %copy-start.7 = (s32[512]{0:T(512)S(1)}, s32[512]{0:T(512)}, u32[]{:S(2)}) copy-start(s32[512]{0:T(512)} %param.6) | copy-start | bytes 6148
  51.3 16.2 %copy-start.8 = (f32[512]{0:T(512)S(1)}, f32[512]{0:T(512)}, u32[]{:S(2)}) copy-start(f32[512]{0:T(512)} %param.9) | copy-start | bytes 6148
  52.6 12.1 %all-to-all-start = ((f32[16,1,128]{2,1,0:T(1,128)}), f32[16,1,128]{2,1,0:T(1,128)S(1)}, u32[]{:S(2)}, u32[]{:S(2)}) async-start(f32[16,1,128]{2,1,0:T(1,128)} %broadcast_select_fusion.1), calls=%async_computation | async-start | bytes 16384 | tf_op jit(solution)/shard_map/all_to_all | solution.py:76
  67.3 1.6 %copy-start.6 = (s32[1024,512]{1,0:T(8,128)S(1)}, s32[1024,512]{1,0:T(8,128)}, u32[]{:S(2)}) copy-start(s32[1024,512]{1,0:T(8,128)} %param.5) | copy-start | bytes 6291460
  75.9 0.8 copy-start.5
  76.7 1.6 %collective-permute-start.6 = (f32[512,128]{1,0:T(8,128)S(1)}, f32[512,128]{1,0:T(8,128)S(1)}, u32[]{:S(2)}, u32[]{:S(2)}) collective-permute-start(f32[512,128]{1,0:T(8,128)S(1)} %constant_dynamic-slice_fusion.1), channel_id=1, source_target_pairs={{0,1},{1,0},{2,3},{3,2},{4,5},{5,4},{6,7},{7,6},{8,9},{9,8},{10,11... | collective-permute-start | bytes 786440 | tf_op jit(solution)/shard_map/ppermute | solution.py:31
  79.3 5.6 %collective-permute-start.7 = (f32[256,128]{1,0:T(8,128)S(1)}, f32[256,128]{1,0:T(8,128)S(1)}, u32[]{:S(2)}, u32[]{:S(2)}) collective-permute-start(f32[256,128]{1,0:T(8,128)S(1)} %constant_dynamic-slice_fusion), channel_id=1, source_target_pairs={{0,2},{1,3},{2,0},{3,1},{4,6},{5,7},{6,4},{7,5},{8,10},{9,11},{10,... | collective-permute-start | bytes 393224 | tf_op jit(solution)/shard_map/ppermute | solution.py:31
  84.9 5.0 %collective-permute-start.8 = (f32[256,128]{1,0:T(8,128)S(1)}, f32[256,128]{1,0:T(8,128)S(1)}, u32[]{:S(2)}, u32[]{:S(2)}) collective-permute-start(f32[256,128]{1,0:T(8,128)S(1)} %dynamic-slice_add_fusion.2), channel_id=1, source_target_pairs={{0,4},{1,5},{2,6},{3,7},{4,0},{5,1},{6,2},{7,3},{8,12},{9,13},{10,... | collective-permute-start | bytes 393224 | tf_op jit(solution)/shard_map/ppermute | solution.py:31
  85.5 17.5 %copy-start.3 = (f32[1024,512]{1,0:T(8,128)S(1)}, f32[1024,512]{1,0:T(8,128)}, u32[]{:S(2)}) copy-start(f32[1024,512]{1,0:T(8,128)} %get-tuple-element.4) | copy-start | bytes 6291460
  90.0 7.3 %collective-permute-start.9 = (f32[256,128]{1,0:T(8,128)S(1)}, f32[256,128]{1,0:T(8,128)S(1)}, u32[]{:S(2)}, u32[]{:S(2)}) collective-permute-start(f32[256,128]{1,0:T(8,128)S(1)} %add.196), channel_id=1, source_target_pairs={{0,8},{1,9},{2,10},{3,11},{4,12},{5,13},{6,14},{7,15},{8,0},{9,1},... | collective-permute-start | bytes 393224 | tf_op jit(solution)/shard_map/ppermute | solution.py:31
  97.3 5.0 %collective-permute-start.10 = (f32[256,128]{1,0:T(8,128)S(1)}, f32[256,128]{1,0:T(8,128)S(1)}, u32[]{:S(2)}, u32[]{:S(2)}) collective-permute-start(f32[256,128]{1,0:T(8,128)S(1)} %add.197), channel_id=1, source_target_pairs={{0,2},{1,3},{2,0},{3,1},{4,6},{5,7},{6,4},{7,5},{8,10},{9,11},{10,... | collective-permute-start | bytes 393224 | tf_op jit(solution)/shard_map/ppermute | solution.py:31
  103.0 3.8 %collective-permute-start.11 = (f32[512,128]{1,0:T(8,128)}, f32[512,128]{1,0:T(8,128)S(1)}, u32[]{:S(2)}, u32[]{:S(2)}) collective-permute-start(f32[512,128]{1,0:T(8,128)} %maximum_select_fusion.3), channel_id=1, source_target_pairs={{0,1},{1,0},{2,3},{3,2},{4,5},{5,4},{6,7},{7,6},{8,9},{9,8},{10,11... | collective-permute-start | bytes 786440 | tf_op jit(solution)/shard_map/ppermute | solution.py:31
  111.1 9.8 %all-to-all-start.1 = ((f32[16,1,128]{2,1,0:T(1,128)}), f32[16,1,128]{2,1,0:T(1,128)S(1)}, u32[]{:S(2)}, u32[]{:S(2)}) async-start(f32[16,1,128]{2,1,0:T(1,128)} %broadcast_select_fusion), calls=%async_computation.1 | async-start | bytes 16384 | tf_op jit(solution)/shard_map/all_to_all | solution.py:76

commit v4 on v3

--- a/solution.py
+++ b/solution.py
@@ -10,8 +10,8 @@
 background = 0.5
 
 
-def product(left, right):
-    return jnp.dot(left, right, precision=lax.Precision.HIGHEST, preferred_element_type=jnp.float32)
+def product(left, right, precision=lax.Precision.HIGHEST):
+    return jnp.dot(left, right, precision=precision, preferred_element_type=jnp.float32)
 
 
 def local_terms(time_factor, user_block, base_block, count_block, start_block):
@@ -90,8 +90,8 @@
         bending = 0.0
         for piece, first in pieces:
             rows = piece.shape[0]
-            tangent_image = product(piece, user_factor.T) + product(
-                lax.dynamic_slice_in_dim(time_factor, first, rows, 0), grad_user.T
+            tangent_image = product(piece, user_factor.T, lax.Precision.HIGH) + product(
+                lax.dynamic_slice_in_dim(time_factor, first, rows, 0), grad_user.T, lax.Precision.HIGH
             )
             weight = lax.dynamic_slice_in_dim(curvature, first, rows, 0)
             bending = bending + jnp.sum(weight * tangent_image * tangent_image)

time: 126 us -> 124 us (0.984)
  matrix products: 43 us -> 39.9 us
  waiting for transfers between devices: 37.2 us -> 38.8 us
    dot_general x18, matrix products: 43 us -> 39.9 us  [product(): jnp.dot(left, right, precision=precision, preferred_element_type=jnp.floa...]
    ppermute x12, waiting for transfers between devices: 27.1 us -> 28.8 us  [exchange(): return lax.ppermute(value, 'user', [(i, i ^ distance) for i in range(n)])]
  transfers between devices with their start and end apart: 14 -> 14, of which waited for: 11 -> 11; matrix products, arithmetic and copies ran while one was open for 20% -> 18% of each run, Pallas kernels for 0% -> 0%
where the time goes in v4:
time: 124 us; the launch traced here: 123 us
  matrix products  39.9 us (32%)
  waiting for transfers between devices  38.8 us (31%)
  starting transfers between devices  21.9 us (18%)
  other arithmetic  9.39 us (8%)
  between operations  8.92 us (7%)
  local copies, waits for them, and re-layouts  4.46 us (4%)
    dot_general x18, matrix products, product(): jnp.dot(left, right, precision=precision, preferred_element_type=jnp.floa...  39.9 us
    ppermute x12, waiting for transfers between devices, exchange(): return lax.ppermute(value, 'user', [(i, i ^ distance) for i in range(n)])  28.8 us
    ppermute x12, starting transfers between devices, exchange(): return lax.ppermute(value, 'user', [(i, i ^ distance) for i in range(n)])  12.7 us
    all_to_all x2, waiting for transfers between devices, sum_scalars(): spread = lax.all_to_all(spread, 'user', 0, 0, tiled=False)  10 us
    all_to_all x2, starting transfers between devices, sum_scalars(): spread = lax.all_to_all(spread, 'user', 0, 0, tiled=False)  9.22 us
    reduce_sum x2, other arithmetic, body(): norm_total = jnp.sum(grad_whole * grad_whole) + user_norm_total  2.6 us
    select_n x4, other arithmetic, sum_scalars(): spread = jnp.where(lane == k, v, spread)  2.51 us
  transfers between devices with their start and end apart: 14, of which 11 were waited for; matrix products, arithmetic and copies ran while one was open for 18% of the time, Pallas kernels for 0%

profile of v4, /device:TPU:0, one launch (start us, length us, event | category | flops | bytes accessed | tf_op | source)
XLA Modules:
  0.0 123.4 jit_solution(627354598288496747)
XLA Ops:
  0.7 7.0 %multiply_select_fusion.2 = (f32[1024,512]{1,0:T(8,128)}, f32[1024,512]{1,0:T(8,128)S(1)}) fusion(s32[512]{0:T(512)} %param.6, f32[512]{0:T(512)} %param.9, s32[1024,512]{1,0:T(8,128)} %param.5, f32[1024,128]{1,0:T(8,128)} %param.7, f32[512,128]{1,0:T(8,128)} %param.8), kind=kOutput, calls=%fused_computation.5 | convolution fusion | flops 815792128 | bytes 7081984 | tf_op jit(solution)/shard_map/dot_general | solution.py:14
  7.7 2.6 %fusion.26 = f32[1024,128]{1,0:T(8,128)} fusion(f32[1024,512]{1,0:T(8,128)S(1)} %get-tuple-element.7, f32[512,128]{1,0:T(8,128)S(1)} %copy-done), kind=kOutput, calls=%fused_computation.75 | convolution fusion | flops 805306368 | bytes 2883584 | tf_op jit(solution)/shard_map/dot_general | solution.py:14
  10.3 1.0 constant_dynamic-slice_fusion.3
  11.3 0.5 collective-permute-start
  11.8 4.0 %multiply_reduce_fusion.3 = (f32[]{:T(128)}, f32[512,128]{1,0:T(8,128)S(1)}) fusion(f32[1024,512]{1,0:T(8,128)S(1)} %get-tuple-element.7, f32[1024,128]{1,0:T(8,128)S(1)} %copy-done.1), kind=kOutput, calls=%fused_computation.42 | convolution fusion | flops 805437440 | bytes 2883588 | tf_op jit(solution)/shard_map/dot_general | solution.py:14
  15.8 0.0 collective-permute-done
  15.8 1.0 dynamic-slice_add_fusion.1
  16.8 2.7 %collective-permute-start.1 = (f32[256,128]{1,0:T(8,128)S(1)}, f32[256,128]{1,0:T(8,128)S(1)}, u32[]{:S(2)}, u32[]{:S(2)}) collective-permute-start(f32[256,128]{1,0:T(8,128)S(1)} %constant_dynamic-slice_fusion.2), channel_id=1, source_target_pairs={{0,2},{1,3},{2,0},{3,1},{4,6},{5,7},{6,4},{7,5},{8,10},{9,11},{10,... | collective-permute-start | bytes 393224 | tf_op jit(solution)/shard_map/ppermute | solution.py:31
  19.5 0.6 fusion.8
  20.1 3.5 %collective-permute-done.1 = f32[256,128]{1,0:T(8,128)S(1)} collective-permute-done((f32[256,128]{1,0:T(8,128)S(1)}, f32[256,128]{1,0:T(8,128)S(1)}, u32[]{:S(2)}, u32[]{:S(2)}) %collective-permute-start.1) | collective-permute-done | bytes 131104 | tf_op jit(solution)/shard_map/ppermute | solution.py:31
  23.6 1.9 %collective-permute-start.2 = (f32[256,128]{1,0:T(8,128)S(1)}, f32[256,128]{1,0:T(8,128)S(1)}, u32[]{:S(2)}, u32[]{:S(2)}) collective-permute-start(f32[256,128]{1,0:T(8,128)S(1)} %dynamic-slice_add_fusion.3), channel_id=1, source_target_pairs={{0,4},{1,5},{2,6},{3,7},{4,0},{5,1},{6,2},{7,3},{8,12},{9,13},{10,... | collective-permute-start | bytes 393224 | tf_op jit(solution)/shard_map/ppermute | solution.py:31
  25.5 0.4 fusion.14
  25.9 3.0 %collective-permute-done.2 = f32[256,128]{1,0:T(8,128)S(1)} collective-permute-done((f32[256,128]{1,0:T(8,128)S(1)}, f32[256,128]{1,0:T(8,128)S(1)}, u32[]{:S(2)}, u32[]{:S(2)}) %collective-permute-start.2) | collective-permute-done | bytes 131104 | tf_op jit(solution)/shard_map/ppermute | solution.py:31
  28.9 2.7 %collective-permute-start.3 = (f32[256,128]{1,0:T(8,128)S(1)}, f32[256,128]{1,0:T(8,128)S(1)}, u32[]{:S(2)}, u32[]{:S(2)}) collective-permute-start(f32[256,128]{1,0:T(8,128)S(1)} %add.175), channel_id=1, source_target_pairs={{0,8},{1,9},{2,10},{3,11},{4,12},{5,13},{6,14},{7,15},{8,0},{9,1},... | collective-permute-start | bytes 393224 | tf_op jit(solution)/shard_map/ppermute | solution.py:31
  31.6 1.2 fusion.16
  32.8 4.2 %collective-permute-done.3 = f32[256,128]{1,0:T(8,128)S(1)} collective-permute-done((f32[256,128]{1,0:T(8,128)S(1)}, f32[256,128]{1,0:T(8,128)S(1)}, u32[]{:S(2)}, u32[]{:S(2)}) %collective-permute-start.3) | collective-permute-done | bytes 131104 | tf_op jit(solution)/shard_map/ppermute | solution.py:31
  37.0 1.4 %collective-permute-start.4 = (f32[256,128]{1,0:T(8,128)S(1)}, f32[256,128]{1,0:T(8,128)S(1)}, u32[]{:S(2)}, u32[]{:S(2)}) collective-permute-start(f32[256,128]{1,0:T(8,128)S(1)} %add.176), channel_id=1, source_target_pairs={{0,2},{1,3},{2,0},{3,1},{4,6},{5,7},{6,4},{7,5},{8,10},{9,11},{10,... | collective-permute-start | bytes 393224 | tf_op jit(solution)/shard_map/ppermute | solution.py:31
  38.5 0.6 compare_select_fusion.1
  39.1 3.0 %collective-permute-done.4 = f32[256,128]{1,0:T(8,128)S(1)} collective-permute-done((f32[256,128]{1,0:T(8,128)S(1)}, f32[256,128]{1,0:T(8,128)S(1)}, u32[]{:S(2)}, u32[]{:S(2)}) %collective-permute-start.4) | collective-permute-done | bytes 131104 | tf_op jit(solution)/shard_map/ppermute | solution.py:31
  42.1 0.1 collective-permute-start.5
  42.2 2.3 %fusion.2 = f32[]{:T(128)} fusion(f32[256,512]{1,0:T(8,128)} %fusion.16, f32[256,128]{1,0:T(8,128)S(1)} %add.176, f32[512,128]{1,0:T(8,128)S(1)} %copy-done, f32[1024,512]{1,0:T(8,128)} %get-tuple-element.6, s32[]{:T(128)S(6)} %select_n.160), kind=kOutput, calls=%fused_computation.25 | convolution fusion | flops 101187584 | bytes 1441800 | tf_op jit(solution)/shard_map/dot_general | solution.py:14
  44.4 2.3 %fusion.3 = f32[]{:T(128)} fusion(f32[256,512]{1,0:T(8,128)S(1)} %fusion.14, f32[256,128]{1,0:T(8,128)S(1)} %collective-permute-done.4, f32[512,128]{1,0:T(8,128)S(1)} %copy-done, f32[1024,512]{1,0:T(8,128)} %get-tuple-element.6, s32[]{:T(128)S(6)} %select_n.161), kind=kOutput, calls=%fused_computation.26 | convolution fusion | flops 101187584 | bytes 1441800 | tf_op jit(solution)/shard_map/dot_general | solution.py:14
  48.1 0.0 collective-permute-done.5
  48.1 2.6 %fusion = f32[]{:T(128)} fusion(f32[512,512]{1,0:T(8,128)S(1)} %fusion.8, f32[512,128]{1,0:T(8,128)S(1)} %collective-permute-done.5, f32[512,128]{1,0:T(8,128)S(1)} %copy-done, f32[1024,512]{1,0:T(8,128)} %get-tuple-element.6, s32[]{:T(128)S(6)} %select_n.162), kind=kOutput, calls=%fused_computation.23 | convolution fusion | flops 202375168 | bytes 2621448 | tf_op jit(solution)/shard_map/dot_general | solution.py:14
  51.3 0.6 broadcast_select_fusion.1
  51.9 5.7 %all-to-all-start = ((f32[16,1,128]{2,1,0:T(1,128)}), f32[16,1,128]{2,1,0:T(1,128)S(1)}, u32[]{:S(2)}, u32[]{:S(2)}) async-start(f32[16,1,128]{2,1,0:T(1,128)} %broadcast_select_fusion.1), calls=%async_computation | async-start | bytes 16384 | tf_op jit(solution)/shard_map/all_to_all | solution.py:76
  57.7 0.7 multiply_reduce_fusion.1
  58.4 5.6 %all-to-all-done = f32[16,1,128]{2,1,0:T(1,128)S(1)} async-done(((f32[16,1,128]{2,1,0:T(1,128)}), f32[16,1,128]{2,1,0:T(1,128)S(1)}, u32[]{:S(2)}, u32[]{:S(2)}) %all-to-all-start) | async-done | bytes 8224 | tf_op jit(solution)/shard_map/all_to_all | solution.py:76
  64.1 0.6 fusion.25
  66.7 0.0 copy-start.6
  66.7 0.1 multiply_subtract_fusion
  66.8 1.4 %copy-done.6 = s32[1024,512]{1,0:T(8,128)S(1)} copy-done((s32[1024,512]{1,0:T(8,128)S(1)}, s32[1024,512]{1,0:T(8,128)}, u32[]{:S(2)}) %copy-start.6) | copy-done | bytes 2097176
  68.3 5.1 %multiply_select_fusion = (f32[1024,512]{1,0:T(8,128)}, f32[1024,512]{1,0:T(8,128)S(1)}) fusion(s32[512]{0:T(512)S(1)} %copy-done.7, f32[512]{0:T(512)S(1)} %copy-done.8, s32[1024,512]{1,0:T(8,128)S(1)} %copy-done.6, f32[1024,128]{1,0:T(8,128)S(1)} %multiply_subtract_fusion, f32[512,128]{1,0:T(8,128)S(1)} %multiply_subtract_fusion.2), kind=kOutput, calls=%fused_computation | convolution fusion | flops 815792128 | bytes 7081984 | tf_op jit(solution)/shard_map/dot_general | solution.py:14
  73.4 1.8 %fusion.27 = f32[1024,128]{1,0:T(8,128)S(1)} fusion(f32[1024,512]{1,0:T(8,128)S(1)} %get-tuple-element.5, f32[512,128]{1,0:T(8,128)S(1)} %multiply_subtract_fusion.2), kind=kOutput, calls=%fused_computation.76 | convolution fusion | flops 805306368 | bytes 2883584 | tf_op jit(solution)/shard_map/dot_general | solution.py:14
  75.2 0.8 copy-done.5
  76.0 0.1 collective-permute-start.6
  76.1 1.5 %collective-permute-done.6 = f32[512,128]{1,0:T(8,128)S(1)} collective-permute-done((f32[512,128]{1,0:T(8,128)S(1)}, f32[512,128]{1,0:T(8,128)S(1)}, u32[]{:S(2)}, u32[]{:S(2)}) %collective-permute-start.6) | collective-permute-done | bytes 262176 | tf_op jit(solution)/shard_map/ppermute | solution.py:31
  77.6 1.0 dynamic-slice_add_fusion
  78.6 0.6 collective-permute-start.7
  79.2 4.0 %multiply_reduce_fusion.2 = (f32[]{:T(128)}, f32[512,128]{1,0:T(8,128)S(1)}) fusion(f32[1024,512]{1,0:T(8,128)S(1)} %get-tuple-element.5, f32[1024,128]{1,0:T(8,128)S(1)} %multiply_subtract_fusion), kind=kOutput, calls=%fused_computation.37 | convolution fusion | flops 805437440 | bytes 2883588 | tf_op jit(solution)/shard_map/dot_general | solution.py:14
  83.2 1.0 collective-permute-done.7
  84.3 0.6 collective-permute-start.8
  84.8 0.6 fusion.6
  85.4 3.9 %collective-permute-done.8 = f32[256,128]{1,0:T(8,128)S(1)} collective-permute-done((f32[256,128]{1,0:T(8,128)S(1)}, f32[256,128]{1,0:T(8,128)S(1)}, u32[]{:S(2)}, u32[]{:S(2)}) %collective-permute-start.8) | collective-permute-done | bytes 131104 | tf_op jit(solution)/shard_map/ppermute | solution.py:31
  89.3 0.6 collective-permute-start.9
  89.9 0.4 fusion.10
  90.3 6.3 %collective-permute-done.9 = f32[256,128]{1,0:T(8,128)S(1)} collective-permute-done((f32[256,128]{1,0:T(8,128)S(1)}, f32[256,128]{1,0:T(8,128)S(1)}, u32[]{:S(2)}, u32[]{:S(2)}) %collective-permute-start.9) | collective-permute-done | bytes 131104 | tf_op jit(solution)/shard_map/ppermute | solution.py:31
  96.6 1.6 %collective-permute-start.10 = (f32[256,128]{1,0:T(8,128)S(1)}, f32[256,128]{1,0:T(8,128)S(1)}, u32[]{:S(2)}, u32[]{:S(2)}) collective-permute-start(f32[256,128]{1,0:T(8,128)S(1)} %add.197), channel_id=1, source_target_pairs={{0,2},{1,3},{2,0},{3,1},{4,6},{5,7},{6,4},{7,5},{8,10},{9,11},{10,... | collective-permute-start | bytes 393224 | tf_op jit(solution)/shard_map/ppermute | solution.py:31
  98.2 0.4 fusion.12
  98.6 0.7 compare_select_fusion
  99.3 2.4 %collective-permute-done.10 = f32[256,128]{1,0:T(8,128)S(1)} collective-permute-done((f32[256,128]{1,0:T(8,128)S(1)}, f32[256,128]{1,0:T(8,128)S(1)}, u32[]{:S(2)}, u32[]{:S(2)}) %collective-permute-start.10) | collective-permute-done | bytes 131104 | tf_op jit(solution)/shard_map/ppermute | solution.py:31
  101.7 0.7 maximum_select_fusion.3
  102.4 0.0 collective-permute-start.11
  102.4 1.1 fusion.4
  103.5 1.1 fusion.5
  105.8 0.0 collective-permute-done.11
  105.8 2.6 %fusion.1 = f32[]{:T(128)} fusion(f32[512,512]{1,0:T(8,128)S(1)} %fusion.6, f32[512,128]{1,0:T(8,128)S(1)} %collective-permute-done.11, f32[512,128]{1,0:T(8,128)S(1)} %multiply_subtract_fusion.2, f32[1024,512]{1,0:T(8,128)} %get-tuple-element.4, s32[]{:T(128)S(6)} %select_n.162), kind=kOutput, calls=%fused_computation.24 | convolution fusion | flops 202375168 | bytes 2621448 | tf_op jit(solution)/shard_map/dot_general | solution.py:14
  109.0 0.6 broadcast_select_fusion
  109.6 3.5 %all-to-all-start.1 = ((f32[16,1,128]{2,1,0:T(1,128)}), f32[16,1,128]{2,1,0:T(1,128)S(1)}, u32[]{:S(2)}, u32[]{:S(2)}) async-start(f32[16,1,128]{2,1,0:T(1,128)} %broadcast_select_fusion), calls=%async_computation.1 | async-start | bytes 16384 | tf_op jit(solution)/shard_map/all_to_all | solution.py:76
  113.1 1.9 %multiply_reduce_fusion = (f32[]{:T(128)}, f32[1024,128]{1,0:T(8,128)S(1)}) fusion(f32[512,128]{1,0:T(8,128)} %maximum_select_fusion.3, f32[512,128]{1,0:T(8,128)S(1)} %collective-permute-done.11, pred[]{:T(512)S(6)} %eq.31), kind=kLoop, calls=%fused_computation.31 | loop fusion | flops 655359 | bytes 1048581 | tf_op jit(solution)/shard_map/reduce_sum | solution.py:99
  115.0 4.4 %all-to-all-done.1 = f32[16,1,128]{2,1,0:T(1,128)S(1)} async-done(((f32[16,1,128]{2,1,0:T(1,128)}), f32[16,1,128]{2,1,0:T(1,128)S(1)}, u32[]{:S(2)}, u32[]{:S(2)}) %all-to-all-start.1) | async-done | bytes 8224 | tf_op jit(solution)/shard_map/all_to_all | solution.py:76
  119.4 0.6 fusion.24
  122.0 0.7 multiply_subtract_fusion.1
  122.8 0.6 dynamic-slice_subtract_fusion
  (29 shorter events, 0.3 us)
Async XLA Ops:
  0.6 7.1 %copy-start = (f32[512,128]{1,0:T(8,128)S(1)}, f32[512,128]{1,0:T(8,128)}, u32[]{:S(2)}) copy-start(f32[512,128]{1,0:T(8,128)} %param.8) | copy-start | bytes 786436
  7.7 4.1 %copy-start.1 = (f32[1024,128]{1,0:T(8,128)S(1)}, f32[1024,128]{1,0:T(8,128)}, u32[]{:S(2)}) copy-start(f32[1024,128]{1,0:T(8,128)} %param.7) | copy-start | bytes 1572868
  11.3 4.5 %collective-permute-start = (f32[512,128]{1,0:T(8,128)S(1)}, f32[512,128]{1,0:T(8,128)}, u32[]{:S(2)}, u32[]{:S(2)}) collective-permute-start(f32[512,128]{1,0:T(8,128)S(1)} %constant_dynamic-slice_fusion.3), channel_id=1, source_target_pairs={{0,1},{1,0},{2,3},{3,2},{4,5},{5,4},{6,7},{7,6},{8,9},{9,8},{10,11... | collective-permute-start | bytes 786440 | tf_op jit(solution)/shard_map/ppermute | solution.py:31
  11.8 4.0 %copy-start.4 = (f32[1024,128]{1,0:T(8,128)S(1)}, f32[1024,128]{1,0:T(8,128)}, u32[]{:S(2)}) copy-start(f32[1024,128]{1,0:T(8,128)} %fusion.26) | copy-start | bytes 1572868
  16.8 6.7 %collective-permute-start.1 = (f32[256,128]{1,0:T(8,128)S(1)}, f32[256,128]{1,0:T(8,128)S(1)}, u32[]{:S(2)}, u32[]{:S(2)}) collective-permute-start(f32[256,128]{1,0:T(8,128)S(1)} %constant_dynamic-slice_fusion.2), channel_id=1, source_target_pairs={{0,2},{1,3},{2,0},{3,1},{4,6},{5,7},{6,4},{7,5},{8,10},{9,11},{10,... | collective-permute-start | bytes 393224 | tf_op jit(solution)/shard_map/ppermute | solution.py:31
  23.6 5.3 %collective-permute-start.2 = (f32[256,128]{1,0:T(8,128)S(1)}, f32[256,128]{1,0:T(8,128)S(1)}, u32[]{:S(2)}, u32[]{:S(2)}) collective-permute-start(f32[256,128]{1,0:T(8,128)S(1)} %dynamic-slice_add_fusion.3), channel_id=1, source_target_pairs={{0,4},{1,5},{2,6},{3,7},{4,0},{5,1},{6,2},{7,3},{8,12},{9,13},{10,... | collective-permute-start | bytes 393224 | tf_op jit(solution)/shard_map/ppermute | solution.py:31
  28.9 8.1 %collective-permute-start.3 = (f32[256,128]{1,0:T(8,128)S(1)}, f32[256,128]{1,0:T(8,128)S(1)}, u32[]{:S(2)}, u32[]{:S(2)}) collective-permute-start(f32[256,128]{1,0:T(8,128)S(1)} %add.175), channel_id=1, source_target_pairs={{0,8},{1,9},{2,10},{3,11},{4,12},{5,13},{6,14},{7,15},{8,0},{9,1},... | collective-permute-start | bytes 393224 | tf_op jit(solution)/shard_map/ppermute | solution.py:31
  37.0 5.0 %collective-permute-start.4 = (f32[256,128]{1,0:T(8,128)S(1)}, f32[256,128]{1,0:T(8,128)S(1)}, u32[]{:S(2)}, u32[]{:S(2)}) collective-permute-start(f32[256,128]{1,0:T(8,128)S(1)} %add.176), channel_id=1, source_target_pairs={{0,2},{1,3},{2,0},{3,1},{4,6},{5,7},{6,4},{7,5},{8,10},{9,11},{10,... | collective-permute-start | bytes 393224 | tf_op jit(solution)/shard_map/ppermute | solution.py:31
  42.1 6.0 %collective-permute-start.5 = (f32[512,128]{1,0:T(8,128)S(1)}, f32[512,128]{1,0:T(8,128)S(1)}, u32[]{:S(2)}, u32[]{:S(2)}) collective-permute-start(f32[512,128]{1,0:T(8,128)S(1)} %maximum_select_fusion.2), channel_id=1, source_target_pairs={{0,1},{1,0},{2,3},{3,2},{4,5},{5,4},{6,7},{7,6},{8,9},{9,8},{10,11... | collective-permute-start | bytes 786440 | tf_op jit(solution)/shard_map/ppermute | solution.py:31
  46.7 20.0 %copy-start.2 = (f32[1024,128]{1,0:T(8,128)S(1)}, f32[1024,128]{1,0:T(8,128)}, u32[]{:S(2)}) copy-start(f32[1024,128]{1,0:T(8,128)} %param.7) | copy-start | bytes 1572868
  50.7 16.2 %copy-start.7 = (s32[512]{0:T(512)S(1)}, s32[512]{0:T(512)}, u32[]{:S(2)}) copy-start(s32[512]{0:T(512)} %param.6) | copy-start | bytes 6148
  50.7 16.2 %copy-start.8 = (f32[512]{0:T(512)S(1)}, f32[512]{0:T(512)}, u32[]{:S(2)}) copy-start(f32[512]{0:T(512)} %param.9) | copy-start | bytes 6148
  51.9 12.1 %all-to-all-start = ((f32[16,1,128]{2,1,0:T(1,128)}), f32[16,1,128]{2,1,0:T(1,128)S(1)}, u32[]{:S(2)}, u32[]{:S(2)}) async-start(f32[16,1,128]{2,1,0:T(1,128)} %broadcast_select_fusion.1), calls=%async_computation | async-start | bytes 16384 | tf_op jit(solution)/shard_map/all_to_all | solution.py:76
  66.7 1.6 %copy-start.6 = (s32[1024,512]{1,0:T(8,128)S(1)}, s32[1024,512]{1,0:T(8,128)}, u32[]{:S(2)}) copy-start(s32[1024,512]{1,0:T(8,128)} %param.5) | copy-start | bytes 6291460
  75.2 0.8 copy-start.5
  76.0 1.6 %collective-permute-start.6 = (f32[512,128]{1,0:T(8,128)S(1)}, f32[512,128]{1,0:T(8,128)S(1)}, u32[]{:S(2)}, u32[]{:S(2)}) collective-permute-start(f32[512,128]{1,0:T(8,128)S(1)} %constant_dynamic-slice_fusion.1), channel_id=1, source_target_pairs={{0,1},{1,0},{2,3},{3,2},{4,5},{5,4},{6,7},{7,6},{8,9},{9,8},{10,11... | collective-permute-start | bytes 786440 | tf_op jit(solution)/shard_map/ppermute | solution.py:31
  78.6 5.6 %collective-permute-start.7 = (f32[256,128]{1,0:T(8,128)S(1)}, f32[256,128]{1,0:T(8,128)S(1)}, u32[]{:S(2)}, u32[]{:S(2)}) collective-permute-start(f32[256,128]{1,0:T(8,128)S(1)} %constant_dynamic-slice_fusion), channel_id=1, source_target_pairs={{0,2},{1,3},{2,0},{3,1},{4,6},{5,7},{6,4},{7,5},{8,10},{9,11},{10,... | collective-permute-start | bytes 393224 | tf_op jit(solution)/shard_map/ppermute | solution.py:31
  84.3 5.0 %collective-permute-start.8 = (f32[256,128]{1,0:T(8,128)S(1)}, f32[256,128]{1,0:T(8,128)S(1)}, u32[]{:S(2)}, u32[]{:S(2)}) collective-permute-start(f32[256,128]{1,0:T(8,128)S(1)} %dynamic-slice_add_fusion.2), channel_id=1, source_target_pairs={{0,4},{1,5},{2,6},{3,7},{4,0},{5,1},{6,2},{7,3},{8,12},{9,13},{10,... | collective-permute-start | bytes 393224 | tf_op jit(solution)/shard_map/ppermute | solution.py:31
  84.8 17.5 %copy-start.3 = (f32[1024,512]{1,0:T(8,128)S(1)}, f32[1024,512]{1,0:T(8,128)}, u32[]{:S(2)}) copy-start(f32[1024,512]{1,0:T(8,128)} %get-tuple-element.4) | copy-start | bytes 6291460
  89.3 7.3 %collective-permute-start.9 = (f32[256,128]{1,0:T(8,128)S(1)}, f32[256,128]{1,0:T(8,128)S(1)}, u32[]{:S(2)}, u32[]{:S(2)}) collective-permute-start(f32[256,128]{1,0:T(8,128)S(1)} %add.196), channel_id=1, source_target_pairs={{0,8},{1,9},{2,10},{3,11},{4,12},{5,13},{6,14},{7,15},{8,0},{9,1},... | collective-permute-start | bytes 393224 | tf_op jit(solution)/shard_map/ppermute | solution.py:31
  96.6 5.0 %collective-permute-start.10 = (f32[256,128]{1,0:T(8,128)S(1)}, f32[256,128]{1,0:T(8,128)S(1)}, u32[]{:S(2)}, u32[]{:S(2)}) collective-permute-start(f32[256,128]{1,0:T(8,128)S(1)} %add.197), channel_id=1, source_target_pairs={{0,2},{1,3},{2,0},{3,1},{4,6},{5,7},{6,4},{7,5},{8,10},{9,11},{10,... | collective-permute-start | bytes 393224 | tf_op jit(solution)/shard_map/ppermute | solution.py:31
  102.4 3.4 %collective-permute-start.11 = (f32[512,128]{1,0:T(8,128)}, f32[512,128]{1,0:T(8,128)S(1)}, u32[]{:S(2)}, u32[]{:S(2)}) collective-permute-start(f32[512,128]{1,0:T(8,128)} %maximum_select_fusion.3), channel_id=1, source_target_pairs={{0,1},{1,0},{2,3},{3,2},{4,5},{5,4},{6,7},{7,6},{8,9},{9,8},{10,11... | collective-permute-start | bytes 786440 | tf_op jit(solution)/shard_map/ppermute | solution.py:31
  109.6 9.8 %all-to-all-start.1 = ((f32[16,1,128]{2,1,0:T(1,128)}), f32[16,1,128]{2,1,0:T(1,128)S(1)}, u32[]{:S(2)}, u32[]{:S(2)}) async-start(f32[16,1,128]{2,1,0:T(1,128)} %broadcast_select_fusion), calls=%async_computation.1 | async-start | bytes 16384 | tf_op jit(solution)/shard_map/all_to_all | solution.py:76

commit v5 on v4

--- a/solution.py
+++ b/solution.py
@@ -32,12 +32,12 @@
 
 
 def sum_over_users(partial, n):
+    me = lax.axis_index("user")
     if n == 1:
-        return partial, [(partial, 0)]
+        return partial, [(partial, 0)], jnp.sum(partial * partial)
     if n & (n - 1) or partial.shape[0] % n:
         total = lax.psum(partial, "user")
-        return total, [(total, 0)]
-    me = lax.axis_index("user")
+        return total, [(total, 0)], jnp.where(me == 0, jnp.sum(total * total), 0.0)
     distances = []
     d = 1
     while d < n:
@@ -54,6 +54,7 @@
         block = keep + exchange(send, n, d)
     for d in butterfly:
         block = block + exchange(block, n, d)
+    share = jnp.where(me < 4, jnp.sum(block * block), 0.0)
     pieces = [(block, offset)]
     for d in reversed(halving):
         rows = block.shape[0]
@@ -64,18 +65,16 @@
         swapped = jnp.concatenate([other, block], axis=0)
         block = jnp.where(upper == 0, both, swapped)
         offset = offset - upper * rows
-    return block, pieces
+    return block, pieces, share
 
 
-def sum_scalars(values, n):
-    lane = lax.broadcasted_iota(jnp.int32, (n, 1, 128), 2)
-    spread = jnp.zeros((n, 1, 128), jnp.float32)
-    for k, v in enumerate(values):
-        spread = jnp.where(lane == k, v, spread)
+def sum_rows(values, n):
+    rows = jnp.stack([jnp.broadcast_to(v, (128,)) for v in values])
+    spread = jnp.broadcast_to(rows[None], (n,) + rows.shape)
     if n > 1:
         spread = lax.all_to_all(spread, "user", 0, 0, tiled=False)
-    total = jnp.sum(spread, axis=(0, 1))
-    return [total[k] for k in range(len(values))]
+    total = jnp.sum(spread, axis=0)
+    return [total[k:k + 1] for k in range(len(values))]
 
 
 def body(n, counts, first_bin, time_factor, user_factor, user_base):
@@ -85,18 +84,17 @@
     for sweep in range(SWEEPS):
         residual, curvature = local_terms(time_factor, user_factor, user_base, counts, first_bin)
         grad_user = product(residual.T, time_factor)
-        grad_whole, pieces = sum_over_users(product(residual, user_factor), n)
+        grad_whole, pieces, time_norm = sum_over_users(product(residual, user_factor), n)
         user_norm = jnp.sum(grad_user * grad_user)
-        bending = 0.0
+        bending = jnp.zeros((user_factor.shape[0],), jnp.float32)
         for piece, first in pieces:
             rows = piece.shape[0]
             tangent_image = product(piece, user_factor.T, lax.Precision.HIGH) + product(
                 lax.dynamic_slice_in_dim(time_factor, first, rows, 0), grad_user.T, lax.Precision.HIGH
             )
             weight = lax.dynamic_slice_in_dim(curvature, first, rows, 0)
-            bending = bending + jnp.sum(weight * tangent_image * tangent_image)
-        user_norm_total, bend_total = sum_scalars([user_norm, bending], n)
-        norm_total = jnp.sum(grad_whole * grad_whole) + user_norm_total
+            bending = bending + jnp.sum(weight * tangent_image * tangent_image, axis=0)
+        norm_total, bend_total = sum_rows([user_norm + time_norm, jnp.sum(bending)], n)
         relax_step = norm_total / (bend_total + damping * norm_total)
         user_factor = user_factor - relax_step * grad_user
         if sweep + 1 < SWEEPS:

time: 124 us -> 111 us (0.90)
  between operations: 8.92 us -> 3.58 us
  matrix products: 39.9 us -> 34.6 us
  other arithmetic: 9.39 us -> 6.29 us
  local copies, waits for them, and re-layouts: 4.46 us -> 6.51 us
  starting transfers between devices: 21.9 us -> 20.6 us
    dot_general x18, matrix products: 39.9 us -> 34.6 us  [product(): jnp.dot(left, right, precision=precision, preferred_element_type=jnp.floa...]
    all_to_all x2, waiting for transfers between devices: 10 us -> 12.8 us  [sum_rows(): spread = lax.all_to_all(spread, 'user', 0, 0, tiled=False)]
    select_n x4 -> x0, other arithmetic: 2.51 us -> none  [sum_scalars(): spread = jnp.where(lane == k, v, spread)]
    ppermute x12, waiting for transfers between devices: 28.8 us -> 26.5 us  [exchange(): return lax.ppermute(value, 'user', [(i, i ^ distance) for i in range(n)])]
    broadcast_in_dim x0 -> x2, local copies, waits for them, and re-layouts: none -> 1.36 us  [sum_rows(): spread = jnp.broadcast_to(rows[None], (n,) + rows.shape)]
    another operation x0 -> x2, local copies, waits for them, and re-layouts: none -> 1.34 us  [sum_rows(): rows = jnp.stack([jnp.broadcast_to(v, (128,)) for v in values])]
    reduce_sum x4 -> x6, other arithmetic: 2.63 us -> 2.61 us  [the longest x2 1.29 us: body(): jnp.sum(bending)]
  transfers between devices with their start and end apart: 14 -> 14, of which waited for: 11 -> 11; matrix products, arithmetic and copies ran while one was open for 18% -> 15% of each run, Pallas kernels for 0% -> 0%
where the time goes in v5:
time: 111 us
  waiting for transfers between devices  39.3 us (35%)
  matrix products  34.6 us (31%)
  starting transfers between devices  20.6 us (19%)
  local copies, waits for them, and re-layouts  6.51 us (6%)
  other arithmetic  6.29 us (6%)
  between operations  3.58 us (3%)
    dot_general x18, matrix products, product(): jnp.dot(left, right, precision=precision, preferred_element_type=jnp.floa...  34.6 us
    ppermute x12, waiting for transfers between devices, exchange(): return lax.ppermute(value, 'user', [(i, i ^ distance) for i in range(n)])  26.5 us
    all_to_all x2, waiting for transfers between devices, sum_rows(): spread = lax.all_to_all(spread, 'user', 0, 0, tiled=False)  12.8 us
    ppermute x12, starting transfers between devices, exchange(): return lax.ppermute(value, 'user', [(i, i ^ distance) for i in range(n)])  11.9 us
    all_to_all x2, starting transfers between devices, sum_rows(): spread = lax.all_to_all(spread, 'user', 0, 0, tiled=False)  8.66 us
  transfers between devices with their start and end apart: 14, of which 11 were waited for; matrix products, arithmetic and copies ran while one was open for 15% of the time, Pallas kernels for 0%

profile of v5, /device:TPU:0, one launch (start us, length us, event | category | flops | bytes accessed | tf_op | source)
XLA Modules:
  0.0 110.8 jit_solution(10726099671532837343)
XLA Ops:
  0.7 7.0 %multiply_select_fusion.2 = (f32[1024,512]{1,0:T(8,128)}, f32[1024,512]{1,0:T(8,128)S(1)}) fusion(s32[512]{0:T(512)} %param.6, f32[512]{0:T(512)} %param.9, s32[1024,512]{1,0:T(8,128)} %param.5, f32[1024,128]{1,0:T(8,128)} %param.7, f32[512,128]{1,0:T(8,128)} %param.8), kind=kOutput, calls=%fused_computation.5 | convolution fusion | flops 815792128 | bytes 7081984 | tf_op jit(solution)/shard_map/dot_general | solution.py:14
  7.7 2.6 %fusion.31 = f32[1024,128]{1,0:T(8,128)} fusion(f32[1024,512]{1,0:T(8,128)S(1)} %get-tuple-element.9, f32[512,128]{1,0:T(8,128)S(1)} %copy-done), kind=kOutput, calls=%fused_computation.80 | convolution fusion | flops 805306368 | bytes 2883584 | tf_op jit(solution)/shard_map/dot_general | solution.py:14
  10.3 1.0 constant_dynamic-slice_fusion.3
  11.3 0.5 collective-permute-start
  11.8 1.3 %collective-permute-done = f32[512,128]{1,0:T(8,128)} collective-permute-done((f32[512,128]{1,0:T(8,128)S(1)}, f32[512,128]{1,0:T(8,128)}, u32[]{:S(2)}, u32[]{:S(2)}) %collective-permute-start) | collective-permute-done | bytes 262176 | tf_op jit(solution)/shard_map/ppermute | solution.py:31
  13.1 1.1 dynamic-slice_add_fusion.1
  14.1 0.7 constant_dynamic-slice_fusion.2
  14.8 2.9 %collective-permute-start.1 = (f32[256,128]{1,0:T(8,128)}, f32[256,128]{1,0:T(8,128)S(1)}, u32[]{:S(2)}, u32[]{:S(2)}) collective-permute-start(f32[256,128]{1,0:T(8,128)} %constant_dynamic-slice_fusion.2), channel_id=1, source_target_pairs={{0,2},{1,3},{2,0},{3,1},{4,6},{5,7},{6,4},{7,5},{8,10},{9,11},{10,... | collective-permute-start | bytes 393224 | tf_op jit(solution)/shard_map/ppermute | solution.py:31
  17.7 4.0 %multiply_reduce_fusion.1 = (f32[]{:T(128)}, f32[512,128]{1,0:T(8,128)S(1)}) fusion(f32[1024,512]{1,0:T(8,128)S(1)} %get-tuple-element.9, f32[1024,128]{1,0:T(8,128)S(1)} %copy-done.1), kind=kOutput, calls=%fused_computation.47 | convolution fusion | flops 805437440 | bytes 2883588 | tf_op jit(solution)/shard_map/dot_general | solution.py:14
  21.7 1.9 %collective-permute-start.2 = (f32[256,128]{1,0:T(8,128)S(1)}, f32[256,128]{1,0:T(8,128)S(1)}, u32[]{:S(2)}, u32[]{:S(2)}) collective-permute-start(f32[256,128]{1,0:T(8,128)S(1)} %dynamic-slice_add_fusion.3), channel_id=1, source_target_pairs={{0,4},{1,5},{2,6},{3,7},{4,0},{5,1},{6,2},{7,3},{8,12},{9,13},{10,... | collective-permute-start | bytes 393224 | tf_op jit(solution)/shard_map/ppermute | solution.py:31
  23.6 0.6 fusion.10
  24.2 2.9 %collective-permute-done.2 = f32[256,128]{1,0:T(8,128)S(1)} collective-permute-done((f32[256,128]{1,0:T(8,128)S(1)}, f32[256,128]{1,0:T(8,128)S(1)}, u32[]{:S(2)}, u32[]{:S(2)}) %collective-permute-start.2) | collective-permute-done | bytes 131104 | tf_op jit(solution)/shard_map/ppermute | solution.py:31
  27.1 2.7 %collective-permute-start.3 = (f32[256,128]{1,0:T(8,128)S(1)}, f32[256,128]{1,0:T(8,128)S(1)}, u32[]{:S(2)}, u32[]{:S(2)}) collective-permute-start(f32[256,128]{1,0:T(8,128)S(1)} %add.179), channel_id=1, source_target_pairs={{0,8},{1,9},{2,10},{3,11},{4,12},{5,13},{6,14},{7,15},{8,0},{9,1},... | collective-permute-start | bytes 393224 | tf_op jit(solution)/shard_map/ppermute | solution.py:31
  29.7 0.4 fusion.16
  30.1 5.1 %collective-permute-done.3 = f32[256,128]{1,0:T(8,128)S(1)} collective-permute-done((f32[256,128]{1,0:T(8,128)S(1)}, f32[256,128]{1,0:T(8,128)S(1)}, u32[]{:S(2)}, u32[]{:S(2)}) %collective-permute-start.3) | collective-permute-done | bytes 131104 | tf_op jit(solution)/shard_map/ppermute | solution.py:31
  35.2 0.6 multiply_reduce_fusion.3
  35.9 0.6 collective-permute-start.4
  36.5 0.4 fusion.18
  38.1 2.7 %collective-permute-done.4 = f32[256,128]{1,0:T(8,128)S(1)} collective-permute-done((f32[256,128]{1,0:T(8,128)S(1)}, f32[256,128]{1,0:T(8,128)S(1)}, u32[]{:S(2)}, u32[]{:S(2)}) %collective-permute-start.4) | collective-permute-done | bytes 131104 | tf_op jit(solution)/shard_map/ppermute | solution.py:31
  40.8 0.7 copy-done.8
  41.5 0.0 copy-start.6
  41.5 0.1 collective-permute-start.5
  41.6 1.5 %fusion.5 = f32[512]{0:T(512)S(1)} fusion(f32[256,512]{1,0:T(8,128)S(1)} %fusion.18, f32[256,128]{1,0:T(8,128)S(1)} %get-tuple-element.5, f32[512,128]{1,0:T(8,128)S(1)} %copy-done, f32[1024,512]{1,0:T(8,128)} %get-tuple-element.8, s32[]{:T(128)S(6)} %select_n.133), kind=kOutput, calls=%fused_computation.28 | convolution fusion | flops 101187072 | bytes 1443844 | tf_op jit(solution)/shard_map/dot_general | solution.py:14
  43.1 1.5 %fusion.4 = f32[512]{0:T(512)S(1)} fusion(f32[256,512]{1,0:T(8,128)S(1)} %fusion.16, f32[256,128]{1,0:T(8,128)} %copy-done.8, f32[512,128]{1,0:T(8,128)S(1)} %copy-done, f32[1024,512]{1,0:T(8,128)} %get-tuple-element.8, s32[]{:T(128)S(6)} %select_n.134), kind=kOutput, calls=%fused_computation.26 | convolution fusion | flops 101187072 | bytes 1443844 | tf_op jit(solution)/shard_map/dot_general | solution.py:14
  44.6 0.0 copy-start.10
  44.6 0.0 copy-start.11
  44.7 0.0 copy-start.7
  44.7 0.6 fusion
  45.3 0.7 add_reduce_fusion.1
  46.0 0.7 stack.6
  46.7 0.7 broadcast_in_dim.15
  47.4 5.2 %all-to-all-start = ((f32[16,2,128]{2,1,0:T(2,128)}), f32[16,2,128]{2,1,0:T(2,128)S(1)}, u32[]{:S(2)}, u32[]{:S(2)}) async-start(f32[16,2,128]{2,1,0:T(2,128)} %broadcast_in_dim.15), calls=%async_computation | async-start | bytes 32768 | tf_op jit(solution)/shard_map/all_to_all | solution.py:75
  52.5 6.3 %all-to-all-done = f32[16,2,128]{2,1,0:T(2,128)S(1)} async-done(((f32[16,2,128]{2,1,0:T(2,128)}), f32[16,2,128]{2,1,0:T(2,128)S(1)}, u32[]{:S(2)}, u32[]{:S(2)}) %all-to-all-start) | async-done | bytes 16416 | tf_op jit(solution)/shard_map/all_to_all | solution.py:75
  59.0 0.1 fusion.7
  59.1 1.4 %copy-done.9 = s32[1024,512]{1,0:T(8,128)S(1)} copy-done((s32[1024,512]{1,0:T(8,128)S(1)}, s32[1024,512]{1,0:T(8,128)}, u32[]{:S(2)}) %copy-start.9) | copy-done | bytes 2097176
  60.5 5.1 %multiply_select_fusion = (f32[1024,512]{1,0:T(8,128)}, f32[1024,512]{1,0:T(8,128)S(1)}) fusion(s32[512]{0:T(512)S(1)} %copy-done.10, f32[512]{0:T(512)S(1)} %copy-done.11, s32[1024,512]{1,0:T(8,128)S(1)} %copy-done.9, f32[1024,128]{1,0:T(8,128)S(1)} %fusion.7, f32[512,128]{1,0:T(8,128)S(1)} %multiply_subtract_fusion.1), kind=kOutput, calls=%fused_computation | convolution fusion | flops 815792128 | bytes 7081984 | tf_op jit(solution)/shard_map/dot_general | solution.py:14
  65.6 1.8 %fusion.32 = f32[1024,128]{1,0:T(8,128)S(1)} fusion(f32[1024,512]{1,0:T(8,128)S(1)} %get-tuple-element.7, f32[512,128]{1,0:T(8,128)S(1)} %multiply_subtract_fusion.1), kind=kOutput, calls=%fused_computation.81 | convolution fusion | flops 805306368 | bytes 2883584 | tf_op jit(solution)/shard_map/dot_general | solution.py:14
  67.5 0.1 collective-permute-start.6
  67.5 1.5 %collective-permute-done.6 = f32[512,128]{1,0:T(8,128)S(1)} collective-permute-done((f32[512,128]{1,0:T(8,128)S(1)}, f32[512,128]{1,0:T(8,128)S(1)}, u32[]{:S(2)}, u32[]{:S(2)}) %collective-permute-start.6) | collective-permute-done | bytes 262176 | tf_op jit(solution)/shard_map/ppermute | solution.py:31
  69.1 0.5 collective-permute-start.7
  69.6 4.1 %multiply_reduce_fusion = (f32[]{:T(128)}, f32[512,128]{1,0:T(8,128)S(1)}) fusion(f32[1024,512]{1,0:T(8,128)S(1)} %get-tuple-element.7, f32[1024,128]{1,0:T(8,128)S(1)} %fusion.7), kind=kOutput, calls=%fused_computation.42 | convolution fusion | flops 805437440 | bytes 2883588 | tf_op jit(solution)/shard_map/dot_general | solution.py:14
  73.7 1.0 collective-permute-done.7
  74.7 0.5 collective-permute-start.8
  75.3 0.6 fusion.8
  75.8 3.9 %collective-permute-done.8 = f32[256,128]{1,0:T(8,128)S(1)} collective-permute-done((f32[256,128]{1,0:T(8,128)S(1)}, f32[256,128]{1,0:T(8,128)S(1)}, u32[]{:S(2)}, u32[]{:S(2)}) %collective-permute-start.8) | collective-permute-done | bytes 131104 | tf_op jit(solution)/shard_map/ppermute | solution.py:31
  79.8 0.5 collective-permute-start.9
  80.3 0.4 fusion.12
  80.7 6.3 %collective-permute-done.9 = f32[256,128]{1,0:T(8,128)S(1)} collective-permute-done((f32[256,128]{1,0:T(8,128)S(1)}, f32[256,128]{1,0:T(8,128)S(1)}, u32[]{:S(2)}, u32[]{:S(2)}) %collective-permute-start.9) | collective-permute-done | bytes 131104 | tf_op jit(solution)/shard_map/ppermute | solution.py:31
  87.0 0.6 multiply_reduce_fusion.2
  87.7 1.7 %collective-permute-start.10 = (f32[256,128]{1,0:T(8,128)S(1)}, f32[256,128]{1,0:T(8,128)}, u32[]{:S(2)}, u32[]{:S(2)}) collective-permute-start(f32[256,128]{1,0:T(8,128)S(1)} %get-tuple-element.3), channel_id=1, source_target_pairs={{0,2},{1,3},{2,0},{3,1},{4,6},{5,7},{6,4},{7,5},{8,10},{9,11},{10,... | collective-permute-start | bytes 393224 | tf_op jit(solution)/shard_map/ppermute | solution.py:31
  89.3 0.4 fusion.14
  91.0 1.7 %collective-permute-done.10 = f32[256,128]{1,0:T(8,128)} collective-permute-done((f32[256,128]{1,0:T(8,128)S(1)}, f32[256,128]{1,0:T(8,128)}, u32[]{:S(2)}, u32[]{:S(2)}) %collective-permute-start.10) | collective-permute-done | bytes 131104 | tf_op jit(solution)/shard_map/ppermute | solution.py:31
  92.7 1.0 maximum_select_fusion.2
  93.8 0.1 collective-permute-start.11
  93.8 1.5 %fusion.3 = f32[512]{0:T(512)S(1)} fusion(f32[256,512]{1,0:T(8,128)S(1)} %fusion.14, f32[256,128]{1,0:T(8,128)S(1)} %get-tuple-element.3, f32[512,128]{1,0:T(8,128)S(1)} %multiply_subtract_fusion.1, f32[1024,512]{1,0:T(8,128)} %get-tuple-element.6, s32[]{:T(128)S(6)} %select_n.133), kind=kOutput, calls=%fused_computation.24 | convolution fusion | flops 101187072 | bytes 1443844 | tf_op jit(solution)/shard_map/dot_general | solution.py:14
  95.3 1.5 %fusion.2 = f32[512]{0:T(512)S(1)} fusion(f32[256,512]{1,0:T(8,128)S(1)} %fusion.12, f32[256,128]{1,0:T(8,128)} %collective-permute-done.10, f32[512,128]{1,0:T(8,128)S(1)} %multiply_subtract_fusion.1, f32[1024,512]{1,0:T(8,128)} %get-tuple-element.6, s32[]{:T(128)S(6)} %select_n.134), kind=kOutput, calls=%fused_computation.22 | convolution fusion | flops 101187072 | bytes 1443844 | tf_op jit(solution)/shard_map/dot_general | solution.py:14
  96.9 0.6 fusion.1
  97.5 0.6 add_reduce_fusion
  98.1 0.6 stack.7
  98.8 0.7 broadcast_in_dim.16
  99.5 3.5 %all-to-all-start.1 = ((f32[16,2,128]{2,1,0:T(2,128)}), f32[16,2,128]{2,1,0:T(2,128)S(1)}, u32[]{:S(2)}, u32[]{:S(2)}) async-start(f32[16,2,128]{2,1,0:T(2,128)} %broadcast_in_dim.16), calls=%async_computation.1 | async-start | bytes 32768 | tf_op jit(solution)/shard_map/all_to_all | solution.py:75
  103.0 6.5 %all-to-all-done.1 = f32[16,2,128]{2,1,0:T(2,128)S(1)} async-done(((f32[16,2,128]{2,1,0:T(2,128)}), f32[16,2,128]{2,1,0:T(2,128)S(1)}, u32[]{:S(2)}, u32[]{:S(2)}) %all-to-all-start.1) | async-done | bytes 16416 | tf_op jit(solution)/shard_map/all_to_all | solution.py:75
  109.5 0.7 multiply_subtract_fusion
  110.2 0.6 dynamic-slice_subtract_fusion
  (34 shorter events, 0.3 us)
Async XLA Ops:
  0.6 7.0 %copy-start = (f32[512,128]{1,0:T(8,128)S(1)}, f32[512,128]{1,0:T(8,128)}, u32[]{:S(2)}) copy-start(f32[512,128]{1,0:T(8,128)} %param.8) | copy-start | bytes 786436
  7.7 10.0 %copy-start.1 = (f32[1024,128]{1,0:T(8,128)S(1)}, f32[1024,128]{1,0:T(8,128)}, u32[]{:S(2)}) copy-start(f32[1024,128]{1,0:T(8,128)} %param.7) | copy-start | bytes 1572868
  11.3 1.8 %collective-permute-start = (f32[512,128]{1,0:T(8,128)S(1)}, f32[512,128]{1,0:T(8,128)}, u32[]{:S(2)}, u32[]{:S(2)}) collective-permute-start(f32[512,128]{1,0:T(8,128)S(1)} %constant_dynamic-slice_fusion.3), channel_id=1, source_target_pairs={{0,1},{1,0},{2,3},{3,2},{4,5},{5,4},{6,7},{7,6},{8,9},{9,8},{10,11... | collective-permute-start | bytes 786440 | tf_op jit(solution)/shard_map/ppermute | solution.py:31
  14.8 6.9 %collective-permute-start.1 = (f32[256,128]{1,0:T(8,128)}, f32[256,128]{1,0:T(8,128)S(1)}, u32[]{:S(2)}, u32[]{:S(2)}) collective-permute-start(f32[256,128]{1,0:T(8,128)} %constant_dynamic-slice_fusion.2), channel_id=1, source_target_pairs={{0,2},{1,3},{2,0},{3,1},{4,6},{5,7},{6,4},{7,5},{8,10},{9,11},{10,... | collective-permute-start | bytes 393224 | tf_op jit(solution)/shard_map/ppermute | solution.py:31
  21.7 5.3 %collective-permute-start.2 = (f32[256,128]{1,0:T(8,128)S(1)}, f32[256,128]{1,0:T(8,128)S(1)}, u32[]{:S(2)}, u32[]{:S(2)}) collective-permute-start(f32[256,128]{1,0:T(8,128)S(1)} %dynamic-slice_add_fusion.3), channel_id=1, source_target_pairs={{0,4},{1,5},{2,6},{3,7},{4,0},{5,1},{6,2},{7,3},{8,12},{9,13},{10,... | collective-permute-start | bytes 393224 | tf_op jit(solution)/shard_map/ppermute | solution.py:31
  27.1 8.2 %collective-permute-start.3 = (f32[256,128]{1,0:T(8,128)S(1)}, f32[256,128]{1,0:T(8,128)S(1)}, u32[]{:S(2)}, u32[]{:S(2)}) collective-permute-start(f32[256,128]{1,0:T(8,128)S(1)} %add.179), channel_id=1, source_target_pairs={{0,8},{1,9},{2,10},{3,11},{4,12},{5,13},{6,14},{7,15},{8,0},{9,1},... | collective-permute-start | bytes 393224 | tf_op jit(solution)/shard_map/ppermute | solution.py:31
  35.9 5.0 %collective-permute-start.4 = (f32[256,128]{1,0:T(8,128)S(1)}, f32[256,128]{1,0:T(8,128)S(1)}, u32[]{:S(2)}, u32[]{:S(2)}) collective-permute-start(f32[256,128]{1,0:T(8,128)S(1)} %get-tuple-element.5), channel_id=1, source_target_pairs={{0,2},{1,3},{2,0},{3,1},{4,6},{5,7},{6,4},{7,5},{8,10},{9,11},{10,... | collective-permute-start | bytes 393224 | tf_op jit(solution)/shard_map/ppermute | solution.py:31
  38.1 6.5 %copy-start.2 = (f32[1024,512]{1,0:T(8,128)S(1)}, f32[1024,512]{1,0:T(8,128)}, u32[]{:S(2)}) copy-start(f32[1024,512]{1,0:T(8,128)} %get-tuple-element.8) | copy-start | bytes 6291460
  40.8 0.7 copy-start.8
  41.5 3.1 %copy-start.6 = (f32[512,128]{1,0:T(8,128)}, f32[512,128]{1,0:T(8,128)S(1)}, u32[]{:S(2)}) copy-start(f32[512,128]{1,0:T(8,128)S(1)} %maximum_select_fusion.1) | copy-start | bytes 786436
  41.5 3.1 %collective-permute-start.5 = (f32[512,128]{1,0:T(8,128)S(1)}, f32[512,128]{1,0:T(8,128)S(1)}, u32[]{:S(2)}, u32[]{:S(2)}) collective-permute-start(f32[512,128]{1,0:T(8,128)S(1)} %maximum_select_fusion.1), channel_id=1, source_target_pairs={{0,1},{1,0},{2,3},{3,2},{4,5},{5,4},{6,7},{7,6},{8,9},{9,8},{10,11... | collective-permute-start | bytes 786440 | tf_op jit(solution)/shard_map/ppermute | solution.py:31
  44.6 14.4 %copy-start.10 = (s32[512]{0:T(512)S(1)}, s32[512]{0:T(512)}, u32[]{:S(2)}) copy-start(s32[512]{0:T(512)} %param.6) | copy-start | bytes 6148
  44.6 14.4 %copy-start.11 = (f32[512]{0:T(512)S(1)}, f32[512]{0:T(512)}, u32[]{:S(2)}) copy-start(f32[512]{0:T(512)} %param.9) | copy-start | bytes 6148
  44.7 14.3 %copy-start.7 = (f32[512,128]{1,0:T(8,128)S(1)}, f32[512,128]{1,0:T(8,128)}, u32[]{:S(2)}) copy-start(f32[512,128]{1,0:T(8,128)} %copy-done.6) | copy-start | bytes 786436
  47.4 11.5 %all-to-all-start = ((f32[16,2,128]{2,1,0:T(2,128)}), f32[16,2,128]{2,1,0:T(2,128)S(1)}, u32[]{:S(2)}, u32[]{:S(2)}) async-start(f32[16,2,128]{2,1,0:T(2,128)} %broadcast_in_dim.15), calls=%async_computation | async-start | bytes 32768 | tf_op jit(solution)/shard_map/all_to_all | solution.py:75
  58.9 1.6 %copy-start.9 = (s32[1024,512]{1,0:T(8,128)S(1)}, s32[1024,512]{1,0:T(8,128)}, u32[]{:S(2)}) copy-start(s32[1024,512]{1,0:T(8,128)} %param.5) | copy-start | bytes 6291460
  67.5 1.6 %collective-permute-start.6 = (f32[512,128]{1,0:T(8,128)S(1)}, f32[512,128]{1,0:T(8,128)S(1)}, u32[]{:S(2)}, u32[]{:S(2)}) collective-permute-start(f32[512,128]{1,0:T(8,128)S(1)} %constant_dynamic-slice_fusion.1), channel_id=1, source_target_pairs={{0,1},{1,0},{2,3},{3,2},{4,5},{5,4},{6,7},{7,6},{8,9},{9,8},{10,11... | collective-permute-start | bytes 786440 | tf_op jit(solution)/shard_map/ppermute | solution.py:31
  69.1 5.6 %collective-permute-start.7 = (f32[256,128]{1,0:T(8,128)S(1)}, f32[256,128]{1,0:T(8,128)S(1)}, u32[]{:S(2)}, u32[]{:S(2)}) collective-permute-start(f32[256,128]{1,0:T(8,128)S(1)} %constant_dynamic-slice_fusion), channel_id=1, source_target_pairs={{0,2},{1,3},{2,0},{3,1},{4,6},{5,7},{6,4},{7,5},{8,10},{9,11},{10,... | collective-permute-start | bytes 393224 | tf_op jit(solution)/shard_map/ppermute | solution.py:31
  74.7 5.0 %collective-permute-start.8 = (f32[256,128]{1,0:T(8,128)S(1)}, f32[256,128]{1,0:T(8,128)S(1)}, u32[]{:S(2)}, u32[]{:S(2)}) collective-permute-start(f32[256,128]{1,0:T(8,128)S(1)} %dynamic-slice_add_fusion.2), channel_id=1, source_target_pairs={{0,4},{1,5},{2,6},{3,7},{4,0},{5,1},{6,2},{7,3},{8,12},{9,13},{10,... | collective-permute-start | bytes 393224 | tf_op jit(solution)/shard_map/ppermute | solution.py:31
  79.8 7.2 %collective-permute-start.9 = (f32[256,128]{1,0:T(8,128)S(1)}, f32[256,128]{1,0:T(8,128)S(1)}, u32[]{:S(2)}, u32[]{:S(2)}) collective-permute-start(f32[256,128]{1,0:T(8,128)S(1)} %add.200), channel_id=1, source_target_pairs={{0,8},{1,9},{2,10},{3,11},{4,12},{5,13},{6,14},{7,15},{8,0},{9,1},... | collective-permute-start | bytes 393224 | tf_op jit(solution)/shard_map/ppermute | solution.py:31
  87.7 5.1 %collective-permute-start.10 = (f32[256,128]{1,0:T(8,128)S(1)}, f32[256,128]{1,0:T(8,128)}, u32[]{:S(2)}, u32[]{:S(2)}) collective-permute-start(f32[256,128]{1,0:T(8,128)S(1)} %get-tuple-element.3), channel_id=1, source_target_pairs={{0,2},{1,3},{2,0},{3,1},{4,6},{5,7},{6,4},{7,5},{8,10},{9,11},{10,... | collective-permute-start | bytes 393224 | tf_op jit(solution)/shard_map/ppermute | solution.py:31
  91.0 5.9 %copy-start.3 = (f32[1024,512]{1,0:T(8,128)S(1)}, f32[1024,512]{1,0:T(8,128)}, u32[]{:S(2)}) copy-start(f32[1024,512]{1,0:T(8,128)} %get-tuple-element.6) | copy-start | bytes 6291460
  93.7 3.1 %copy-start.4 = (f32[512,128]{1,0:T(8,128)}, f32[512,128]{1,0:T(8,128)S(1)}, u32[]{:S(2)}) copy-start(f32[512,128]{1,0:T(8,128)S(1)} %maximum_select_fusion.2) | copy-start | bytes 786436
  93.8 3.1 %collective-permute-start.11 = (f32[512,128]{1,0:T(8,128)S(1)}, f32[512,128]{1,0:T(8,128)S(1)}, u32[]{:S(2)}, u32[]{:S(2)}) collective-permute-start(f32[512,128]{1,0:T(8,128)S(1)} %maximum_select_fusion.2), channel_id=1, source_target_pairs={{0,1},{1,0},{2,3},{3,2},{4,5},{5,4},{6,7},{7,6},{8,9},{9,8},{10,11... | collective-permute-start | bytes 786440 | tf_op jit(solution)/shard_map/ppermute | solution.py:31
  96.9 13.3 %copy-start.5 = (f32[512,128]{1,0:T(8,128)S(1)}, f32[512,128]{1,0:T(8,128)}, u32[]{:S(2)}) copy-start(f32[512,128]{1,0:T(8,128)} %copy-done.4) | copy-start | bytes 786436
  99.5 10.0 %all-to-all-start.1 = ((f32[16,2,128]{2,1,0:T(2,128)}), f32[16,2,128]{2,1,0:T(2,128)S(1)}, u32[]{:S(2)}, u32[]{:S(2)}) async-start(f32[16,2,128]{2,1,0:T(2,128)} %broadcast_in_dim.16), calls=%async_computation.1 | async-start | bytes 32768 | tf_op jit(solution)/shard_map/all_to_all | solution.py:75

commit v6 on v5

--- a/solution.py
+++ b/solution.py
@@ -20,10 +20,10 @@
     observed = time_bins >= start_block[None, :]
     decay = jnp.exp(-jnp.abs(linear))
     intensity = jnp.maximum(linear, 0.0) + jnp.log1p(decay) + background
-    gate_value = jnp.where(linear >= 0, 1.0, decay) / (1.0 + decay)
-    inverse = 1.0 / intensity
-    residual = jnp.where(observed, gate_value * (1.0 - count_block.astype(jnp.float32) * inverse), 0.0)
-    curvature = jnp.where(observed, gate_value * gate_value * inverse, 0.0)
+    gated = jnp.where(linear >= 0, 1.0, decay) / ((1.0 + decay) * intensity)
+    gate_value = gated * intensity
+    residual = jnp.where(observed, gate_value - count_block.astype(jnp.float32) * gated, 0.0)
+    curvature = jnp.where(observed, gate_value * gated, 0.0)
     return (residual, curvature)
 
 
@@ -69,8 +69,10 @@
 
 
 def sum_rows(values, n):
-    rows = jnp.stack([jnp.broadcast_to(v, (128,)) for v in values])
-    spread = jnp.broadcast_to(rows[None], (n,) + rows.shape)
+    row = lax.broadcasted_iota(jnp.int32, (n, len(values), 128), 1)
+    spread = jnp.zeros(row.shape, jnp.float32)
+    for k, v in enumerate(values):
+        spread = jnp.where(row == k, v, spread)
     if n > 1:
         spread = lax.all_to_all(spread, "user", 0, 0, tiled=False)
     total = jnp.sum(spread, axis=0)

time: 111 us -> 112 us (level)
  waiting for transfers between devices: 39.3 us -> 43.8 us
  local copies, waits for them, and re-layouts: 6.51 us -> 2.36 us
  other arithmetic: 6.29 us -> 7.8 us
    ppermute x12, waiting for transfers between devices: 26.5 us -> 31 us  [exchange(): return lax.ppermute(value, 'user', [(i, i ^ distance) for i in range(n)])]
    select_n x0 -> x4, other arithmetic: none -> 2.66 us  [sum_rows(): spread = jnp.where(row == k, v, spread)]
    broadcast_in_dim x2 -> x0, local copies, waits for them, and re-layouts: 1.36 us -> none  [sum_rows(): spread = jnp.broadcast_to(rows[None], (n,) + rows.shape)]
    another operation x2 -> x0, local copies, waits for them, and re-layouts: 1.34 us -> none  [sum_rows(): rows = jnp.stack([jnp.broadcast_to(v, (128,)) for v in values])]
where the time goes in v6:
time: 112 us
  waiting for transfers between devices  43.8 us (39%)
  matrix products  33.9 us (30%)
  starting transfers between devices  20.4 us (18%)
  other arithmetic  7.8 us (7%)
  between operations  3.6 us (3%)
  local copies, waits for them, and re-layouts  2.36 us (2%)
    dot_general x18, matrix products, product(): jnp.dot(left, right, precision=precision, preferred_element_type=jnp.floa...  33.9 us
    ppermute x12, waiting for transfers between devices, exchange(): return lax.ppermute(value, 'user', [(i, i ^ distance) for i in range(n)])  31 us
    all_to_all x2, waiting for transfers between devices, sum_rows(): spread = lax.all_to_all(spread, 'user', 0, 0, tiled=False)  12.8 us
    ppermute x12, starting transfers between devices, exchange(): return lax.ppermute(value, 'user', [(i, i ^ distance) for i in range(n)])  11 us
    all_to_all x2, starting transfers between devices, sum_rows(): spread = lax.all_to_all(spread, 'user', 0, 0, tiled=False)  9.36 us
    select_n x4, other arithmetic, sum_rows(): spread = jnp.where(row == k, v, spread)  2.66 us
  transfers between devices with their start and end apart: 14, of which 11 were waited for; matrix products, arithmetic and copies ran while one was open for 15% of the time, Pallas kernels for 0%

profile of v6, /device:TPU:0, one launch (start us, length us, event | category | flops | bytes accessed | tf_op | source)
XLA Modules:
  0.0 111.8 jit_solution(15479782123277713934)
XLA Ops:
  0.7 7.0 %multiply_select_fusion.1 = (f32[1024,512]{1,0:T(8,128)}, f32[1024,512]{1,0:T(8,128)S(1)}) fusion(f32[512]{0:T(512)} %param.9, s32[512]{0:T(512)} %param.6, s32[1024,512]{1,0:T(8,128)} %param.5, f32[1024,128]{1,0:T(8,128)} %param.7, f32[512,128]{1,0:T(8,128)} %param.8), kind=kOutput, calls=%fused_computation.7 | convolution fusion | flops 815267840 | bytes 7081984 | tf_op jit(solution)/shard_map/dot_general | solution.py:14
  7.7 0.0 copy-done
  7.7 1.8 %fusion.33 = f32[1024,128]{1,0:T(8,128)S(1)} fusion(f32[1024,512]{1,0:T(8,128)S(1)} %get-tuple-element.9, f32[512,128]{1,0:T(8,128)S(1)} %copy-done), kind=kOutput, calls=%fused_computation.87 | convolution fusion | flops 805306368 | bytes 2883584 | tf_op jit(solution)/shard_map/dot_general | solution.py:14
  9.5 0.8 constant_dynamic-slice_fusion.3
  10.3 0.4 collective-permute-start
  10.7 0.0 copy-done.4
  10.8 4.1 %multiply_reduce_fusion.1 = (f32[]{:T(128)}, f32[512,128]{1,0:T(8,128)S(1)}) fusion(f32[1024,512]{1,0:T(8,128)S(1)} %get-tuple-element.9, f32[1024,128]{1,0:T(8,128)S(1)} %copy-done.1), kind=kOutput, calls=%fused_computation.46 | convolution fusion | flops 805437440 | bytes 2883588 | tf_op jit(solution)/shard_map/dot_general | solution.py:14
  14.8 0.0 collective-permute-done
  14.8 1.0 dynamic-slice_add_fusion.1
  15.9 2.6 %collective-permute-start.1 = (f32[256,128]{1,0:T(8,128)S(1)}, f32[256,128]{1,0:T(8,128)S(1)}, u32[]{:S(2)}, u32[]{:S(2)}) collective-permute-start(f32[256,128]{1,0:T(8,128)S(1)} %constant_dynamic-slice_fusion.2), channel_id=1, source_target_pairs={{0,2},{1,3},{2,0},{3,1},{4,6},{5,7},{6,4},{7,5},{8,10},{9,11},{10,... | collective-permute-start | bytes 393224 | tf_op jit(solution)/shard_map/ppermute | solution.py:31
  18.5 0.6 fusion.12
  19.0 3.5 %collective-permute-done.1 = f32[256,128]{1,0:T(8,128)S(1)} collective-permute-done((f32[256,128]{1,0:T(8,128)S(1)}, f32[256,128]{1,0:T(8,128)S(1)}, u32[]{:S(2)}, u32[]{:S(2)}) %collective-permute-start.1) | collective-permute-done | bytes 131104 | tf_op jit(solution)/shard_map/ppermute | solution.py:31
  22.6 1.9 %collective-permute-start.2 = (f32[256,128]{1,0:T(8,128)S(1)}, f32[256,128]{1,0:T(8,128)S(1)}, u32[]{:S(2)}, u32[]{:S(2)}) collective-permute-start(f32[256,128]{1,0:T(8,128)S(1)} %dynamic-slice_add_fusion.3), channel_id=1, source_target_pairs={{0,4},{1,5},{2,6},{3,7},{4,0},{5,1},{6,2},{7,3},{8,12},{9,13},{10,... | collective-permute-start | bytes 393224 | tf_op jit(solution)/shard_map/ppermute | solution.py:31
  24.5 0.4 fusion.18
  24.9 3.1 %collective-permute-done.2 = f32[256,128]{1,0:T(8,128)S(1)} collective-permute-done((f32[256,128]{1,0:T(8,128)S(1)}, f32[256,128]{1,0:T(8,128)S(1)}, u32[]{:S(2)}, u32[]{:S(2)}) %collective-permute-start.2) | collective-permute-done | bytes 131104 | tf_op jit(solution)/shard_map/ppermute | solution.py:31
  28.0 2.7 %collective-permute-start.3 = (f32[256,128]{1,0:T(8,128)S(1)}, f32[256,128]{1,0:T(8,128)S(1)}, u32[]{:S(2)}, u32[]{:S(2)}) collective-permute-start(f32[256,128]{1,0:T(8,128)S(1)} %add.177), channel_id=1, source_target_pairs={{0,8},{1,9},{2,10},{3,11},{4,12},{5,13},{6,14},{7,15},{8,0},{9,1},... | collective-permute-start | bytes 393224 | tf_op jit(solution)/shard_map/ppermute | solution.py:31
  30.7 0.4 fusion.20
  31.1 5.1 %collective-permute-done.3 = f32[256,128]{1,0:T(8,128)S(1)} collective-permute-done((f32[256,128]{1,0:T(8,128)S(1)}, f32[256,128]{1,0:T(8,128)S(1)}, u32[]{:S(2)}, u32[]{:S(2)}) %collective-permute-start.3) | collective-permute-done | bytes 131104 | tf_op jit(solution)/shard_map/ppermute | solution.py:31
  36.2 0.6 multiply_reduce_fusion.3
  36.8 1.3 %collective-permute-start.4 = (f32[256,128]{1,0:T(8,128)S(1)}, f32[256,128]{1,0:T(8,128)S(1)}, u32[]{:S(2)}, u32[]{:S(2)}) collective-permute-start(f32[256,128]{1,0:T(8,128)S(1)} %get-tuple-element.5), channel_id=1, source_target_pairs={{0,2},{1,3},{2,0},{3,1},{4,6},{5,7},{6,4},{7,5},{8,10},{9,11},{10,... | collective-permute-start | bytes 393224 | tf_op jit(solution)/shard_map/ppermute | solution.py:31
  39.4 1.6 %fusion.7 = f32[512]{0:T(512)S(1)} fusion(f32[256,512]{1,0:T(8,128)S(1)} %fusion.20, f32[256,128]{1,0:T(8,128)S(1)} %get-tuple-element.5, f32[512,128]{1,0:T(8,128)S(1)} %copy-done, f32[1024,512]{1,0:T(8,128)} %get-tuple-element.8, s32[]{:T(128)S(6)} %select_n.142), kind=kOutput, calls=%fused_computation.30 | convolution fusion | flops 101187072 | bytes 1443844 | tf_op jit(solution)/shard_map/dot_general | solution.py:14
  41.0 0.7 collective-permute-done.4
  41.8 0.1 collective-permute-start.5
  41.9 1.5 %fusion.6 = f32[512]{0:T(512)S(1)} fusion(f32[256,512]{1,0:T(8,128)S(1)} %fusion.18, f32[256,128]{1,0:T(8,128)S(1)} %collective-permute-done.4, f32[512,128]{1,0:T(8,128)S(1)} %copy-done, f32[1024,512]{1,0:T(8,128)} %get-tuple-element.8, s32[]{:T(128)S(6)} %select_n.148), kind=kOutput, calls=%fused_computation.28 | convolution fusion | flops 101187072 | bytes 1443844 | tf_op jit(solution)/shard_map/dot_general | solution.py:14
  43.3 0.0 copy-start.7
  43.4 0.0 copy-start.8
  43.4 0.0 collective-permute-done.5
  43.4 0.0 copy-done.2
  43.4 0.6 fusion.2
  44.0 0.6 add_reduce_fusion.1
  44.6 1.3 %broadcast_select_fusion.1 = f32[16,2,128]{2,1,0:T(2,128)} fusion(pred[2]{0:T(512)(128)(4,1)S(1)} %iota_compare_fusion.1, f32[]{:T(128)} %add_reduce_fusion.1, f32[2]{0:T(128)S(1)} %compare_select_fusion.1), kind=kLoop, calls=%fused_computation.67 | loop fusion | flops 4096 | bytes 16398 | tf_op jit(solution)/shard_map/jit(_where)/select_n | solution.py:75
  46.0 5.9 %all-to-all-start = ((f32[16,2,128]{2,1,0:T(2,128)}), f32[16,2,128]{2,1,0:T(2,128)S(1)}, u32[]{:S(2)}, u32[]{:S(2)}) async-start(f32[16,2,128]{2,1,0:T(2,128)} %broadcast_select_fusion.1), calls=%async_computation | async-start | bytes 32768 | tf_op jit(solution)/shard_map/all_to_all | solution.py:77
  51.8 6.3 %all-to-all-done = f32[16,2,128]{2,1,0:T(2,128)S(1)} async-done(((f32[16,2,128]{2,1,0:T(2,128)}), f32[16,2,128]{2,1,0:T(2,128)S(1)}, u32[]{:S(2)}, u32[]{:S(2)}) %all-to-all-start) | async-done | bytes 16416 | tf_op jit(solution)/shard_map/all_to_all | solution.py:77
  58.2 0.1 fusion.9
  58.3 0.0 copy-done.7
  58.3 1.4 %copy-done.6 = s32[1024,512]{1,0:T(8,128)S(1)} copy-done((s32[1024,512]{1,0:T(8,128)S(1)}, s32[1024,512]{1,0:T(8,128)}, u32[]{:S(2)}) %copy-start.6) | copy-done | bytes 2097176
  59.8 5.1 %multiply_select_fusion = (f32[1024,512]{1,0:T(8,128)}, f32[1024,512]{1,0:T(8,128)S(1)}) fusion(f32[512]{0:T(512)S(1)} %copy-done.7, s32[512]{0:T(512)S(1)} %copy-done.8, s32[1024,512]{1,0:T(8,128)S(1)} %copy-done.6, f32[1024,128]{1,0:T(8,128)S(1)} %fusion.9, f32[512,128]{1,0:T(8,128)S(1)} %multiply_subtract_fusion.1), kind=kOutput, calls=%fused_computation.1 | convolution fusion | flops 815267840 | bytes 7081984 | tf_op jit(solution)/shard_map/dot_general | solution.py:14
  64.9 1.8 %fusion.34 = f32[1024,128]{1,0:T(8,128)S(1)} fusion(f32[1024,512]{1,0:T(8,128)S(1)} %get-tuple-element.7, f32[512,128]{1,0:T(8,128)S(1)} %multiply_subtract_fusion.1), kind=kOutput, calls=%fused_computation.88 | convolution fusion | flops 805306368 | bytes 2883584 | tf_op jit(solution)/shard_map/dot_general | solution.py:14
  66.7 0.1 collective-permute-start.6
  66.8 4.1 %multiply_reduce_fusion = (f32[]{:T(128)}, f32[512,128]{1,0:T(8,128)S(1)}) fusion(f32[1024,512]{1,0:T(8,128)S(1)} %get-tuple-element.7, f32[1024,128]{1,0:T(8,128)S(1)} %fusion.9), kind=kOutput, calls=%fused_computation.41 | convolution fusion | flops 805437440 | bytes 2883588 | tf_op jit(solution)/shard_map/dot_general | solution.py:14
  70.9 0.0 collective-permute-done.6
  70.9 0.6 collective-permute-start.7
  71.6 0.6 fusion.10
  72.1 4.7 %collective-permute-done.7 = f32[256,128]{1,0:T(8,128)S(1)} collective-permute-done((f32[256,128]{1,0:T(8,128)S(1)}, f32[256,128]{1,0:T(8,128)S(1)}, u32[]{:S(2)}, u32[]{:S(2)}) %collective-permute-start.7) | collective-permute-done | bytes 131104 | tf_op jit(solution)/shard_map/ppermute | solution.py:31
  76.9 0.6 collective-permute-start.8
  77.5 0.4 fusion.14
  77.8 4.2 %collective-permute-done.8 = f32[256,128]{1,0:T(8,128)S(1)} collective-permute-done((f32[256,128]{1,0:T(8,128)S(1)}, f32[256,128]{1,0:T(8,128)S(1)}, u32[]{:S(2)}, u32[]{:S(2)}) %collective-permute-start.8) | collective-permute-done | bytes 131104 | tf_op jit(solution)/shard_map/ppermute | solution.py:31
  82.1 0.5 collective-permute-start.9
  82.6 0.4 fusion.16
  83.0 6.9 %collective-permute-done.9 = f32[256,128]{1,0:T(8,128)S(1)} collective-permute-done((f32[256,128]{1,0:T(8,128)S(1)}, f32[256,128]{1,0:T(8,128)S(1)}, u32[]{:S(2)}, u32[]{:S(2)}) %collective-permute-start.9) | collective-permute-done | bytes 131104 | tf_op jit(solution)/shard_map/ppermute | solution.py:31
  89.9 0.6 multiply_reduce_fusion.2
  91.2 0.2 collective-permute-start.10
  92.0 1.6 %fusion.5 = f32[512]{0:T(512)S(1)} fusion(f32[256,512]{1,0:T(8,128)S(1)} %fusion.16, f32[256,128]{1,0:T(8,128)S(1)} %get-tuple-element.3, f32[512,128]{1,0:T(8,128)S(1)} %multiply_subtract_fusion.1, f32[1024,512]{1,0:T(8,128)} %get-tuple-element.6, s32[]{:T(128)S(6)} %select_n.142), kind=kOutput, calls=%fused_computation.26 | convolution fusion | flops 101187072 | bytes 1443844 | tf_op jit(solution)/shard_map/dot_general | solution.py:14
  93.6 2.6 %collective-permute-done.10 = f32[256,128]{1,0:T(8,128)S(1)} collective-permute-done((f32[256,128]{1,0:T(8,128)S(1)}, f32[256,128]{1,0:T(8,128)S(1)}, u32[]{:S(2)}, u32[]{:S(2)}) %collective-permute-start.10) | collective-permute-done | bytes 131104 | tf_op jit(solution)/shard_map/ppermute | solution.py:31
  96.2 0.1 collective-permute-start.11
  96.3 1.5 %fusion.4 = f32[512]{0:T(512)S(1)} fusion(f32[256,512]{1,0:T(8,128)S(1)} %fusion.14, f32[256,128]{1,0:T(8,128)S(1)} %collective-permute-done.10, f32[512,128]{1,0:T(8,128)S(1)} %multiply_subtract_fusion.1, f32[1024,512]{1,0:T(8,128)} %get-tuple-element.6, s32[]{:T(128)S(6)} %select_n.148), kind=kOutput, calls=%fused_computation.24 | convolution fusion | flops 101187072 | bytes 1443844 | tf_op jit(solution)/shard_map/dot_general | solution.py:14
  97.8 0.1 collective-permute-done.11
  97.8 0.6 fusion.3
  98.5 0.6 add_reduce_fusion
  99.1 1.3 %broadcast_select_fusion = f32[16,2,128]{2,1,0:T(2,128)} fusion(pred[2]{0:T(512)(128)(4,1)S(1)} %iota_compare_fusion.1, f32[]{:T(128)} %add_reduce_fusion, f32[2]{0:T(128)S(1)} %compare_select_fusion), kind=kLoop, calls=%fused_computation.66 | loop fusion | flops 4096 | bytes 16398 | tf_op jit(solution)/shard_map/jit(_where)/select_n | solution.py:75
  100.4 3.5 %all-to-all-start.1 = ((f32[16,2,128]{2,1,0:T(2,128)}), f32[16,2,128]{2,1,0:T(2,128)S(1)}, u32[]{:S(2)}, u32[]{:S(2)}) async-start(f32[16,2,128]{2,1,0:T(2,128)} %broadcast_select_fusion), calls=%async_computation.1 | async-start | bytes 32768 | tf_op jit(solution)/shard_map/all_to_all | solution.py:77
  103.9 6.5 %all-to-all-done.1 = f32[16,2,128]{2,1,0:T(2,128)S(1)} async-done(((f32[16,2,128]{2,1,0:T(2,128)}), f32[16,2,128]{2,1,0:T(2,128)S(1)}, u32[]{:S(2)}, u32[]{:S(2)}) %all-to-all-start.1) | async-done | bytes 16416 | tf_op jit(solution)/shard_map/all_to_all | solution.py:77
  110.4 0.7 multiply_subtract_fusion
  111.1 0.6 dynamic-slice_subtract_fusion
  (29 shorter events, 0.3 us)
Async XLA Ops:
  0.6 7.0 %copy-start = (f32[512,128]{1,0:T(8,128)S(1)}, f32[512,128]{1,0:T(8,128)}, u32[]{:S(2)}) copy-start(f32[512,128]{1,0:T(8,128)} %param.8) | copy-start | bytes 786436
  7.7 3.1 %copy-start.1 = (f32[1024,128]{1,0:T(8,128)S(1)}, f32[1024,128]{1,0:T(8,128)}, u32[]{:S(2)}) copy-start(f32[1024,128]{1,0:T(8,128)} %param.7) | copy-start | bytes 1572868
  9.5 1.3 %copy-start.4 = (f32[1024,128]{1,0:T(8,128)}, f32[1024,128]{1,0:T(8,128)S(1)}, u32[]{:S(2)}) copy-start(f32[1024,128]{1,0:T(8,128)S(1)} %fusion.33) | copy-start | bytes 1572868
  10.3 4.5 %collective-permute-start = (f32[512,128]{1,0:T(8,128)}, f32[512,128]{1,0:T(8,128)}, u32[]{:S(2)}, u32[]{:S(2)}) collective-permute-start(f32[512,128]{1,0:T(8,128)} %constant_dynamic-slice_fusion.3), channel_id=1, source_target_pairs={{0,1},{1,0},{2,3},{3,2},{4,5},{5,4},{6,7},{7,6},{8,9},{9,8},{10,11... | collective-permute-start | bytes 786440 | tf_op jit(solution)/shard_map/ppermute | solution.py:31
  10.8 4.1 %copy-start.5 = (f32[1024,128]{1,0:T(8,128)S(1)}, f32[1024,128]{1,0:T(8,128)}, u32[]{:S(2)}) copy-start(f32[1024,128]{1,0:T(8,128)} %copy-done.4) | copy-start | bytes 1572868
  15.9 6.7 %collective-permute-start.1 = (f32[256,128]{1,0:T(8,128)S(1)}, f32[256,128]{1,0:T(8,128)S(1)}, u32[]{:S(2)}, u32[]{:S(2)}) collective-permute-start(f32[256,128]{1,0:T(8,128)S(1)} %constant_dynamic-slice_fusion.2), channel_id=1, source_target_pairs={{0,2},{1,3},{2,0},{3,1},{4,6},{5,7},{6,4},{7,5},{8,10},{9,11},{10,... | collective-permute-start | bytes 393224 | tf_op jit(solution)/shard_map/ppermute | solution.py:31
  22.6 5.4 %collective-permute-start.2 = (f32[256,128]{1,0:T(8,128)S(1)}, f32[256,128]{1,0:T(8,128)S(1)}, u32[]{:S(2)}, u32[]{:S(2)}) collective-permute-start(f32[256,128]{1,0:T(8,128)S(1)} %dynamic-slice_add_fusion.3), channel_id=1, source_target_pairs={{0,4},{1,5},{2,6},{3,7},{4,0},{5,1},{6,2},{7,3},{8,12},{9,13},{10,... | collective-permute-start | bytes 393224 | tf_op jit(solution)/shard_map/ppermute | solution.py:31
  28.0 8.2 %collective-permute-start.3 = (f32[256,128]{1,0:T(8,128)S(1)}, f32[256,128]{1,0:T(8,128)S(1)}, u32[]{:S(2)}, u32[]{:S(2)}) collective-permute-start(f32[256,128]{1,0:T(8,128)S(1)} %add.177), channel_id=1, source_target_pairs={{0,8},{1,9},{2,10},{3,11},{4,12},{5,13},{6,14},{7,15},{8,0},{9,1},... | collective-permute-start | bytes 393224 | tf_op jit(solution)/shard_map/ppermute | solution.py:31
  36.8 5.0 %collective-permute-start.4 = (f32[256,128]{1,0:T(8,128)S(1)}, f32[256,128]{1,0:T(8,128)S(1)}, u32[]{:S(2)}, u32[]{:S(2)}) collective-permute-start(f32[256,128]{1,0:T(8,128)S(1)} %get-tuple-element.5), channel_id=1, source_target_pairs={{0,2},{1,3},{2,0},{3,1},{4,6},{5,7},{6,4},{7,5},{8,10},{9,11},{10,... | collective-permute-start | bytes 393224 | tf_op jit(solution)/shard_map/ppermute | solution.py:31
  39.4 4.0 %copy-start.2 = (f32[1024,512]{1,0:T(8,128)S(1)}, f32[1024,512]{1,0:T(8,128)}, u32[]{:S(2)}) copy-start(f32[1024,512]{1,0:T(8,128)} %get-tuple-element.8) | copy-start | bytes 6291460
  41.8 1.6 %collective-permute-start.5 = (f32[512,128]{1,0:T(8,128)S(1)}, f32[512,128]{1,0:T(8,128)S(1)}, u32[]{:S(2)}, u32[]{:S(2)}) collective-permute-start(f32[512,128]{1,0:T(8,128)S(1)} %maximum_select_fusion.1), channel_id=1, source_target_pairs={{0,1},{1,0},{2,3},{3,2},{4,5},{5,4},{6,7},{7,6},{8,9},{9,8},{10,11... | collective-permute-start | bytes 786440 | tf_op jit(solution)/shard_map/ppermute | solution.py:31
  43.3 15.0 %copy-start.7 = (f32[512]{0:T(512)S(1)}, f32[512]{0:T(512)}, u32[]{:S(2)}) copy-start(f32[512]{0:T(512)} %param.9) | copy-start | bytes 6148
  43.4 15.0 %copy-start.8 = (s32[512]{0:T(512)S(1)}, s32[512]{0:T(512)}, u32[]{:S(2)}) copy-start(s32[512]{0:T(512)} %param.6) | copy-start | bytes 6148
  46.0 12.2 %all-to-all-start = ((f32[16,2,128]{2,1,0:T(2,128)}), f32[16,2,128]{2,1,0:T(2,128)S(1)}, u32[]{:S(2)}, u32[]{:S(2)}) async-start(f32[16,2,128]{2,1,0:T(2,128)} %broadcast_select_fusion.1), calls=%async_computation | async-start | bytes 32768 | tf_op jit(solution)/shard_map/all_to_all | solution.py:77
  58.2 1.6 %copy-start.6 = (s32[1024,512]{1,0:T(8,128)S(1)}, s32[1024,512]{1,0:T(8,128)}, u32[]{:S(2)}) copy-start(s32[1024,512]{1,0:T(8,128)} %param.5) | copy-start | bytes 6291460
  66.7 4.2 %collective-permute-start.6 = (f32[512,128]{1,0:T(8,128)S(1)}, f32[512,128]{1,0:T(8,128)S(1)}, u32[]{:S(2)}, u32[]{:S(2)}) collective-permute-start(f32[512,128]{1,0:T(8,128)S(1)} %constant_dynamic-slice_fusion.1), channel_id=1, source_target_pairs={{0,1},{1,0},{2,3},{3,2},{4,5},{5,4},{6,7},{7,6},{8,9},{9,8},{10,11... | collective-permute-start | bytes 786440 | tf_op jit(solution)/shard_map/ppermute | solution.py:31
  70.9 6.0 %collective-permute-start.7 = (f32[256,128]{1,0:T(8,128)S(1)}, f32[256,128]{1,0:T(8,128)S(1)}, u32[]{:S(2)}, u32[]{:S(2)}) collective-permute-start(f32[256,128]{1,0:T(8,128)S(1)} %constant_dynamic-slice_fusion), channel_id=1, source_target_pairs={{0,2},{1,3},{2,0},{3,1},{4,6},{5,7},{6,4},{7,5},{8,10},{9,11},{10,... | collective-permute-start | bytes 393224 | tf_op jit(solution)/shard_map/ppermute | solution.py:31
  76.9 5.2 %collective-permute-start.8 = (f32[256,128]{1,0:T(8,128)S(1)}, f32[256,128]{1,0:T(8,128)S(1)}, u32[]{:S(2)}, u32[]{:S(2)}) collective-permute-start(f32[256,128]{1,0:T(8,128)S(1)} %dynamic-slice_add_fusion.2), channel_id=1, source_target_pairs={{0,4},{1,5},{2,6},{3,7},{4,0},{5,1},{6,2},{7,3},{8,12},{9,13},{10,... | collective-permute-start | bytes 393224 | tf_op jit(solution)/shard_map/ppermute | solution.py:31
  82.1 7.8 %collective-permute-start.9 = (f32[256,128]{1,0:T(8,128)S(1)}, f32[256,128]{1,0:T(8,128)S(1)}, u32[]{:S(2)}, u32[]{:S(2)}) collective-permute-start(f32[256,128]{1,0:T(8,128)S(1)} %add.196), channel_id=1, source_target_pairs={{0,8},{1,9},{2,10},{3,11},{4,12},{5,13},{6,14},{7,15},{8,0},{9,1},... | collective-permute-start | bytes 393224 | tf_op jit(solution)/shard_map/ppermute | solution.py:31
  91.2 5.0 %collective-permute-start.10 = (f32[256,128]{1,0:T(8,128)S(1)}, f32[256,128]{1,0:T(8,128)S(1)}, u32[]{:S(2)}, u32[]{:S(2)}) collective-permute-start(f32[256,128]{1,0:T(8,128)S(1)} %get-tuple-element.3), channel_id=1, source_target_pairs={{0,2},{1,3},{2,0},{3,1},{4,6},{5,7},{6,4},{7,5},{8,10},{9,11},{10,... | collective-permute-start | bytes 393224 | tf_op jit(solution)/shard_map/ppermute | solution.py:31
  92.0 5.8 %copy-start.3 = (f32[1024,512]{1,0:T(8,128)S(1)}, f32[1024,512]{1,0:T(8,128)}, u32[]{:S(2)}) copy-start(f32[1024,512]{1,0:T(8,128)} %get-tuple-element.6) | copy-start | bytes 6291460
  96.2 1.6 %collective-permute-start.11 = (f32[512,128]{1,0:T(8,128)S(1)}, f32[512,128]{1,0:T(8,128)S(1)}, u32[]{:S(2)}, u32[]{:S(2)}) collective-permute-start(f32[512,128]{1,0:T(8,128)S(1)} %maximum_select_fusion.2), channel_id=1, source_target_pairs={{0,1},{1,0},{2,3},{3,2},{4,5},{5,4},{6,7},{7,6},{8,9},{9,8},{10,11... | collective-permute-start | bytes 786440 | tf_op jit(solution)/shard_map/ppermute | solution.py:31
  100.4 10.0 %all-to-all-start.1 = ((f32[16,2,128]{2,1,0:T(2,128)}), f32[16,2,128]{2,1,0:T(2,128)S(1)}, u32[]{:S(2)}, u32[]{:S(2)}) async-start(f32[16,2,128]{2,1,0:T(2,128)} %broadcast_select_fusion), calls=%async_computation.1 | async-start | bytes 32768 | tf_op jit(solution)/shard_map/all_to_all | solution.py:77

commit v7 on v6

--- a/solution.py
+++ b/solution.py
@@ -14,9 +14,9 @@
     return jnp.dot(left, right, precision=precision, preferred_element_type=jnp.float32)
 
 
-def local_terms(time_factor, user_block, base_block, count_block, start_block):
+def local_terms(time_factor, user_block, base_block, count_block, start_block, first_bin=0):
     linear = product(time_factor, user_block.T) + base_block[None, :]
-    time_bins = jnp.arange(time_factor.shape[0], dtype=jnp.int32)[:, None]
+    time_bins = first_bin + jnp.arange(time_factor.shape[0], dtype=jnp.int32)[:, None]
     observed = time_bins >= start_block[None, :]
     decay = jnp.exp(-jnp.abs(linear))
     intensity = jnp.maximum(linear, 0.0) + jnp.log1p(decay) + background
@@ -31,21 +31,18 @@
     return lax.ppermute(value, "user", [(i, i ^ distance) for i in range(n)])
 
 
-def sum_over_users(partial, n):
-    me = lax.axis_index("user")
-    if n == 1:
-        return partial, [(partial, 0)], jnp.sum(partial * partial)
-    if n & (n - 1) or partial.shape[0] % n:
-        total = lax.psum(partial, "user")
-        return total, [(total, 0)], jnp.where(me == 0, jnp.sum(total * total), 0.0)
+def distances_of(n):
     distances = []
     d = 1
     while d < n:
         distances.append(d)
         d *= 2
-    halving, butterfly = distances[:2], distances[2:]
-    block, offset = partial, 0
-    for d in halving:
+    return distances
+
+
+def finish_sum(block, offset, n, halving, butterfly):
+    me = lax.axis_index("user")
+    for d in halving[1:]:
         half = block.shape[0] // 2
         upper = (me // d) % 2
         keep = lax.dynamic_slice_in_dim(block, upper * half, half, 0)
@@ -54,9 +51,9 @@
         block = keep + exchange(send, n, d)
     for d in butterfly:
         block = block + exchange(block, n, d)
-    share = jnp.where(me < 4, jnp.sum(block * block), 0.0)
+    share = jnp.where(me < 2 ** len(halving), jnp.sum(block * block), 0.0)
     pieces = [(block, offset)]
-    for d in reversed(halving):
+    for d in reversed(halving[1:]):
         rows = block.shape[0]
         other = exchange(block, n, d)
         upper = (me // d) % 2
@@ -79,24 +76,70 @@
     return [total[k:k + 1] for k in range(len(values))]
 
 
+def bending_of(pieces, time_factor, user_factor, grad_user):
+    bending = jnp.zeros((user_factor.shape[0],), jnp.float32)
+    for piece, first, weight in pieces:
+        rows = piece.shape[0]
+        tangent_image = product(piece, user_factor.T, lax.Precision.HIGH) + product(
+            lax.dynamic_slice_in_dim(time_factor, first, rows, 0), grad_user.T, lax.Precision.HIGH
+        )
+        bending = bending + jnp.sum(weight * tangent_image * tangent_image, axis=0)
+    return jnp.sum(bending)
+
+
+def gradients_split(n, counts, first_bin, time_factor, user_factor, user_base):
+    me = lax.axis_index("user")
+    distances = distances_of(n)
+    halving, butterfly = distances[:2], distances[2:]
+    half = time_factor.shape[0] // 2
+    upper = me % 2
+    sent_first, kept_first = (1 - upper) * half, upper * half
+
+    def terms(first):
+        rows = lax.dynamic_slice_in_dim(time_factor, first, half, 0)
+        block = lax.dynamic_slice_in_dim(counts, first, half, 0)
+        residual, curvature = local_terms(rows, user_factor, user_base, block, first_bin, first)
+        return rows, residual, curvature
+
+    sent_rows, sent_residual, sent_curvature = terms(sent_first)
+    arrived = exchange(product(sent_residual, user_factor), n, 1)
+    kept_rows, kept_residual, kept_curvature = terms(kept_first)
+    grad_user = product(sent_residual.T, sent_rows) + product(kept_residual.T, kept_rows)
+    kept, pieces, time_norm = finish_sum(
+        product(kept_residual, user_factor) + arrived, kept_first, n, halving, butterfly
+    )
+    other = exchange(kept, n, 1)
+    grad_whole = jnp.where(upper == 0, jnp.concatenate([kept, other]), jnp.concatenate([other, kept]))
+    weighted = [
+        (piece, first, lax.dynamic_slice_in_dim(kept_curvature, first - kept_first, piece.shape[0], 0))
+        for piece, first in pieces
+    ]
+    weighted.append((other, sent_first, sent_curvature))
+    return grad_user, grad_whole, time_norm, bending_of(weighted, time_factor, user_factor, grad_user)
+
+
+def gradients_whole(n, counts, first_bin, time_factor, user_factor, user_base):
+    me = lax.axis_index("user")
+    residual, curvature = local_terms(time_factor, user_factor, user_base, counts, first_bin)
+    grad_user = product(residual.T, time_factor)
+    grad_whole = lax.psum(product(residual, user_factor), "user") if n > 1 else product(residual, user_factor)
+    time_norm = jnp.where(me == 0, jnp.sum(grad_whole * grad_whole), 0.0)
+    bending = bending_of([(grad_whole, 0, curvature)], time_factor, user_factor, grad_user)
+    return grad_user, grad_whole, time_norm, bending
+
+
 def body(n, counts, first_bin, time_factor, user_factor, user_base):
     shard_rows = time_factor.shape[0] // n
     offset = lax.axis_index("user") * shard_rows
+    split = n >= 4 and not n & (n - 1) and time_factor.shape[0] % n == 0
+    gradients = gradients_split if split else gradients_whole
     mine_rows = time_factor
     for sweep in range(SWEEPS):
-        residual, curvature = local_terms(time_factor, user_factor, user_base, counts, first_bin)
-        grad_user = product(residual.T, time_factor)
-        grad_whole, pieces, time_norm = sum_over_users(product(residual, user_factor), n)
+        grad_user, grad_whole, time_norm, bending = gradients(
+            n, counts, first_bin, time_factor, user_factor, user_base
+        )
         user_norm = jnp.sum(grad_user * grad_user)
-        bending = jnp.zeros((user_factor.shape[0],), jnp.float32)
-        for piece, first in pieces:
-            rows = piece.shape[0]
-            tangent_image = product(piece, user_factor.T, lax.Precision.HIGH) + product(
-                lax.dynamic_slice_in_dim(time_factor, first, rows, 0), grad_user.T, lax.Precision.HIGH
-            )
-            weight = lax.dynamic_slice_in_dim(curvature, first, rows, 0)
-            bending = bending + jnp.sum(weight * tangent_image * tangent_image, axis=0)
-        norm_total, bend_total = sum_rows([user_norm + time_norm, jnp.sum(bending)], n)
+        norm_total, bend_total = sum_rows([user_norm + time_norm, bending], n)
         relax_step = norm_total / (bend_total + damping * norm_total)
         user_factor = user_factor - relax_step * grad_user
         if sweep + 1 < SWEEPS:

time: 112 us -> 116 us (1.036)
  matrix products: 33.9 us -> 40.5 us
  local copies, waits for them, and re-layouts: 2.36 us -> 0.52 us
  waiting for transfers between devices: 43.8 us -> 42.3 us
    dot_general x18 -> x24, matrix products: 33.9 us -> 40.5 us  [product(): jnp.dot(left, right, precision=precision, preferred_element_type=jnp.floa...]
    ppermute x12, waiting for transfers between devices: 31 us -> 29.4 us  [exchange(): return lax.ppermute(value, 'user', [(i, i ^ distance) for i in range(n)])]
  transfers between devices with their start and end apart: 14 -> 14, of which waited for: 11 -> 10; matrix products, arithmetic and copies ran while one was open for 15% -> 15% of each run, Pallas kernels for 0% -> 0%
where the time goes in v7:
time: 116 us; the launch traced here: 115 us
  waiting for transfers between devices  42.3 us (36%)
  matrix products  40.5 us (35%)
  starting transfers between devices  20.3 us (18%)
  other arithmetic  7.81 us (7%)
  between operations  3.54 us (3%)
    dot_general x24, matrix products, product(): jnp.dot(left, right, precision=precision, preferred_element_type=jnp.floa...  40.5 us
    ppermute x12, waiting for transfers between devices, exchange(): return lax.ppermute(value, 'user', [(i, i ^ distance) for i in range(n)])  29.4 us
    all_to_all x2, waiting for transfers between devices, sum_rows(): spread = lax.all_to_all(spread, 'user', 0, 0, tiled=False)  12.9 us
    ppermute x12, starting transfers between devices, exchange(): return lax.ppermute(value, 'user', [(i, i ^ distance) for i in range(n)])  11.2 us
    all_to_all x2, starting transfers between devices, sum_rows(): spread = lax.all_to_all(spread, 'user', 0, 0, tiled=False)  9.16 us
    select_n x4, other arithmetic, sum_rows(): spread = jnp.where(row == k, v, spread)  2.66 us
  transfers between devices with their start and end apart: 14, of which 10 were waited for; matrix products, arithmetic and copies ran while one was open for 15% of the time, Pallas kernels for 0%

profile of v7, /device:TPU:0, one launch (start us, length us, event | category | flops | bytes accessed | tf_op | source)
XLA Modules:
  0.0 115.0 jit_solution(14124335116994747201)
XLA Ops:
  0.7 2.0 %convolution_add_fusion.4 = f32[512,512]{1,0:T(8,128)S(1)} fusion(f32[512,128]{1,0:T(8,128)} %param.8, f32[512]{0:T(512)} %param.9, f32[1024,128]{1,0:T(8,128)} %param.7, s32[]{:T(128)S(6)} %select_n.157), kind=kOutput, calls=%fused_computation.14 | convolution fusion | flops 402915328 | bytes 1574916 | tf_op jit(solution)/shard_map/dot_general | solution.py:14
  2.7 0.0 copy-start
  2.7 0.0 copy-start.1
  2.7 5.9 %compare_select_fusion.6 = (f32[512,512]{1,0:T(8,128)S(1)}, f32[512,512]{1,0:T(8,128)S(1)}, f32[512,512]{1,0:T(8,128)}) fusion(s32[1024,512]{1,0:T(8,128)} %param.5, s32[]{:T(128)S(6)} %select_n.150, s32[512]{0:T(512)} %param.6, s32[512]{0:T(512)S(1)} %get-tuple-element.17, s32[]{:T(128)S(6)} %select_n.157, f32[512,512]{1,0:T(8,128)S(1)} %convolution_add_fusion.4, ...), kind=kOutput, calls=%fused_computation.6 | convolution fusion | flops 411828224 | bytes 6825472 | tf_op jit(solution)/shard_map/dot_general | solution.py:14
  8.6 1.7 %fusion.53 = f32[512,128]{1,0:T(8,128)} fusion(f32[512,512]{1,0:T(8,128)S(1)} %get-tuple-element.9, f32[512,128]{1,0:T(8,128)S(1)} %copy-done), kind=kOutput, calls=%fused_computation.122 | convolution fusion | flops 402653184 | bytes 1572864 | tf_op jit(solution)/shard_map/dot_general | solution.py:14
  10.3 0.5 collective-permute-start
  10.7 1.8 %fusion.23 = f32[512,128]{1,0:T(8,128)S(1)} fusion(f32[512,512]{1,0:T(8,128)S(1)} %get-tuple-element.9, f32[1024,128]{1,0:T(8,128)S(1)} %copy-done.1, s32[]{:T(128)S(6)} %select_n.157), kind=kOutput, calls=%fused_computation.74 | convolution fusion | flops 402653184 | bytes 1572868 | tf_op jit(solution)/shard_map/dot_general | solution.py:14
  12.6 2.4 %multiply_reduce_fusion.1 = (f32[]{:T(128)}, f32[512,128]{1,0:T(8,128)S(1)}) fusion(f32[512,128]{1,0:T(8,128)S(1)} %fusion.23, f32[512,512]{1,0:T(8,128)S(1)} %get-tuple-element.8, f32[1024,128]{1,0:T(8,128)S(1)} %copy-done.1, s32[]{:T(128)S(6)} %select_n.150), kind=kOutput, calls=%fused_computation.62 | convolution fusion | flops 402849792 | bytes 1835016 | tf_op jit(solution)/shard_map/dot_general | solution.py:14
  15.0 1.9 %convolution_add_fusion.13 = f32[512,128]{1,0:T(8,128)S(1)} fusion(f32[512,128]{1,0:T(8,128)} %collective-permute-done, f32[512,512]{1,0:T(8,128)S(1)} %get-tuple-element.8, f32[512,128]{1,0:T(8,128)S(1)} %copy-done), kind=kOutput, calls=%fused_computation.25 | convolution fusion | flops 402718720 | bytes 1835008 | tf_op jit(solution)/shard_map/dot_general | solution.py:14
  17.0 2.5 %collective-permute-start.1 = (f32[256,128]{1,0:T(8,128)S(1)}, f32[256,128]{1,0:T(8,128)S(1)}, u32[]{:S(2)}, u32[]{:S(2)}) collective-permute-start(f32[256,128]{1,0:T(8,128)S(1)} %constant_dynamic-slice_fusion.1), channel_id=1, source_target_pairs={{0,2},{1,3},{2,0},{3,1},{4,6},{5,7},{6,4},{7,5},{8,10},{9,11},{10,... | collective-permute-start | bytes 393224 | tf_op jit(solution)/shard_map/ppermute | solution.py:31
  19.5 1.6 %fusion.21 = f32[512,512]{1,0:T(8,128)} fusion(f32[512,128]{1,0:T(8,128)S(1)} %get-tuple-element.13, f32[1024,128]{1,0:T(8,128)S(1)} %copy-done.1, s32[]{:T(128)S(6)} %select_n.157), kind=kOutput, calls=%fused_computation.72 | convolution fusion | flops 201326592 | bytes 1572868 | tf_op jit(solution)/shard_map/dot_general | solution.py:14
  21.1 2.6 %collective-permute-done.1 = f32[256,128]{1,0:T(8,128)S(1)} collective-permute-done((f32[256,128]{1,0:T(8,128)S(1)}, f32[256,128]{1,0:T(8,128)S(1)}, u32[]{:S(2)}, u32[]{:S(2)}) %collective-permute-start.1) | collective-permute-done | bytes 131104 | tf_op jit(solution)/shard_map/ppermute | solution.py:31
  23.7 1.9 %collective-permute-start.2 = (f32[256,128]{1,0:T(8,128)S(1)}, f32[256,128]{1,0:T(8,128)S(1)}, u32[]{:S(2)}, u32[]{:S(2)}) collective-permute-start(f32[256,128]{1,0:T(8,128)S(1)} %dynamic-slice_add_fusion.1), channel_id=1, source_target_pairs={{0,4},{1,5},{2,6},{3,7},{4,0},{5,1},{6,2},{7,3},{8,12},{9,13},{10,... | collective-permute-start | bytes 393224 | tf_op jit(solution)/shard_map/ppermute | solution.py:31
  25.6 0.4 fusion.30
  26.0 3.1 %collective-permute-done.2 = f32[256,128]{1,0:T(8,128)S(1)} collective-permute-done((f32[256,128]{1,0:T(8,128)S(1)}, f32[256,128]{1,0:T(8,128)S(1)}, u32[]{:S(2)}, u32[]{:S(2)}) %collective-permute-start.2) | collective-permute-done | bytes 131104 | tf_op jit(solution)/shard_map/ppermute | solution.py:31
  29.2 2.7 %collective-permute-start.3 = (f32[256,128]{1,0:T(8,128)S(1)}, f32[256,128]{1,0:T(8,128)S(1)}, u32[]{:S(2)}, u32[]{:S(2)}) collective-permute-start(f32[256,128]{1,0:T(8,128)S(1)} %add.240), channel_id=1, source_target_pairs={{0,8},{1,9},{2,10},{3,11},{4,12},{5,13},{6,14},{7,15},{8,0},{9,1},... | collective-permute-start | bytes 393224 | tf_op jit(solution)/shard_map/ppermute | solution.py:31
  31.8 0.4 fusion.32
  32.2 0.0 copy-start.8
  32.3 5.1 %collective-permute-done.3 = f32[256,128]{1,0:T(8,128)S(1)} collective-permute-done((f32[256,128]{1,0:T(8,128)S(1)}, f32[256,128]{1,0:T(8,128)S(1)}, u32[]{:S(2)}, u32[]{:S(2)}) %collective-permute-start.3) | collective-permute-done | bytes 131104 | tf_op jit(solution)/shard_map/ppermute | solution.py:31
  37.4 0.6 multiply_reduce_fusion.3
  38.0 1.3 %collective-permute-start.4 = (f32[256,128]{1,0:T(8,128)S(1)}, f32[256,128]{1,0:T(8,128)S(1)}, u32[]{:S(2)}, u32[]{:S(2)}) collective-permute-start(f32[256,128]{1,0:T(8,128)S(1)} %get-tuple-element.5), channel_id=1, source_target_pairs={{0,2},{1,3},{2,0},{3,1},{4,6},{5,7},{6,4},{7,5},{8,10},{9,11},{10,... | collective-permute-start | bytes 393224 | tf_op jit(solution)/shard_map/ppermute | solution.py:31
  40.5 1.6 %fusion.9 = f32[512]{0:T(512)S(1)} fusion(f32[256,512]{1,0:T(8,128)S(1)} %fusion.32, f32[256,128]{1,0:T(8,128)S(1)} %get-tuple-element.5, f32[512,128]{1,0:T(8,128)S(1)} %copy-done, f32[512,512]{1,0:T(8,128)} %get-tuple-element.11, s32[]{:T(128)S(6)} %select_n.155), kind=kOutput, calls=%fused_computation.49 | convolution fusion | flops 101187072 | bytes 1443844 | tf_op jit(solution)/shard_map/dot_general | solution.py:14
  42.1 0.9 collective-permute-done.4
  43.0 0.3 collective-permute-start.5
  43.3 1.5 %fusion.8 = f32[512]{0:T(512)S(1)} fusion(f32[256,512]{1,0:T(8,128)S(1)} %fusion.30, f32[256,128]{1,0:T(8,128)S(1)} %collective-permute-done.4, f32[512,128]{1,0:T(8,128)S(1)} %copy-done, f32[512,512]{1,0:T(8,128)} %get-tuple-element.11, s32[]{:T(128)S(6)} %select_n.162), kind=kOutput, calls=%fused_computation.47 | convolution fusion | flops 101187072 | bytes 1443844 | tf_op jit(solution)/shard_map/dot_general | solution.py:14
  44.8 0.0 collective-permute-done.5
  44.8 1.5 %fusion = f32[512]{0:T(512)S(1)} fusion(f32[512,512]{1,0:T(8,128)S(1)} %copy-done.4, f32[512,128]{1,0:T(8,128)S(1)} %collective-permute-done.5, f32[512,128]{1,0:T(8,128)S(1)} %copy-done, f32[512,512]{1,0:T(8,128)S(1)} %copy-done.3, s32[512]{0:T(512)S(1)} %copy-done.8, s32[512]{0:T(512)S(1)} %get-tuple-element.16), kind=kOutput, calls=%fused_computation.16 | convolution fusion | flops 206044672 | bytes 2627584 | tf_op jit(solution)/shard_map/dot_general | solution.py:14
  46.3 0.0 copy-start.6
  46.3 0.6 add_reduce_fusion.1
  46.9 1.3 %broadcast_select_fusion.1 = f32[16,2,128]{2,1,0:T(2,128)} fusion(pred[2]{0:T(512)(128)(4,1)S(1)} %iota_compare_fusion, f32[]{:T(128)} %add_reduce_fusion.1, f32[2]{0:T(128)S(1)} %compare_select_fusion.9), kind=kLoop, calls=%fused_computation.94 | loop fusion | flops 4096 | bytes 16398 | tf_op jit(solution)/shard_map/jit(_where)/select_n | solution.py:72
  48.3 5.7 %all-to-all-start = ((f32[16,2,128]{2,1,0:T(2,128)}), f32[16,2,128]{2,1,0:T(2,128)S(1)}, u32[]{:S(2)}, u32[]{:S(2)}) async-start(f32[16,2,128]{2,1,0:T(2,128)} %broadcast_select_fusion.1), calls=%async_computation | async-start | bytes 32768 | tf_op jit(solution)/shard_map/all_to_all | solution.py:74
  53.9 6.5 %all-to-all-done = f32[16,2,128]{2,1,0:T(2,128)S(1)} async-done(((f32[16,2,128]{2,1,0:T(2,128)}), f32[16,2,128]{2,1,0:T(2,128)S(1)}, u32[]{:S(2)}, u32[]{:S(2)}) %all-to-all-start) | async-done | bytes 16416 | tf_op jit(solution)/shard_map/all_to_all | solution.py:74
  60.5 0.1 fusion.11
  60.6 1.0 convolution_add_fusion.1
  61.6 0.4 copy-done.7
  62.1 3.7 %compare_select_fusion.4 = (f32[512,512]{1,0:T(8,128)S(1)}, f32[512,512]{1,0:T(8,128)S(1)}, f32[512,512]{1,0:T(8,128)}) fusion(s32[1024,512]{1,0:T(8,128)S(1)} %copy-done.7, s32[]{:T(128)S(6)} %select_n.150, s32[512]{0:T(512)S(1)} %copy-done.8, s32[512]{0:T(512)S(1)} %get-tuple-element.17, s32[]{:T(128)S(6)} %select_n.157, ...), kind=kOutput, calls=%fused_computation.4 | convolution fusion | flops 411828224 | bytes 6825472 | tf_op jit(solution)/shard_map/dot_general | solution.py:14
  65.8 1.8 %fusion.18 = f32[512,128]{1,0:T(8,128)S(1)} fusion(f32[512,512]{1,0:T(8,128)S(1)} %get-tuple-element.7, f32[1024,128]{1,0:T(8,128)S(1)} %fusion.11, s32[]{:T(128)S(6)} %select_n.157), kind=kOutput, calls=%fused_computation.69 | convolution fusion | flops 402653184 | bytes 1572868 | tf_op jit(solution)/shard_map/dot_general | solution.py:14
  67.6 1.0 fusion.54
  68.6 0.1 collective-permute-start.6
  68.7 2.5 %multiply_reduce_fusion = (f32[]{:T(128)}, f32[512,128]{1,0:T(8,128)S(1)}) fusion(f32[512,128]{1,0:T(8,128)S(1)} %fusion.18, f32[512,512]{1,0:T(8,128)S(1)} %get-tuple-element.6, f32[1024,128]{1,0:T(8,128)S(1)} %fusion.11, s32[]{:T(128)S(6)} %select_n.150), kind=kOutput, calls=%fused_computation.60 | convolution fusion | flops 402849792 | bytes 1835016 | tf_op jit(solution)/shard_map/dot_general | solution.py:14
  71.2 1.0 convolution_add_fusion.11
  72.2 0.7 collective-permute-start.7
  72.8 1.6 %fusion.16 = f32[512,512]{1,0:T(8,128)} fusion(f32[512,128]{1,0:T(8,128)S(1)} %get-tuple-element.15, f32[1024,128]{1,0:T(8,128)S(1)} %fusion.11, s32[]{:T(128)S(6)} %select_n.157), kind=kOutput, calls=%fused_computation.67 | convolution fusion | flops 201326592 | bytes 1572868 | tf_op jit(solution)/shard_map/dot_general | solution.py:14
  74.4 3.7 %collective-permute-done.7 = f32[256,128]{1,0:T(8,128)S(1)} collective-permute-done((f32[256,128]{1,0:T(8,128)S(1)}, f32[256,128]{1,0:T(8,128)S(1)}, u32[]{:S(2)}, u32[]{:S(2)}) %collective-permute-start.7) | collective-permute-done | bytes 131104 | tf_op jit(solution)/shard_map/ppermute | solution.py:31
  78.2 0.6 collective-permute-start.8
  78.7 0.4 fusion.26
  79.1 4.2 %collective-permute-done.8 = f32[256,128]{1,0:T(8,128)S(1)} collective-permute-done((f32[256,128]{1,0:T(8,128)S(1)}, f32[256,128]{1,0:T(8,128)S(1)}, u32[]{:S(2)}, u32[]{:S(2)}) %collective-permute-start.8) | collective-permute-done | bytes 131104 | tf_op jit(solution)/shard_map/ppermute | solution.py:31
  83.4 0.5 collective-permute-start.9
  83.9 0.4 fusion.28
  84.2 6.9 %collective-permute-done.9 = f32[256,128]{1,0:T(8,128)S(1)} collective-permute-done((f32[256,128]{1,0:T(8,128)S(1)}, f32[256,128]{1,0:T(8,128)S(1)}, u32[]{:S(2)}, u32[]{:S(2)}) %collective-permute-start.9) | collective-permute-done | bytes 131104 | tf_op jit(solution)/shard_map/ppermute | solution.py:31
  91.1 0.6 multiply_reduce_fusion.2
  92.4 0.2 collective-permute-start.10
  93.3 1.6 %fusion.7 = f32[512]{0:T(512)S(1)} fusion(f32[256,512]{1,0:T(8,128)S(1)} %fusion.28, f32[256,128]{1,0:T(8,128)S(1)} %get-tuple-element.3, f32[512,128]{1,0:T(8,128)S(1)} %multiply_subtract_fusion.1, f32[512,512]{1,0:T(8,128)} %get-tuple-element.10, s32[]{:T(128)S(6)} %select_n.155), kind=kOutput, calls=%fused_computation.45 | convolution fusion | flops 101187072 | bytes 1443844 | tf_op jit(solution)/shard_map/dot_general | solution.py:14
  94.8 2.7 %collective-permute-done.10 = f32[256,128]{1,0:T(8,128)} collective-permute-done((f32[256,128]{1,0:T(8,128)S(1)}, f32[256,128]{1,0:T(8,128)}, u32[]{:S(2)}, u32[]{:S(2)}) %collective-permute-start.10) | collective-permute-done | bytes 131104 | tf_op jit(solution)/shard_map/ppermute | solution.py:31
  97.5 1.0 maximum_select_fusion.2
  98.5 0.1 collective-permute-start.11
  98.6 1.6 %fusion.6 = f32[512]{0:T(512)S(1)} fusion(f32[256,512]{1,0:T(8,128)S(1)} %fusion.26, f32[256,128]{1,0:T(8,128)} %collective-permute-done.10, f32[512,128]{1,0:T(8,128)S(1)} %multiply_subtract_fusion.1, f32[512,512]{1,0:T(8,128)} %get-tuple-element.10, s32[]{:T(128)S(6)} %select_n.162), kind=kOutput, calls=%fused_computation.43 | convolution fusion | flops 101187072 | bytes 1443844 | tf_op jit(solution)/shard_map/dot_general | solution.py:14
  100.2 1.5 %fusion.1 = f32[512]{0:T(512)S(1)} fusion(f32[512,512]{1,0:T(8,128)S(1)} %copy-done.5, f32[512,128]{1,0:T(8,128)S(1)} %collective-permute-done.11, f32[512,128]{1,0:T(8,128)S(1)} %multiply_subtract_fusion.1, f32[512,512]{1,0:T(8,128)S(1)} %convolution_add_fusion.1, s32[512]{0:T(512)S(1)} %copy-done.8, s32[512]{0:T(512)S(1)} %get-tuple-element.16), kind=kOutput, calls=%fused_computation.17 | convolution fusion | flops 206044672 | bytes 2627584 | tf_op jit(solution)/shard_map/dot_general | solution.py:14
  101.7 0.6 add_reduce_fusion
  102.3 1.3 %broadcast_select_fusion = f32[16,2,128]{2,1,0:T(2,128)} fusion(pred[2]{0:T(512)(128)(4,1)S(1)} %iota_compare_fusion, f32[]{:T(128)} %add_reduce_fusion, f32[2]{0:T(128)S(1)} %compare_select_fusion.8), kind=kLoop, calls=%fused_computation.93 | loop fusion | flops 4096 | bytes 16398 | tf_op jit(solution)/shard_map/jit(_where)/select_n | solution.py:72
  103.6 3.5 %all-to-all-start.1 = ((f32[16,2,128]{2,1,0:T(2,128)}), f32[16,2,128]{2,1,0:T(2,128)S(1)}, u32[]{:S(2)}, u32[]{:S(2)}) async-start(f32[16,2,128]{2,1,0:T(2,128)} %broadcast_select_fusion), calls=%async_computation.1 | async-start | bytes 32768 | tf_op jit(solution)/shard_map/all_to_all | solution.py:74
  107.1 6.5 %all-to-all-done.1 = f32[16,2,128]{2,1,0:T(2,128)S(1)} async-done(((f32[16,2,128]{2,1,0:T(2,128)}), f32[16,2,128]{2,1,0:T(2,128)S(1)}, u32[]{:S(2)}, u32[]{:S(2)}) %all-to-all-start.1) | async-done | bytes 16416 | tf_op jit(solution)/shard_map/all_to_all | solution.py:74
  113.6 0.8 multiply_subtract_fusion
  114.4 0.6 dynamic-slice_subtract_fusion
  (32 shorter events, 0.3 us)
Async XLA Ops:
  2.7 5.9 %copy-start.2 = (f32[512,512]{1,0:T(8,128)}, f32[512,512]{1,0:T(8,128)S(1)}, u32[]{:S(2)}) copy-start(f32[512,512]{1,0:T(8,128)S(1)} %convolution_add_fusion.4) | copy-start | bytes 3145732
  2.7 5.9 %copy-start = (f32[512,128]{1,0:T(8,128)S(1)}, f32[512,128]{1,0:T(8,128)}, u32[]{:S(2)}) copy-start(f32[512,128]{1,0:T(8,128)} %param.8) | copy-start | bytes 786436
  2.7 8.0 %copy-start.1 = (f32[1024,128]{1,0:T(8,128)S(1)}, f32[1024,128]{1,0:T(8,128)}, u32[]{:S(2)}) copy-start(f32[1024,128]{1,0:T(8,128)} %param.7) | copy-start | bytes 1572868
  10.3 4.7 %collective-permute-start = (f32[512,128]{1,0:T(8,128)}, f32[512,128]{1,0:T(8,128)}, u32[]{:S(2)}, u32[]{:S(2)}) collective-permute-start(f32[512,128]{1,0:T(8,128)} %fusion.53), channel_id=1, source_target_pairs={{0,1},{1,0},{2,3},{3,2},{4,5},{5,4},{6,7},{7,6},{8,9},{9,8},{10,11... | collective-permute-start | bytes 786440 | tf_op jit(solution)/shard_map/ppermute | solution.py:31
  17.0 6.7 %collective-permute-start.1 = (f32[256,128]{1,0:T(8,128)S(1)}, f32[256,128]{1,0:T(8,128)S(1)}, u32[]{:S(2)}, u32[]{:S(2)}) collective-permute-start(f32[256,128]{1,0:T(8,128)S(1)} %constant_dynamic-slice_fusion.1), channel_id=1, source_target_pairs={{0,2},{1,3},{2,0},{3,1},{4,6},{5,7},{6,4},{7,5},{8,10},{9,11},{10,... | collective-permute-start | bytes 393224 | tf_op jit(solution)/shard_map/ppermute | solution.py:31
  23.7 5.4 %collective-permute-start.2 = (f32[256,128]{1,0:T(8,128)S(1)}, f32[256,128]{1,0:T(8,128)S(1)}, u32[]{:S(2)}, u32[]{:S(2)}) collective-permute-start(f32[256,128]{1,0:T(8,128)S(1)} %dynamic-slice_add_fusion.1), channel_id=1, source_target_pairs={{0,4},{1,5},{2,6},{3,7},{4,0},{5,1},{6,2},{7,3},{8,12},{9,13},{10,... | collective-permute-start | bytes 393224 | tf_op jit(solution)/shard_map/ppermute | solution.py:31
  29.2 8.3 %collective-permute-start.3 = (f32[256,128]{1,0:T(8,128)S(1)}, f32[256,128]{1,0:T(8,128)S(1)}, u32[]{:S(2)}, u32[]{:S(2)}) collective-permute-start(f32[256,128]{1,0:T(8,128)S(1)} %add.240), channel_id=1, source_target_pairs={{0,8},{1,9},{2,10},{3,11},{4,12},{5,13},{6,14},{7,15},{8,0},{9,1},... | collective-permute-start | bytes 393224 | tf_op jit(solution)/shard_map/ppermute | solution.py:31
  32.2 12.6 %copy-start.3 = (f32[512,512]{1,0:T(8,128)S(1)}, f32[512,512]{1,0:T(8,128)}, u32[]{:S(2)}) copy-start(f32[512,512]{1,0:T(8,128)} %copy-done.2) | copy-start | bytes 3145732
  32.2 12.6 %copy-start.8 = (s32[512]{0:T(512)S(1)}, s32[512]{0:T(512)}, u32[]{:S(2)}) copy-start(s32[512]{0:T(512)} %param.6) | copy-start | bytes 6148
  38.0 5.0 %collective-permute-start.4 = (f32[256,128]{1,0:T(8,128)S(1)}, f32[256,128]{1,0:T(8,128)S(1)}, u32[]{:S(2)}, u32[]{:S(2)}) collective-permute-start(f32[256,128]{1,0:T(8,128)S(1)} %get-tuple-element.5), channel_id=1, source_target_pairs={{0,2},{1,3},{2,0},{3,1},{4,6},{5,7},{6,4},{7,5},{8,10},{9,11},{10,... | collective-permute-start | bytes 393224 | tf_op jit(solution)/shard_map/ppermute | solution.py:31
  40.5 4.3 %copy-start.4 = (f32[512,512]{1,0:T(8,128)S(1)}, f32[512,512]{1,0:T(8,128)}, u32[]{:S(2)}) copy-start(f32[512,512]{1,0:T(8,128)} %fusion.21) | copy-start | bytes 3145732
  43.0 1.8 %collective-permute-start.5 = (f32[512,128]{1,0:T(8,128)S(1)}, f32[512,128]{1,0:T(8,128)S(1)}, u32[]{:S(2)}, u32[]{:S(2)}) collective-permute-start(f32[512,128]{1,0:T(8,128)S(1)} %maximum_select_fusion.1), channel_id=1, source_target_pairs={{0,1},{1,0},{2,3},{3,2},{4,5},{5,4},{6,7},{7,6},{8,9},{9,8},{10,11... | collective-permute-start | bytes 786440 | tf_op jit(solution)/shard_map/ppermute | solution.py:31
  46.3 14.3 %copy-start.6 = (f32[512]{0:T(512)S(1)}, f32[512]{0:T(512)}, u32[]{:S(2)}) copy-start(f32[512]{0:T(512)} %param.9) | copy-start | bytes 6148
  48.3 12.2 %all-to-all-start = ((f32[16,2,128]{2,1,0:T(2,128)}), f32[16,2,128]{2,1,0:T(2,128)S(1)}, u32[]{:S(2)}, u32[]{:S(2)}) async-start(f32[16,2,128]{2,1,0:T(2,128)} %broadcast_select_fusion.1), calls=%async_computation | async-start | bytes 32768 | tf_op jit(solution)/shard_map/all_to_all | solution.py:74
  60.5 1.6 %copy-start.7 = (s32[1024,512]{1,0:T(8,128)S(1)}, s32[1024,512]{1,0:T(8,128)}, u32[]{:S(2)}) copy-start(s32[1024,512]{1,0:T(8,128)} %param.5) | copy-start | bytes 6291460
  68.6 2.5 %collective-permute-start.6 = (f32[512,128]{1,0:T(8,128)S(1)}, f32[512,128]{1,0:T(8,128)S(1)}, u32[]{:S(2)}, u32[]{:S(2)}) collective-permute-start(f32[512,128]{1,0:T(8,128)S(1)} %fusion.54), channel_id=1, source_target_pairs={{0,1},{1,0},{2,3},{3,2},{4,5},{5,4},{6,7},{7,6},{8,9},{9,8},{10,11... | collective-permute-start | bytes 786440 | tf_op jit(solution)/shard_map/ppermute | solution.py:31
  72.2 6.0 %collective-permute-start.7 = (f32[256,128]{1,0:T(8,128)S(1)}, f32[256,128]{1,0:T(8,128)S(1)}, u32[]{:S(2)}, u32[]{:S(2)}) collective-permute-start(f32[256,128]{1,0:T(8,128)S(1)} %constant_dynamic-slice_fusion), channel_id=1, source_target_pairs={{0,2},{1,3},{2,0},{3,1},{4,6},{5,7},{6,4},{7,5},{8,10},{9,11},{10,... | collective-permute-start | bytes 393224 | tf_op jit(solution)/shard_map/ppermute | solution.py:31
  78.2 5.2 %collective-permute-start.8 = (f32[256,128]{1,0:T(8,128)S(1)}, f32[256,128]{1,0:T(8,128)S(1)}, u32[]{:S(2)}, u32[]{:S(2)}) collective-permute-start(f32[256,128]{1,0:T(8,128)S(1)} %dynamic-slice_add_fusion), channel_id=1, source_target_pairs={{0,4},{1,5},{2,6},{3,7},{4,0},{5,1},{6,2},{7,3},{8,12},{9,13},{10,... | collective-permute-start | bytes 393224 | tf_op jit(solution)/shard_map/ppermute | solution.py:31
  83.4 7.8 %collective-permute-start.9 = (f32[256,128]{1,0:T(8,128)S(1)}, f32[256,128]{1,0:T(8,128)S(1)}, u32[]{:S(2)}, u32[]{:S(2)}) collective-permute-start(f32[256,128]{1,0:T(8,128)S(1)} %add.265), channel_id=1, source_target_pairs={{0,8},{1,9},{2,10},{3,11},{4,12},{5,13},{6,14},{7,15},{8,0},{9,1},... | collective-permute-start | bytes 393224 | tf_op jit(solution)/shard_map/ppermute | solution.py:31
  92.4 5.1 %collective-permute-start.10 = (f32[256,128]{1,0:T(8,128)S(1)}, f32[256,128]{1,0:T(8,128)}, u32[]{:S(2)}, u32[]{:S(2)}) collective-permute-start(f32[256,128]{1,0:T(8,128)S(1)} %get-tuple-element.3), channel_id=1, source_target_pairs={{0,2},{1,3},{2,0},{3,1},{4,6},{5,7},{6,4},{7,5},{8,10},{9,11},{10,... | collective-permute-start | bytes 393224 | tf_op jit(solution)/shard_map/ppermute | solution.py:31
  93.3 7.0 %copy-start.5 = (f32[512,512]{1,0:T(8,128)S(1)}, f32[512,512]{1,0:T(8,128)}, u32[]{:S(2)}) copy-start(f32[512,512]{1,0:T(8,128)} %fusion.16) | copy-start | bytes 3145732
  98.5 1.6 %collective-permute-start.11 = (f32[512,128]{1,0:T(8,128)S(1)}, f32[512,128]{1,0:T(8,128)S(1)}, u32[]{:S(2)}, u32[]{:S(2)}) collective-permute-start(f32[512,128]{1,0:T(8,128)S(1)} %maximum_select_fusion.2), channel_id=1, source_target_pairs={{0,1},{1,0},{2,3},{3,2},{4,5},{5,4},{6,7},{7,6},{8,9},{9,8},{10,11... | collective-permute-start | bytes 786440 | tf_op jit(solution)/shard_map/ppermute | solution.py:31
  103.6 10.0 %all-to-all-start.1 = ((f32[16,2,128]{2,1,0:T(2,128)}), f32[16,2,128]{2,1,0:T(2,128)S(1)}, u32[]{:S(2)}, u32[]{:S(2)}) async-start(f32[16,2,128]{2,1,0:T(2,128)} %broadcast_select_fusion), calls=%async_computation.1 | async-start | bytes 32768 | tf_op jit(solution)/shard_map/all_to_all | solution.py:74

commit v8 on v5

--- a/solution.py
+++ b/solution.py
@@ -14,10 +14,8 @@
     return jnp.dot(left, right, precision=precision, preferred_element_type=jnp.float32)
 
 
-def local_terms(time_factor, user_block, base_block, count_block, start_block):
+def local_terms(time_factor, user_block, base_block, count_block, observed):
     linear = product(time_factor, user_block.T) + base_block[None, :]
-    time_bins = jnp.arange(time_factor.shape[0], dtype=jnp.int32)[:, None]
-    observed = time_bins >= start_block[None, :]
     decay = jnp.exp(-jnp.abs(linear))
     intensity = jnp.maximum(linear, 0.0) + jnp.log1p(decay) + background
     gate_value = jnp.where(linear >= 0, 1.0, decay) / (1.0 + decay)
@@ -25,6 +23,11 @@
     residual = jnp.where(observed, gate_value * (1.0 - count_block.astype(jnp.float32) * inverse), 0.0)
     curvature = jnp.where(observed, gate_value * gate_value * inverse, 0.0)
     return (residual, curvature)
+
+
+def observed_of(counts, first_bin):
+    time_bins = jnp.arange(counts.shape[0], dtype=jnp.int32)[:, None]
+    return time_bins >= first_bin[None, :]
 
 
 def exchange(value, n, distance):
@@ -81,8 +84,11 @@
     shard_rows = time_factor.shape[0] // n
     offset = lax.axis_index("user") * shard_rows
     mine_rows = time_factor
+    observed = observed_of(counts, first_bin)
     for sweep in range(SWEEPS):
-        residual, curvature = local_terms(time_factor, user_factor, user_base, counts, first_bin)
+        residual, curvature = local_terms(time_factor, user_factor, user_base, counts, observed)
+        if sweep + 1 < SWEEPS:
+            code = lax.optimization_barrier(jnp.where(observed, counts, -1).astype(jnp.int8))
         grad_user = product(residual.T, time_factor)
         grad_whole, pieces, time_norm = sum_over_users(product(residual, user_factor), n)
         user_norm = jnp.sum(grad_user * grad_user)
@@ -99,6 +105,7 @@
         user_factor = user_factor - relax_step * grad_user
         if sweep + 1 < SWEEPS:
             time_factor = time_factor - relax_step * grad_whole
+            counts, observed = code, code >= 0
         else:
             mine_rows = lax.dynamic_slice_in_dim(
                 time_factor - relax_step * grad_whole, offset, shard_rows, 0

time: 111 us -> 114 us (1.027)
  matrix products: 34.6 us -> 38.3 us
  waiting for transfers between devices: 39.3 us -> 37.4 us
    dot_general x18, matrix products: 34.6 us -> 38.3 us  [product(): jnp.dot(left, right, precision=precision, preferred_element_type=jnp.floa...]
    convert_element_type x0 -> x1, other arithmetic: none -> 2.08 us  [body(): jnp.where(observed, counts, -1).astype(jnp.int8)]
    all_to_all x2, waiting for transfers between devices: 12.8 us -> 10.8 us  [sum_rows(): spread = lax.all_to_all(spread, 'user', 0, 0, tiled=False)]
  transfers between devices with their start and end apart: 14 -> 14, of which waited for: 11 -> 10; matrix products, arithmetic and copies ran while one was open for 15% -> 18% of each run, Pallas kernels for 0% -> 0%
where the time goes in v8:
time: 114 us; the launch traced here: 113 us
  matrix products  38.3 us (34%)
  waiting for transfers between devices  37.4 us (33%)
  starting transfers between devices  20.5 us (18%)
  other arithmetic  7.38 us (6%)
  local copies, waits for them, and re-layouts  5.92 us (5%)
  between operations  3.58 us (3%)
    dot_general x18, matrix products, product(): jnp.dot(left, right, precision=precision, preferred_element_type=jnp.floa...  38.3 us
    ppermute x12, waiting for transfers between devices, exchange(): return lax.ppermute(value, 'user', [(i, i ^ distance) for i in range(n)])  26.5 us
    ppermute x12, starting transfers between devices, exchange(): return lax.ppermute(value, 'user', [(i, i ^ distance) for i in range(n)])  12 us
    all_to_all x2, waiting for transfers between devices, sum_rows(): spread = lax.all_to_all(spread, 'user', 0, 0, tiled=False)  10.8 us
    all_to_all x2, starting transfers between devices, sum_rows(): spread = lax.all_to_all(spread, 'user', 0, 0, tiled=False)  8.48 us
  transfers between devices with their start and end apart: 14, of which 10 were waited for; matrix products, arithmetic and copies ran while one was open for 18% of the time, Pallas kernels for 0%

profile of v8, /device:TPU:0, one launch (start us, length us, event | category | flops | bytes accessed | tf_op | source)
XLA Modules:
  0.0 113.1 jit_solution(9769186694647583755)
XLA Ops:
  0.7 7.0 %multiply_select_fusion.2 = (f32[1024,512]{1,0:T(8,128)}, f32[1024,512]{1,0:T(8,128)S(1)}) fusion(s32[512]{0:T(512)} %param.6, f32[512]{0:T(512)} %param.9, s32[1024,512]{1,0:T(8,128)} %param.5, f32[1024,128]{1,0:T(8,128)} %param.7, f32[512,128]{1,0:T(8,128)} %param.8), kind=kOutput, calls=%fused_computation.6 | convolution fusion | flops 815792128 | bytes 7081984 | tf_op jit(solution)/shard_map/dot_general | solution.py:14
  7.7 2.6 %fusion.39 = f32[1024,128]{1,0:T(8,128)} fusion(f32[1024,512]{1,0:T(8,128)S(1)} %get-tuple-element.7, f32[512,128]{1,0:T(8,128)S(1)} %copy-done), kind=kOutput, calls=%fused_computation.89 | convolution fusion | flops 805306368 | bytes 2883584 | tf_op jit(solution)/shard_map/dot_general | solution.py:14
  10.3 1.0 constant_dynamic-slice_fusion.3
  11.3 0.5 collective-permute-start
  11.8 1.3 %collective-permute-done = f32[512,128]{1,0:T(8,128)} collective-permute-done((f32[512,128]{1,0:T(8,128)S(1)}, f32[512,128]{1,0:T(8,128)}, u32[]{:S(2)}, u32[]{:S(2)}) %collective-permute-start) | collective-permute-done | bytes 262176 | tf_op jit(solution)/shard_map/ppermute | solution.py:34
  13.1 1.1 dynamic-slice_add_fusion.1
  14.1 0.7 constant_dynamic-slice_fusion.2
  14.8 2.9 %collective-permute-start.1 = (f32[256,128]{1,0:T(8,128)}, f32[256,128]{1,0:T(8,128)S(1)}, u32[]{:S(2)}, u32[]{:S(2)}) collective-permute-start(f32[256,128]{1,0:T(8,128)} %constant_dynamic-slice_fusion.2), channel_id=1, source_target_pairs={{0,2},{1,3},{2,0},{3,1},{4,6},{5,7},{6,4},{7,5},{8,10},{9,11},{10,... | collective-permute-start | bytes 393224 | tf_op jit(solution)/shard_map/ppermute | solution.py:34
  17.7 4.0 %multiply_reduce_fusion.1 = (f32[]{:T(128)}, f32[512,128]{1,0:T(8,128)S(1)}) fusion(f32[1024,512]{1,0:T(8,128)S(1)} %get-tuple-element.7, f32[1024,128]{1,0:T(8,128)S(1)} %copy-done.1), kind=kOutput, calls=%fused_computation.48 | convolution fusion | flops 805437440 | bytes 2883588 | tf_op jit(solution)/shard_map/dot_general | solution.py:14
  21.7 1.9 %collective-permute-start.2 = (f32[256,128]{1,0:T(8,128)S(1)}, f32[256,128]{1,0:T(8,128)S(1)}, u32[]{:S(2)}, u32[]{:S(2)}) collective-permute-start(f32[256,128]{1,0:T(8,128)S(1)} %dynamic-slice_add_fusion.3), channel_id=1, source_target_pairs={{0,4},{1,5},{2,6},{3,7},{4,0},{5,1},{6,2},{7,3},{8,12},{9,13},{10,... | collective-permute-start | bytes 393224 | tf_op jit(solution)/shard_map/ppermute | solution.py:34
  23.6 0.6 fusion.10
  24.2 2.9 %collective-permute-done.2 = f32[256,128]{1,0:T(8,128)S(1)} collective-permute-done((f32[256,128]{1,0:T(8,128)S(1)}, f32[256,128]{1,0:T(8,128)S(1)}, u32[]{:S(2)}, u32[]{:S(2)}) %collective-permute-start.2) | collective-permute-done | bytes 131104 | tf_op jit(solution)/shard_map/ppermute | solution.py:34
  27.1 2.7 %collective-permute-start.3 = (f32[256,128]{1,0:T(8,128)S(1)}, f32[256,128]{1,0:T(8,128)S(1)}, u32[]{:S(2)}, u32[]{:S(2)}) collective-permute-start(f32[256,128]{1,0:T(8,128)S(1)} %add.179), channel_id=1, source_target_pairs={{0,8},{1,9},{2,10},{3,11},{4,12},{5,13},{6,14},{7,15},{8,0},{9,1},... | collective-permute-start | bytes 393224 | tf_op jit(solution)/shard_map/ppermute | solution.py:34
  29.7 0.4 fusion.18
  30.1 5.1 %collective-permute-done.3 = f32[256,128]{1,0:T(8,128)S(1)} collective-permute-done((f32[256,128]{1,0:T(8,128)S(1)}, f32[256,128]{1,0:T(8,128)S(1)}, u32[]{:S(2)}, u32[]{:S(2)}) %collective-permute-start.3) | collective-permute-done | bytes 131104 | tf_op jit(solution)/shard_map/ppermute | solution.py:34
  35.2 0.6 multiply_reduce_fusion.3
  35.9 0.6 collective-permute-start.4
  36.5 0.4 fusion.20
  38.1 2.7 %collective-permute-done.4 = f32[256,128]{1,0:T(8,128)S(1)} collective-permute-done((f32[256,128]{1,0:T(8,128)S(1)}, f32[256,128]{1,0:T(8,128)S(1)}, u32[]{:S(2)}, u32[]{:S(2)}) %collective-permute-start.4) | collective-permute-done | bytes 131104 | tf_op jit(solution)/shard_map/ppermute | solution.py:34
  40.8 0.7 copy-done.9
  41.5 0.0 copy-start.6
  41.5 0.1 collective-permute-start.5
  41.6 1.5 %fusion.5 = f32[512]{0:T(512)S(1)} fusion(f32[256,512]{1,0:T(8,128)S(1)} %fusion.20, f32[256,128]{1,0:T(8,128)S(1)} %get-tuple-element.5, f32[512,128]{1,0:T(8,128)S(1)} %copy-done, f32[1024,512]{1,0:T(8,128)} %get-tuple-element.6, s32[]{:T(128)S(6)} %select_n.137), kind=kOutput, calls=%fused_computation.29 | convolution fusion | flops 101187072 | bytes 1443844 | tf_op jit(solution)/shard_map/dot_general | solution.py:14
  43.1 0.0 copy-start.10
  43.1 1.5 %fusion.4 = f32[512]{0:T(512)S(1)} fusion(f32[256,512]{1,0:T(8,128)S(1)} %fusion.18, f32[256,128]{1,0:T(8,128)} %copy-done.9, f32[512,128]{1,0:T(8,128)S(1)} %copy-done, f32[1024,512]{1,0:T(8,128)} %get-tuple-element.6, s32[]{:T(128)S(6)} %select_n.138), kind=kOutput, calls=%fused_computation.27 | convolution fusion | flops 101187072 | bytes 1443844 | tf_op jit(solution)/shard_map/dot_general | solution.py:14
  44.6 0.2 copy-done.2
  44.8 0.6 fusion
  45.5 0.0 copy-start.7
  45.5 0.7 add_reduce_fusion.1
  46.2 0.7 stack.6
  46.9 0.7 broadcast_in_dim.31
  47.5 5.0 %all-to-all-start = ((f32[16,2,128]{2,1,0:T(2,128)}), f32[16,2,128]{2,1,0:T(2,128)S(1)}, u32[]{:S(2)}, u32[]{:S(2)}) async-start(f32[16,2,128]{2,1,0:T(2,128)} %broadcast_in_dim.31), calls=%async_computation | async-start | bytes 32768 | tf_op jit(solution)/shard_map/all_to_all | solution.py:78
  52.5 0.0 copy-start.11
  52.6 2.1 %select_convert_fusion = s8[1024,512]{1,0:T(32,128)(4,1)S(1)} fusion(s32[1024,512]{1,0:T(8,128)} %param.5, s32[512]{0:T(512)S(1)} %copy-done.10), kind=kLoop, calls=%fused_computation.5 | loop fusion | flops 1572864 | bytes 2623488 | tf_op jit(solution)/shard_map/convert_element_type | solution.py:91
  54.6 4.4 %all-to-all-done = f32[16,2,128]{2,1,0:T(2,128)S(1)} async-done(((f32[16,2,128]{2,1,0:T(2,128)}), f32[16,2,128]{2,1,0:T(2,128)S(1)}, u32[]{:S(2)}, u32[]{:S(2)}) %all-to-all-start) | async-done | bytes 16416 | tf_op jit(solution)/shard_map/all_to_all | solution.py:78
  59.1 0.1 fusion.7
  59.2 4.9 %multiply_select_fusion = (f32[1024,512]{1,0:T(8,128)}, f32[1024,512]{1,0:T(8,128)S(1)}) fusion(s8[1024,512]{1,0:T(32,128)(4,1)S(1)} %select_convert_fusion, f32[512]{0:T(512)S(1)} %copy-done.11, f32[1024,128]{1,0:T(8,128)S(1)} %fusion.7, f32[512,128]{1,0:T(8,128)S(1)} %multiply_subtract_fusion.1), kind=kOutput, calls=%fused_computation | convolution fusion | flops 813170688 | bytes 5507072 | tf_op jit(solution)/shard_map/dot_general | solution.py:14
  64.1 3.7 %fusion.12 = f32[1024,128]{1,0:T(8,128)S(1)} fusion(f32[512,128]{1,0:T(8,128)S(1)} %multiply_subtract_fusion.1, s8[1024,512]{1,0:T(32,128)(4,1)S(1)} %select_convert_fusion, f32[1024,512]{1,0:T(8,128)S(1)} %get-tuple-element.13, f32[512]{0:T(512)S(1)} %copy-done.11), kind=kOutput, calls=%fused_computation.49 | convolution fusion | flops 814219264 | bytes 3409920 | tf_op jit(solution)/shard_map/dot_general | solution.py:14
  67.9 0.1 collective-permute-start.6
  67.9 1.5 %collective-permute-done.6 = f32[512,128]{1,0:T(8,128)S(1)} collective-permute-done((f32[512,128]{1,0:T(8,128)S(1)}, f32[512,128]{1,0:T(8,128)S(1)}, u32[]{:S(2)}, u32[]{:S(2)}) %collective-permute-start.6) | collective-permute-done | bytes 262176 | tf_op jit(solution)/shard_map/ppermute | solution.py:34
  69.5 0.5 collective-permute-start.7
  70.0 6.1 %multiply_reduce_fusion = (f32[]{:T(128)}, f32[512,128]{1,0:T(8,128)S(1)}) fusion(f32[1024,128]{1,0:T(8,128)S(1)} %fusion.7, s8[1024,512]{1,0:T(32,128)(4,1)S(1)} %select_convert_fusion, f32[1024,512]{1,0:T(8,128)S(1)} %get-tuple-element.13, f32[512]{0:T(512)S(1)} %copy-done.11), kind=kOutput, calls=%fused_computation.43 | convolution fusion | flops 814350336 | bytes 3409924 | tf_op jit(solution)/shard_map/dot_general | solution.py:14
  76.2 0.6 collective-permute-start.8
  76.8 0.6 fusion.8
  77.4 4.1 %collective-permute-done.8 = f32[256,128]{1,0:T(8,128)S(1)} collective-permute-done((f32[256,128]{1,0:T(8,128)S(1)}, f32[256,128]{1,0:T(8,128)S(1)}, u32[]{:S(2)}, u32[]{:S(2)}) %collective-permute-start.8) | collective-permute-done | bytes 131104 | tf_op jit(solution)/shard_map/ppermute | solution.py:34
  81.5 0.7 collective-permute-start.9
  82.2 0.4 fusion.14
  82.6 7.1 %collective-permute-done.9 = f32[256,128]{1,0:T(8,128)S(1)} collective-permute-done((f32[256,128]{1,0:T(8,128)S(1)}, f32[256,128]{1,0:T(8,128)S(1)}, u32[]{:S(2)}, u32[]{:S(2)}) %collective-permute-start.9) | collective-permute-done | bytes 131104 | tf_op jit(solution)/shard_map/ppermute | solution.py:34
  89.7 0.6 multiply_reduce_fusion.2
  90.3 1.5 %collective-permute-start.10 = (f32[256,128]{1,0:T(8,128)S(1)}, f32[256,128]{1,0:T(8,128)S(1)}, u32[]{:S(2)}, u32[]{:S(2)}) collective-permute-start(f32[256,128]{1,0:T(8,128)S(1)} %get-tuple-element.3), channel_id=1, source_target_pairs={{0,2},{1,3},{2,0},{3,1},{4,6},{5,7},{6,4},{7,5},{8,10},{9,11},{10,... | collective-permute-start | bytes 393224 | tf_op jit(solution)/shard_map/ppermute | solution.py:34
  91.8 0.4 fusion.16
  93.5 1.8 %collective-permute-done.10 = f32[256,128]{1,0:T(8,128)S(1)} collective-permute-done((f32[256,128]{1,0:T(8,128)S(1)}, f32[256,128]{1,0:T(8,128)S(1)}, u32[]{:S(2)}, u32[]{:S(2)}) %collective-permute-start.10) | collective-permute-done | bytes 131104 | tf_op jit(solution)/shard_map/ppermute | solution.py:34
  95.3 0.7 copy-done.8
  96.0 0.1 collective-permute-start.11
  96.1 1.5 %fusion.3 = f32[512]{0:T(512)S(1)} fusion(f32[256,512]{1,0:T(8,128)S(1)} %fusion.16, f32[256,128]{1,0:T(8,128)S(1)} %get-tuple-element.3, f32[512,128]{1,0:T(8,128)S(1)} %multiply_subtract_fusion.1, f32[1024,512]{1,0:T(8,128)} %get-tuple-element.12, s32[]{:T(128)S(6)} %select_n.137), kind=kOutput, calls=%fused_computation.25 | convolution fusion | flops 101187072 | bytes 1443844 | tf_op jit(solution)/shard_map/dot_general | solution.py:14
  97.5 1.5 %fusion.2 = f32[512]{0:T(512)S(1)} fusion(f32[256,512]{1,0:T(8,128)S(1)} %fusion.14, f32[256,128]{1,0:T(8,128)} %copy-done.8, f32[512,128]{1,0:T(8,128)S(1)} %multiply_subtract_fusion.1, f32[1024,512]{1,0:T(8,128)} %get-tuple-element.12, s32[]{:T(128)S(6)} %select_n.138), kind=kOutput, calls=%fused_computation.23 | convolution fusion | flops 101187072 | bytes 1443844 | tf_op jit(solution)/shard_map/dot_general | solution.py:14
  99.1 0.6 fusion.1
  99.7 0.6 add_reduce_fusion
  100.4 0.6 stack.7
  101.0 0.7 broadcast_in_dim.33
  101.7 3.5 %all-to-all-start.1 = ((f32[16,2,128]{2,1,0:T(2,128)}), f32[16,2,128]{2,1,0:T(2,128)S(1)}, u32[]{:S(2)}, u32[]{:S(2)}) async-start(f32[16,2,128]{2,1,0:T(2,128)} %broadcast_in_dim.33), calls=%async_computation.1 | async-start | bytes 32768 | tf_op jit(solution)/shard_map/all_to_all | solution.py:78
  105.2 6.5 %all-to-all-done.1 = f32[16,2,128]{2,1,0:T(2,128)S(1)} async-done(((f32[16,2,128]{2,1,0:T(2,128)}), f32[16,2,128]{2,1,0:T(2,128)S(1)}, u32[]{:S(2)}, u32[]{:S(2)}) %all-to-all-start.1) | async-done | bytes 16416 | tf_op jit(solution)/shard_map/all_to_all | solution.py:78
  111.7 0.7 multiply_subtract_fusion
  112.4 0.6 dynamic-slice_subtract_fusion
  (35 shorter events, 0.3 us)
Async XLA Ops:
  0.6 7.0 %copy-start = (f32[512,128]{1,0:T(8,128)S(1)}, f32[512,128]{1,0:T(8,128)}, u32[]{:S(2)}) copy-start(f32[512,128]{1,0:T(8,128)} %param.8) | copy-start | bytes 786436
  7.7 10.0 %copy-start.1 = (f32[1024,128]{1,0:T(8,128)S(1)}, f32[1024,128]{1,0:T(8,128)}, u32[]{:S(2)}) copy-start(f32[1024,128]{1,0:T(8,128)} %param.7) | copy-start | bytes 1572868
  11.3 1.8 %collective-permute-start = (f32[512,128]{1,0:T(8,128)S(1)}, f32[512,128]{1,0:T(8,128)}, u32[]{:S(2)}, u32[]{:S(2)}) collective-permute-start(f32[512,128]{1,0:T(8,128)S(1)} %constant_dynamic-slice_fusion.3), channel_id=1, source_target_pairs={{0,1},{1,0},{2,3},{3,2},{4,5},{5,4},{6,7},{7,6},{8,9},{9,8},{10,11... | collective-permute-start | bytes 786440 | tf_op jit(solution)/shard_map/ppermute | solution.py:34
  14.8 6.9 %collective-permute-start.1 = (f32[256,128]{1,0:T(8,128)}, f32[256,128]{1,0:T(8,128)S(1)}, u32[]{:S(2)}, u32[]{:S(2)}) collective-permute-start(f32[256,128]{1,0:T(8,128)} %constant_dynamic-slice_fusion.2), channel_id=1, source_target_pairs={{0,2},{1,3},{2,0},{3,1},{4,6},{5,7},{6,4},{7,5},{8,10},{9,11},{10,... | collective-permute-start | bytes 393224 | tf_op jit(solution)/shard_map/ppermute | solution.py:34
  21.7 5.3 %collective-permute-start.2 = (f32[256,128]{1,0:T(8,128)S(1)}, f32[256,128]{1,0:T(8,128)S(1)}, u32[]{:S(2)}, u32[]{:S(2)}) collective-permute-start(f32[256,128]{1,0:T(8,128)S(1)} %dynamic-slice_add_fusion.3), channel_id=1, source_target_pairs={{0,4},{1,5},{2,6},{3,7},{4,0},{5,1},{6,2},{7,3},{8,12},{9,13},{10,... | collective-permute-start | bytes 393224 | tf_op jit(solution)/shard_map/ppermute | solution.py:34
  27.1 8.2 %collective-permute-start.3 = (f32[256,128]{1,0:T(8,128)S(1)}, f32[256,128]{1,0:T(8,128)S(1)}, u32[]{:S(2)}, u32[]{:S(2)}) collective-permute-start(f32[256,128]{1,0:T(8,128)S(1)} %add.179), channel_id=1, source_target_pairs={{0,8},{1,9},{2,10},{3,11},{4,12},{5,13},{6,14},{7,15},{8,0},{9,1},... | collective-permute-start | bytes 393224 | tf_op jit(solution)/shard_map/ppermute | solution.py:34
  35.9 5.0 %collective-permute-start.4 = (f32[256,128]{1,0:T(8,128)S(1)}, f32[256,128]{1,0:T(8,128)S(1)}, u32[]{:S(2)}, u32[]{:S(2)}) collective-permute-start(f32[256,128]{1,0:T(8,128)S(1)} %get-tuple-element.5), channel_id=1, source_target_pairs={{0,2},{1,3},{2,0},{3,1},{4,6},{5,7},{6,4},{7,5},{8,10},{9,11},{10,... | collective-permute-start | bytes 393224 | tf_op jit(solution)/shard_map/ppermute | solution.py:34
  38.1 6.7 %copy-start.2 = (f32[1024,512]{1,0:T(8,128)S(1)}, f32[1024,512]{1,0:T(8,128)}, u32[]{:S(2)}) copy-start(f32[1024,512]{1,0:T(8,128)} %get-tuple-element.6) | copy-start | bytes 6291460
  40.8 0.7 copy-start.9
  41.5 3.1 %copy-start.6 = (f32[512,128]{1,0:T(8,128)}, f32[512,128]{1,0:T(8,128)S(1)}, u32[]{:S(2)}) copy-start(f32[512,128]{1,0:T(8,128)S(1)} %maximum_select_fusion.1) | copy-start | bytes 786436
  41.5 3.1 %collective-permute-start.5 = (f32[512,128]{1,0:T(8,128)S(1)}, f32[512,128]{1,0:T(8,128)S(1)}, u32[]{:S(2)}, u32[]{:S(2)}) collective-permute-start(f32[512,128]{1,0:T(8,128)S(1)} %maximum_select_fusion.1), channel_id=1, source_target_pairs={{0,1},{1,0},{2,3},{3,2},{4,5},{5,4},{6,7},{7,6},{8,9},{9,8},{10,11... | collective-permute-start | bytes 786440 | tf_op jit(solution)/shard_map/ppermute | solution.py:34
  43.1 9.5 %copy-start.10 = (s32[512]{0:T(512)S(1)}, s32[512]{0:T(512)}, u32[]{:S(2)}) copy-start(s32[512]{0:T(512)} %param.6) | copy-start | bytes 6148
  45.5 13.6 %copy-start.7 = (f32[512,128]{1,0:T(8,128)S(1)}, f32[512,128]{1,0:T(8,128)}, u32[]{:S(2)}) copy-start(f32[512,128]{1,0:T(8,128)} %copy-done.6) | copy-start | bytes 786436
  47.5 11.5 %all-to-all-start = ((f32[16,2,128]{2,1,0:T(2,128)}), f32[16,2,128]{2,1,0:T(2,128)S(1)}, u32[]{:S(2)}, u32[]{:S(2)}) async-start(f32[16,2,128]{2,1,0:T(2,128)} %broadcast_in_dim.31), calls=%async_computation | async-start | bytes 32768 | tf_op jit(solution)/shard_map/all_to_all | solution.py:78
  52.5 6.7 %copy-start.11 = (f32[512]{0:T(512)S(1)}, f32[512]{0:T(512)}, u32[]{:S(2)}) copy-start(f32[512]{0:T(512)} %param.9) | copy-start | bytes 6148
  67.9 1.6 %collective-permute-start.6 = (f32[512,128]{1,0:T(8,128)S(1)}, f32[512,128]{1,0:T(8,128)S(1)}, u32[]{:S(2)}, u32[]{:S(2)}) collective-permute-start(f32[512,128]{1,0:T(8,128)S(1)} %constant_dynamic-slice_fusion.1), channel_id=1, source_target_pairs={{0,1},{1,0},{2,3},{3,2},{4,5},{5,4},{6,7},{7,6},{8,9},{9,8},{10,11... | collective-permute-start | bytes 786440 | tf_op jit(solution)/shard_map/ppermute | solution.py:34
  69.5 6.7 %collective-permute-start.7 = (f32[256,128]{1,0:T(8,128)S(1)}, f32[256,128]{1,0:T(8,128)S(1)}, u32[]{:S(2)}, u32[]{:S(2)}) collective-permute-start(f32[256,128]{1,0:T(8,128)S(1)} %constant_dynamic-slice_fusion), channel_id=1, source_target_pairs={{0,2},{1,3},{2,0},{3,1},{4,6},{5,7},{6,4},{7,5},{8,10},{9,11},{10,... | collective-permute-start | bytes 393224 | tf_op jit(solution)/shard_map/ppermute | solution.py:34
  76.2 5.3 %collective-permute-start.8 = (f32[256,128]{1,0:T(8,128)S(1)}, f32[256,128]{1,0:T(8,128)S(1)}, u32[]{:S(2)}, u32[]{:S(2)}) collective-permute-start(f32[256,128]{1,0:T(8,128)S(1)} %dynamic-slice_add_fusion.2), channel_id=1, source_target_pairs={{0,4},{1,5},{2,6},{3,7},{4,0},{5,1},{6,2},{7,3},{8,12},{9,13},{10,... | collective-permute-start | bytes 393224 | tf_op jit(solution)/shard_map/ppermute | solution.py:34
  81.5 8.2 %collective-permute-start.9 = (f32[256,128]{1,0:T(8,128)S(1)}, f32[256,128]{1,0:T(8,128)S(1)}, u32[]{:S(2)}, u32[]{:S(2)}) collective-permute-start(f32[256,128]{1,0:T(8,128)S(1)} %add.200), channel_id=1, source_target_pairs={{0,8},{1,9},{2,10},{3,11},{4,12},{5,13},{6,14},{7,15},{8,0},{9,1},... | collective-permute-start | bytes 393224 | tf_op jit(solution)/shard_map/ppermute | solution.py:34
  90.3 5.0 %collective-permute-start.10 = (f32[256,128]{1,0:T(8,128)S(1)}, f32[256,128]{1,0:T(8,128)S(1)}, u32[]{:S(2)}, u32[]{:S(2)}) collective-permute-start(f32[256,128]{1,0:T(8,128)S(1)} %get-tuple-element.3), channel_id=1, source_target_pairs={{0,2},{1,3},{2,0},{3,1},{4,6},{5,7},{6,4},{7,5},{8,10},{9,11},{10,... | collective-permute-start | bytes 393224 | tf_op jit(solution)/shard_map/ppermute | solution.py:34
  93.5 5.6 %copy-start.3 = (f32[1024,512]{1,0:T(8,128)S(1)}, f32[1024,512]{1,0:T(8,128)}, u32[]{:S(2)}) copy-start(f32[1024,512]{1,0:T(8,128)} %get-tuple-element.12) | copy-start | bytes 6291460
  95.3 0.7 copy-start.8
  96.0 3.1 %copy-start.4 = (f32[512,128]{1,0:T(8,128)}, f32[512,128]{1,0:T(8,128)S(1)}, u32[]{:S(2)}) copy-start(f32[512,128]{1,0:T(8,128)S(1)} %maximum_select_fusion.2) | copy-start | bytes 786436
  96.0 3.1 %collective-permute-start.11 = (f32[512,128]{1,0:T(8,128)S(1)}, f32[512,128]{1,0:T(8,128)S(1)}, u32[]{:S(2)}, u32[]{:S(2)}) collective-permute-start(f32[512,128]{1,0:T(8,128)S(1)} %maximum_select_fusion.2), channel_id=1, source_target_pairs={{0,1},{1,0},{2,3},{3,2},{4,5},{5,4},{6,7},{7,6},{8,9},{9,8},{10,11... | collective-permute-start | bytes 786440 | tf_op jit(solution)/shard_map/ppermute | solution.py:34
  99.1 13.3 %copy-start.5 = (f32[512,128]{1,0:T(8,128)S(1)}, f32[512,128]{1,0:T(8,128)}, u32[]{:S(2)}) copy-start(f32[512,128]{1,0:T(8,128)} %copy-done.4) | copy-start | bytes 786436
  101.7 10.0 %all-to-all-start.1 = ((f32[16,2,128]{2,1,0:T(2,128)}), f32[16,2,128]{2,1,0:T(2,128)S(1)}, u32[]{:S(2)}, u32[]{:S(2)}) async-start(f32[16,2,128]{2,1,0:T(2,128)} %broadcast_in_dim.33), calls=%async_computation.1 | async-start | bytes 32768 | tf_op jit(solution)/shard_map/all_to_all | solution.py:78

commit v9 on v5

--- a/solution.py
+++ b/solution.py
@@ -10,7 +10,7 @@
 background = 0.5
 
 
-def product(left, right, precision=lax.Precision.HIGHEST):
+def product(left, right, precision=lax.Precision.HIGH):
     return jnp.dot(left, right, precision=precision, preferred_element_type=jnp.float32)
 
 
@@ -89,8 +89,8 @@
         bending = jnp.zeros((user_factor.shape[0],), jnp.float32)
         for piece, first in pieces:
             rows = piece.shape[0]
-            tangent_image = product(piece, user_factor.T, lax.Precision.HIGH) + product(
-                lax.dynamic_slice_in_dim(time_factor, first, rows, 0), grad_user.T, lax.Precision.HIGH
+            tangent_image = product(piece, user_factor.T) + product(
+                lax.dynamic_slice_in_dim(time_factor, first, rows, 0), grad_user.T
             )
             weight = lax.dynamic_slice_in_dim(curvature, first, rows, 0)
             bending = bending + jnp.sum(weight * tangent_image * tangent_image, axis=0)

time: 111 us -> 108 us (0.973)
  matrix products: 34.6 us -> 28.1 us
  waiting for transfers between devices: 39.3 us -> 42.6 us
    dot_general x18, matrix products: 34.6 us -> 28.1 us  [product(): jnp.dot(left, right, precision=precision, preferred_element_type=jnp.floa...]
    ppermute x12, waiting for transfers between devices: 26.5 us -> 29.6 us  [exchange(): return lax.ppermute(value, 'user', [(i, i ^ distance) for i in range(n)])]
  transfers between devices with their start and end apart: 14 -> 14, of which waited for: 11 -> 12; matrix products, arithmetic and copies ran while one was open for 15% -> 13% of each run, Pallas kernels for 0% -> 0%
where the time goes in v9:
time: 108 us
  waiting for transfers between devices  42.6 us (39%)
  matrix products  28.1 us (26%)
  starting transfers between devices  20.6 us (19%)
  local copies, waits for them, and re-layouts  6.51 us (6%)
  other arithmetic  6.29 us (6%)
  between operations  3.58 us (3%)
    ppermute x12, waiting for transfers between devices, exchange(): return lax.ppermute(value, 'user', [(i, i ^ distance) for i in range(n)])  29.6 us
    dot_general x18, matrix products, product(): jnp.dot(left, right, precision=precision, preferred_element_type=jnp.floa...  28.1 us
    all_to_all x2, waiting for transfers between devices, sum_rows(): spread = lax.all_to_all(spread, 'user', 0, 0, tiled=False)  12.9 us
    ppermute x12, starting transfers between devices, exchange(): return lax.ppermute(value, 'user', [(i, i ^ distance) for i in range(n)])  11.6 us
    all_to_all x2, starting transfers between devices, sum_rows(): spread = lax.all_to_all(spread, 'user', 0, 0, tiled=False)  9.01 us
  transfers between devices with their start and end apart: 14, of which 12 were waited for; matrix products, arithmetic and copies ran while one was open for 13% of the time, Pallas kernels for 0%

profile of v9, /device:TPU:0, one launch (start us, length us, event | category | flops | bytes accessed | tf_op | source)
XLA Modules:
  0.0 107.6 jit_solution(14261508605619229301)
XLA Ops:
  0.7 6.2 %multiply_select_fusion.2 = (f32[1024,512]{1,0:T(8,128)}, f32[1024,512]{1,0:T(8,128)S(1)}) fusion(s32[512]{0:T(512)} %param.6, f32[512]{0:T(512)} %param.9, s32[1024,512]{1,0:T(8,128)} %param.5, f32[1024,128]{1,0:T(8,128)} %param.7, f32[512,128]{1,0:T(8,128)} %param.8), kind=kOutput, calls=%fused_computation.5 | convolution fusion | flops 413138944 | bytes 7081984 | tf_op jit(solution)/shard_map/dot_general | solution.py:14
  6.9 1.8 %fusion.31 = f32[1024,128]{1,0:T(8,128)} fusion(f32[1024,512]{1,0:T(8,128)S(1)} %get-tuple-element.9, f32[512,128]{1,0:T(8,128)S(1)} %copy-done), kind=kOutput, calls=%fused_computation.80 | convolution fusion | flops 402653184 | bytes 2883584 | tf_op jit(solution)/shard_map/dot_general | solution.py:14
  8.7 1.0 constant_dynamic-slice_fusion.3
  9.6 0.5 collective-permute-start
  10.2 1.3 %collective-permute-done = f32[512,128]{1,0:T(8,128)} collective-permute-done((f32[512,128]{1,0:T(8,128)S(1)}, f32[512,128]{1,0:T(8,128)}, u32[]{:S(2)}, u32[]{:S(2)}) %collective-permute-start) | collective-permute-done | bytes 262176 | tf_op jit(solution)/shard_map/ppermute | solution.py:31
  11.5 1.1 dynamic-slice_add_fusion.1
  12.5 0.7 constant_dynamic-slice_fusion.2
  13.2 2.9 %collective-permute-start.1 = (f32[256,128]{1,0:T(8,128)}, f32[256,128]{1,0:T(8,128)S(1)}, u32[]{:S(2)}, u32[]{:S(2)}) collective-permute-start(f32[256,128]{1,0:T(8,128)} %constant_dynamic-slice_fusion.2), channel_id=1, source_target_pairs={{0,2},{1,3},{2,0},{3,1},{4,6},{5,7},{6,4},{7,5},{8,10},{9,11},{10,... | collective-permute-start | bytes 393224 | tf_op jit(solution)/shard_map/ppermute | solution.py:31
  16.1 2.4 %multiply_reduce_fusion.1 = (f32[]{:T(128)}, f32[512,128]{1,0:T(8,128)S(1)}) fusion(f32[1024,512]{1,0:T(8,128)S(1)} %get-tuple-element.9, f32[1024,128]{1,0:T(8,128)S(1)} %copy-done.1), kind=kOutput, calls=%fused_computation.47 | convolution fusion | flops 402784256 | bytes 2883588 | tf_op jit(solution)/shard_map/dot_general | solution.py:14
  18.5 1.6 %collective-permute-done.1 = f32[256,128]{1,0:T(8,128)S(1)} collective-permute-done((f32[256,128]{1,0:T(8,128)}, f32[256,128]{1,0:T(8,128)S(1)}, u32[]{:S(2)}, u32[]{:S(2)}) %collective-permute-start.1) | collective-permute-done | bytes 131104 | tf_op jit(solution)/shard_map/ppermute | solution.py:31
  20.1 1.9 %collective-permute-start.2 = (f32[256,128]{1,0:T(8,128)S(1)}, f32[256,128]{1,0:T(8,128)S(1)}, u32[]{:S(2)}, u32[]{:S(2)}) collective-permute-start(f32[256,128]{1,0:T(8,128)S(1)} %dynamic-slice_add_fusion.3), channel_id=1, source_target_pairs={{0,4},{1,5},{2,6},{3,7},{4,0},{5,1},{6,2},{7,3},{8,12},{9,13},{10,... | collective-permute-start | bytes 393224 | tf_op jit(solution)/shard_map/ppermute | solution.py:31
  22.0 0.6 fusion.10
  22.6 2.6 %collective-permute-done.2 = f32[256,128]{1,0:T(8,128)S(1)} collective-permute-done((f32[256,128]{1,0:T(8,128)S(1)}, f32[256,128]{1,0:T(8,128)S(1)}, u32[]{:S(2)}, u32[]{:S(2)}) %collective-permute-start.2) | collective-permute-done | bytes 131104 | tf_op jit(solution)/shard_map/ppermute | solution.py:31
  25.2 2.8 %collective-permute-start.3 = (f32[256,128]{1,0:T(8,128)S(1)}, f32[256,128]{1,0:T(8,128)S(1)}, u32[]{:S(2)}, u32[]{:S(2)}) collective-permute-start(f32[256,128]{1,0:T(8,128)S(1)} %add.179), channel_id=1, source_target_pairs={{0,8},{1,9},{2,10},{3,11},{4,12},{5,13},{6,14},{7,15},{8,0},{9,1},... | collective-permute-start | bytes 393224 | tf_op jit(solution)/shard_map/ppermute | solution.py:31
  28.0 0.4 fusion.16
  28.4 4.7 %collective-permute-done.3 = f32[256,128]{1,0:T(8,128)S(1)} collective-permute-done((f32[256,128]{1,0:T(8,128)S(1)}, f32[256,128]{1,0:T(8,128)S(1)}, u32[]{:S(2)}, u32[]{:S(2)}) %collective-permute-start.3) | collective-permute-done | bytes 131104 | tf_op jit(solution)/shard_map/ppermute | solution.py:31
  33.1 0.6 multiply_reduce_fusion.3
  33.7 1.1 %collective-permute-start.4 = (f32[256,128]{1,0:T(8,128)S(1)}, f32[256,128]{1,0:T(8,128)S(1)}, u32[]{:S(2)}, u32[]{:S(2)}) collective-permute-start(f32[256,128]{1,0:T(8,128)S(1)} %get-tuple-element.5), channel_id=1, source_target_pairs={{0,2},{1,3},{2,0},{3,1},{4,6},{5,7},{6,4},{7,5},{8,10},{9,11},{10,... | collective-permute-start | bytes 393224 | tf_op jit(solution)/shard_map/ppermute | solution.py:31
  34.8 0.4 fusion.18
  36.5 2.2 %collective-permute-done.4 = f32[256,128]{1,0:T(8,128)S(1)} collective-permute-done((f32[256,128]{1,0:T(8,128)S(1)}, f32[256,128]{1,0:T(8,128)S(1)}, u32[]{:S(2)}, u32[]{:S(2)}) %collective-permute-start.4) | collective-permute-done | bytes 131104 | tf_op jit(solution)/shard_map/ppermute | solution.py:31
  38.7 0.7 copy-done.8
  39.4 0.0 copy-start.6
  39.4 0.1 collective-permute-start.5
  39.5 1.5 %fusion.5 = f32[512]{0:T(512)S(1)} fusion(f32[256,512]{1,0:T(8,128)S(1)} %fusion.18, f32[256,128]{1,0:T(8,128)S(1)} %get-tuple-element.5, f32[512,128]{1,0:T(8,128)S(1)} %copy-done, f32[1024,512]{1,0:T(8,128)} %get-tuple-element.8, s32[]{:T(128)S(6)} %select_n.133), kind=kOutput, calls=%fused_computation.28 | convolution fusion | flops 101187072 | bytes 1443844 | tf_op jit(solution)/shard_map/dot_general | solution.py:14
  40.9 1.5 %fusion.4 = f32[512]{0:T(512)S(1)} fusion(f32[256,512]{1,0:T(8,128)S(1)} %fusion.16, f32[256,128]{1,0:T(8,128)} %copy-done.8, f32[512,128]{1,0:T(8,128)S(1)} %copy-done, f32[1024,512]{1,0:T(8,128)} %get-tuple-element.8, s32[]{:T(128)S(6)} %select_n.134), kind=kOutput, calls=%fused_computation.26 | convolution fusion | flops 101187072 | bytes 1443844 | tf_op jit(solution)/shard_map/dot_general | solution.py:14
  42.5 0.0 copy-start.10
  42.5 0.0 copy-start.7
  42.5 0.6 fusion
  43.2 0.7 add_reduce_fusion.1
  43.9 0.7 stack.6
  44.6 0.7 broadcast_in_dim.15
  45.2 5.5 %all-to-all-start = ((f32[16,2,128]{2,1,0:T(2,128)}), f32[16,2,128]{2,1,0:T(2,128)S(1)}, u32[]{:S(2)}, u32[]{:S(2)}) async-start(f32[16,2,128]{2,1,0:T(2,128)} %broadcast_in_dim.15), calls=%async_computation | async-start | bytes 32768 | tf_op jit(solution)/shard_map/all_to_all | solution.py:75
  50.8 6.5 %all-to-all-done = f32[16,2,128]{2,1,0:T(2,128)S(1)} async-done(((f32[16,2,128]{2,1,0:T(2,128)}), f32[16,2,128]{2,1,0:T(2,128)S(1)}, u32[]{:S(2)}, u32[]{:S(2)}) %all-to-all-start) | async-done | bytes 16416 | tf_op jit(solution)/shard_map/all_to_all | solution.py:75
  57.3 0.1 fusion.7
  57.4 1.4 %copy-done.9 = s32[1024,512]{1,0:T(8,128)S(1)} copy-done((s32[1024,512]{1,0:T(8,128)S(1)}, s32[1024,512]{1,0:T(8,128)}, u32[]{:S(2)}) %copy-start.9) | copy-done | bytes 2097176
  58.9 4.3 %multiply_select_fusion = (f32[1024,512]{1,0:T(8,128)}, f32[1024,512]{1,0:T(8,128)S(1)}) fusion(s32[512]{0:T(512)S(1)} %copy-done.10, f32[512]{0:T(512)S(1)} %copy-done.11, s32[1024,512]{1,0:T(8,128)S(1)} %copy-done.9, f32[1024,128]{1,0:T(8,128)S(1)} %fusion.7, f32[512,128]{1,0:T(8,128)S(1)} %multiply_subtract_fusion.1), kind=kOutput, calls=%fused_computation | convolution fusion | flops 413138944 | bytes 7081984 | tf_op jit(solution)/shard_map/dot_general | solution.py:14
  63.2 1.0 fusion.32
  64.2 0.1 collective-permute-start.6
  64.3 1.5 %collective-permute-done.6 = f32[512,128]{1,0:T(8,128)S(1)} collective-permute-done((f32[512,128]{1,0:T(8,128)S(1)}, f32[512,128]{1,0:T(8,128)S(1)}, u32[]{:S(2)}, u32[]{:S(2)}) %collective-permute-start.6) | collective-permute-done | bytes 262176 | tf_op jit(solution)/shard_map/ppermute | solution.py:31
  65.9 0.5 collective-permute-start.7
  66.4 2.4 %multiply_reduce_fusion = (f32[]{:T(128)}, f32[512,128]{1,0:T(8,128)S(1)}) fusion(f32[1024,512]{1,0:T(8,128)S(1)} %get-tuple-element.7, f32[1024,128]{1,0:T(8,128)S(1)} %fusion.7), kind=kOutput, calls=%fused_computation.42 | convolution fusion | flops 402784256 | bytes 2883588 | tf_op jit(solution)/shard_map/dot_general | solution.py:14
  68.8 2.7 %collective-permute-done.7 = f32[256,128]{1,0:T(8,128)S(1)} collective-permute-done((f32[256,128]{1,0:T(8,128)S(1)}, f32[256,128]{1,0:T(8,128)S(1)}, u32[]{:S(2)}, u32[]{:S(2)}) %collective-permute-start.7) | collective-permute-done | bytes 131104 | tf_op jit(solution)/shard_map/ppermute | solution.py:31
  71.5 0.5 collective-permute-start.8
  72.0 0.6 fusion.8
  72.6 3.9 %collective-permute-done.8 = f32[256,128]{1,0:T(8,128)S(1)} collective-permute-done((f32[256,128]{1,0:T(8,128)S(1)}, f32[256,128]{1,0:T(8,128)S(1)}, u32[]{:S(2)}, u32[]{:S(2)}) %collective-permute-start.8) | collective-permute-done | bytes 131104 | tf_op jit(solution)/shard_map/ppermute | solution.py:31
  76.6 0.5 collective-permute-start.9
  77.1 0.4 fusion.12
  77.5 6.3 %collective-permute-done.9 = f32[256,128]{1,0:T(8,128)S(1)} collective-permute-done((f32[256,128]{1,0:T(8,128)S(1)}, f32[256,128]{1,0:T(8,128)S(1)}, u32[]{:S(2)}, u32[]{:S(2)}) %collective-permute-start.9) | collective-permute-done | bytes 131104 | tf_op jit(solution)/shard_map/ppermute | solution.py:31
  83.8 0.6 multiply_reduce_fusion.2
  84.4 0.6 collective-permute-start.10
  85.0 0.4 fusion.14
  86.7 2.8 %collective-permute-done.10 = f32[256,128]{1,0:T(8,128)} collective-permute-done((f32[256,128]{1,0:T(8,128)S(1)}, f32[256,128]{1,0:T(8,128)}, u32[]{:S(2)}, u32[]{:S(2)}) %collective-permute-start.10) | collective-permute-done | bytes 131104 | tf_op jit(solution)/shard_map/ppermute | solution.py:31
  89.5 1.0 maximum_select_fusion.2
  90.5 0.1 collective-permute-start.11
  90.6 1.5 %fusion.3 = f32[512]{0:T(512)S(1)} fusion(f32[256,512]{1,0:T(8,128)S(1)} %fusion.14, f32[256,128]{1,0:T(8,128)S(1)} %get-tuple-element.3, f32[512,128]{1,0:T(8,128)S(1)} %multiply_subtract_fusion.1, f32[1024,512]{1,0:T(8,128)} %get-tuple-element.6, s32[]{:T(128)S(6)} %select_n.133), kind=kOutput, calls=%fused_computation.24 | convolution fusion | flops 101187072 | bytes 1443844 | tf_op jit(solution)/shard_map/dot_general | solution.py:14
  92.1 1.5 %fusion.2 = f32[512]{0:T(512)S(1)} fusion(f32[256,512]{1,0:T(8,128)S(1)} %fusion.12, f32[256,128]{1,0:T(8,128)} %collective-permute-done.10, f32[512,128]{1,0:T(8,128)S(1)} %multiply_subtract_fusion.1, f32[1024,512]{1,0:T(8,128)} %get-tuple-element.6, s32[]{:T(128)S(6)} %select_n.134), kind=kOutput, calls=%fused_computation.22 | convolution fusion | flops 101187072 | bytes 1443844 | tf_op jit(solution)/shard_map/dot_general | solution.py:14
  93.6 0.6 fusion.1
  94.3 0.6 add_reduce_fusion
  94.9 0.6 stack.7
  95.5 0.7 broadcast_in_dim.16
  96.2 3.5 %all-to-all-start.1 = ((f32[16,2,128]{2,1,0:T(2,128)}), f32[16,2,128]{2,1,0:T(2,128)S(1)}, u32[]{:S(2)}, u32[]{:S(2)}) async-start(f32[16,2,128]{2,1,0:T(2,128)} %broadcast_in_dim.16), calls=%async_computation.1 | async-start | bytes 32768 | tf_op jit(solution)/shard_map/all_to_all | solution.py:75
  99.7 6.5 %all-to-all-done.1 = f32[16,2,128]{2,1,0:T(2,128)S(1)} async-done(((f32[16,2,128]{2,1,0:T(2,128)}), f32[16,2,128]{2,1,0:T(2,128)S(1)}, u32[]{:S(2)}, u32[]{:S(2)}) %all-to-all-start.1) | async-done | bytes 16416 | tf_op jit(solution)/shard_map/all_to_all | solution.py:75
  106.2 0.7 multiply_subtract_fusion
  107.0 0.6 dynamic-slice_subtract_fusion
  (34 shorter events, 0.3 us)
Async XLA Ops:
  0.6 6.2 %copy-start = (f32[512,128]{1,0:T(8,128)S(1)}, f32[512,128]{1,0:T(8,128)}, u32[]{:S(2)}) copy-start(f32[512,128]{1,0:T(8,128)} %param.8) | copy-start | bytes 786436
  6.9 9.2 %copy-start.1 = (f32[1024,128]{1,0:T(8,128)S(1)}, f32[1024,128]{1,0:T(8,128)}, u32[]{:S(2)}) copy-start(f32[1024,128]{1,0:T(8,128)} %param.7) | copy-start | bytes 1572868
  9.6 1.8 %collective-permute-start = (f32[512,128]{1,0:T(8,128)S(1)}, f32[512,128]{1,0:T(8,128)}, u32[]{:S(2)}, u32[]{:S(2)}) collective-permute-start(f32[512,128]{1,0:T(8,128)S(1)} %constant_dynamic-slice_fusion.3), channel_id=1, source_target_pairs={{0,1},{1,0},{2,3},{3,2},{4,5},{5,4},{6,7},{7,6},{8,9},{9,8},{10,11... | collective-permute-start | bytes 786440 | tf_op jit(solution)/shard_map/ppermute | solution.py:31
  13.2 6.9 %collective-permute-start.1 = (f32[256,128]{1,0:T(8,128)}, f32[256,128]{1,0:T(8,128)S(1)}, u32[]{:S(2)}, u32[]{:S(2)}) collective-permute-start(f32[256,128]{1,0:T(8,128)} %constant_dynamic-slice_fusion.2), channel_id=1, source_target_pairs={{0,2},{1,3},{2,0},{3,1},{4,6},{5,7},{6,4},{7,5},{8,10},{9,11},{10,... | collective-permute-start | bytes 393224 | tf_op jit(solution)/shard_map/ppermute | solution.py:31
  20.1 5.1 %collective-permute-start.2 = (f32[256,128]{1,0:T(8,128)S(1)}, f32[256,128]{1,0:T(8,128)S(1)}, u32[]{:S(2)}, u32[]{:S(2)}) collective-permute-start(f32[256,128]{1,0:T(8,128)S(1)} %dynamic-slice_add_fusion.3), channel_id=1, source_target_pairs={{0,4},{1,5},{2,6},{3,7},{4,0},{5,1},{6,2},{7,3},{8,12},{9,13},{10,... | collective-permute-start | bytes 393224 | tf_op jit(solution)/shard_map/ppermute | solution.py:31
  25.2 7.9 %collective-permute-start.3 = (f32[256,128]{1,0:T(8,128)S(1)}, f32[256,128]{1,0:T(8,128)S(1)}, u32[]{:S(2)}, u32[]{:S(2)}) collective-permute-start(f32[256,128]{1,0:T(8,128)S(1)} %add.179), channel_id=1, source_target_pairs={{0,8},{1,9},{2,10},{3,11},{4,12},{5,13},{6,14},{7,15},{8,0},{9,1},... | collective-permute-start | bytes 393224 | tf_op jit(solution)/shard_map/ppermute | solution.py:31
  33.7 5.0 %collective-permute-start.4 = (f32[256,128]{1,0:T(8,128)S(1)}, f32[256,128]{1,0:T(8,128)S(1)}, u32[]{:S(2)}, u32[]{:S(2)}) collective-permute-start(f32[256,128]{1,0:T(8,128)S(1)} %get-tuple-element.5), channel_id=1, source_target_pairs={{0,2},{1,3},{2,0},{3,1},{4,6},{5,7},{6,4},{7,5},{8,10},{9,11},{10,... | collective-permute-start | bytes 393224 | tf_op jit(solution)/shard_map/ppermute | solution.py:31
  36.5 6.0 %copy-start.2 = (f32[1024,512]{1,0:T(8,128)S(1)}, f32[1024,512]{1,0:T(8,128)}, u32[]{:S(2)}) copy-start(f32[1024,512]{1,0:T(8,128)} %get-tuple-element.8) | copy-start | bytes 6291460
  38.7 0.7 copy-start.8
  39.4 3.1 %copy-start.6 = (f32[512,128]{1,0:T(8,128)}, f32[512,128]{1,0:T(8,128)S(1)}, u32[]{:S(2)}) copy-start(f32[512,128]{1,0:T(8,128)S(1)} %maximum_select_fusion.1) | copy-start | bytes 786436
  39.4 3.1 %collective-permute-start.5 = (f32[512,128]{1,0:T(8,128)S(1)}, f32[512,128]{1,0:T(8,128)S(1)}, u32[]{:S(2)}, u32[]{:S(2)}) collective-permute-start(f32[512,128]{1,0:T(8,128)S(1)} %maximum_select_fusion.1), channel_id=1, source_target_pairs={{0,1},{1,0},{2,3},{3,2},{4,5},{5,4},{6,7},{7,6},{8,9},{9,8},{10,11... | collective-permute-start | bytes 786440 | tf_op jit(solution)/shard_map/ppermute | solution.py:31
  42.5 14.9 %copy-start.10 = (s32[512]{0:T(512)S(1)}, s32[512]{0:T(512)}, u32[]{:S(2)}) copy-start(s32[512]{0:T(512)} %param.6) | copy-start | bytes 6148
  42.5 14.9 %copy-start.11 = (f32[512]{0:T(512)S(1)}, f32[512]{0:T(512)}, u32[]{:S(2)}) copy-start(f32[512]{0:T(512)} %param.9) | copy-start | bytes 6148
  42.5 14.8 %copy-start.7 = (f32[512,128]{1,0:T(8,128)S(1)}, f32[512,128]{1,0:T(8,128)}, u32[]{:S(2)}) copy-start(f32[512,128]{1,0:T(8,128)} %copy-done.6) | copy-start | bytes 786436
  45.2 12.0 %all-to-all-start = ((f32[16,2,128]{2,1,0:T(2,128)}), f32[16,2,128]{2,1,0:T(2,128)S(1)}, u32[]{:S(2)}, u32[]{:S(2)}) async-start(f32[16,2,128]{2,1,0:T(2,128)} %broadcast_in_dim.15), calls=%async_computation | async-start | bytes 32768 | tf_op jit(solution)/shard_map/all_to_all | solution.py:75
  57.3 1.6 %copy-start.9 = (s32[1024,512]{1,0:T(8,128)S(1)}, s32[1024,512]{1,0:T(8,128)}, u32[]{:S(2)}) copy-start(s32[1024,512]{1,0:T(8,128)} %param.5) | copy-start | bytes 6291460
  64.2 1.6 %collective-permute-start.6 = (f32[512,128]{1,0:T(8,128)S(1)}, f32[512,128]{1,0:T(8,128)S(1)}, u32[]{:S(2)}, u32[]{:S(2)}) collective-permute-start(f32[512,128]{1,0:T(8,128)S(1)} %constant_dynamic-slice_fusion.1), channel_id=1, source_target_pairs={{0,1},{1,0},{2,3},{3,2},{4,5},{5,4},{6,7},{7,6},{8,9},{9,8},{10,11... | collective-permute-start | bytes 786440 | tf_op jit(solution)/shard_map/ppermute | solution.py:31
  65.9 5.6 %collective-permute-start.7 = (f32[256,128]{1,0:T(8,128)S(1)}, f32[256,128]{1,0:T(8,128)S(1)}, u32[]{:S(2)}, u32[]{:S(2)}) collective-permute-start(f32[256,128]{1,0:T(8,128)S(1)} %constant_dynamic-slice_fusion), channel_id=1, source_target_pairs={{0,2},{1,3},{2,0},{3,1},{4,6},{5,7},{6,4},{7,5},{8,10},{9,11},{10,... | collective-permute-start | bytes 393224 | tf_op jit(solution)/shard_map/ppermute | solution.py:31
  71.5 5.0 %collective-permute-start.8 = (f32[256,128]{1,0:T(8,128)S(1)}, f32[256,128]{1,0:T(8,128)S(1)}, u32[]{:S(2)}, u32[]{:S(2)}) collective-permute-start(f32[256,128]{1,0:T(8,128)S(1)} %dynamic-slice_add_fusion.2), channel_id=1, source_target_pairs={{0,4},{1,5},{2,6},{3,7},{4,0},{5,1},{6,2},{7,3},{8,12},{9,13},{10,... | collective-permute-start | bytes 393224 | tf_op jit(solution)/shard_map/ppermute | solution.py:31
  76.6 7.2 %collective-permute-start.9 = (f32[256,128]{1,0:T(8,128)S(1)}, f32[256,128]{1,0:T(8,128)S(1)}, u32[]{:S(2)}, u32[]{:S(2)}) collective-permute-start(f32[256,128]{1,0:T(8,128)S(1)} %add.200), channel_id=1, source_target_pairs={{0,8},{1,9},{2,10},{3,11},{4,12},{5,13},{6,14},{7,15},{8,0},{9,1},... | collective-permute-start | bytes 393224 | tf_op jit(solution)/shard_map/ppermute | solution.py:31
  84.4 5.1 %collective-permute-start.10 = (f32[256,128]{1,0:T(8,128)S(1)}, f32[256,128]{1,0:T(8,128)}, u32[]{:S(2)}, u32[]{:S(2)}) collective-permute-start(f32[256,128]{1,0:T(8,128)S(1)} %get-tuple-element.3), channel_id=1, source_target_pairs={{0,2},{1,3},{2,0},{3,1},{4,6},{5,7},{6,4},{7,5},{8,10},{9,11},{10,... | collective-permute-start | bytes 393224 | tf_op jit(solution)/shard_map/ppermute | solution.py:31
  86.7 7.0 %copy-start.3 = (f32[1024,512]{1,0:T(8,128)S(1)}, f32[1024,512]{1,0:T(8,128)}, u32[]{:S(2)}) copy-start(f32[1024,512]{1,0:T(8,128)} %get-tuple-element.6) | copy-start | bytes 6291460
  90.5 3.1 %copy-start.4 = (f32[512,128]{1,0:T(8,128)}, f32[512,128]{1,0:T(8,128)S(1)}, u32[]{:S(2)}) copy-start(f32[512,128]{1,0:T(8,128)S(1)} %maximum_select_fusion.2) | copy-start | bytes 786436
  90.5 3.1 %collective-permute-start.11 = (f32[512,128]{1,0:T(8,128)S(1)}, f32[512,128]{1,0:T(8,128)S(1)}, u32[]{:S(2)}, u32[]{:S(2)}) collective-permute-start(f32[512,128]{1,0:T(8,128)S(1)} %maximum_select_fusion.2), channel_id=1, source_target_pairs={{0,1},{1,0},{2,3},{3,2},{4,5},{5,4},{6,7},{7,6},{8,9},{9,8},{10,11... | collective-permute-start | bytes 786440 | tf_op jit(solution)/shard_map/ppermute | solution.py:31
  93.6 13.3 %copy-start.5 = (f32[512,128]{1,0:T(8,128)S(1)}, f32[512,128]{1,0:T(8,128)}, u32[]{:S(2)}) copy-start(f32[512,128]{1,0:T(8,128)} %copy-done.4) | copy-start | bytes 786436
  96.2 10.0 %all-to-all-start.1 = ((f32[16,2,128]{2,1,0:T(2,128)}), f32[16,2,128]{2,1,0:T(2,128)S(1)}, u32[]{:S(2)}, u32[]{:S(2)}) async-start(f32[16,2,128]{2,1,0:T(2,128)} %broadcast_in_dim.16), calls=%async_computation.1 | async-start | bytes 32768 | tf_op jit(solution)/shard_map/all_to_all | solution.py:75

commit v10 on v9

--- a/solution.py
+++ b/solution.py
@@ -56,15 +56,13 @@
         block = block + exchange(block, n, d)
     share = jnp.where(me < 4, jnp.sum(block * block), 0.0)
     pieces = [(block, offset)]
-    for d in reversed(halving):
-        rows = block.shape[0]
-        other = exchange(block, n, d)
-        upper = (me // d) % 2
-        pieces.append((other, offset + (1 - 2 * upper) * rows))
-        both = jnp.concatenate([block, other], axis=0)
-        swapped = jnp.concatenate([other, block], axis=0)
-        block = jnp.where(upper == 0, both, swapped)
-        offset = offset - upper * rows
+    for level in reversed(range(len(halving))):
+        d = halving[level]
+        shift = (1 - 2 * ((me // d) % 2)) * (partial.shape[0] >> (level + 1))
+        pieces = pieces + [(exchange(piece, n, d), first + shift) for piece, first in pieces]
+    block = jnp.zeros_like(partial)
+    for piece, first in pieces:
+        block = lax.dynamic_update_slice_in_dim(block, piece, first, 0)
     return block, pieces, share
 
 

time: 108 us -> 107 us (level)
    dot_general x18 -> x22, matrix products: 28.1 us -> 28.5 us  [product(): jnp.dot(left, right, precision=precision, preferred_element_type=jnp.floa...]
    ppermute x12 -> x14, starting transfers between devices: 11.6 us -> 11.3 us  [exchange(): return lax.ppermute(value, 'user', [(i, i ^ distance) for i in range(n)])]
    ppermute x12 -> x14, waiting for transfers between devices: 29.6 us -> 29.5 us  [exchange(): return lax.ppermute(value, 'user', [(i, i ^ distance) for i in range(n)])]
  transfers between devices with their start and end apart: 14 -> 16, of which waited for: 12 -> 12; matrix products, arithmetic and copies ran while one was open for 13% -> 13% of each run, Pallas kernels for 0% -> 0%
where the time goes in v10:
time: 107 us; the launch traced here: 106 us
  waiting for transfers between devices  41.7 us (39%)
  matrix products  28.5 us (27%)
  starting transfers between devices  20.5 us (19%)
  local copies, waits for them, and re-layouts  6.02 us (6%)
  other arithmetic  5.91 us (6%)
  between operations  3.69 us (3%)
    ppermute x14, waiting for transfers between devices, exchange(): return lax.ppermute(value, 'user', [(i, i ^ distance) for i in range(n)])  29.5 us
    dot_general x22, matrix products, product(): jnp.dot(left, right, precision=precision, preferred_element_type=jnp.floa...  28.5 us
    all_to_all x2, waiting for transfers between devices, sum_rows(): spread = lax.all_to_all(spread, 'user', 0, 0, tiled=False)  12.3 us
    ppermute x14, starting transfers between devices, exchange(): return lax.ppermute(value, 'user', [(i, i ^ distance) for i in range(n)])  11.3 us
    all_to_all x2, starting transfers between devices, sum_rows(): spread = lax.all_to_all(spread, 'user', 0, 0, tiled=False)  9.21 us
  transfers between devices with their start and end apart: 16, of which 12 were waited for; matrix products, arithmetic and copies ran while one was open for 13% of the time, Pallas kernels for 0%

profile of v10, /device:TPU:0, one launch (start us, length us, event | category | flops | bytes accessed | tf_op | source)
XLA Modules:
  0.0 106.4 jit_solution(3639953262292941725)
XLA Ops:
  0.7 6.2 %multiply_select_fusion.2 = (f32[1024,512]{1,0:T(8,128)}, f32[1024,512]{1,0:T(8,128)S(1)}) fusion(s32[512]{0:T(512)} %param.6, f32[512]{0:T(512)} %param.9, s32[1024,512]{1,0:T(8,128)} %param.5, f32[1024,128]{1,0:T(8,128)} %param.7, f32[512,128]{1,0:T(8,128)} %param.8), kind=kOutput, calls=%fused_computation.5 | convolution fusion | flops 413138944 | bytes 7081984 | tf_op jit(solution)/shard_map/dot_general | solution.py:14
  6.9 1.8 %fusion.31 = f32[1024,128]{1,0:T(8,128)} fusion(f32[1024,512]{1,0:T(8,128)S(1)} %get-tuple-element.9, f32[512,128]{1,0:T(8,128)S(1)} %copy-done), kind=kOutput, calls=%fused_computation.87 | convolution fusion | flops 402653184 | bytes 2883584 | tf_op jit(solution)/shard_map/dot_general | solution.py:14
  8.7 1.0 constant_dynamic-slice_fusion.3
  9.6 0.5 collective-permute-start
  10.2 2.4 %multiply_reduce_fusion.1 = (f32[]{:T(128)}, f32[512,128]{1,0:T(8,128)S(1)}) fusion(f32[1024,512]{1,0:T(8,128)S(1)} %get-tuple-element.9, f32[1024,128]{1,0:T(8,128)S(1)} %copy-done.1), kind=kOutput, calls=%fused_computation.41 | convolution fusion | flops 402784256 | bytes 2883588 | tf_op jit(solution)/shard_map/dot_general | solution.py:14
  12.6 0.4 fusion.17
  13.0 1.1 %dynamic-slice_add_fusion.1 = f32[512,128]{1,0:T(8,128)S(1)} fusion(f32[512,128]{1,0:T(8,128)} %collective-permute-done, f32[1024,128]{1,0:T(8,128)} %fusion.31, s32[]{:T(128)S(6)} %select_n.115), kind=kLoop, calls=%fused_computation.40 | loop fusion | flops 65536 | bytes 786436 | tf_op jit(solution)/shard_map/add | solution.py:54
  14.1 2.6 %collective-permute-start.1 = (f32[256,128]{1,0:T(8,128)S(1)}, f32[256,128]{1,0:T(8,128)S(1)}, u32[]{:S(2)}, u32[]{:S(2)}) collective-permute-start(f32[256,128]{1,0:T(8,128)S(1)} %constant_dynamic-slice_fusion.2), channel_id=1, source_target_pairs={{0,2},{1,3},{2,0},{3,1},{4,6},{5,7},{6,4},{7,5},{8,10},{9,11},{10,... | collective-permute-start | bytes 393224 | tf_op jit(solution)/shard_map/ppermute | solution.py:31
  16.6 0.4 fusion.19
  17.0 3.8 %collective-permute-done.1 = f32[256,128]{1,0:T(8,128)S(1)} collective-permute-done((f32[256,128]{1,0:T(8,128)S(1)}, f32[256,128]{1,0:T(8,128)S(1)}, u32[]{:S(2)}, u32[]{:S(2)}) %collective-permute-start.1) | collective-permute-done | bytes 131104 | tf_op jit(solution)/shard_map/ppermute | solution.py:31
  20.8 1.9 %collective-permute-start.2 = (f32[256,128]{1,0:T(8,128)S(1)}, f32[256,128]{1,0:T(8,128)S(1)}, u32[]{:S(2)}, u32[]{:S(2)}) collective-permute-start(f32[256,128]{1,0:T(8,128)S(1)} %dynamic-slice_add_fusion.3), channel_id=1, source_target_pairs={{0,4},{1,5},{2,6},{3,7},{4,0},{5,1},{6,2},{7,3},{8,12},{9,13},{10,... | collective-permute-start | bytes 393224 | tf_op jit(solution)/shard_map/ppermute | solution.py:31
  22.7 0.4 fusion.15
  23.1 3.1 %collective-permute-done.2 = f32[256,128]{1,0:T(8,128)S(1)} collective-permute-done((f32[256,128]{1,0:T(8,128)S(1)}, f32[256,128]{1,0:T(8,128)S(1)}, u32[]{:S(2)}, u32[]{:S(2)}) %collective-permute-start.2) | collective-permute-done | bytes 131104 | tf_op jit(solution)/shard_map/ppermute | solution.py:31
  26.2 2.7 %collective-permute-start.3 = (f32[256,128]{1,0:T(8,128)S(1)}, f32[256,128]{1,0:T(8,128)S(1)}, u32[]{:S(2)}, u32[]{:S(2)}) collective-permute-start(f32[256,128]{1,0:T(8,128)S(1)} %add.209), channel_id=1, source_target_pairs={{0,8},{1,9},{2,10},{3,11},{4,12},{5,13},{6,14},{7,15},{8,0},{9,1},... | collective-permute-start | bytes 393224 | tf_op jit(solution)/shard_map/ppermute | solution.py:31
  28.9 0.4 fusion.13
  29.3 5.1 %collective-permute-done.3 = f32[256,128]{1,0:T(8,128)S(1)} collective-permute-done((f32[256,128]{1,0:T(8,128)S(1)}, f32[256,128]{1,0:T(8,128)S(1)}, u32[]{:S(2)}, u32[]{:S(2)}) %collective-permute-start.3) | collective-permute-done | bytes 131104 | tf_op jit(solution)/shard_map/ppermute | solution.py:31
  34.4 0.6 multiply_reduce_fusion.3
  35.1 1.3 %collective-permute-start.4 = (f32[256,128]{1,0:T(8,128)S(1)}, f32[256,128]{1,0:T(8,128)S(1)}, u32[]{:S(2)}, u32[]{:S(2)}) collective-permute-start(f32[256,128]{1,0:T(8,128)S(1)} %get-tuple-element.5), channel_id=1, source_target_pairs={{0,2},{1,3},{2,0},{3,1},{4,6},{5,7},{6,4},{7,5},{8,10},{9,11},{10,... | collective-permute-start | bytes 393224 | tf_op jit(solution)/shard_map/ppermute | solution.py:31
  36.4 1.5 %fusion.7 = f32[512]{0:T(512)S(1)} fusion(f32[256,512]{1,0:T(8,128)S(1)} %fusion.19, f32[256,128]{1,0:T(8,128)S(1)} %get-tuple-element.5, f32[512,128]{1,0:T(8,128)S(1)} %copy-done, f32[1024,512]{1,0:T(8,128)} %get-tuple-element.8, s32[]{:T(128)S(6)} %select_n.123), kind=kOutput, calls=%fused_computation.34 | convolution fusion | flops 101187072 | bytes 1443844 | tf_op jit(solution)/shard_map/dot_general | solution.py:14
  39.2 0.8 collective-permute-done.4
  40.0 1.5 %fusion.6 = f32[512]{0:T(512)S(1)} fusion(f32[256,512]{1,0:T(8,128)S(1)} %fusion.17, f32[256,128]{1,0:T(8,128)S(1)} %collective-permute-done.4, f32[512,128]{1,0:T(8,128)S(1)} %copy-done, f32[1024,512]{1,0:T(8,128)} %get-tuple-element.8, s32[]{:T(128)S(6)} %select_n.124), kind=kOutput, calls=%fused_computation.32 | convolution fusion | flops 101187072 | bytes 1443844 | tf_op jit(solution)/shard_map/dot_general | solution.py:14
  41.5 0.0 copy-start.2
  41.5 0.4 fusion.5
  42.0 0.4 fusion.4
  42.5 0.6 add_reduce_fusion.1
  43.1 0.6 stack.6
  43.7 0.7 broadcast_in_dim.15
  44.4 5.7 %all-to-all-start = ((f32[16,2,128]{2,1,0:T(2,128)}), f32[16,2,128]{2,1,0:T(2,128)S(1)}, u32[]{:S(2)}, u32[]{:S(2)}) async-start(f32[16,2,128]{2,1,0:T(2,128)} %broadcast_in_dim.15), calls=%async_computation | async-start | bytes 32768 | tf_op jit(solution)/shard_map/all_to_all | solution.py:73
  50.2 6.5 %all-to-all-done = f32[16,2,128]{2,1,0:T(2,128)S(1)} async-done(((f32[16,2,128]{2,1,0:T(2,128)}), f32[16,2,128]{2,1,0:T(2,128)S(1)}, u32[]{:S(2)}, u32[]{:S(2)}) %all-to-all-start) | async-done | bytes 16416 | tf_op jit(solution)/shard_map/all_to_all | solution.py:73
  56.7 0.1 multiply_subtract_fusion
  56.8 1.4 %copy-done.7 = s32[1024,512]{1,0:T(8,128)S(1)} copy-done((s32[1024,512]{1,0:T(8,128)S(1)}, s32[1024,512]{1,0:T(8,128)}, u32[]{:S(2)}) %copy-start.7) | copy-done | bytes 2097176
  58.3 4.3 %multiply_select_fusion = (f32[1024,512]{1,0:T(8,128)}, f32[1024,512]{1,0:T(8,128)S(1)}) fusion(s32[512]{0:T(512)S(1)} %copy-done.8, f32[512]{0:T(512)S(1)} %copy-done.9, s32[1024,512]{1,0:T(8,128)S(1)} %copy-done.7, f32[1024,128]{1,0:T(8,128)S(1)} %multiply_subtract_fusion, f32[512,128]{1,0:T(8,128)S(1)} %multiply_subtract_fusion.2), kind=kOutput, calls=%fused_computation | convolution fusion | flops 413138944 | bytes 7081984 | tf_op jit(solution)/shard_map/dot_general | solution.py:14
  62.6 1.0 fusion.32
  63.6 0.1 collective-permute-start.7
  63.7 1.5 %collective-permute-done.7 = f32[512,128]{1,0:T(8,128)S(1)} collective-permute-done((f32[512,128]{1,0:T(8,128)S(1)}, f32[512,128]{1,0:T(8,128)S(1)}, u32[]{:S(2)}, u32[]{:S(2)}) %collective-permute-start.7) | collective-permute-done | bytes 262176 | tf_op jit(solution)/shard_map/ppermute | solution.py:31
  65.3 0.5 collective-permute-start.8
  65.8 5.1 %collective-permute-done.8 = f32[256,128]{1,0:T(8,128)S(1)} collective-permute-done((f32[256,128]{1,0:T(8,128)S(1)}, f32[256,128]{1,0:T(8,128)S(1)}, u32[]{:S(2)}, u32[]{:S(2)}) %collective-permute-start.8) | collective-permute-done | bytes 131104 | tf_op jit(solution)/shard_map/ppermute | solution.py:31
  70.9 0.5 collective-permute-start.9
  71.4 2.4 %multiply_reduce_fusion = (f32[]{:T(128)}, f32[512,128]{1,0:T(8,128)S(1)}) fusion(f32[1024,512]{1,0:T(8,128)S(1)} %get-tuple-element.7, f32[1024,128]{1,0:T(8,128)S(1)} %multiply_subtract_fusion), kind=kOutput, calls=%fused_computation.38 | convolution fusion | flops 402784256 | bytes 2883588 | tf_op jit(solution)/shard_map/dot_general | solution.py:14
  73.8 2.1 %collective-permute-done.9 = f32[256,128]{1,0:T(8,128)S(1)} collective-permute-done((f32[256,128]{1,0:T(8,128)S(1)}, f32[256,128]{1,0:T(8,128)S(1)}, u32[]{:S(2)}, u32[]{:S(2)}) %collective-permute-start.9) | collective-permute-done | bytes 131104 | tf_op jit(solution)/shard_map/ppermute | solution.py:31
  76.0 0.5 collective-permute-start.10
  76.5 1.2 %fusion.8 = f32[256,512]{1,0:T(8,128)} fusion(f32[512,128]{1,0:T(8,128)S(1)} %get-tuple-element.13, f32[1024,128]{1,0:T(8,128)S(1)} %multiply_subtract_fusion, s32[]{:T(128)S(6)} %select_n.126), kind=kOutput, calls=%fused_computation.42 | convolution fusion | flops 100663296 | bytes 917508 | tf_op jit(solution)/shard_map/dot_general | solution.py:14
  77.7 5.5 %collective-permute-done.10 = f32[256,128]{1,0:T(8,128)S(1)} collective-permute-done((f32[256,128]{1,0:T(8,128)S(1)}, f32[256,128]{1,0:T(8,128)S(1)}, u32[]{:S(2)}, u32[]{:S(2)}) %collective-permute-start.10) | collective-permute-done | bytes 131104 | tf_op jit(solution)/shard_map/ppermute | solution.py:31
  83.2 0.6 multiply_reduce_fusion.2
  83.8 0.6 collective-permute-start.11
  84.4 0.4 fusion.33
  84.8 0.1 collective-permute-start.12
  84.8 1.5 %fusion.3 = f32[512]{0:T(512)S(1)} fusion(f32[256,512]{1,0:T(8,128)S(1)} %fusion.33, f32[512,128]{1,0:T(8,128)S(1)} %get-tuple-element.13, f32[1024,512]{1,0:T(8,128)} %get-tuple-element.6, s32[]{:T(128)S(6)} %select_n.123, f32[1024,128]{1,0:T(8,128)S(1)} %multiply_subtract_fusion), kind=kOutput, calls=%fused_computation.26 | convolution fusion | flops 101187072 | bytes 1444864 | tf_op jit(solution)/shard_map/dot_general | solution.py:14
  87.7 1.1 %collective-permute-done.11 = f32[256,128]{1,0:T(8,128)S(1)} collective-permute-done((f32[256,128]{1,0:T(8,128)S(1)}, f32[256,128]{1,0:T(8,128)S(1)}, u32[]{:S(2)}, u32[]{:S(2)}) %collective-permute-start.11) | collective-permute-done | bytes 131104 | tf_op jit(solution)/shard_map/ppermute | solution.py:31
  88.8 0.4 fusion.34
  89.2 0.4 fusion.2
  89.6 0.4 fusion.35
  90.0 0.4 fusion.1
  90.5 0.1 collective-permute-start.13
  90.6 1.3 %collective-permute-done.13 = f32[256,128]{1,0:T(8,128)S(1)} collective-permute-done((f32[256,128]{1,0:T(8,128)S(1)}, f32[256,128]{1,0:T(8,128)S(1)}, u32[]{:S(2)}, u32[]{:S(2)}) %collective-permute-start.13) | collective-permute-done | bytes 131104 | tf_op jit(solution)/shard_map/ppermute | solution.py:31
  91.9 0.4 fusion
  92.3 0.6 add_reduce_fusion
  92.9 0.6 stack.7
  93.6 0.7 broadcast_in_dim.16
  94.3 3.5 %all-to-all-start.1 = ((f32[16,2,128]{2,1,0:T(2,128)}), f32[16,2,128]{2,1,0:T(2,128)S(1)}, u32[]{:S(2)}, u32[]{:S(2)}) async-start(f32[16,2,128]{2,1,0:T(2,128)} %broadcast_in_dim.16), calls=%async_computation.1 | async-start | bytes 32768 | tf_op jit(solution)/shard_map/all_to_all | solution.py:73
  97.8 0.7 constant_dynamic-update-slice_fusion.3
  98.4 5.8 %all-to-all-done.1 = f32[16,2,128]{2,1,0:T(2,128)S(1)} async-done(((f32[16,2,128]{2,1,0:T(2,128)}), f32[16,2,128]{2,1,0:T(2,128)S(1)}, u32[]{:S(2)}, u32[]{:S(2)}) %all-to-all-start.1) | async-done | bytes 16416 | tf_op jit(solution)/shard_map/all_to_all | solution.py:73
  104.3 0.7 multiply_subtract_fusion.1
  105.0 1.4 %dynamic-slice_subtract_fusion = f32[64,128]{1,0:T(8,128)} fusion(f32[1024,128]{1,0:T(8,128)S(1)} %multiply_subtract_fusion, s32[]{:T(128)S(6)} %select_n.131, f32[1024,128]{1,0:T(8,128)} %constant_dynamic-update-slice_fusion.3, f32[128]{0:T(128)S(1)} %fusion.30), kind=kLoop, calls=%fused_computation.59 | loop fusion | flops 16384 | bytes 98820 | tf_op jit(solution)/shard_map/sub | solution.py:102
  (46 shorter events, 0.5 us)
Async XLA Ops:
  0.6 6.2 %copy-start = (f32[512,128]{1,0:T(8,128)S(1)}, f32[512,128]{1,0:T(8,128)}, u32[]{:S(2)}) copy-start(f32[512,128]{1,0:T(8,128)} %param.8) | copy-start | bytes 786436
  6.9 3.3 %copy-start.1 = (f32[1024,128]{1,0:T(8,128)S(1)}, f32[1024,128]{1,0:T(8,128)}, u32[]{:S(2)}) copy-start(f32[1024,128]{1,0:T(8,128)} %param.7) | copy-start | bytes 1572868
  9.6 3.3 %collective-permute-start = (f32[512,128]{1,0:T(8,128)S(1)}, f32[512,128]{1,0:T(8,128)}, u32[]{:S(2)}, u32[]{:S(2)}) collective-permute-start(f32[512,128]{1,0:T(8,128)S(1)} %constant_dynamic-slice_fusion.3), channel_id=1, source_target_pairs={{0,1},{1,0},{2,3},{3,2},{4,5},{5,4},{6,7},{7,6},{8,9},{9,8},{10,11... | collective-permute-start | bytes 786440 | tf_op jit(solution)/shard_map/ppermute | solution.py:31
  14.1 6.7 %collective-permute-start.1 = (f32[256,128]{1,0:T(8,128)S(1)}, f32[256,128]{1,0:T(8,128)S(1)}, u32[]{:S(2)}, u32[]{:S(2)}) collective-permute-start(f32[256,128]{1,0:T(8,128)S(1)} %constant_dynamic-slice_fusion.2), channel_id=1, source_target_pairs={{0,2},{1,3},{2,0},{3,1},{4,6},{5,7},{6,4},{7,5},{8,10},{9,11},{10,... | collective-permute-start | bytes 393224 | tf_op jit(solution)/shard_map/ppermute | solution.py:31
  20.8 5.4 %collective-permute-start.2 = (f32[256,128]{1,0:T(8,128)S(1)}, f32[256,128]{1,0:T(8,128)S(1)}, u32[]{:S(2)}, u32[]{:S(2)}) collective-permute-start(f32[256,128]{1,0:T(8,128)S(1)} %dynamic-slice_add_fusion.3), channel_id=1, source_target_pairs={{0,4},{1,5},{2,6},{3,7},{4,0},{5,1},{6,2},{7,3},{8,12},{9,13},{10,... | collective-permute-start | bytes 393224 | tf_op jit(solution)/shard_map/ppermute | solution.py:31
  26.2 8.2 %collective-permute-start.3 = (f32[256,128]{1,0:T(8,128)S(1)}, f32[256,128]{1,0:T(8,128)S(1)}, u32[]{:S(2)}, u32[]{:S(2)}) collective-permute-start(f32[256,128]{1,0:T(8,128)S(1)} %add.209), channel_id=1, source_target_pairs={{0,8},{1,9},{2,10},{3,11},{4,12},{5,13},{6,14},{7,15},{8,0},{9,1},... | collective-permute-start | bytes 393224 | tf_op jit(solution)/shard_map/ppermute | solution.py:31
  35.1 5.0 %collective-permute-start.4 = (f32[256,128]{1,0:T(8,128)S(1)}, f32[256,128]{1,0:T(8,128)S(1)}, u32[]{:S(2)}, u32[]{:S(2)}) collective-permute-start(f32[256,128]{1,0:T(8,128)S(1)} %get-tuple-element.5), channel_id=1, source_target_pairs={{0,2},{1,3},{2,0},{3,1},{4,6},{5,7},{6,4},{7,5},{8,10},{9,11},{10,... | collective-permute-start | bytes 393224 | tf_op jit(solution)/shard_map/ppermute | solution.py:31
  36.4 5.1 %collective-permute-start.5 = (f32[256,128]{1,0:T(8,128)S(1)}, f32[256,128]{1,0:T(8,128)S(1)}, u32[]{:S(2)}, u32[]{:S(2)}) collective-permute-start(f32[256,128]{1,0:T(8,128)S(1)} %get-tuple-element.5), channel_id=1, source_target_pairs={{0,1},{1,0},{2,3},{3,2},{4,5},{5,4},{6,7},{7,6},{8,9},{9,8},{10,11... | collective-permute-start | bytes 393224 | tf_op jit(solution)/shard_map/ppermute | solution.py:31
  39.1 2.4 %copy-start.5 = (f32[1024,512]{1,0:T(8,128)S(1)}, f32[1024,512]{1,0:T(8,128)}, u32[]{:S(2)}) copy-start(f32[1024,512]{1,0:T(8,128)} %get-tuple-element.8) | copy-start | bytes 6291460
  40.0 2.0 %collective-permute-start.6 = (f32[256,128]{1,0:T(8,128)S(1)}, f32[256,128]{1,0:T(8,128)S(1)}, u32[]{:S(2)}, u32[]{:S(2)}) collective-permute-start(f32[256,128]{1,0:T(8,128)S(1)} %collective-permute-done.4), channel_id=1, source_target_pairs={{0,1},{1,0},{2,3},{3,2},{4,5},{5,4},{6,7},{7,6},{8,9},{9,8},{10,11... | collective-permute-start | bytes 393224 | tf_op jit(solution)/shard_map/ppermute | solution.py:31
  41.5 15.2 %copy-start.2 = (f32[1024,128]{1,0:T(8,128)S(1)}, f32[1024,128]{1,0:T(8,128)}, u32[]{:S(2)}) copy-start(f32[1024,128]{1,0:T(8,128)} %param.7) | copy-start | bytes 1572868
  42.0 14.8 %copy-start.8 = (s32[512]{0:T(512)S(1)}, s32[512]{0:T(512)}, u32[]{:S(2)}) copy-start(s32[512]{0:T(512)} %param.6) | copy-start | bytes 6148
  42.0 14.8 %copy-start.9 = (f32[512]{0:T(512)S(1)}, f32[512]{0:T(512)}, u32[]{:S(2)}) copy-start(f32[512]{0:T(512)} %param.9) | copy-start | bytes 6148
  44.4 12.2 %all-to-all-start = ((f32[16,2,128]{2,1,0:T(2,128)}), f32[16,2,128]{2,1,0:T(2,128)S(1)}, u32[]{:S(2)}, u32[]{:S(2)}) async-start(f32[16,2,128]{2,1,0:T(2,128)} %broadcast_in_dim.15), calls=%async_computation | async-start | bytes 32768 | tf_op jit(solution)/shard_map/all_to_all | solution.py:73
  56.7 1.6 %copy-start.7 = (s32[1024,512]{1,0:T(8,128)S(1)}, s32[1024,512]{1,0:T(8,128)}, u32[]{:S(2)}) copy-start(s32[1024,512]{1,0:T(8,128)} %param.5) | copy-start | bytes 6291460
  63.6 1.6 %collective-permute-start.7 = (f32[512,128]{1,0:T(8,128)S(1)}, f32[512,128]{1,0:T(8,128)S(1)}, u32[]{:S(2)}, u32[]{:S(2)}) collective-permute-start(f32[512,128]{1,0:T(8,128)S(1)} %constant_dynamic-slice_fusion.1), channel_id=1, source_target_pairs={{0,1},{1,0},{2,3},{3,2},{4,5},{5,4},{6,7},{7,6},{8,9},{9,8},{10,11... | collective-permute-start | bytes 786440 | tf_op jit(solution)/shard_map/ppermute | solution.py:31
  65.3 5.6 %collective-permute-start.8 = (f32[256,128]{1,0:T(8,128)S(1)}, f32[256,128]{1,0:T(8,128)S(1)}, u32[]{:S(2)}, u32[]{:S(2)}) collective-permute-start(f32[256,128]{1,0:T(8,128)S(1)} %constant_dynamic-slice_fusion), channel_id=1, source_target_pairs={{0,2},{1,3},{2,0},{3,1},{4,6},{5,7},{6,4},{7,5},{8,10},{9,11},{10,... | collective-permute-start | bytes 393224 | tf_op jit(solution)/shard_map/ppermute | solution.py:31
  70.9 5.0 %collective-permute-start.9 = (f32[256,128]{1,0:T(8,128)S(1)}, f32[256,128]{1,0:T(8,128)S(1)}, u32[]{:S(2)}, u32[]{:S(2)}) collective-permute-start(f32[256,128]{1,0:T(8,128)S(1)} %dynamic-slice_add_fusion.2), channel_id=1, source_target_pairs={{0,4},{1,5},{2,6},{3,7},{4,0},{5,1},{6,2},{7,3},{8,12},{9,13},{10,... | collective-permute-start | bytes 393224 | tf_op jit(solution)/shard_map/ppermute | solution.py:31
  76.0 7.2 %collective-permute-start.10 = (f32[256,128]{1,0:T(8,128)S(1)}, f32[256,128]{1,0:T(8,128)S(1)}, u32[]{:S(2)}, u32[]{:S(2)}) collective-permute-start(f32[256,128]{1,0:T(8,128)S(1)} %add.234), channel_id=1, source_target_pairs={{0,8},{1,9},{2,10},{3,11},{4,12},{5,13},{6,14},{7,15},{8,0},{9,1},... | collective-permute-start | bytes 393224 | tf_op jit(solution)/shard_map/ppermute | solution.py:31
  83.8 5.4 %copy-start.3 = (f32[1024,512]{1,0:T(8,128)S(1)}, f32[1024,512]{1,0:T(8,128)}, u32[]{:S(2)}) copy-start(f32[1024,512]{1,0:T(8,128)} %get-tuple-element.6) | copy-start | bytes 6291460
  83.8 5.0 %collective-permute-start.11 = (f32[256,128]{1,0:T(8,128)S(1)}, f32[256,128]{1,0:T(8,128)S(1)}, u32[]{:S(2)}, u32[]{:S(2)}) collective-permute-start(f32[256,128]{1,0:T(8,128)S(1)} %get-tuple-element.3), channel_id=1, source_target_pairs={{0,2},{1,3},{2,0},{3,1},{4,6},{5,7},{6,4},{7,5},{8,10},{9,11},{10,... | collective-permute-start | bytes 393224 | tf_op jit(solution)/shard_map/ppermute | solution.py:31
  84.8 4.9 %collective-permute-start.12 = (f32[256,128]{1,0:T(8,128)S(1)}, f32[256,128]{1,0:T(8,128)S(1)}, u32[]{:S(2)}, u32[]{:S(2)}) collective-permute-start(f32[256,128]{1,0:T(8,128)S(1)} %get-tuple-element.3), channel_id=1, source_target_pairs={{0,1},{1,0},{2,3},{3,2},{4,5},{5,4},{6,7},{7,6},{8,9},{9,8},{10,11... | collective-permute-start | bytes 393224 | tf_op jit(solution)/shard_map/ppermute | solution.py:31
  89.2 2.7 %copy-start.4 = (f32[256,512]{1,0:T(8,128)S(1)}, f32[256,512]{1,0:T(8,128)}, u32[]{:S(2)}) copy-start(f32[256,512]{1,0:T(8,128)} %fusion.8) | copy-start | bytes 1572868
  90.5 1.4 %collective-permute-start.13 = (f32[256,128]{1,0:T(8,128)S(1)}, f32[256,128]{1,0:T(8,128)S(1)}, u32[]{:S(2)}, u32[]{:S(2)}) collective-permute-start(f32[256,128]{1,0:T(8,128)S(1)} %collective-permute-done.11), channel_id=1, source_target_pairs={{0,1},{1,0},{2,3},{3,2},{4,5},{5,4},{6,7},{7,6},{8,9},{9,8},{10,11... | collective-permute-start | bytes 393224 | tf_op jit(solution)/shard_map/ppermute | solution.py:31
  90.6 1.7 %copy-start.6 = (f32[1024,128]{1,0:T(8,128)}, f32[1024,128]{1,0:T(8,128)S(1)}, u32[]{:S(2)}) copy-start(f32[1024,128]{1,0:T(8,128)S(1)} %constant_dynamic-update-slice_fusion) | copy-start | bytes 1572868
  94.3 10.0 %all-to-all-start.1 = ((f32[16,2,128]{2,1,0:T(2,128)}), f32[16,2,128]{2,1,0:T(2,128)S(1)}, u32[]{:S(2)}, u32[]{:S(2)}) async-start(f32[16,2,128]{2,1,0:T(2,128)} %broadcast_in_dim.16), calls=%async_computation.1 | async-start | bytes 32768 | tf_op jit(solution)/shard_map/all_to_all | solution.py:73

commit v11 on v10

--- a/solution.py
+++ b/solution.py
@@ -92,15 +92,18 @@
             )
             weight = lax.dynamic_slice_in_dim(curvature, first, rows, 0)
             bending = bending + jnp.sum(weight * tangent_image * tangent_image, axis=0)
+        if sweep + 1 == SWEEPS:
+            mine_time, mine_grad = lax.optimization_barrier((
+                lax.dynamic_slice_in_dim(time_factor, offset, shard_rows, 0),
+                lax.dynamic_slice_in_dim(grad_whole, offset, shard_rows, 0),
+            ))
         norm_total, bend_total = sum_rows([user_norm + time_norm, jnp.sum(bending)], n)
         relax_step = norm_total / (bend_total + damping * norm_total)
         user_factor = user_factor - relax_step * grad_user
         if sweep + 1 < SWEEPS:
             time_factor = time_factor - relax_step * grad_whole
         else:
-            mine_rows = lax.dynamic_slice_in_dim(
-                time_factor - relax_step * grad_whole, offset, shard_rows, 0
-            )
+            mine_rows = mine_time - relax_step * mine_grad
     return (mine_rows, user_factor)
 
 

time: 107 us -> 109 us (1.019)
  local copies, waits for them, and re-layouts: 6.02 us -> 8.34 us
  waiting for transfers between devices: 41.7 us -> 40.4 us
    add x4, other arithmetic: 1.14 us -> 2.74 us  [sum_over_users(): block = keep + exchange(send, n, d)]
    dynamic_slice x0 -> x2, local copies, waits for them, and re-layouts: none -> 1.38 us  [the longest x1 0.76 us: body(): lax.dynamic_slice_in_dim(grad_whole, offset, shard_rows, 0)]
  transfers between devices with their start and end apart: 16 -> 16, of which waited for: 12 -> 12; matrix products, arithmetic and copies ran while one was open for 13% -> 15% of each run, Pallas kernels for 0% -> 0%
where the time goes in v11:
time: 109 us; the launch traced here: 108 us
  waiting for transfers between devices  40.4 us (37%)
  matrix products  28.5 us (26%)
  starting transfers between devices  20.5 us (19%)
  local copies, waits for them, and re-layouts  8.34 us (8%)
  other arithmetic  6.85 us (6%)
  between operations  3.66 us (3%)
    ppermute x14, waiting for transfers between devices, exchange(): return lax.ppermute(value, 'user', [(i, i ^ distance) for i in range(n)])  28.9 us
    dot_general x22, matrix products, product(): jnp.dot(left, right, precision=precision, preferred_element_type=jnp.floa...  28.5 us
    all_to_all x2, waiting for transfers between devices, sum_rows(): spread = lax.all_to_all(spread, 'user', 0, 0, tiled=False)  11.5 us
    ppermute x14, starting transfers between devices, exchange(): return lax.ppermute(value, 'user', [(i, i ^ distance) for i in range(n)])  11.3 us
    all_to_all x2, starting transfers between devices, sum_rows(): spread = lax.all_to_all(spread, 'user', 0, 0, tiled=False)  9.21 us
    add x4, other arithmetic, sum_over_users(): block = keep + exchange(send, n, d)  2.74 us
  transfers between devices with their start and end apart: 16, of which 12 were waited for; matrix products, arithmetic and copies ran while one was open for 15% of the time, Pallas kernels for 0%

profile of v11, /device:TPU:0, one launch (start us, length us, event | category | flops | bytes accessed | tf_op | source)
XLA Modules:
  0.0 108.3 jit_solution(18354194627066675326)
XLA Ops:
  0.7 6.2 %multiply_select_fusion.2 = (f32[1024,512]{1,0:T(8,128)}, f32[1024,512]{1,0:T(8,128)S(1)}) fusion(s32[512]{0:T(512)} %param.6, f32[512]{0:T(512)} %param.9, s32[1024,512]{1,0:T(8,128)} %param.5, f32[1024,128]{1,0:T(8,128)} %param.7, f32[512,128]{1,0:T(8,128)} %param.8), kind=kOutput, calls=%fused_computation.5 | convolution fusion | flops 413138944 | bytes 7081984 | tf_op jit(solution)/shard_map/dot_general | solution.py:14
  6.9 1.8 %fusion.31 = f32[1024,128]{1,0:T(8,128)} fusion(f32[1024,512]{1,0:T(8,128)S(1)} %get-tuple-element.13, f32[512,128]{1,0:T(8,128)S(1)} %copy-done), kind=kOutput, calls=%fused_computation.88 | convolution fusion | flops 402653184 | bytes 2883584 | tf_op jit(solution)/shard_map/dot_general | solution.py:14
  8.7 1.0 constant_dynamic-slice_fusion.5
  9.6 0.5 collective-permute-start
  10.2 2.4 %multiply_reduce_fusion.1 = (f32[]{:T(128)}, f32[512,128]{1,0:T(8,128)S(1)}) fusion(f32[1024,512]{1,0:T(8,128)S(1)} %get-tuple-element.13, f32[1024,128]{1,0:T(8,128)S(1)} %copy-done.1), kind=kOutput, calls=%fused_computation.41 | convolution fusion | flops 402784256 | bytes 2883588 | tf_op jit(solution)/shard_map/dot_general | solution.py:14
  12.6 0.4 fusion.17
  13.0 1.1 dynamic-slice_add_fusion.1
  14.1 2.6 %collective-permute-start.1 = (f32[256,128]{1,0:T(8,128)S(1)}, f32[256,128]{1,0:T(8,128)S(1)}, u32[]{:S(2)}, u32[]{:S(2)}) collective-permute-start(f32[256,128]{1,0:T(8,128)S(1)} %constant_dynamic-slice_fusion.4), channel_id=1, source_target_pairs={{0,2},{1,3},{2,0},{3,1},{4,6},{5,7},{6,4},{7,5},{8,10},{9,11},{10,... | collective-permute-start | bytes 393224 | tf_op jit(solution)/shard_map/ppermute | solution.py:31
  16.6 0.4 fusion.19
  17.0 3.8 %collective-permute-done.1 = f32[256,128]{1,0:T(8,128)S(1)} collective-permute-done((f32[256,128]{1,0:T(8,128)S(1)}, f32[256,128]{1,0:T(8,128)S(1)}, u32[]{:S(2)}, u32[]{:S(2)}) %collective-permute-start.1) | collective-permute-done | bytes 131104 | tf_op jit(solution)/shard_map/ppermute | solution.py:31
  20.8 1.9 %collective-permute-start.2 = (f32[256,128]{1,0:T(8,128)S(1)}, f32[256,128]{1,0:T(8,128)S(1)}, u32[]{:S(2)}, u32[]{:S(2)}) collective-permute-start(f32[256,128]{1,0:T(8,128)S(1)} %dynamic-slice_add_fusion.3), channel_id=1, source_target_pairs={{0,4},{1,5},{2,6},{3,7},{4,0},{5,1},{6,2},{7,3},{8,12},{9,13},{10,... | collective-permute-start | bytes 393224 | tf_op jit(solution)/shard_map/ppermute | solution.py:31
  22.7 0.4 fusion.15
  23.1 3.1 %collective-permute-done.2 = f32[256,128]{1,0:T(8,128)S(1)} collective-permute-done((f32[256,128]{1,0:T(8,128)S(1)}, f32[256,128]{1,0:T(8,128)S(1)}, u32[]{:S(2)}, u32[]{:S(2)}) %collective-permute-start.2) | collective-permute-done | bytes 131104 | tf_op jit(solution)/shard_map/ppermute | solution.py:31
  26.2 2.7 %collective-permute-start.3 = (f32[256,128]{1,0:T(8,128)S(1)}, f32[256,128]{1,0:T(8,128)S(1)}, u32[]{:S(2)}, u32[]{:S(2)}) collective-permute-start(f32[256,128]{1,0:T(8,128)S(1)} %add.210), channel_id=1, source_target_pairs={{0,8},{1,9},{2,10},{3,11},{4,12},{5,13},{6,14},{7,15},{8,0},{9,1},... | collective-permute-start | bytes 393224 | tf_op jit(solution)/shard_map/ppermute | solution.py:31
  28.9 0.4 fusion.13
  29.3 5.1 %collective-permute-done.3 = f32[256,128]{1,0:T(8,128)S(1)} collective-permute-done((f32[256,128]{1,0:T(8,128)S(1)}, f32[256,128]{1,0:T(8,128)S(1)}, u32[]{:S(2)}, u32[]{:S(2)}) %collective-permute-start.3) | collective-permute-done | bytes 131104 | tf_op jit(solution)/shard_map/ppermute | solution.py:31
  34.4 0.6 multiply_reduce_fusion.3
  35.1 1.3 %collective-permute-start.4 = (f32[256,128]{1,0:T(8,128)S(1)}, f32[256,128]{1,0:T(8,128)S(1)}, u32[]{:S(2)}, u32[]{:S(2)}) collective-permute-start(f32[256,128]{1,0:T(8,128)S(1)} %get-tuple-element.9), channel_id=1, source_target_pairs={{0,2},{1,3},{2,0},{3,1},{4,6},{5,7},{6,4},{7,5},{8,10},{9,11},{10,... | collective-permute-start | bytes 393224 | tf_op jit(solution)/shard_map/ppermute | solution.py:31
  36.4 1.5 %fusion.7 = f32[512]{0:T(512)S(1)} fusion(f32[256,512]{1,0:T(8,128)S(1)} %fusion.19, f32[256,128]{1,0:T(8,128)S(1)} %get-tuple-element.9, f32[512,128]{1,0:T(8,128)S(1)} %copy-done, f32[1024,512]{1,0:T(8,128)} %get-tuple-element.12, s32[]{:T(128)S(6)} %select_n.124), kind=kOutput, calls=%fused_computation.34 | convolution fusion | flops 101187072 | bytes 1443844 | tf_op jit(solution)/shard_map/dot_general | solution.py:14
  39.2 0.8 collective-permute-done.4
  40.0 1.5 %fusion.6 = f32[512]{0:T(512)S(1)} fusion(f32[256,512]{1,0:T(8,128)S(1)} %fusion.17, f32[256,128]{1,0:T(8,128)S(1)} %collective-permute-done.4, f32[512,128]{1,0:T(8,128)S(1)} %copy-done, f32[1024,512]{1,0:T(8,128)} %get-tuple-element.12, s32[]{:T(128)S(6)} %select_n.125), kind=kOutput, calls=%fused_computation.32 | convolution fusion | flops 101187072 | bytes 1443844 | tf_op jit(solution)/shard_map/dot_general | solution.py:14
  41.5 0.4 fusion.5
  42.0 0.4 fusion.4
  42.5 0.6 add_reduce_fusion.1
  43.1 0.6 stack.6
  43.7 0.7 broadcast_in_dim.15
  44.4 5.7 %all-to-all-start = ((f32[16,2,128]{2,1,0:T(2,128)}), f32[16,2,128]{2,1,0:T(2,128)S(1)}, u32[]{:S(2)}, u32[]{:S(2)}) async-start(f32[16,2,128]{2,1,0:T(2,128)} %broadcast_in_dim.15), calls=%async_computation | async-start | bytes 32768 | tf_op jit(solution)/shard_map/all_to_all | solution.py:73
  50.2 6.5 %all-to-all-done = f32[16,2,128]{2,1,0:T(2,128)S(1)} async-done(((f32[16,2,128]{2,1,0:T(2,128)}), f32[16,2,128]{2,1,0:T(2,128)S(1)}, u32[]{:S(2)}, u32[]{:S(2)}) %all-to-all-start) | async-done | bytes 16416 | tf_op jit(solution)/shard_map/all_to_all | solution.py:73
  56.8 1.4 %copy-done.8 = s32[1024,512]{1,0:T(8,128)S(1)} copy-done((s32[1024,512]{1,0:T(8,128)S(1)}, s32[1024,512]{1,0:T(8,128)}, u32[]{:S(2)}) %copy-start.8) | copy-done | bytes 2097176
  58.3 4.3 %multiply_select_fusion = (f32[1024,512]{1,0:T(8,128)}, f32[1024,512]{1,0:T(8,128)S(1)}) fusion(s32[512]{0:T(512)S(1)} %copy-done.9, f32[512]{0:T(512)S(1)} %copy-done.10, s32[1024,512]{1,0:T(8,128)S(1)} %copy-done.8, f32[1024,128]{1,0:T(8,128)S(1)} %multiply_subtract_fusion, f32[512,128]{1,0:T(8,128)S(1)} %multiply_subtract_fusion.2), kind=kOutput, calls=%fused_computation | convolution fusion | flops 413138944 | bytes 7081984 | tf_op jit(solution)/shard_map/dot_general | solution.py:14
  62.6 1.0 fusion.32
  63.7 1.5 %collective-permute-done.7 = f32[512,128]{1,0:T(8,128)S(1)} collective-permute-done((f32[512,128]{1,0:T(8,128)S(1)}, f32[512,128]{1,0:T(8,128)S(1)}, u32[]{:S(2)}, u32[]{:S(2)}) %collective-permute-start.7) | collective-permute-done | bytes 262176 | tf_op jit(solution)/shard_map/ppermute | solution.py:31
  65.2 0.7 dynamic-slice_add_fusion
  66.0 0.9 constant_dynamic-slice_fusion.1
  66.9 0.5 collective-permute-start.8
  67.4 5.1 %collective-permute-done.8 = f32[256,128]{1,0:T(8,128)S(1)} collective-permute-done((f32[256,128]{1,0:T(8,128)S(1)}, f32[256,128]{1,0:T(8,128)S(1)}, u32[]{:S(2)}, u32[]{:S(2)}) %collective-permute-start.8) | collective-permute-done | bytes 131104 | tf_op jit(solution)/shard_map/ppermute | solution.py:31
  72.5 0.9 dynamic-slice_add_fusion.2
  73.4 0.5 collective-permute-start.9
  73.9 2.4 %multiply_reduce_fusion = (f32[]{:T(128)}, f32[512,128]{1,0:T(8,128)S(1)}) fusion(f32[1024,512]{1,0:T(8,128)S(1)} %get-tuple-element.11, f32[1024,128]{1,0:T(8,128)S(1)} %multiply_subtract_fusion), kind=kOutput, calls=%fused_computation.37 | convolution fusion | flops 402784256 | bytes 2883588 | tf_op jit(solution)/shard_map/dot_general | solution.py:14
  76.3 2.1 %collective-permute-done.9 = f32[256,128]{1,0:T(8,128)S(1)} collective-permute-done((f32[256,128]{1,0:T(8,128)S(1)}, f32[256,128]{1,0:T(8,128)S(1)}, u32[]{:S(2)}, u32[]{:S(2)}) %collective-permute-start.9) | collective-permute-done | bytes 131104 | tf_op jit(solution)/shard_map/ppermute | solution.py:31
  78.5 0.5 collective-permute-start.10
  79.0 1.2 %fusion.8 = f32[256,512]{1,0:T(8,128)} fusion(f32[512,128]{1,0:T(8,128)S(1)} %get-tuple-element.17, f32[1024,128]{1,0:T(8,128)S(1)} %multiply_subtract_fusion, s32[]{:T(128)S(6)} %select_n.127), kind=kOutput, calls=%fused_computation.42 | convolution fusion | flops 100663296 | bytes 917508 | tf_op jit(solution)/shard_map/dot_general | solution.py:14
  80.2 0.6 constant_dynamic-slice_fusion.3
  80.8 4.9 %collective-permute-done.10 = f32[256,128]{1,0:T(8,128)S(1)} collective-permute-done((f32[256,128]{1,0:T(8,128)S(1)}, f32[256,128]{1,0:T(8,128)S(1)}, u32[]{:S(2)}, u32[]{:S(2)}) %collective-permute-start.10) | collective-permute-done | bytes 131104 | tf_op jit(solution)/shard_map/ppermute | solution.py:31
  85.7 0.6 multiply_reduce_fusion.2
  86.3 0.6 collective-permute-start.11
  86.9 0.4 fusion.33
  87.3 1.5 %fusion.3 = f32[512]{0:T(512)S(1)} fusion(f32[256,512]{1,0:T(8,128)S(1)} %fusion.33, f32[512,128]{1,0:T(8,128)S(1)} %get-tuple-element.17, f32[1024,512]{1,0:T(8,128)} %get-tuple-element.10, s32[]{:T(128)S(6)} %select_n.124, f32[1024,128]{1,0:T(8,128)S(1)} %multiply_subtract_fusion), kind=kOutput, calls=%fused_computation.26 | convolution fusion | flops 101187072 | bytes 1444864 | tf_op jit(solution)/shard_map/dot_general | solution.py:14
  90.2 1.1 %collective-permute-done.11 = f32[256,128]{1,0:T(8,128)S(1)} collective-permute-done((f32[256,128]{1,0:T(8,128)S(1)}, f32[256,128]{1,0:T(8,128)S(1)}, u32[]{:S(2)}, u32[]{:S(2)}) %collective-permute-start.11) | collective-permute-done | bytes 131104 | tf_op jit(solution)/shard_map/ppermute | solution.py:31
  91.3 0.4 fusion.34
  91.7 0.4 fusion.2
  92.1 0.4 fusion.35
  92.5 0.4 fusion.1
  93.1 1.3 %collective-permute-done.13 = f32[256,128]{1,0:T(8,128)S(1)} collective-permute-done((f32[256,128]{1,0:T(8,128)S(1)}, f32[256,128]{1,0:T(8,128)S(1)}, u32[]{:S(2)}, u32[]{:S(2)}) %collective-permute-start.13) | collective-permute-done | bytes 131104 | tf_op jit(solution)/shard_map/ppermute | solution.py:31
  94.4 0.4 fusion
  94.8 0.7 add_reduce_fusion
  95.5 0.7 stack.7
  96.2 0.7 broadcast_in_dim.16
  96.9 3.5 %all-to-all-start.1 = ((f32[16,2,128]{2,1,0:T(2,128)}), f32[16,2,128]{2,1,0:T(2,128)S(1)}, u32[]{:S(2)}, u32[]{:S(2)}) async-start(f32[16,2,128]{2,1,0:T(2,128)} %broadcast_in_dim.16), calls=%async_computation.1 | async-start | bytes 32768 | tf_op jit(solution)/shard_map/all_to_all | solution.py:73
  100.4 0.7 constant_dynamic-update-slice_fusion
  101.1 0.8 constant_dynamic-slice_fusion
  101.8 5.0 %all-to-all-done.1 = f32[16,2,128]{2,1,0:T(2,128)S(1)} async-done(((f32[16,2,128]{2,1,0:T(2,128)}), f32[16,2,128]{2,1,0:T(2,128)S(1)}, u32[]{:S(2)}, u32[]{:S(2)}) %all-to-all-start.1) | async-done | bytes 16416 | tf_op jit(solution)/shard_map/all_to_all | solution.py:73
  106.9 0.7 multiply_subtract_fusion.1
  107.6 0.6 multiply_subtract_fusion.3
  (50 shorter events, 0.7 us)
Async XLA Ops:
  0.6 6.2 %copy-start = (f32[512,128]{1,0:T(8,128)S(1)}, f32[512,128]{1,0:T(8,128)}, u32[]{:S(2)}) copy-start(f32[512,128]{1,0:T(8,128)} %param.8) | copy-start | bytes 786436
  6.9 3.3 %copy-start.1 = (f32[1024,128]{1,0:T(8,128)S(1)}, f32[1024,128]{1,0:T(8,128)}, u32[]{:S(2)}) copy-start(f32[1024,128]{1,0:T(8,128)} %param.7) | copy-start | bytes 1572868
  9.6 3.3 %collective-permute-start = (f32[512,128]{1,0:T(8,128)S(1)}, f32[512,128]{1,0:T(8,128)}, u32[]{:S(2)}, u32[]{:S(2)}) collective-permute-start(f32[512,128]{1,0:T(8,128)S(1)} %constant_dynamic-slice_fusion.5), channel_id=1, source_target_pairs={{0,1},{1,0},{2,3},{3,2},{4,5},{5,4},{6,7},{7,6},{8,9},{9,8},{10,11... | collective-permute-start | bytes 786440 | tf_op jit(solution)/shard_map/ppermute | solution.py:31
  14.1 6.7 %collective-permute-start.1 = (f32[256,128]{1,0:T(8,128)S(1)}, f32[256,128]{1,0:T(8,128)S(1)}, u32[]{:S(2)}, u32[]{:S(2)}) collective-permute-start(f32[256,128]{1,0:T(8,128)S(1)} %constant_dynamic-slice_fusion.4), channel_id=1, source_target_pairs={{0,2},{1,3},{2,0},{3,1},{4,6},{5,7},{6,4},{7,5},{8,10},{9,11},{10,... | collective-permute-start | bytes 393224 | tf_op jit(solution)/shard_map/ppermute | solution.py:31
  20.8 5.4 %collective-permute-start.2 = (f32[256,128]{1,0:T(8,128)S(1)}, f32[256,128]{1,0:T(8,128)S(1)}, u32[]{:S(2)}, u32[]{:S(2)}) collective-permute-start(f32[256,128]{1,0:T(8,128)S(1)} %dynamic-slice_add_fusion.3), channel_id=1, source_target_pairs={{0,4},{1,5},{2,6},{3,7},{4,0},{5,1},{6,2},{7,3},{8,12},{9,13},{10,... | collective-permute-start | bytes 393224 | tf_op jit(solution)/shard_map/ppermute | solution.py:31
  26.2 8.2 %collective-permute-start.3 = (f32[256,128]{1,0:T(8,128)S(1)}, f32[256,128]{1,0:T(8,128)S(1)}, u32[]{:S(2)}, u32[]{:S(2)}) collective-permute-start(f32[256,128]{1,0:T(8,128)S(1)} %add.210), channel_id=1, source_target_pairs={{0,8},{1,9},{2,10},{3,11},{4,12},{5,13},{6,14},{7,15},{8,0},{9,1},... | collective-permute-start | bytes 393224 | tf_op jit(solution)/shard_map/ppermute | solution.py:31
  35.1 5.0 %collective-permute-start.4 = (f32[256,128]{1,0:T(8,128)S(1)}, f32[256,128]{1,0:T(8,128)S(1)}, u32[]{:S(2)}, u32[]{:S(2)}) collective-permute-start(f32[256,128]{1,0:T(8,128)S(1)} %get-tuple-element.9), channel_id=1, source_target_pairs={{0,2},{1,3},{2,0},{3,1},{4,6},{5,7},{6,4},{7,5},{8,10},{9,11},{10,... | collective-permute-start | bytes 393224 | tf_op jit(solution)/shard_map/ppermute | solution.py:31
  36.4 5.1 %collective-permute-start.5 = (f32[256,128]{1,0:T(8,128)S(1)}, f32[256,128]{1,0:T(8,128)S(1)}, u32[]{:S(2)}, u32[]{:S(2)}) collective-permute-start(f32[256,128]{1,0:T(8,128)S(1)} %get-tuple-element.9), channel_id=1, source_target_pairs={{0,1},{1,0},{2,3},{3,2},{4,5},{5,4},{6,7},{7,6},{8,9},{9,8},{10,11... | collective-permute-start | bytes 393224 | tf_op jit(solution)/shard_map/ppermute | solution.py:31
  39.1 2.4 %copy-start.5 = (f32[1024,512]{1,0:T(8,128)S(1)}, f32[1024,512]{1,0:T(8,128)}, u32[]{:S(2)}) copy-start(f32[1024,512]{1,0:T(8,128)} %get-tuple-element.12) | copy-start | bytes 6291460
  40.0 2.0 %collective-permute-start.6 = (f32[256,128]{1,0:T(8,128)S(1)}, f32[256,128]{1,0:T(8,128)S(1)}, u32[]{:S(2)}, u32[]{:S(2)}) collective-permute-start(f32[256,128]{1,0:T(8,128)S(1)} %collective-permute-done.4), channel_id=1, source_target_pairs={{0,1},{1,0},{2,3},{3,2},{4,5},{5,4},{6,7},{7,6},{8,9},{9,8},{10,11... | collective-permute-start | bytes 393224 | tf_op jit(solution)/shard_map/ppermute | solution.py:31
  41.5 15.2 %copy-start.2 = (f32[1024,128]{1,0:T(8,128)S(1)}, f32[1024,128]{1,0:T(8,128)}, u32[]{:S(2)}) copy-start(f32[1024,128]{1,0:T(8,128)} %param.7) | copy-start | bytes 1572868
  42.0 14.8 %copy-start.9 = (s32[512]{0:T(512)S(1)}, s32[512]{0:T(512)}, u32[]{:S(2)}) copy-start(s32[512]{0:T(512)} %param.6) | copy-start | bytes 6148
  42.0 14.8 %copy-start.10 = (f32[512]{0:T(512)S(1)}, f32[512]{0:T(512)}, u32[]{:S(2)}) copy-start(f32[512]{0:T(512)} %param.9) | copy-start | bytes 6148
  44.4 12.2 %all-to-all-start = ((f32[16,2,128]{2,1,0:T(2,128)}), f32[16,2,128]{2,1,0:T(2,128)S(1)}, u32[]{:S(2)}, u32[]{:S(2)}) async-start(f32[16,2,128]{2,1,0:T(2,128)} %broadcast_in_dim.15), calls=%async_computation | async-start | bytes 32768 | tf_op jit(solution)/shard_map/all_to_all | solution.py:73
  56.7 1.6 %copy-start.8 = (s32[1024,512]{1,0:T(8,128)S(1)}, s32[1024,512]{1,0:T(8,128)}, u32[]{:S(2)}) copy-start(s32[1024,512]{1,0:T(8,128)} %param.5) | copy-start | bytes 6291460
  63.6 1.6 %collective-permute-start.7 = (f32[512,128]{1,0:T(8,128)S(1)}, f32[512,128]{1,0:T(8,128)S(1)}, u32[]{:S(2)}, u32[]{:S(2)}) collective-permute-start(f32[512,128]{1,0:T(8,128)S(1)} %constant_dynamic-slice_fusion.2), channel_id=1, source_target_pairs={{0,1},{1,0},{2,3},{3,2},{4,5},{5,4},{6,7},{7,6},{8,9},{9,8},{10,11... | collective-permute-start | bytes 786440 | tf_op jit(solution)/shard_map/ppermute | solution.py:31
  66.9 5.6 %collective-permute-start.8 = (f32[256,128]{1,0:T(8,128)S(1)}, f32[256,128]{1,0:T(8,128)S(1)}, u32[]{:S(2)}, u32[]{:S(2)}) collective-permute-start(f32[256,128]{1,0:T(8,128)S(1)} %constant_dynamic-slice_fusion.1), channel_id=1, source_target_pairs={{0,2},{1,3},{2,0},{3,1},{4,6},{5,7},{6,4},{7,5},{8,10},{9,11},{10,... | collective-permute-start | bytes 393224 | tf_op jit(solution)/shard_map/ppermute | solution.py:31
  73.4 5.0 %collective-permute-start.9 = (f32[256,128]{1,0:T(8,128)S(1)}, f32[256,128]{1,0:T(8,128)S(1)}, u32[]{:S(2)}, u32[]{:S(2)}) collective-permute-start(f32[256,128]{1,0:T(8,128)S(1)} %dynamic-slice_add_fusion.2), channel_id=1, source_target_pairs={{0,4},{1,5},{2,6},{3,7},{4,0},{5,1},{6,2},{7,3},{8,12},{9,13},{10,... | collective-permute-start | bytes 393224 | tf_op jit(solution)/shard_map/ppermute | solution.py:31
  78.5 7.2 %collective-permute-start.10 = (f32[256,128]{1,0:T(8,128)S(1)}, f32[256,128]{1,0:T(8,128)S(1)}, u32[]{:S(2)}, u32[]{:S(2)}) collective-permute-start(f32[256,128]{1,0:T(8,128)S(1)} %add.236), channel_id=1, source_target_pairs={{0,8},{1,9},{2,10},{3,11},{4,12},{5,13},{6,14},{7,15},{8,0},{9,1},... | collective-permute-start | bytes 393224 | tf_op jit(solution)/shard_map/ppermute | solution.py:31
  86.3 5.4 %copy-start.3 = (f32[1024,512]{1,0:T(8,128)S(1)}, f32[1024,512]{1,0:T(8,128)}, u32[]{:S(2)}) copy-start(f32[1024,512]{1,0:T(8,128)} %get-tuple-element.10) | copy-start | bytes 6291460
  86.3 5.0 %collective-permute-start.11 = (f32[256,128]{1,0:T(8,128)S(1)}, f32[256,128]{1,0:T(8,128)S(1)}, u32[]{:S(2)}, u32[]{:S(2)}) collective-permute-start(f32[256,128]{1,0:T(8,128)S(1)} %get-tuple-element.7), channel_id=1, source_target_pairs={{0,2},{1,3},{2,0},{3,1},{4,6},{5,7},{6,4},{7,5},{8,10},{9,11},{10,... | collective-permute-start | bytes 393224 | tf_op jit(solution)/shard_map/ppermute | solution.py:31
  87.3 4.9 %collective-permute-start.12 = (f32[256,128]{1,0:T(8,128)S(1)}, f32[256,128]{1,0:T(8,128)S(1)}, u32[]{:S(2)}, u32[]{:S(2)}) collective-permute-start(f32[256,128]{1,0:T(8,128)S(1)} %get-tuple-element.7), channel_id=1, source_target_pairs={{0,1},{1,0},{2,3},{3,2},{4,5},{5,4},{6,7},{7,6},{8,9},{9,8},{10,11... | collective-permute-start | bytes 393224 | tf_op jit(solution)/shard_map/ppermute | solution.py:31
  91.7 2.7 %copy-start.4 = (f32[256,512]{1,0:T(8,128)S(1)}, f32[256,512]{1,0:T(8,128)}, u32[]{:S(2)}) copy-start(f32[256,512]{1,0:T(8,128)} %fusion.8) | copy-start | bytes 1572868
  93.0 14.7 %copy-start.7 = (f32[64,128]{1,0:T(8,128)S(1)}, f32[64,128]{1,0:T(8,128)}, u32[]{:S(2)}) copy-start(f32[64,128]{1,0:T(8,128)} %constant_dynamic-slice_fusion.3) | copy-start | bytes 98308
  93.0 1.4 %collective-permute-start.13 = (f32[256,128]{1,0:T(8,128)S(1)}, f32[256,128]{1,0:T(8,128)S(1)}, u32[]{:S(2)}, u32[]{:S(2)}) collective-permute-start(f32[256,128]{1,0:T(8,128)S(1)} %collective-permute-done.11), channel_id=1, source_target_pairs={{0,1},{1,0},{2,3},{3,2},{4,5},{5,4},{6,7},{7,6},{8,9},{9,8},{10,11... | collective-permute-start | bytes 393224 | tf_op jit(solution)/shard_map/ppermute | solution.py:31
  93.1 1.7 %copy-start.6 = (f32[1024,128]{1,0:T(8,128)}, f32[1024,128]{1,0:T(8,128)S(1)}, u32[]{:S(2)}) copy-start(f32[1024,128]{1,0:T(8,128)S(1)} %constant_dynamic-update-slice_fusion.1) | copy-start | bytes 1572868
  96.9 10.0 %all-to-all-start.1 = ((f32[16,2,128]{2,1,0:T(2,128)}), f32[16,2,128]{2,1,0:T(2,128)S(1)}, u32[]{:S(2)}, u32[]{:S(2)}) async-start(f32[16,2,128]{2,1,0:T(2,128)} %broadcast_in_dim.16), calls=%async_computation.1 | async-start | bytes 32768 | tf_op jit(solution)/shard_map/all_to_all | solution.py:73

commit v12 on v10

--- a/solution.py
+++ b/solution.py
@@ -55,11 +55,12 @@
     for d in butterfly:
         block = block + exchange(block, n, d)
     share = jnp.where(me < 4, jnp.sum(block * block), 0.0)
-    pieces = [(block, offset)]
-    for level in reversed(range(len(halving))):
-        d = halving[level]
-        shift = (1 - 2 * ((me // d) % 2)) * (partial.shape[0] >> (level + 1))
-        pieces = pieces + [(exchange(piece, n, d), first + shift) for piece, first in pieces]
+    def first_row(j):
+        return sum(((j // d) % 2) * (partial.shape[0] >> (level + 1)) for level, d in enumerate(halving))
+
+    pieces = [(block, offset)] + [
+        (exchange(block, n, x), first_row(me ^ x)) for x in range(1, 2 ** len(halving))
+    ]
     block = jnp.zeros_like(partial)
     for piece, first in pieces:
         block = lax.dynamic_update_slice_in_dim(block, piece, first, 0)

time: 107 us -> 117 us (1.093)
  matrix products: 28.5 us -> 34.9 us
  starting transfers between devices: 20.5 us -> 22.1 us
  waiting for transfers between devices: 41.7 us -> 43.2 us
  local copies, waits for them, and re-layouts: 6.02 us -> 7.24 us
    dot_general x22, matrix products: 28.5 us -> 34.9 us  [product(): jnp.dot(left, right, precision=precision, preferred_element_type=jnp.floa...]
    ppermute x14, waiting for transfers between devices: 29.5 us -> 32.2 us  [exchange(): return lax.ppermute(value, 'user', [(i, i ^ distance) for i in range(n)])]
    ppermute x14, starting transfers between devices: 11.3 us -> 13 us  [exchange(): return lax.ppermute(value, 'user', [(i, i ^ distance) for i in range(n)])]
    all_to_all x2, waiting for transfers between devices: 12.3 us -> 11 us  [sum_rows(): spread = lax.all_to_all(spread, 'user', 0, 0, tiled=False)]
  transfers between devices with their start and end apart: 16 -> 16, of which waited for: 12 -> 11; matrix products, arithmetic and copies ran while one was open for 13% -> 14% of each run, Pallas kernels for 0% -> 0%
where the time goes in v12:
time: 117 us; the launch traced here: 116 us
  waiting for transfers between devices  43.2 us (37%)
  matrix products  34.9 us (30%)
  starting transfers between devices  22.1 us (19%)
  local copies, waits for them, and re-layouts  7.24 us (6%)
  other arithmetic  5.15 us (4%)
  between operations  3.66 us (3%)
    dot_general x22, matrix products, product(): jnp.dot(left, right, precision=precision, preferred_element_type=jnp.floa...  34.9 us
    ppermute x14, waiting for transfers between devices, exchange(): return lax.ppermute(value, 'user', [(i, i ^ distance) for i in range(n)])  32.2 us
    ppermute x14, starting transfers between devices, exchange(): return lax.ppermute(value, 'user', [(i, i ^ distance) for i in range(n)])  13 us
    all_to_all x2, waiting for transfers between devices, sum_rows(): spread = lax.all_to_all(spread, 'user', 0, 0, tiled=False)  11 us
    all_to_all x2, starting transfers between devices, sum_rows(): spread = lax.all_to_all(spread, 'user', 0, 0, tiled=False)  9.1 us
  transfers between devices with their start and end apart: 16, of which 11 were waited for; matrix products, arithmetic and copies ran while one was open for 14% of the time, Pallas kernels for 0%

profile of v12, /device:TPU:0, one launch (start us, length us, event | category | flops | bytes accessed | tf_op | source)
XLA Modules:
  0.0 116.2 jit_solution(13968454399052639198)
XLA Ops:
  0.7 6.2 %multiply_select_fusion.2 = (f32[1024,512]{1,0:T(8,128)}, f32[1024,512]{1,0:T(8,128)S(1)}) fusion(s32[512]{0:T(512)} %param.6, f32[512]{0:T(512)} %param.9, s32[1024,512]{1,0:T(8,128)} %param.5, f32[1024,128]{1,0:T(8,128)} %param.7, f32[512,128]{1,0:T(8,128)} %param.8), kind=kOutput, calls=%fused_computation.5 | convolution fusion | flops 413138944 | bytes 7081984 | tf_op jit(solution)/shard_map/dot_general | solution.py:14
  6.9 1.8 %fusion.34 = f32[1024,128]{1,0:T(8,128)} fusion(f32[1024,512]{1,0:T(8,128)S(1)} %get-tuple-element.9, f32[512,128]{1,0:T(8,128)S(1)} %copy-done), kind=kOutput, calls=%fused_computation.90 | convolution fusion | flops 402653184 | bytes 2883584 | tf_op jit(solution)/shard_map/dot_general | solution.py:14
  8.7 1.0 constant_dynamic-slice_fusion.3
  9.6 0.5 collective-permute-start
  10.2 2.4 %multiply_reduce_fusion.1 = (f32[]{:T(128)}, f32[512,128]{1,0:T(8,128)S(1)}) fusion(f32[1024,512]{1,0:T(8,128)S(1)} %get-tuple-element.9, f32[1024,128]{1,0:T(8,128)S(1)} %copy-done.1), kind=kOutput, calls=%fused_computation.41 | convolution fusion | flops 402784256 | bytes 2883588 | tf_op jit(solution)/shard_map/dot_general | solution.py:14
  12.6 0.4 fusion.20
  13.0 1.1 dynamic-slice_add_fusion.1
  14.1 2.6 %collective-permute-start.1 = (f32[256,128]{1,0:T(8,128)S(1)}, f32[256,128]{1,0:T(8,128)S(1)}, u32[]{:S(2)}, u32[]{:S(2)}) collective-permute-start(f32[256,128]{1,0:T(8,128)S(1)} %constant_dynamic-slice_fusion.2), channel_id=1, source_target_pairs={{0,2},{1,3},{2,0},{3,1},{4,6},{5,7},{6,4},{7,5},{8,10},{9,11},{10,... | collective-permute-start | bytes 393224 | tf_op jit(solution)/shard_map/ppermute | solution.py:31
  16.6 0.4 fusion.22
  17.0 3.8 %collective-permute-done.1 = f32[256,128]{1,0:T(8,128)S(1)} collective-permute-done((f32[256,128]{1,0:T(8,128)S(1)}, f32[256,128]{1,0:T(8,128)S(1)}, u32[]{:S(2)}, u32[]{:S(2)}) %collective-permute-start.1) | collective-permute-done | bytes 131104 | tf_op jit(solution)/shard_map/ppermute | solution.py:31
  20.8 1.9 %collective-permute-start.2 = (f32[256,128]{1,0:T(8,128)S(1)}, f32[256,128]{1,0:T(8,128)S(1)}, u32[]{:S(2)}, u32[]{:S(2)}) collective-permute-start(f32[256,128]{1,0:T(8,128)S(1)} %dynamic-slice_add_fusion.3), channel_id=1, source_target_pairs={{0,4},{1,5},{2,6},{3,7},{4,0},{5,1},{6,2},{7,3},{8,12},{9,13},{10,... | collective-permute-start | bytes 393224 | tf_op jit(solution)/shard_map/ppermute | solution.py:31
  22.7 0.4 fusion.18
  23.1 3.1 %collective-permute-done.2 = f32[256,128]{1,0:T(8,128)S(1)} collective-permute-done((f32[256,128]{1,0:T(8,128)S(1)}, f32[256,128]{1,0:T(8,128)S(1)}, u32[]{:S(2)}, u32[]{:S(2)}) %collective-permute-start.2) | collective-permute-done | bytes 131104 | tf_op jit(solution)/shard_map/ppermute | solution.py:31
  26.2 2.7 %collective-permute-start.3 = (f32[256,128]{1,0:T(8,128)S(1)}, f32[256,128]{1,0:T(8,128)S(1)}, u32[]{:S(2)}, u32[]{:S(2)}) collective-permute-start(f32[256,128]{1,0:T(8,128)S(1)} %add.235), channel_id=1, source_target_pairs={{0,8},{1,9},{2,10},{3,11},{4,12},{5,13},{6,14},{7,15},{8,0},{9,1},... | collective-permute-start | bytes 393224 | tf_op jit(solution)/shard_map/ppermute | solution.py:31
  28.9 0.4 fusion.16
  29.3 5.1 %collective-permute-done.3 = f32[256,128]{1,0:T(8,128)S(1)} collective-permute-done((f32[256,128]{1,0:T(8,128)S(1)}, f32[256,128]{1,0:T(8,128)S(1)}, u32[]{:S(2)}, u32[]{:S(2)}) %collective-permute-start.3) | collective-permute-done | bytes 131104 | tf_op jit(solution)/shard_map/ppermute | solution.py:31
  34.4 0.6 multiply_reduce_fusion.3
  35.1 1.3 %collective-permute-start.5 = (f32[256,128]{1,0:T(8,128)S(1)}, f32[256,128]{1,0:T(8,128)S(1)}, u32[]{:S(2)}, u32[]{:S(2)}) collective-permute-start(f32[256,128]{1,0:T(8,128)S(1)} %get-tuple-element.5), channel_id=1, source_target_pairs={{0,2},{1,3},{2,0},{3,1},{4,6},{5,7},{6,4},{7,5},{8,10},{9,11},{10,... | collective-permute-start | bytes 393224 | tf_op jit(solution)/shard_map/ppermute | solution.py:31
  36.4 0.6 collective-permute-start.6
  36.9 1.4 %fusion.7 = f32[512]{0:T(512)S(1)} fusion(f32[256,512]{1,0:T(8,128)S(1)} %fusion.22, f32[256,128]{1,0:T(8,128)S(1)} %get-tuple-element.5, f32[512,128]{1,0:T(8,128)S(1)} %copy-done, f32[1024,512]{1,0:T(8,128)} %get-tuple-element.8, s32[]{:T(128)S(6)} %select_n.165), kind=kOutput, calls=%fused_computation.34 | convolution fusion | flops 101187072 | bytes 1443844 | tf_op jit(solution)/shard_map/dot_general | solution.py:14
  39.8 1.6 %fusion.6 = f32[512]{0:T(512)S(1)} fusion(f32[256,512]{1,0:T(8,128)S(1)} %fusion.20, f32[256,128]{1,0:T(8,128)S(1)} %collective-permute-done.4, f32[512,128]{1,0:T(8,128)S(1)} %copy-done, f32[1024,512]{1,0:T(8,128)} %get-tuple-element.8, s32[]{:T(128)S(6)} %select_n.169), kind=kOutput, calls=%fused_computation.32 | convolution fusion | flops 101187072 | bytes 1443844 | tf_op jit(solution)/shard_map/dot_general | solution.py:14
  41.4 0.1 copy-done.2
  41.4 0.4 fusion.5
  41.9 1.6 %collective-permute-done.6 = f32[256,128]{1,0:T(8,128)} collective-permute-done((f32[256,128]{1,0:T(8,128)S(1)}, f32[256,128]{1,0:T(8,128)}, u32[]{:S(2)}, u32[]{:S(2)}) %collective-permute-start.6) | collective-permute-done | bytes 131104 | tf_op jit(solution)/shard_map/ppermute | solution.py:31
  43.5 1.3 %fusion.4 = f32[512]{0:T(512)S(1)} fusion(f32[256,512]{1,0:T(8,128)S(1)} %fusion.16, f32[256,128]{1,0:T(8,128)} %collective-permute-done.6, f32[512,128]{1,0:T(8,128)S(1)} %copy-done, f32[1024,512]{1,0:T(8,128)S(1)} %copy-done.2, s32[]{:T(128)S(6)} %select_n.177), kind=kOutput, calls=%fused_computation.28 | convolution fusion | flops 101187072 | bytes 1443844 | tf_op jit(solution)/shard_map/dot_general | solution.py:14
  44.8 0.6 add_reduce_fusion.1
  45.5 0.6 stack.6
  46.1 0.7 broadcast_in_dim.15
  46.8 5.6 %all-to-all-start = ((f32[16,2,128]{2,1,0:T(2,128)}), f32[16,2,128]{2,1,0:T(2,128)S(1)}, u32[]{:S(2)}, u32[]{:S(2)}) async-start(f32[16,2,128]{2,1,0:T(2,128)} %broadcast_in_dim.15), calls=%async_computation | async-start | bytes 32768 | tf_op jit(solution)/shard_map/all_to_all | solution.py:74
  52.4 0.9 constant_dynamic-update-slice_fusion.4
  53.4 5.5 %all-to-all-done = f32[16,2,128]{2,1,0:T(2,128)S(1)} async-done(((f32[16,2,128]{2,1,0:T(2,128)}), f32[16,2,128]{2,1,0:T(2,128)S(1)}, u32[]{:S(2)}, u32[]{:S(2)}) %all-to-all-start) | async-done | bytes 16416 | tf_op jit(solution)/shard_map/all_to_all | solution.py:74
  59.0 0.1 multiply_subtract_fusion
  59.1 1.5 %copy-done.5 = s32[1024,512]{1,0:T(8,128)S(1)} copy-done((s32[1024,512]{1,0:T(8,128)S(1)}, s32[1024,512]{1,0:T(8,128)}, u32[]{:S(2)}) %copy-start.5) | copy-done | bytes 2097176
  60.5 9.4 %multiply_select_fusion = (f32[1024,512]{1,0:T(8,128)S(1)}, f32[1024,512]{1,0:T(8,128)S(1)}) fusion(s32[512]{0:T(512)S(1)} %copy-done.6, f32[512]{0:T(512)S(1)} %copy-done.7, s32[1024,512]{1,0:T(8,128)S(1)} %copy-done.5, f32[1024,128]{1,0:T(8,128)S(1)} %multiply_subtract_fusion, f32[512,128]{1,0:T(8,128)S(1)} %multiply_subtract_fusion.2), kind=kOutput, calls=%fused_computation | convolution fusion | flops 413138944 | bytes 7081984 | tf_op jit(solution)/shard_map/dot_general | solution.py:14
  70.0 1.0 fusion.35
  71.0 0.1 collective-permute-start.7
  71.1 2.4 %multiply_reduce_fusion = (f32[]{:T(128)}, f32[512,128]{1,0:T(8,128)S(1)}) fusion(f32[1024,512]{1,0:T(8,128)S(1)} %get-tuple-element.7, f32[1024,128]{1,0:T(8,128)S(1)} %multiply_subtract_fusion), kind=kOutput, calls=%fused_computation.38 | convolution fusion | flops 402784256 | bytes 2883588 | tf_op jit(solution)/shard_map/dot_general | solution.py:14
  73.5 0.4 fusion.12
  74.0 0.6 collective-permute-start.8
  74.6 0.4 fusion.14
  74.9 5.0 %collective-permute-done.8 = f32[256,128]{1,0:T(8,128)S(1)} collective-permute-done((f32[256,128]{1,0:T(8,128)S(1)}, f32[256,128]{1,0:T(8,128)S(1)}, u32[]{:S(2)}, u32[]{:S(2)}) %collective-permute-start.8) | collective-permute-done | bytes 131104 | tf_op jit(solution)/shard_map/ppermute | solution.py:31
  79.9 0.5 collective-permute-start.9
  80.4 0.4 fusion.10
  80.8 4.3 %collective-permute-done.9 = f32[256,128]{1,0:T(8,128)S(1)} collective-permute-done((f32[256,128]{1,0:T(8,128)S(1)}, f32[256,128]{1,0:T(8,128)S(1)}, u32[]{:S(2)}, u32[]{:S(2)}) %collective-permute-start.9) | collective-permute-done | bytes 131104 | tf_op jit(solution)/shard_map/ppermute | solution.py:31
  85.1 0.4 collective-permute-start.10
  85.5 0.4 fusion.8
  85.9 6.6 %collective-permute-done.10 = f32[256,128]{1,0:T(8,128)S(1)} collective-permute-done((f32[256,128]{1,0:T(8,128)S(1)}, f32[256,128]{1,0:T(8,128)S(1)}, u32[]{:S(2)}, u32[]{:S(2)}) %collective-permute-start.10) | collective-permute-done | bytes 131104 | tf_op jit(solution)/shard_map/ppermute | solution.py:31
  92.5 0.6 multiply_reduce_fusion.2
  93.1 1.0 collective-permute-start.12
  94.1 0.9 collective-permute-start.13
  95.0 0.4 fusion.3
  96.8 1.6 %fusion.2 = f32[512]{0:T(512)S(1)} fusion(f32[256,512]{1,0:T(8,128)S(1)} %fusion.12, f32[256,128]{1,0:T(8,128)S(1)} %collective-permute-done.11, f32[512,128]{1,0:T(8,128)S(1)} %multiply_subtract_fusion.2, f32[1024,512]{1,0:T(8,128)} %copy-done.3, s32[]{:T(128)S(6)} %select_n.169), kind=kOutput, calls=%fused_computation.24 | convolution fusion | flops 101187072 | bytes 1443844 | tf_op jit(solution)/shard_map/dot_general | solution.py:14
  98.4 1.0 collective-permute-done.12
  99.4 0.4 fusion.1
  99.8 1.7 %collective-permute-done.13 = f32[256,128]{1,0:T(8,128)} collective-permute-done((f32[256,128]{1,0:T(8,128)S(1)}, f32[256,128]{1,0:T(8,128)}, u32[]{:S(2)}, u32[]{:S(2)}) %collective-permute-start.13) | collective-permute-done | bytes 131104 | tf_op jit(solution)/shard_map/ppermute | solution.py:31
  101.5 1.3 %fusion = f32[512]{0:T(512)S(1)} fusion(f32[256,512]{1,0:T(8,128)S(1)} %fusion.8, f32[256,128]{1,0:T(8,128)} %collective-permute-done.13, f32[512,128]{1,0:T(8,128)S(1)} %multiply_subtract_fusion.2, f32[1024,512]{1,0:T(8,128)S(1)} %copy-done.4, s32[]{:T(128)S(6)} %select_n.177), kind=kOutput, calls=%fused_computation.20 | convolution fusion | flops 101187072 | bytes 1443844 | tf_op jit(solution)/shard_map/dot_general | solution.py:14
  102.9 0.6 add_reduce_fusion
  103.5 0.6 stack.7
  104.1 0.7 broadcast_in_dim.16
  104.8 3.5 %all-to-all-start.1 = ((f32[16,2,128]{2,1,0:T(2,128)}), f32[16,2,128]{2,1,0:T(2,128)S(1)}, u32[]{:S(2)}, u32[]{:S(2)}) async-start(f32[16,2,128]{2,1,0:T(2,128)} %broadcast_in_dim.16), calls=%async_computation.1 | async-start | bytes 32768 | tf_op jit(solution)/shard_map/all_to_all | solution.py:74
  108.4 0.9 constant_dynamic-update-slice_fusion
  109.3 5.5 %all-to-all-done.1 = f32[16,2,128]{2,1,0:T(2,128)S(1)} async-done(((f32[16,2,128]{2,1,0:T(2,128)}), f32[16,2,128]{2,1,0:T(2,128)S(1)}, u32[]{:S(2)}, u32[]{:S(2)}) %all-to-all-start.1) | async-done | bytes 16416 | tf_op jit(solution)/shard_map/all_to_all | solution.py:74
  114.8 0.7 multiply_subtract_fusion.1
  115.6 0.6 dynamic-slice_subtract_fusion
  (42 shorter events, 0.5 us)
Async XLA Ops:
  0.6 6.2 %copy-start = (f32[512,128]{1,0:T(8,128)S(1)}, f32[512,128]{1,0:T(8,128)}, u32[]{:S(2)}) copy-start(f32[512,128]{1,0:T(8,128)} %param.8) | copy-start | bytes 786436
  6.9 3.3 %copy-start.1 = (f32[1024,128]{1,0:T(8,128)S(1)}, f32[1024,128]{1,0:T(8,128)}, u32[]{:S(2)}) copy-start(f32[1024,128]{1,0:T(8,128)} %param.7) | copy-start | bytes 1572868
  9.6 3.3 %collective-permute-start = (f32[512,128]{1,0:T(8,128)S(1)}, f32[512,128]{1,0:T(8,128)}, u32[]{:S(2)}, u32[]{:S(2)}) collective-permute-start(f32[512,128]{1,0:T(8,128)S(1)} %constant_dynamic-slice_fusion.3), channel_id=1, source_target_pairs={{0,1},{1,0},{2,3},{3,2},{4,5},{5,4},{6,7},{7,6},{8,9},{9,8},{10,11... | collective-permute-start | bytes 786440 | tf_op jit(solution)/shard_map/ppermute | solution.py:31
  14.1 6.7 %collective-permute-start.1 = (f32[256,128]{1,0:T(8,128)S(1)}, f32[256,128]{1,0:T(8,128)S(1)}, u32[]{:S(2)}, u32[]{:S(2)}) collective-permute-start(f32[256,128]{1,0:T(8,128)S(1)} %constant_dynamic-slice_fusion.2), channel_id=1, source_target_pairs={{0,2},{1,3},{2,0},{3,1},{4,6},{5,7},{6,4},{7,5},{8,10},{9,11},{10,... | collective-permute-start | bytes 393224 | tf_op jit(solution)/shard_map/ppermute | solution.py:31
  20.8 5.4 %collective-permute-start.2 = (f32[256,128]{1,0:T(8,128)S(1)}, f32[256,128]{1,0:T(8,128)S(1)}, u32[]{:S(2)}, u32[]{:S(2)}) collective-permute-start(f32[256,128]{1,0:T(8,128)S(1)} %dynamic-slice_add_fusion.3), channel_id=1, source_target_pairs={{0,4},{1,5},{2,6},{3,7},{4,0},{5,1},{6,2},{7,3},{8,12},{9,13},{10,... | collective-permute-start | bytes 393224 | tf_op jit(solution)/shard_map/ppermute | solution.py:31
  26.2 8.2 %collective-permute-start.3 = (f32[256,128]{1,0:T(8,128)S(1)}, f32[256,128]{1,0:T(8,128)S(1)}, u32[]{:S(2)}, u32[]{:S(2)}) collective-permute-start(f32[256,128]{1,0:T(8,128)S(1)} %add.235), channel_id=1, source_target_pairs={{0,8},{1,9},{2,10},{3,11},{4,12},{5,13},{6,14},{7,15},{8,0},{9,1},... | collective-permute-start | bytes 393224 | tf_op jit(solution)/shard_map/ppermute | solution.py:31
  35.1 4.7 %collective-permute-start.4 = (f32[256,128]{1,0:T(8,128)S(1)}, f32[256,128]{1,0:T(8,128)S(1)}, u32[]{:S(2)}, u32[]{:S(2)}) collective-permute-start(f32[256,128]{1,0:T(8,128)S(1)} %get-tuple-element.5), channel_id=1, source_target_pairs={{0,1},{1,0},{2,3},{3,2},{4,5},{5,4},{6,7},{7,6},{8,9},{9,8},{10,11... | collective-permute-start | bytes 393224 | tf_op jit(solution)/shard_map/ppermute | solution.py:31
  35.1 6.3 %collective-permute-start.5 = (f32[256,128]{1,0:T(8,128)S(1)}, f32[256,128]{1,0:T(8,128)S(1)}, u32[]{:S(2)}, u32[]{:S(2)}) collective-permute-start(f32[256,128]{1,0:T(8,128)S(1)} %get-tuple-element.5), channel_id=1, source_target_pairs={{0,2},{1,3},{2,0},{3,1},{4,6},{5,7},{6,4},{7,5},{8,10},{9,11},{10,... | collective-permute-start | bytes 393224 | tf_op jit(solution)/shard_map/ppermute | solution.py:31
  36.4 7.1 %collective-permute-start.6 = (f32[256,128]{1,0:T(8,128)S(1)}, f32[256,128]{1,0:T(8,128)}, u32[]{:S(2)}, u32[]{:S(2)}) collective-permute-start(f32[256,128]{1,0:T(8,128)S(1)} %get-tuple-element.5), channel_id=1, source_target_pairs={{0,3},{1,2},{2,1},{3,0},{4,7},{5,6},{6,5},{7,4},{8,11},{9,10},{10,... | collective-permute-start | bytes 393224 | tf_op jit(solution)/shard_map/ppermute | solution.py:31
  39.7 1.7 %copy-start.2 = (f32[1024,512]{1,0:T(8,128)S(1)}, f32[1024,512]{1,0:T(8,128)}, u32[]{:S(2)}) copy-start(f32[1024,512]{1,0:T(8,128)} %get-tuple-element.8) | copy-start | bytes 6291460
  41.9 17.2 %copy-start.6 = (s32[512]{0:T(512)S(1)}, s32[512]{0:T(512)}, u32[]{:S(2)}) copy-start(s32[512]{0:T(512)} %param.6) | copy-start | bytes 6148
  41.9 17.2 %copy-start.7 = (f32[512]{0:T(512)S(1)}, f32[512]{0:T(512)}, u32[]{:S(2)}) copy-start(f32[512]{0:T(512)} %param.9) | copy-start | bytes 6148
  46.8 12.1 %all-to-all-start = ((f32[16,2,128]{2,1,0:T(2,128)}), f32[16,2,128]{2,1,0:T(2,128)S(1)}, u32[]{:S(2)}, u32[]{:S(2)}) async-start(f32[16,2,128]{2,1,0:T(2,128)} %broadcast_in_dim.15), calls=%async_computation | async-start | bytes 32768 | tf_op jit(solution)/shard_map/all_to_all | solution.py:74
  58.9 1.6 %copy-start.5 = (s32[1024,512]{1,0:T(8,128)S(1)}, s32[1024,512]{1,0:T(8,128)}, u32[]{:S(2)}) copy-start(s32[1024,512]{1,0:T(8,128)} %param.5) | copy-start | bytes 6291460
  69.9 25.0 %copy-start.3 = (f32[1024,512]{1,0:T(8,128)}, f32[1024,512]{1,0:T(8,128)S(1)}, u32[]{:S(2)}) copy-start(f32[1024,512]{1,0:T(8,128)S(1)} %get-tuple-element.6) | copy-start | bytes 6291460
  71.0 2.9 %collective-permute-start.7 = (f32[512,128]{1,0:T(8,128)S(1)}, f32[512,128]{1,0:T(8,128)S(1)}, u32[]{:S(2)}, u32[]{:S(2)}) collective-permute-start(f32[512,128]{1,0:T(8,128)S(1)} %constant_dynamic-slice_fusion.1), channel_id=1, source_target_pairs={{0,1},{1,0},{2,3},{3,2},{4,5},{5,4},{6,7},{7,6},{8,9},{9,8},{10,11... | collective-permute-start | bytes 786440 | tf_op jit(solution)/shard_map/ppermute | solution.py:31
  74.0 6.0 %collective-permute-start.8 = (f32[256,128]{1,0:T(8,128)S(1)}, f32[256,128]{1,0:T(8,128)S(1)}, u32[]{:S(2)}, u32[]{:S(2)}) collective-permute-start(f32[256,128]{1,0:T(8,128)S(1)} %constant_dynamic-slice_fusion), channel_id=1, source_target_pairs={{0,2},{1,3},{2,0},{3,1},{4,6},{5,7},{6,4},{7,5},{8,10},{9,11},{10,... | collective-permute-start | bytes 393224 | tf_op jit(solution)/shard_map/ppermute | solution.py:31
  79.9 5.2 %collective-permute-start.9 = (f32[256,128]{1,0:T(8,128)S(1)}, f32[256,128]{1,0:T(8,128)S(1)}, u32[]{:S(2)}, u32[]{:S(2)}) collective-permute-start(f32[256,128]{1,0:T(8,128)S(1)} %dynamic-slice_add_fusion.2), channel_id=1, source_target_pairs={{0,4},{1,5},{2,6},{3,7},{4,0},{5,1},{6,2},{7,3},{8,12},{9,13},{10,... | collective-permute-start | bytes 393224 | tf_op jit(solution)/shard_map/ppermute | solution.py:31
  85.1 7.3 %collective-permute-start.10 = (f32[256,128]{1,0:T(8,128)S(1)}, f32[256,128]{1,0:T(8,128)S(1)}, u32[]{:S(2)}, u32[]{:S(2)}) collective-permute-start(f32[256,128]{1,0:T(8,128)S(1)} %add.266), channel_id=1, source_target_pairs={{0,8},{1,9},{2,10},{3,11},{4,12},{5,13},{6,14},{7,15},{8,0},{9,1},... | collective-permute-start | bytes 393224 | tf_op jit(solution)/shard_map/ppermute | solution.py:31
  93.1 3.7 %collective-permute-start.11 = (f32[256,128]{1,0:T(8,128)S(1)}, f32[256,128]{1,0:T(8,128)S(1)}, u32[]{:S(2)}, u32[]{:S(2)}) collective-permute-start(f32[256,128]{1,0:T(8,128)S(1)} %get-tuple-element.3), channel_id=1, source_target_pairs={{0,1},{1,0},{2,3},{3,2},{4,5},{5,4},{6,7},{7,6},{8,9},{9,8},{10,11... | collective-permute-start | bytes 393224 | tf_op jit(solution)/shard_map/ppermute | solution.py:31
  93.1 6.3 %collective-permute-start.12 = (f32[256,128]{1,0:T(8,128)S(1)}, f32[256,128]{1,0:T(8,128)S(1)}, u32[]{:S(2)}, u32[]{:S(2)}) collective-permute-start(f32[256,128]{1,0:T(8,128)S(1)} %get-tuple-element.3), channel_id=1, source_target_pairs={{0,2},{1,3},{2,0},{3,1},{4,6},{5,7},{6,4},{7,5},{8,10},{9,11},{10,... | collective-permute-start | bytes 393224 | tf_op jit(solution)/shard_map/ppermute | solution.py:31
  94.1 7.4 %collective-permute-start.13 = (f32[256,128]{1,0:T(8,128)S(1)}, f32[256,128]{1,0:T(8,128)}, u32[]{:S(2)}, u32[]{:S(2)}) collective-permute-start(f32[256,128]{1,0:T(8,128)S(1)} %get-tuple-element.3), channel_id=1, source_target_pairs={{0,3},{1,2},{2,1},{3,0},{4,7},{5,6},{6,5},{7,4},{8,11},{9,10},{10,... | collective-permute-start | bytes 393224 | tf_op jit(solution)/shard_map/ppermute | solution.py:31
  96.7 2.7 %copy-start.4 = (f32[1024,512]{1,0:T(8,128)S(1)}, f32[1024,512]{1,0:T(8,128)}, u32[]{:S(2)}) copy-start(f32[1024,512]{1,0:T(8,128)} %copy-done.3) | copy-start | bytes 6291460
  104.8 10.0 %all-to-all-start.1 = ((f32[16,2,128]{2,1,0:T(2,128)}), f32[16,2,128]{2,1,0:T(2,128)S(1)}, u32[]{:S(2)}, u32[]{:S(2)}) async-start(f32[16,2,128]{2,1,0:T(2,128)} %broadcast_in_dim.16), calls=%async_computation.1 | async-start | bytes 32768 | tf_op jit(solution)/shard_map/all_to_all | solution.py:74

commit v13 on v10

--- a/solution.py
+++ b/solution.py
@@ -67,8 +67,10 @@
 
 
 def sum_rows(values, n):
-    rows = jnp.stack([jnp.broadcast_to(v, (128,)) for v in values])
-    spread = jnp.broadcast_to(rows[None], (n,) + rows.shape)
+    row = lax.broadcasted_iota(jnp.int32, (n, len(values), 128), 1)
+    spread = jnp.zeros(row.shape, jnp.float32)
+    for k, v in enumerate(values):
+        spread = jnp.where(row == k, v, spread)
     if n > 1:
         spread = lax.all_to_all(spread, "user", 0, 0, tiled=False)
     total = jnp.sum(spread, axis=0)

time: 107 us -> 106 us (level)
  local copies, waits for them, and re-layouts: 6.02 us -> 2.71 us
  other arithmetic: 5.91 us -> 7.82 us
  waiting for transfers between devices: 41.7 us -> 43 us
    select_n x0 -> x4, other arithmetic: none -> 2.66 us  [sum_rows(): spread = jnp.where(row == k, v, spread)]
    broadcast_in_dim x2 -> x0, local copies, waits for them, and re-layouts: 1.36 us -> none  [sum_rows(): spread = jnp.broadcast_to(rows[None], (n,) + rows.shape)]
    another operation x4 -> x2, local copies, waits for them, and re-layouts: 1.37 us -> 0.07 us  [the longest x2 1.29 us: sum_rows(): rows = jnp.stack([jnp.broadcast_to(v, (128,)) for v in values])]
  transfers between devices with their start and end apart: 16 -> 16, of which waited for: 12 -> 12; matrix products, arithmetic and copies ran while one was open for 13% -> 12% of each run, Pallas kernels for 0% -> 0%
where the time goes in v13:
time: 106 us
  waiting for transfers between devices  43 us (41%)
  matrix products  27.8 us (26%)
  starting transfers between devices  20.6 us (19%)
  other arithmetic  7.82 us (7%)
  between operations  3.69 us (3%)
  local copies, waits for them, and re-layouts  2.71 us (3%)
    ppermute x14, waiting for transfers between devices, exchange(): return lax.ppermute(value, 'user', [(i, i ^ distance) for i in range(n)])  30.1 us
    dot_general x22, matrix products, product(): jnp.dot(left, right, precision=precision, preferred_element_type=jnp.floa...  27.8 us
    all_to_all x2, waiting for transfers between devices, sum_rows(): spread = lax.all_to_all(spread, 'user', 0, 0, tiled=False)  12.9 us
    ppermute x14, starting transfers between devices, exchange(): return lax.ppermute(value, 'user', [(i, i ^ distance) for i in range(n)])  11.3 us
    all_to_all x2, starting transfers between devices, sum_rows(): spread = lax.all_to_all(spread, 'user', 0, 0, tiled=False)  9.21 us
    select_n x4, other arithmetic, sum_rows(): spread = jnp.where(row == k, v, spread)  2.66 us
  transfers between devices with their start and end apart: 16, of which 12 were waited for; matrix products, arithmetic and copies ran while one was open for 12% of the time, Pallas kernels for 0%

profile of v13, /device:TPU:0, one launch (start us, length us, event | category | flops | bytes accessed | tf_op | source)
XLA Modules:
  0.0 105.6 jit_solution(4911296919982665715)
XLA Ops:
  0.7 6.2 %multiply_select_fusion.3 = (f32[1024,512]{1,0:T(8,128)}, f32[1024,512]{1,0:T(8,128)S(1)}) fusion(s32[512]{0:T(512)} %param.6, f32[512]{0:T(512)} %param.9, s32[1024,512]{1,0:T(8,128)} %param.5, f32[1024,128]{1,0:T(8,128)} %param.7, f32[512,128]{1,0:T(8,128)} %param.8), kind=kOutput, calls=%fused_computation.6 | convolution fusion | flops 413138944 | bytes 7081984 | tf_op jit(solution)/shard_map/dot_general | solution.py:14
  6.9 1.8 %fusion.31 = f32[1024,128]{1,0:T(8,128)} fusion(f32[1024,512]{1,0:T(8,128)S(1)} %get-tuple-element.9, f32[512,128]{1,0:T(8,128)S(1)} %copy-done), kind=kOutput, calls=%fused_computation.92 | convolution fusion | flops 402653184 | bytes 2883584 | tf_op jit(solution)/shard_map/dot_general | solution.py:14
  8.7 1.0 constant_dynamic-slice_fusion.3
  9.6 0.5 collective-permute-start
  10.2 2.4 %multiply_reduce_fusion.1 = (f32[]{:T(128)}, f32[512,128]{1,0:T(8,128)S(1)}) fusion(f32[1024,512]{1,0:T(8,128)S(1)} %get-tuple-element.9, f32[1024,128]{1,0:T(8,128)S(1)} %copy-done.1), kind=kOutput, calls=%fused_computation.40 | convolution fusion | flops 402784256 | bytes 2883588 | tf_op jit(solution)/shard_map/dot_general | solution.py:14
  12.6 0.4 fusion.17
  13.0 0.0 collective-permute-done
  13.0 1.1 %dynamic-slice_add_fusion.1 = f32[512,128]{1,0:T(8,128)S(1)} fusion(f32[512,128]{1,0:T(8,128)} %collective-permute-done, f32[1024,128]{1,0:T(8,128)} %fusion.31, s32[]{:T(128)S(6)} %select_n.134), kind=kLoop, calls=%fused_computation.41 | loop fusion | flops 65536 | bytes 786436 | tf_op jit(solution)/shard_map/add | solution.py:54
  14.1 2.6 %collective-permute-start.1 = (f32[256,128]{1,0:T(8,128)S(1)}, f32[256,128]{1,0:T(8,128)S(1)}, u32[]{:S(2)}, u32[]{:S(2)}) collective-permute-start(f32[256,128]{1,0:T(8,128)S(1)} %constant_dynamic-slice_fusion.2), channel_id=1, source_target_pairs={{0,2},{1,3},{2,0},{3,1},{4,6},{5,7},{6,4},{7,5},{8,10},{9,11},{10,... | collective-permute-start | bytes 393224 | tf_op jit(solution)/shard_map/ppermute | solution.py:31
  16.6 0.4 fusion.19
  17.0 3.8 %collective-permute-done.1 = f32[256,128]{1,0:T(8,128)S(1)} collective-permute-done((f32[256,128]{1,0:T(8,128)S(1)}, f32[256,128]{1,0:T(8,128)S(1)}, u32[]{:S(2)}, u32[]{:S(2)}) %collective-permute-start.1) | collective-permute-done | bytes 131104 | tf_op jit(solution)/shard_map/ppermute | solution.py:31
  20.8 1.9 %collective-permute-start.2 = (f32[256,128]{1,0:T(8,128)S(1)}, f32[256,128]{1,0:T(8,128)S(1)}, u32[]{:S(2)}, u32[]{:S(2)}) collective-permute-start(f32[256,128]{1,0:T(8,128)S(1)} %dynamic-slice_add_fusion.3), channel_id=1, source_target_pairs={{0,4},{1,5},{2,6},{3,7},{4,0},{5,1},{6,2},{7,3},{8,12},{9,13},{10,... | collective-permute-start | bytes 393224 | tf_op jit(solution)/shard_map/ppermute | solution.py:31
  22.7 0.4 fusion.15
  23.1 3.1 %collective-permute-done.2 = f32[256,128]{1,0:T(8,128)S(1)} collective-permute-done((f32[256,128]{1,0:T(8,128)S(1)}, f32[256,128]{1,0:T(8,128)S(1)}, u32[]{:S(2)}, u32[]{:S(2)}) %collective-permute-start.2) | collective-permute-done | bytes 131104 | tf_op jit(solution)/shard_map/ppermute | solution.py:31
  26.2 2.7 %collective-permute-start.3 = (f32[256,128]{1,0:T(8,128)S(1)}, f32[256,128]{1,0:T(8,128)S(1)}, u32[]{:S(2)}, u32[]{:S(2)}) collective-permute-start(f32[256,128]{1,0:T(8,128)S(1)} %add.207), channel_id=1, source_target_pairs={{0,8},{1,9},{2,10},{3,11},{4,12},{5,13},{6,14},{7,15},{8,0},{9,1},... | collective-permute-start | bytes 393224 | tf_op jit(solution)/shard_map/ppermute | solution.py:31
  28.9 0.4 fusion.13
  29.3 5.1 %collective-permute-done.3 = f32[256,128]{1,0:T(8,128)S(1)} collective-permute-done((f32[256,128]{1,0:T(8,128)S(1)}, f32[256,128]{1,0:T(8,128)S(1)}, u32[]{:S(2)}, u32[]{:S(2)}) %collective-permute-start.3) | collective-permute-done | bytes 131104 | tf_op jit(solution)/shard_map/ppermute | solution.py:31
  34.4 0.6 multiply_reduce_fusion.3
  35.1 1.3 %collective-permute-start.4 = (f32[256,128]{1,0:T(8,128)S(1)}, f32[256,128]{1,0:T(8,128)S(1)}, u32[]{:S(2)}, u32[]{:S(2)}) collective-permute-start(f32[256,128]{1,0:T(8,128)S(1)} %get-tuple-element.5), channel_id=1, source_target_pairs={{0,2},{1,3},{2,0},{3,1},{4,6},{5,7},{6,4},{7,5},{8,10},{9,11},{10,... | collective-permute-start | bytes 393224 | tf_op jit(solution)/shard_map/ppermute | solution.py:31
  36.4 1.5 %fusion.7 = f32[512]{0:T(512)S(1)} fusion(f32[256,512]{1,0:T(8,128)S(1)} %fusion.19, f32[256,128]{1,0:T(8,128)S(1)} %get-tuple-element.5, f32[512,128]{1,0:T(8,128)S(1)} %copy-done, f32[1024,512]{1,0:T(8,128)} %get-tuple-element.8, s32[]{:T(128)S(6)} %select_n.132), kind=kOutput, calls=%fused_computation.34 | convolution fusion | flops 101187072 | bytes 1443844 | tf_op jit(solution)/shard_map/dot_general | solution.py:14
  39.2 0.8 collective-permute-done.4
  40.0 1.5 %fusion.6 = f32[512]{0:T(512)S(1)} fusion(f32[256,512]{1,0:T(8,128)S(1)} %fusion.17, f32[256,128]{1,0:T(8,128)S(1)} %collective-permute-done.4, f32[512,128]{1,0:T(8,128)S(1)} %copy-done, f32[1024,512]{1,0:T(8,128)} %get-tuple-element.8, s32[]{:T(128)S(6)} %select_n.138), kind=kOutput, calls=%fused_computation.32 | convolution fusion | flops 101187072 | bytes 1443844 | tf_op jit(solution)/shard_map/dot_general | solution.py:14
  41.5 0.0 copy-start.2
  41.5 0.4 fusion.5
  42.0 0.0 copy-start.6
  42.0 0.0 copy-start.7
  42.0 0.4 fusion.4
  42.5 0.6 add_reduce_fusion.1
  43.1 1.3 %broadcast_select_fusion.1 = f32[16,2,128]{2,1,0:T(2,128)} fusion(pred[2]{0:T(512)(128)(4,1)S(1)} %iota_compare_fusion.1, f32[]{:T(128)} %add_reduce_fusion.1, f32[2]{0:T(128)S(1)} %compare_select_fusion.1), kind=kLoop, calls=%fused_computation.62 | loop fusion | flops 4096 | bytes 16398 | tf_op jit(solution)/shard_map/jit(_where)/select_n | solution.py:73
  44.4 5.7 %all-to-all-start = ((f32[16,2,128]{2,1,0:T(2,128)}), f32[16,2,128]{2,1,0:T(2,128)S(1)}, u32[]{:S(2)}, u32[]{:S(2)}) async-start(f32[16,2,128]{2,1,0:T(2,128)} %broadcast_select_fusion.1), calls=%async_computation | async-start | bytes 32768 | tf_op jit(solution)/shard_map/all_to_all | solution.py:75
  50.2 6.5 %all-to-all-done = f32[16,2,128]{2,1,0:T(2,128)S(1)} async-done(((f32[16,2,128]{2,1,0:T(2,128)}), f32[16,2,128]{2,1,0:T(2,128)S(1)}, u32[]{:S(2)}, u32[]{:S(2)}) %all-to-all-start) | async-done | bytes 16416 | tf_op jit(solution)/shard_map/all_to_all | solution.py:75
  56.7 0.1 multiply_subtract_fusion
  56.8 1.4 %copy-done.5 = s32[1024,512]{1,0:T(8,128)S(1)} copy-done((s32[1024,512]{1,0:T(8,128)S(1)}, s32[1024,512]{1,0:T(8,128)}, u32[]{:S(2)}) %copy-start.5) | copy-done | bytes 2097176
  58.2 4.3 %multiply_select_fusion.1 = (f32[1024,512]{1,0:T(8,128)}, f32[1024,512]{1,0:T(8,128)S(1)}) fusion(s32[512]{0:T(512)S(1)} %copy-done.6, f32[512]{0:T(512)S(1)} %copy-done.7, s32[1024,512]{1,0:T(8,128)S(1)} %copy-done.5, f32[1024,128]{1,0:T(8,128)S(1)} %multiply_subtract_fusion, f32[512,128]{1,0:T(8,128)S(1)} %multiply_subtract_fusion.2), kind=kOutput, calls=%fused_computation.1 | convolution fusion | flops 413138944 | bytes 7081984 | tf_op jit(solution)/shard_map/dot_general | solution.py:14
  62.6 1.0 fusion.32
  63.6 0.1 collective-permute-start.7
  63.7 1.5 %collective-permute-done.7 = f32[512,128]{1,0:T(8,128)S(1)} collective-permute-done((f32[512,128]{1,0:T(8,128)S(1)}, f32[512,128]{1,0:T(8,128)S(1)}, u32[]{:S(2)}, u32[]{:S(2)}) %collective-permute-start.7) | collective-permute-done | bytes 262176 | tf_op jit(solution)/shard_map/ppermute | solution.py:31
  65.3 0.5 collective-permute-start.8
  65.8 5.1 %collective-permute-done.8 = f32[256,128]{1,0:T(8,128)S(1)} collective-permute-done((f32[256,128]{1,0:T(8,128)S(1)}, f32[256,128]{1,0:T(8,128)S(1)}, u32[]{:S(2)}, u32[]{:S(2)}) %collective-permute-start.8) | collective-permute-done | bytes 131104 | tf_op jit(solution)/shard_map/ppermute | solution.py:31
  70.9 0.5 collective-permute-start.9
  71.4 2.4 %multiply_reduce_fusion = (f32[]{:T(128)}, f32[512,128]{1,0:T(8,128)S(1)}) fusion(f32[1024,512]{1,0:T(8,128)S(1)} %get-tuple-element.7, f32[1024,128]{1,0:T(8,128)S(1)} %multiply_subtract_fusion), kind=kOutput, calls=%fused_computation.37 | convolution fusion | flops 402784256 | bytes 2883588 | tf_op jit(solution)/shard_map/dot_general | solution.py:14
  73.8 2.1 %collective-permute-done.9 = f32[256,128]{1,0:T(8,128)S(1)} collective-permute-done((f32[256,128]{1,0:T(8,128)S(1)}, f32[256,128]{1,0:T(8,128)S(1)}, u32[]{:S(2)}, u32[]{:S(2)}) %collective-permute-start.9) | collective-permute-done | bytes 131104 | tf_op jit(solution)/shard_map/ppermute | solution.py:31
  76.0 0.5 collective-permute-start.10
  76.5 0.4 fusion.8
  76.9 6.3 %collective-permute-done.10 = f32[256,128]{1,0:T(8,128)S(1)} collective-permute-done((f32[256,128]{1,0:T(8,128)S(1)}, f32[256,128]{1,0:T(8,128)S(1)}, u32[]{:S(2)}, u32[]{:S(2)}) %collective-permute-start.10) | collective-permute-done | bytes 131104 | tf_op jit(solution)/shard_map/ppermute | solution.py:31
  83.2 0.6 multiply_reduce_fusion.2
  83.8 0.6 collective-permute-start.11
  84.4 0.4 fusion.33
  84.8 0.1 collective-permute-start.12
  86.1 1.6 %fusion.3 = f32[512]{0:T(512)S(1)} fusion(f32[256,512]{1,0:T(8,128)S(1)} %fusion.33, f32[512,128]{1,0:T(8,128)S(1)} %get-tuple-element.13, f32[1024,512]{1,0:T(8,128)} %get-tuple-element.6, s32[]{:T(128)S(6)} %select_n.132, f32[1024,128]{1,0:T(8,128)S(1)} %multiply_subtract_fusion), kind=kOutput, calls=%fused_computation.26 | convolution fusion | flops 101187072 | bytes 1444864 | tf_op jit(solution)/shard_map/dot_general | solution.py:14
  87.8 0.9 collective-permute-done.11
  88.8 0.4 fusion.34
  89.2 0.4 fusion.2
  89.6 0.4 fusion.35
  90.0 0.4 fusion.1
  90.4 0.1 collective-permute-start.13
  90.6 1.3 %collective-permute-done.13 = f32[256,128]{1,0:T(8,128)S(1)} collective-permute-done((f32[256,128]{1,0:T(8,128)S(1)}, f32[256,128]{1,0:T(8,128)S(1)}, u32[]{:S(2)}, u32[]{:S(2)}) %collective-permute-start.13) | collective-permute-done | bytes 131104 | tf_op jit(solution)/shard_map/ppermute | solution.py:31
  91.9 0.4 fusion
  92.3 0.6 add_reduce_fusion
  92.9 1.3 %broadcast_select_fusion = f32[16,2,128]{2,1,0:T(2,128)} fusion(pred[2]{0:T(512)(128)(4,1)S(1)} %iota_compare_fusion.1, f32[]{:T(128)} %add_reduce_fusion, f32[2]{0:T(128)S(1)} %compare_select_fusion), kind=kLoop, calls=%fused_computation.61 | loop fusion | flops 4096 | bytes 16398 | tf_op jit(solution)/shard_map/jit(_where)/select_n | solution.py:73
  94.2 3.5 %all-to-all-start.1 = ((f32[16,2,128]{2,1,0:T(2,128)}), f32[16,2,128]{2,1,0:T(2,128)S(1)}, u32[]{:S(2)}, u32[]{:S(2)}) async-start(f32[16,2,128]{2,1,0:T(2,128)} %broadcast_select_fusion), calls=%async_computation.1 | async-start | bytes 32768 | tf_op jit(solution)/shard_map/all_to_all | solution.py:75
  97.7 6.4 %all-to-all-done.1 = f32[16,2,128]{2,1,0:T(2,128)S(1)} async-done(((f32[16,2,128]{2,1,0:T(2,128)}), f32[16,2,128]{2,1,0:T(2,128)S(1)}, u32[]{:S(2)}, u32[]{:S(2)}) %all-to-all-start.1) | async-done | bytes 16416 | tf_op jit(solution)/shard_map/all_to_all | solution.py:75
  104.2 0.7 multiply_subtract_fusion.1
  105.0 0.6 dynamic-slice_subtract_fusion
  (43 shorter events, 0.5 us)
Async XLA Ops:
  0.6 6.2 %copy-start = (f32[512,128]{1,0:T(8,128)S(1)}, f32[512,128]{1,0:T(8,128)}, u32[]{:S(2)}) copy-start(f32[512,128]{1,0:T(8,128)} %param.8) | copy-start | bytes 786436
  6.9 3.3 %copy-start.1 = (f32[1024,128]{1,0:T(8,128)S(1)}, f32[1024,128]{1,0:T(8,128)}, u32[]{:S(2)}) copy-start(f32[1024,128]{1,0:T(8,128)} %param.7) | copy-start | bytes 1572868
  9.6 3.3 %collective-permute-start = (f32[512,128]{1,0:T(8,128)S(1)}, f32[512,128]{1,0:T(8,128)}, u32[]{:S(2)}, u32[]{:S(2)}) collective-permute-start(f32[512,128]{1,0:T(8,128)S(1)} %constant_dynamic-slice_fusion.3), channel_id=1, source_target_pairs={{0,1},{1,0},{2,3},{3,2},{4,5},{5,4},{6,7},{7,6},{8,9},{9,8},{10,11... | collective-permute-start | bytes 786440 | tf_op jit(solution)/shard_map/ppermute | solution.py:31
  14.1 6.7 %collective-permute-start.1 = (f32[256,128]{1,0:T(8,128)S(1)}, f32[256,128]{1,0:T(8,128)S(1)}, u32[]{:S(2)}, u32[]{:S(2)}) collective-permute-start(f32[256,128]{1,0:T(8,128)S(1)} %constant_dynamic-slice_fusion.2), channel_id=1, source_target_pairs={{0,2},{1,3},{2,0},{3,1},{4,6},{5,7},{6,4},{7,5},{8,10},{9,11},{10,... | collective-permute-start | bytes 393224 | tf_op jit(solution)/shard_map/ppermute | solution.py:31
  20.8 5.4 %collective-permute-start.2 = (f32[256,128]{1,0:T(8,128)S(1)}, f32[256,128]{1,0:T(8,128)S(1)}, u32[]{:S(2)}, u32[]{:S(2)}) collective-permute-start(f32[256,128]{1,0:T(8,128)S(1)} %dynamic-slice_add_fusion.3), channel_id=1, source_target_pairs={{0,4},{1,5},{2,6},{3,7},{4,0},{5,1},{6,2},{7,3},{8,12},{9,13},{10,... | collective-permute-start | bytes 393224 | tf_op jit(solution)/shard_map/ppermute | solution.py:31
  26.2 8.2 %collective-permute-start.3 = (f32[256,128]{1,0:T(8,128)S(1)}, f32[256,128]{1,0:T(8,128)S(1)}, u32[]{:S(2)}, u32[]{:S(2)}) collective-permute-start(f32[256,128]{1,0:T(8,128)S(1)} %add.207), channel_id=1, source_target_pairs={{0,8},{1,9},{2,10},{3,11},{4,12},{5,13},{6,14},{7,15},{8,0},{9,1},... | collective-permute-start | bytes 393224 | tf_op jit(solution)/shard_map/ppermute | solution.py:31
  35.1 5.0 %collective-permute-start.4 = (f32[256,128]{1,0:T(8,128)S(1)}, f32[256,128]{1,0:T(8,128)S(1)}, u32[]{:S(2)}, u32[]{:S(2)}) collective-permute-start(f32[256,128]{1,0:T(8,128)S(1)} %get-tuple-element.5), channel_id=1, source_target_pairs={{0,2},{1,3},{2,0},{3,1},{4,6},{5,7},{6,4},{7,5},{8,10},{9,11},{10,... | collective-permute-start | bytes 393224 | tf_op jit(solution)/shard_map/ppermute | solution.py:31
  36.4 5.1 %collective-permute-start.5 = (f32[256,128]{1,0:T(8,128)S(1)}, f32[256,128]{1,0:T(8,128)S(1)}, u32[]{:S(2)}, u32[]{:S(2)}) collective-permute-start(f32[256,128]{1,0:T(8,128)S(1)} %get-tuple-element.5), channel_id=1, source_target_pairs={{0,1},{1,0},{2,3},{3,2},{4,5},{5,4},{6,7},{7,6},{8,9},{9,8},{10,11... | collective-permute-start | bytes 393224 | tf_op jit(solution)/shard_map/ppermute | solution.py:31
  39.1 2.4 %copy-start.4 = (f32[1024,512]{1,0:T(8,128)S(1)}, f32[1024,512]{1,0:T(8,128)}, u32[]{:S(2)}) copy-start(f32[1024,512]{1,0:T(8,128)} %get-tuple-element.8) | copy-start | bytes 6291460
  40.0 2.0 %collective-permute-start.6 = (f32[256,128]{1,0:T(8,128)S(1)}, f32[256,128]{1,0:T(8,128)S(1)}, u32[]{:S(2)}, u32[]{:S(2)}) collective-permute-start(f32[256,128]{1,0:T(8,128)S(1)} %collective-permute-done.4), channel_id=1, source_target_pairs={{0,1},{1,0},{2,3},{3,2},{4,5},{5,4},{6,7},{7,6},{8,9},{9,8},{10,11... | collective-permute-start | bytes 393224 | tf_op jit(solution)/shard_map/ppermute | solution.py:31
  41.5 15.2 %copy-start.2 = (f32[1024,128]{1,0:T(8,128)S(1)}, f32[1024,128]{1,0:T(8,128)}, u32[]{:S(2)}) copy-start(f32[1024,128]{1,0:T(8,128)} %param.7) | copy-start | bytes 1572868
  42.0 14.8 %copy-start.6 = (s32[512]{0:T(512)S(1)}, s32[512]{0:T(512)}, u32[]{:S(2)}) copy-start(s32[512]{0:T(512)} %param.6) | copy-start | bytes 6148
  42.0 14.8 %copy-start.7 = (f32[512]{0:T(512)S(1)}, f32[512]{0:T(512)}, u32[]{:S(2)}) copy-start(f32[512]{0:T(512)} %param.9) | copy-start | bytes 6148
  44.4 12.2 %all-to-all-start = ((f32[16,2,128]{2,1,0:T(2,128)}), f32[16,2,128]{2,1,0:T(2,128)S(1)}, u32[]{:S(2)}, u32[]{:S(2)}) async-start(f32[16,2,128]{2,1,0:T(2,128)} %broadcast_select_fusion.1), calls=%async_computation | async-start | bytes 32768 | tf_op jit(solution)/shard_map/all_to_all | solution.py:75
  56.7 1.6 %copy-start.5 = (s32[1024,512]{1,0:T(8,128)S(1)}, s32[1024,512]{1,0:T(8,128)}, u32[]{:S(2)}) copy-start(s32[1024,512]{1,0:T(8,128)} %param.5) | copy-start | bytes 6291460
  63.6 1.6 %collective-permute-start.7 = (f32[512,128]{1,0:T(8,128)S(1)}, f32[512,128]{1,0:T(8,128)S(1)}, u32[]{:S(2)}, u32[]{:S(2)}) collective-permute-start(f32[512,128]{1,0:T(8,128)S(1)} %constant_dynamic-slice_fusion.1), channel_id=1, source_target_pairs={{0,1},{1,0},{2,3},{3,2},{4,5},{5,4},{6,7},{7,6},{8,9},{9,8},{10,11... | collective-permute-start | bytes 786440 | tf_op jit(solution)/shard_map/ppermute | solution.py:31
  65.3 5.6 %collective-permute-start.8 = (f32[256,128]{1,0:T(8,128)S(1)}, f32[256,128]{1,0:T(8,128)S(1)}, u32[]{:S(2)}, u32[]{:S(2)}) collective-permute-start(f32[256,128]{1,0:T(8,128)S(1)} %constant_dynamic-slice_fusion), channel_id=1, source_target_pairs={{0,2},{1,3},{2,0},{3,1},{4,6},{5,7},{6,4},{7,5},{8,10},{9,11},{10,... | collective-permute-start | bytes 393224 | tf_op jit(solution)/shard_map/ppermute | solution.py:31
  70.9 5.0 %collective-permute-start.9 = (f32[256,128]{1,0:T(8,128)S(1)}, f32[256,128]{1,0:T(8,128)S(1)}, u32[]{:S(2)}, u32[]{:S(2)}) collective-permute-start(f32[256,128]{1,0:T(8,128)S(1)} %dynamic-slice_add_fusion.2), channel_id=1, source_target_pairs={{0,4},{1,5},{2,6},{3,7},{4,0},{5,1},{6,2},{7,3},{8,12},{9,13},{10,... | collective-permute-start | bytes 393224 | tf_op jit(solution)/shard_map/ppermute | solution.py:31
  76.0 7.2 %collective-permute-start.10 = (f32[256,128]{1,0:T(8,128)S(1)}, f32[256,128]{1,0:T(8,128)S(1)}, u32[]{:S(2)}, u32[]{:S(2)}) collective-permute-start(f32[256,128]{1,0:T(8,128)S(1)} %add.230), channel_id=1, source_target_pairs={{0,8},{1,9},{2,10},{3,11},{4,12},{5,13},{6,14},{7,15},{8,0},{9,1},... | collective-permute-start | bytes 393224 | tf_op jit(solution)/shard_map/ppermute | solution.py:31
  83.8 5.0 %collective-permute-start.11 = (f32[256,128]{1,0:T(8,128)S(1)}, f32[256,128]{1,0:T(8,128)S(1)}, u32[]{:S(2)}, u32[]{:S(2)}) collective-permute-start(f32[256,128]{1,0:T(8,128)S(1)} %get-tuple-element.3), channel_id=1, source_target_pairs={{0,2},{1,3},{2,0},{3,1},{4,6},{5,7},{6,4},{7,5},{8,10},{9,11},{10,... | collective-permute-start | bytes 393224 | tf_op jit(solution)/shard_map/ppermute | solution.py:31
  84.8 4.8 %collective-permute-start.12 = (f32[256,128]{1,0:T(8,128)S(1)}, f32[256,128]{1,0:T(8,128)S(1)}, u32[]{:S(2)}, u32[]{:S(2)}) collective-permute-start(f32[256,128]{1,0:T(8,128)S(1)} %get-tuple-element.3), channel_id=1, source_target_pairs={{0,1},{1,0},{2,3},{3,2},{4,5},{5,4},{6,7},{7,6},{8,9},{9,8},{10,11... | collective-permute-start | bytes 393224 | tf_op jit(solution)/shard_map/ppermute | solution.py:31
  86.1 3.0 %copy-start.3 = (f32[1024,512]{1,0:T(8,128)S(1)}, f32[1024,512]{1,0:T(8,128)}, u32[]{:S(2)}) copy-start(f32[1024,512]{1,0:T(8,128)} %get-tuple-element.6) | copy-start | bytes 6291460
  90.4 1.4 %collective-permute-start.13 = (f32[256,128]{1,0:T(8,128)S(1)}, f32[256,128]{1,0:T(8,128)S(1)}, u32[]{:S(2)}, u32[]{:S(2)}) collective-permute-start(f32[256,128]{1,0:T(8,128)S(1)} %collective-permute-done.11), channel_id=1, source_target_pairs={{0,1},{1,0},{2,3},{3,2},{4,5},{5,4},{6,7},{7,6},{8,9},{9,8},{10,11... | collective-permute-start | bytes 393224 | tf_op jit(solution)/shard_map/ppermute | solution.py:31
  94.2 10.0 %all-to-all-start.1 = ((f32[16,2,128]{2,1,0:T(2,128)}), f32[16,2,128]{2,1,0:T(2,128)S(1)}, u32[]{:S(2)}, u32[]{:S(2)}) async-start(f32[16,2,128]{2,1,0:T(2,128)} %broadcast_select_fusion), calls=%async_computation.1 | async-start | bytes 32768 | tf_op jit(solution)/shard_map/all_to_all | solution.py:75

commit v14 on v13

--- a/solution.py
+++ b/solution.py
@@ -14,10 +14,8 @@
     return jnp.dot(left, right, precision=precision, preferred_element_type=jnp.float32)
 
 
-def local_terms(time_factor, user_block, base_block, count_block, start_block):
+def local_terms(time_factor, user_block, base_block, count_block, observed):
     linear = product(time_factor, user_block.T) + base_block[None, :]
-    time_bins = jnp.arange(time_factor.shape[0], dtype=jnp.int32)[:, None]
-    observed = time_bins >= start_block[None, :]
     decay = jnp.exp(-jnp.abs(linear))
     intensity = jnp.maximum(linear, 0.0) + jnp.log1p(decay) + background
     gate_value = jnp.where(linear >= 0, 1.0, decay) / (1.0 + decay)
@@ -25,6 +23,11 @@
     residual = jnp.where(observed, gate_value * (1.0 - count_block.astype(jnp.float32) * inverse), 0.0)
     curvature = jnp.where(observed, gate_value * gate_value * inverse, 0.0)
     return (residual, curvature)
+
+
+def observed_of(counts, first_bin):
+    time_bins = jnp.arange(counts.shape[0], dtype=jnp.int32)[:, None]
+    return time_bins >= first_bin[None, :]
 
 
 def exchange(value, n, distance):
@@ -81,8 +84,11 @@
     shard_rows = time_factor.shape[0] // n
     offset = lax.axis_index("user") * shard_rows
     mine_rows = time_factor
+    observed = observed_of(counts, first_bin)
     for sweep in range(SWEEPS):
-        residual, curvature = local_terms(time_factor, user_factor, user_base, counts, first_bin)
+        residual, curvature = local_terms(time_factor, user_factor, user_base, counts, observed)
+        if sweep + 1 < SWEEPS:
+            code = lax.optimization_barrier(jnp.where(observed, counts, -1).astype(jnp.int8))
         grad_user = product(residual.T, time_factor)
         grad_whole, pieces, time_norm = sum_over_users(product(residual, user_factor), n)
         user_norm = jnp.sum(grad_user * grad_user)
@@ -99,6 +105,7 @@
         user_factor = user_factor - relax_step * grad_user
         if sweep + 1 < SWEEPS:
             time_factor = time_factor - relax_step * grad_whole
+            counts, observed = code, code >= 0
         else:
             mine_rows = lax.dynamic_slice_in_dim(
                 time_factor - relax_step * grad_whole, offset, shard_rows, 0

time: 106 us -> 112 us (1.057)
  matrix products: 27.8 us -> 33.9 us
  waiting for transfers between devices: 43 us -> 41.5 us
  other arithmetic: 7.82 us -> 8.95 us
    dot_general x22, matrix products: 27.8 us -> 33.9 us  [product(): jnp.dot(left, right, precision=precision, preferred_element_type=jnp.floa...]
    unnamed x16 -> x20, local copies, waits for them, and re-layouts: 1.48 us -> 0.04 us
    ppermute x14, waiting for transfers between devices: 30.1 us -> 28.8 us  [exchange(): return lax.ppermute(value, 'user', [(i, i ^ distance) for i in range(n)])]
    convert_element_type x0 -> x1, other arithmetic: none -> 1.2 us  [body(): jnp.where(observed, counts, -1).astype(jnp.int8)]
  transfers between devices with their start and end apart: 16 -> 16, of which waited for: 12 -> 11; matrix products, arithmetic and copies ran while one was open for 12% -> 18% of each run, Pallas kernels for 0% -> 0%
where the time goes in v14:
time: 112 us; the launch traced here: 111 us
  waiting for transfers between devices  41.5 us (37%)
  matrix products  33.9 us (30%)
  starting transfers between devices  20.9 us (19%)
  other arithmetic  8.95 us (8%)
  between operations  3.69 us (3%)
  local copies, waits for them, and re-layouts  2.33 us (2%)
    dot_general x22, matrix products, product(): jnp.dot(left, right, precision=precision, preferred_element_type=jnp.floa...  33.9 us
    ppermute x14, waiting for transfers between devices, exchange(): return lax.ppermute(value, 'user', [(i, i ^ distance) for i in range(n)])  28.8 us
    all_to_all x2, waiting for transfers between devices, sum_rows(): spread = lax.all_to_all(spread, 'user', 0, 0, tiled=False)  12.7 us
    ppermute x14, starting transfers between devices, exchange(): return lax.ppermute(value, 'user', [(i, i ^ distance) for i in range(n)])  11.5 us
    all_to_all x2, starting transfers between devices, sum_rows(): spread = lax.all_to_all(spread, 'user', 0, 0, tiled=False)  9.4 us
    select_n x4, other arithmetic, sum_rows(): spread = jnp.where(row == k, v, spread)  2.66 us
  transfers between devices with their start and end apart: 16, of which 11 were waited for; matrix products, arithmetic and copies ran while one was open for 18% of the time, Pallas kernels for 0%

profile of v14, /device:TPU:0, one launch (start us, length us, event | category | flops | bytes accessed | tf_op | source)
XLA Modules:
  0.0 111.3 jit_solution(15449084596026056632)
XLA Ops:
  0.7 6.2 %multiply_select_fusion.3 = (f32[1024,512]{1,0:T(8,128)}, f32[1024,512]{1,0:T(8,128)S(1)}) fusion(s32[512]{0:T(512)} %param.6, f32[512]{0:T(512)} %param.9, s32[1024,512]{1,0:T(8,128)} %param.5, f32[1024,128]{1,0:T(8,128)} %param.7, f32[512,128]{1,0:T(8,128)} %param.8), kind=kOutput, calls=%fused_computation.7 | convolution fusion | flops 413138944 | bytes 7081984 | tf_op jit(solution)/shard_map/dot_general | solution.py:14
  6.9 1.8 %fusion.39 = f32[1024,128]{1,0:T(8,128)} fusion(f32[1024,512]{1,0:T(8,128)S(1)} %get-tuple-element.7, f32[512,128]{1,0:T(8,128)S(1)} %copy-done), kind=kOutput, calls=%fused_computation.101 | convolution fusion | flops 402653184 | bytes 2883584 | tf_op jit(solution)/shard_map/dot_general | solution.py:14
  8.7 1.1 %constant_dynamic-slice_fusion.3 = f32[512,128]{1,0:T(8,128)S(1)} fusion(f32[1024,128]{1,0:T(8,128)} %fusion.39, s32[]{:T(128)S(6)} %select_n.139), kind=kLoop, calls=%fused_computation.85 | loop fusion | bytes 524292 | tf_op jit(solution)/shard_map/dynamic_slice | solution.py:55
  9.8 0.5 collective-permute-start
  10.3 2.4 %multiply_reduce_fusion.1 = (f32[]{:T(128)}, f32[512,128]{1,0:T(8,128)S(1)}) fusion(f32[1024,512]{1,0:T(8,128)S(1)} %get-tuple-element.7, f32[1024,128]{1,0:T(8,128)S(1)} %copy-done.1), kind=kOutput, calls=%fused_computation.41 | convolution fusion | flops 402784256 | bytes 2883588 | tf_op jit(solution)/shard_map/dot_general | solution.py:14
  12.8 1.2 %select_convert_fusion = s8[1024,512]{1,0:T(32,128)(4,1)} fusion(s32[1024,512]{1,0:T(8,128)S(1)} %copy-done.3, s32[512]{0:T(512)S(1)} %copy-done.7), kind=kLoop, calls=%fused_computation.5 | loop fusion | flops 1572864 | bytes 2623488 | tf_op jit(solution)/shard_map/convert_element_type | solution.py:91
  14.0 0.4 fusion.19
  14.4 1.0 dynamic-slice_add_fusion.1
  15.4 2.6 %collective-permute-start.1 = (f32[256,128]{1,0:T(8,128)S(1)}, f32[256,128]{1,0:T(8,128)S(1)}, u32[]{:S(2)}, u32[]{:S(2)}) collective-permute-start(f32[256,128]{1,0:T(8,128)S(1)} %constant_dynamic-slice_fusion.2), channel_id=1, source_target_pairs={{0,2},{1,3},{2,0},{3,1},{4,6},{5,7},{6,4},{7,5},{8,10},{9,11},{10,... | collective-permute-start | bytes 393224 | tf_op jit(solution)/shard_map/ppermute | solution.py:34
  17.9 0.4 fusion.21
  18.3 3.8 %collective-permute-done.1 = f32[256,128]{1,0:T(8,128)S(1)} collective-permute-done((f32[256,128]{1,0:T(8,128)S(1)}, f32[256,128]{1,0:T(8,128)S(1)}, u32[]{:S(2)}, u32[]{:S(2)}) %collective-permute-start.1) | collective-permute-done | bytes 131104 | tf_op jit(solution)/shard_map/ppermute | solution.py:34
  22.1 1.9 %collective-permute-start.2 = (f32[256,128]{1,0:T(8,128)S(1)}, f32[256,128]{1,0:T(8,128)S(1)}, u32[]{:S(2)}, u32[]{:S(2)}) collective-permute-start(f32[256,128]{1,0:T(8,128)S(1)} %dynamic-slice_add_fusion.3), channel_id=1, source_target_pairs={{0,4},{1,5},{2,6},{3,7},{4,0},{5,1},{6,2},{7,3},{8,12},{9,13},{10,... | collective-permute-start | bytes 393224 | tf_op jit(solution)/shard_map/ppermute | solution.py:34
  24.0 0.4 fusion.17
  24.4 3.1 %collective-permute-done.2 = f32[256,128]{1,0:T(8,128)S(1)} collective-permute-done((f32[256,128]{1,0:T(8,128)S(1)}, f32[256,128]{1,0:T(8,128)S(1)}, u32[]{:S(2)}, u32[]{:S(2)}) %collective-permute-start.2) | collective-permute-done | bytes 131104 | tf_op jit(solution)/shard_map/ppermute | solution.py:34
  27.5 2.7 %collective-permute-start.3 = (f32[256,128]{1,0:T(8,128)S(1)}, f32[256,128]{1,0:T(8,128)S(1)}, u32[]{:S(2)}, u32[]{:S(2)}) collective-permute-start(f32[256,128]{1,0:T(8,128)S(1)} %add.207), channel_id=1, source_target_pairs={{0,8},{1,9},{2,10},{3,11},{4,12},{5,13},{6,14},{7,15},{8,0},{9,1},... | collective-permute-start | bytes 393224 | tf_op jit(solution)/shard_map/ppermute | solution.py:34
  30.2 0.4 fusion.15
  30.6 5.1 %collective-permute-done.3 = f32[256,128]{1,0:T(8,128)S(1)} collective-permute-done((f32[256,128]{1,0:T(8,128)S(1)}, f32[256,128]{1,0:T(8,128)S(1)}, u32[]{:S(2)}, u32[]{:S(2)}) %collective-permute-start.3) | collective-permute-done | bytes 131104 | tf_op jit(solution)/shard_map/ppermute | solution.py:34
  35.7 0.6 multiply_reduce_fusion.3
  36.4 1.3 %collective-permute-start.4 = (f32[256,128]{1,0:T(8,128)S(1)}, f32[256,128]{1,0:T(8,128)S(1)}, u32[]{:S(2)}, u32[]{:S(2)}) collective-permute-start(f32[256,128]{1,0:T(8,128)S(1)} %get-tuple-element.5), channel_id=1, source_target_pairs={{0,2},{1,3},{2,0},{3,1},{4,6},{5,7},{6,4},{7,5},{8,10},{9,11},{10,... | collective-permute-start | bytes 393224 | tf_op jit(solution)/shard_map/ppermute | solution.py:34
  37.7 0.0 collective-permute-start.5
  37.7 1.4 %fusion.7 = f32[512]{0:T(512)S(1)} fusion(f32[256,512]{1,0:T(8,128)S(1)} %fusion.21, f32[256,128]{1,0:T(8,128)S(1)} %get-tuple-element.5, f32[512,128]{1,0:T(8,128)S(1)} %copy-done, f32[1024,512]{1,0:T(8,128)} %get-tuple-element.6, s32[]{:T(128)S(6)} %select_n.136), kind=kOutput, calls=%fused_computation.35 | convolution fusion | flops 101187072 | bytes 1443844 | tf_op jit(solution)/shard_map/dot_general | solution.py:14
  40.5 0.8 collective-permute-done.4
  41.3 1.5 %fusion.6 = f32[512]{0:T(512)S(1)} fusion(f32[256,512]{1,0:T(8,128)S(1)} %fusion.19, f32[256,128]{1,0:T(8,128)S(1)} %collective-permute-done.4, f32[512,128]{1,0:T(8,128)S(1)} %copy-done, f32[1024,512]{1,0:T(8,128)} %get-tuple-element.6, s32[]{:T(128)S(6)} %select_n.142), kind=kOutput, calls=%fused_computation.33 | convolution fusion | flops 101187072 | bytes 1443844 | tf_op jit(solution)/shard_map/dot_general | solution.py:14
  42.8 1.3 %fusion.5 = f32[512]{0:T(512)S(1)} fusion(f32[256,512]{1,0:T(8,128)S(1)} %fusion.17, f32[256,128]{1,0:T(8,128)} %collective-permute-done.5, f32[512,128]{1,0:T(8,128)S(1)} %copy-done, f32[1024,512]{1,0:T(8,128)S(1)} %copy-done.5, s32[]{:T(128)S(6)} %select_n.143), kind=kOutput, calls=%fused_computation.31 | convolution fusion | flops 101187072 | bytes 1443844 | tf_op jit(solution)/shard_map/dot_general | solution.py:14
  44.2 0.9 constant_dynamic-update-slice_fusion.5
  45.1 0.0 copy-start.8
  45.1 0.4 fusion.4
  45.6 0.6 add_reduce_fusion.1
  46.2 1.3 %broadcast_select_fusion.1 = f32[16,2,128]{2,1,0:T(2,128)} fusion(pred[2]{0:T(512)(128)(4,1)S(1)} %iota_compare_fusion.1, f32[]{:T(128)} %add_reduce_fusion.1, f32[2]{0:T(128)S(1)} %compare_select_fusion.1), kind=kLoop, calls=%fused_computation.65 | loop fusion | flops 4096 | bytes 16398 | tf_op jit(solution)/shard_map/jit(_where)/select_n | solution.py:76
  47.5 5.9 %all-to-all-start = ((f32[16,2,128]{2,1,0:T(2,128)}), f32[16,2,128]{2,1,0:T(2,128)S(1)}, u32[]{:S(2)}, u32[]{:S(2)}) async-start(f32[16,2,128]{2,1,0:T(2,128)} %broadcast_select_fusion.1), calls=%async_computation | async-start | bytes 32768 | tf_op jit(solution)/shard_map/all_to_all | solution.py:78
  53.5 6.3 %all-to-all-done = f32[16,2,128]{2,1,0:T(2,128)S(1)} async-done(((f32[16,2,128]{2,1,0:T(2,128)}), f32[16,2,128]{2,1,0:T(2,128)S(1)}, u32[]{:S(2)}, u32[]{:S(2)}) %all-to-all-start) | async-done | bytes 16416 | tf_op jit(solution)/shard_map/all_to_all | solution.py:78
  59.8 0.1 multiply_subtract_fusion
  59.9 4.1 %multiply_select_fusion.1 = (f32[1024,512]{1,0:T(8,128)}, f32[1024,512]{1,0:T(8,128)S(1)}) fusion(s8[1024,512]{1,0:T(32,128)(4,1)S(1)} %copy-done.6, f32[512]{0:T(512)S(1)} %copy-done.8, f32[1024,128]{1,0:T(8,128)S(1)} %multiply_subtract_fusion, f32[512,128]{1,0:T(8,128)S(1)} %multiply_subtract_fusion.2), kind=kOutput, calls=%fused_computation.1 | convolution fusion | flops 410517504 | bytes 5507072 | tf_op jit(solution)/shard_map/dot_general | solution.py:14
  64.0 2.9 %fusion.9 = f32[1024,128]{1,0:T(8,128)S(1)} fusion(f32[512,128]{1,0:T(8,128)S(1)} %multiply_subtract_fusion.2, s8[1024,512]{1,0:T(32,128)(4,1)S(1)} %copy-done.6, f32[1024,512]{1,0:T(8,128)S(1)} %get-tuple-element.11, f32[512]{0:T(512)S(1)} %copy-done.8), kind=kOutput, calls=%fused_computation.44 | convolution fusion | flops 411566080 | bytes 3409920 | tf_op jit(solution)/shard_map/dot_general | solution.py:14
  67.0 0.1 collective-permute-start.7
  67.1 1.5 %collective-permute-done.7 = f32[512,128]{1,0:T(8,128)S(1)} collective-permute-done((f32[512,128]{1,0:T(8,128)S(1)}, f32[512,128]{1,0:T(8,128)S(1)}, u32[]{:S(2)}, u32[]{:S(2)}) %collective-permute-start.7) | collective-permute-done | bytes 262176 | tf_op jit(solution)/shard_map/ppermute | solution.py:34
  68.6 0.5 collective-permute-start.8
  69.2 5.1 %collective-permute-done.8 = f32[256,128]{1,0:T(8,128)S(1)} collective-permute-done((f32[256,128]{1,0:T(8,128)S(1)}, f32[256,128]{1,0:T(8,128)S(1)}, u32[]{:S(2)}, u32[]{:S(2)}) %collective-permute-start.8) | collective-permute-done | bytes 131104 | tf_op jit(solution)/shard_map/ppermute | solution.py:34
  74.3 0.5 collective-permute-start.9
  74.8 5.9 %multiply_reduce_fusion = (f32[]{:T(128)}, f32[512,128]{1,0:T(8,128)S(1)}) fusion(f32[1024,128]{1,0:T(8,128)S(1)} %multiply_subtract_fusion, s8[1024,512]{1,0:T(32,128)(4,1)S(1)} %copy-done.6, f32[1024,512]{1,0:T(8,128)} %copy-done.9, f32[512]{0:T(512)S(1)} %copy-done.8), kind=kOutput, calls=%fused_computation.38 | convolution fusion | flops 411697152 | bytes 3409924 | tf_op jit(solution)/shard_map/dot_general | solution.py:14
  80.6 0.0 collective-permute-done.9
  80.7 0.7 collective-permute-start.10
  81.4 0.4 fusion.10
  81.8 7.1 %collective-permute-done.10 = f32[256,128]{1,0:T(8,128)S(1)} collective-permute-done((f32[256,128]{1,0:T(8,128)S(1)}, f32[256,128]{1,0:T(8,128)S(1)}, u32[]{:S(2)}, u32[]{:S(2)}) %collective-permute-start.10) | collective-permute-done | bytes 131104 | tf_op jit(solution)/shard_map/ppermute | solution.py:34
  88.9 0.6 multiply_reduce_fusion.2
  89.5 0.6 collective-permute-start.11
  90.1 0.4 fusion.40
  90.5 0.1 collective-permute-start.12
  91.9 1.6 %fusion.3 = f32[512]{0:T(512)S(1)} fusion(f32[256,512]{1,0:T(8,128)S(1)} %fusion.40, f32[512,128]{1,0:T(8,128)S(1)} %get-tuple-element.13, f32[1024,512]{1,0:T(8,128)} %get-tuple-element.10, s32[]{:T(128)S(6)} %select_n.136, f32[1024,128]{1,0:T(8,128)S(1)} %multiply_subtract_fusion), kind=kOutput, calls=%fused_computation.27 | convolution fusion | flops 101187072 | bytes 1444864 | tf_op jit(solution)/shard_map/dot_general | solution.py:14
  93.6 0.9 collective-permute-done.11
  94.5 0.4 fusion.41
  94.9 0.4 fusion.2
  95.3 0.0 collective-permute-done.12
  95.3 0.4 fusion.42
  95.7 0.4 fusion.1
  96.1 0.1 collective-permute-start.13
  96.3 1.3 %collective-permute-done.13 = f32[256,128]{1,0:T(8,128)S(1)} collective-permute-done((f32[256,128]{1,0:T(8,128)S(1)}, f32[256,128]{1,0:T(8,128)S(1)}, u32[]{:S(2)}, u32[]{:S(2)}) %collective-permute-start.13) | collective-permute-done | bytes 131104 | tf_op jit(solution)/shard_map/ppermute | solution.py:34
  97.6 0.4 fusion
  98.0 0.6 add_reduce_fusion
  98.6 1.3 %broadcast_select_fusion = f32[16,2,128]{2,1,0:T(2,128)} fusion(pred[2]{0:T(512)(128)(4,1)S(1)} %iota_compare_fusion.1, f32[]{:T(128)} %add_reduce_fusion, f32[2]{0:T(128)S(1)} %compare_select_fusion), kind=kLoop, calls=%fused_computation.64 | loop fusion | flops 4096 | bytes 16398 | tf_op jit(solution)/shard_map/jit(_where)/select_n | solution.py:76
  99.9 3.5 %all-to-all-start.1 = ((f32[16,2,128]{2,1,0:T(2,128)}), f32[16,2,128]{2,1,0:T(2,128)S(1)}, u32[]{:S(2)}, u32[]{:S(2)}) async-start(f32[16,2,128]{2,1,0:T(2,128)} %broadcast_select_fusion), calls=%async_computation.1 | async-start | bytes 32768 | tf_op jit(solution)/shard_map/all_to_all | solution.py:78
  103.4 6.4 %all-to-all-done.1 = f32[16,2,128]{2,1,0:T(2,128)S(1)} async-done(((f32[16,2,128]{2,1,0:T(2,128)}), f32[16,2,128]{2,1,0:T(2,128)S(1)}, u32[]{:S(2)}, u32[]{:S(2)}) %all-to-all-start.1) | async-done | bytes 16416 | tf_op jit(solution)/shard_map/all_to_all | solution.py:78
  109.9 0.7 multiply_subtract_fusion.1
  110.7 0.6 dynamic-slice_subtract_fusion
  (48 shorter events, 0.5 us)
Async XLA Ops:
  0.6 6.2 %copy-start = (f32[512,128]{1,0:T(8,128)S(1)}, f32[512,128]{1,0:T(8,128)}, u32[]{:S(2)}) copy-start(f32[512,128]{1,0:T(8,128)} %param.8) | copy-start | bytes 786436
  6.9 3.5 %copy-start.1 = (f32[1024,128]{1,0:T(8,128)S(1)}, f32[1024,128]{1,0:T(8,128)}, u32[]{:S(2)}) copy-start(f32[1024,128]{1,0:T(8,128)} %param.7) | copy-start | bytes 1572868
  8.7 4.1 %copy-start.7 = (s32[512]{0:T(512)S(1)}, s32[512]{0:T(512)}, u32[]{:S(2)}) copy-start(s32[512]{0:T(512)} %param.6) | copy-start | bytes 6148
  8.7 4.1 %copy-start.3 = (s32[1024,512]{1,0:T(8,128)S(1)}, s32[1024,512]{1,0:T(8,128)}, u32[]{:S(2)}) copy-start(s32[1024,512]{1,0:T(8,128)} %param.5) | copy-start | bytes 6291460
  9.8 4.5 %collective-permute-start = (f32[512,128]{1,0:T(8,128)S(1)}, f32[512,128]{1,0:T(8,128)}, u32[]{:S(2)}, u32[]{:S(2)}) collective-permute-start(f32[512,128]{1,0:T(8,128)S(1)} %constant_dynamic-slice_fusion.3), channel_id=1, source_target_pairs={{0,1},{1,0},{2,3},{3,2},{4,5},{5,4},{6,7},{7,6},{8,9},{9,8},{10,11... | collective-permute-start | bytes 786440 | tf_op jit(solution)/shard_map/ppermute | solution.py:34
  12.8 1.6 %copy-start.4 = (f32[1024,128]{1,0:T(8,128)S(1)}, f32[1024,128]{1,0:T(8,128)}, u32[]{:S(2)}) copy-start(f32[1024,128]{1,0:T(8,128)} %fusion.39) | copy-start | bytes 1572868
  15.4 6.7 %collective-permute-start.1 = (f32[256,128]{1,0:T(8,128)S(1)}, f32[256,128]{1,0:T(8,128)S(1)}, u32[]{:S(2)}, u32[]{:S(2)}) collective-permute-start(f32[256,128]{1,0:T(8,128)S(1)} %constant_dynamic-slice_fusion.2), channel_id=1, source_target_pairs={{0,2},{1,3},{2,0},{3,1},{4,6},{5,7},{6,4},{7,5},{8,10},{9,11},{10,... | collective-permute-start | bytes 393224 | tf_op jit(solution)/shard_map/ppermute | solution.py:34
  22.1 5.4 %collective-permute-start.2 = (f32[256,128]{1,0:T(8,128)S(1)}, f32[256,128]{1,0:T(8,128)S(1)}, u32[]{:S(2)}, u32[]{:S(2)}) collective-permute-start(f32[256,128]{1,0:T(8,128)S(1)} %dynamic-slice_add_fusion.3), channel_id=1, source_target_pairs={{0,4},{1,5},{2,6},{3,7},{4,0},{5,1},{6,2},{7,3},{8,12},{9,13},{10,... | collective-permute-start | bytes 393224 | tf_op jit(solution)/shard_map/ppermute | solution.py:34
  27.5 8.2 %collective-permute-start.3 = (f32[256,128]{1,0:T(8,128)S(1)}, f32[256,128]{1,0:T(8,128)S(1)}, u32[]{:S(2)}, u32[]{:S(2)}) collective-permute-start(f32[256,128]{1,0:T(8,128)S(1)} %add.207), channel_id=1, source_target_pairs={{0,8},{1,9},{2,10},{3,11},{4,12},{5,13},{6,14},{7,15},{8,0},{9,1},... | collective-permute-start | bytes 393224 | tf_op jit(solution)/shard_map/ppermute | solution.py:34
  36.4 5.0 %collective-permute-start.4 = (f32[256,128]{1,0:T(8,128)S(1)}, f32[256,128]{1,0:T(8,128)S(1)}, u32[]{:S(2)}, u32[]{:S(2)}) collective-permute-start(f32[256,128]{1,0:T(8,128)S(1)} %get-tuple-element.5), channel_id=1, source_target_pairs={{0,2},{1,3},{2,0},{3,1},{4,6},{5,7},{6,4},{7,5},{8,10},{9,11},{10,... | collective-permute-start | bytes 393224 | tf_op jit(solution)/shard_map/ppermute | solution.py:34
  37.7 5.1 %collective-permute-start.5 = (f32[256,128]{1,0:T(8,128)S(1)}, f32[256,128]{1,0:T(8,128)}, u32[]{:S(2)}, u32[]{:S(2)}) collective-permute-start(f32[256,128]{1,0:T(8,128)S(1)} %get-tuple-element.5), channel_id=1, source_target_pairs={{0,1},{1,0},{2,3},{3,2},{4,5},{5,4},{6,7},{7,6},{8,9},{9,8},{10,11... | collective-permute-start | bytes 393224 | tf_op jit(solution)/shard_map/ppermute | solution.py:34
  40.4 2.4 %copy-start.5 = (f32[1024,512]{1,0:T(8,128)S(1)}, f32[1024,512]{1,0:T(8,128)}, u32[]{:S(2)}) copy-start(f32[1024,512]{1,0:T(8,128)} %get-tuple-element.6) | copy-start | bytes 6291460
  41.3 3.8 %collective-permute-start.6 = (f32[256,128]{1,0:T(8,128)S(1)}, f32[256,128]{1,0:T(8,128)S(1)}, u32[]{:S(2)}, u32[]{:S(2)}) collective-permute-start(f32[256,128]{1,0:T(8,128)S(1)} %collective-permute-done.4), channel_id=1, source_target_pairs={{0,1},{1,0},{2,3},{3,2},{4,5},{5,4},{6,7},{7,6},{8,9},{9,8},{10,11... | collective-permute-start | bytes 393224 | tf_op jit(solution)/shard_map/ppermute | solution.py:34
  45.1 14.8 %copy-start.6 = (s8[1024,512]{1,0:T(32,128)(4,1)S(1)}, s8[1024,512]{1,0:T(32,128)(4,1)}, u32[]{:S(2)}) copy-start(s8[1024,512]{1,0:T(32,128)(4,1)} %select_convert_fusion) | copy-start | bytes 1572868
  45.1 14.8 %copy-start.8 = (f32[512]{0:T(512)S(1)}, f32[512]{0:T(512)}, u32[]{:S(2)}) copy-start(f32[512]{0:T(512)} %param.9) | copy-start | bytes 6148
  47.5 12.2 %all-to-all-start = ((f32[16,2,128]{2,1,0:T(2,128)}), f32[16,2,128]{2,1,0:T(2,128)S(1)}, u32[]{:S(2)}, u32[]{:S(2)}) async-start(f32[16,2,128]{2,1,0:T(2,128)} %broadcast_select_fusion.1), calls=%async_computation | async-start | bytes 32768 | tf_op jit(solution)/shard_map/all_to_all | solution.py:78
  64.0 2.9 %copy-start.9 = (f32[1024,512]{1,0:T(8,128)}, f32[1024,512]{1,0:T(8,128)S(1)}, u32[]{:S(2)}) copy-start(f32[1024,512]{1,0:T(8,128)S(1)} %get-tuple-element.11) | copy-start | bytes 6291460
  67.0 1.6 %collective-permute-start.7 = (f32[512,128]{1,0:T(8,128)S(1)}, f32[512,128]{1,0:T(8,128)S(1)}, u32[]{:S(2)}, u32[]{:S(2)}) collective-permute-start(f32[512,128]{1,0:T(8,128)S(1)} %constant_dynamic-slice_fusion.1), channel_id=1, source_target_pairs={{0,1},{1,0},{2,3},{3,2},{4,5},{5,4},{6,7},{7,6},{8,9},{9,8},{10,11... | collective-permute-start | bytes 786440 | tf_op jit(solution)/shard_map/ppermute | solution.py:34
  68.6 5.6 %collective-permute-start.8 = (f32[256,128]{1,0:T(8,128)S(1)}, f32[256,128]{1,0:T(8,128)S(1)}, u32[]{:S(2)}, u32[]{:S(2)}) collective-permute-start(f32[256,128]{1,0:T(8,128)S(1)} %constant_dynamic-slice_fusion), channel_id=1, source_target_pairs={{0,2},{1,3},{2,0},{3,1},{4,6},{5,7},{6,4},{7,5},{8,10},{9,11},{10,... | collective-permute-start | bytes 393224 | tf_op jit(solution)/shard_map/ppermute | solution.py:34
  74.3 6.4 %collective-permute-start.9 = (f32[256,128]{1,0:T(8,128)S(1)}, f32[256,128]{1,0:T(8,128)S(1)}, u32[]{:S(2)}, u32[]{:S(2)}) collective-permute-start(f32[256,128]{1,0:T(8,128)S(1)} %dynamic-slice_add_fusion.2), channel_id=1, source_target_pairs={{0,4},{1,5},{2,6},{3,7},{4,0},{5,1},{6,2},{7,3},{8,12},{9,13},{10,... | collective-permute-start | bytes 393224 | tf_op jit(solution)/shard_map/ppermute | solution.py:34
  80.7 8.2 %collective-permute-start.10 = (f32[256,128]{1,0:T(8,128)S(1)}, f32[256,128]{1,0:T(8,128)S(1)}, u32[]{:S(2)}, u32[]{:S(2)}) collective-permute-start(f32[256,128]{1,0:T(8,128)S(1)} %add.230), channel_id=1, source_target_pairs={{0,8},{1,9},{2,10},{3,11},{4,12},{5,13},{6,14},{7,15},{8,0},{9,1},... | collective-permute-start | bytes 393224 | tf_op jit(solution)/shard_map/ppermute | solution.py:34
  89.5 5.0 %collective-permute-start.11 = (f32[256,128]{1,0:T(8,128)S(1)}, f32[256,128]{1,0:T(8,128)S(1)}, u32[]{:S(2)}, u32[]{:S(2)}) collective-permute-start(f32[256,128]{1,0:T(8,128)S(1)} %get-tuple-element.3), channel_id=1, source_target_pairs={{0,2},{1,3},{2,0},{3,1},{4,6},{5,7},{6,4},{7,5},{8,10},{9,11},{10,... | collective-permute-start | bytes 393224 | tf_op jit(solution)/shard_map/ppermute | solution.py:34
  90.5 4.8 %collective-permute-start.12 = (f32[256,128]{1,0:T(8,128)S(1)}, f32[256,128]{1,0:T(8,128)S(1)}, u32[]{:S(2)}, u32[]{:S(2)}) collective-permute-start(f32[256,128]{1,0:T(8,128)S(1)} %get-tuple-element.3), channel_id=1, source_target_pairs={{0,1},{1,0},{2,3},{3,2},{4,5},{5,4},{6,7},{7,6},{8,9},{9,8},{10,11... | collective-permute-start | bytes 393224 | tf_op jit(solution)/shard_map/ppermute | solution.py:34
  91.9 3.0 %copy-start.2 = (f32[1024,512]{1,0:T(8,128)S(1)}, f32[1024,512]{1,0:T(8,128)}, u32[]{:S(2)}) copy-start(f32[1024,512]{1,0:T(8,128)} %get-tuple-element.10) | copy-start | bytes 6291460
  96.1 1.4 %collective-permute-start.13 = (f32[256,128]{1,0:T(8,128)S(1)}, f32[256,128]{1,0:T(8,128)S(1)}, u32[]{:S(2)}, u32[]{:S(2)}) collective-permute-start(f32[256,128]{1,0:T(8,128)S(1)} %collective-permute-done.11), channel_id=1, source_target_pairs={{0,1},{1,0},{2,3},{3,2},{4,5},{5,4},{6,7},{7,6},{8,9},{9,8},{10,11... | collective-permute-start | bytes 393224 | tf_op jit(solution)/shard_map/ppermute | solution.py:34
  99.9 10.0 %all-to-all-start.1 = ((f32[16,2,128]{2,1,0:T(2,128)}), f32[16,2,128]{2,1,0:T(2,128)S(1)}, u32[]{:S(2)}, u32[]{:S(2)}) async-start(f32[16,2,128]{2,1,0:T(2,128)} %broadcast_select_fusion), calls=%async_computation.1 | async-start | bytes 32768 | tf_op jit(solution)/shard_map/all_to_all | solution.py:78

commit v15 on v13

--- a/solution.py
+++ b/solution.py
@@ -94,7 +94,9 @@
             )
             weight = lax.dynamic_slice_in_dim(curvature, first, rows, 0)
             bending = bending + jnp.sum(weight * tangent_image * tangent_image, axis=0)
-        norm_total, bend_total = sum_rows([user_norm + time_norm, jnp.sum(bending)], n)
+        lanes = jnp.sum(bending.reshape(-1, 128), axis=0)
+        norm_total, bend_lanes = sum_rows([user_norm + time_norm, lanes], n)
+        bend_total = jnp.sum(bend_lanes, axis=1, keepdims=True)
         relax_step = norm_total / (bend_total + damping * norm_total)
         user_factor = user_factor - relax_step * grad_user
         if sweep + 1 < SWEEPS:

time: 106 us -> 105 us (level)
  local copies, waits for them, and re-layouts: 2.71 us -> 1.44 us
    select_n x4, other arithmetic: 2.66 us -> 1.37 us  [sum_rows(): spread = jnp.where(row == k, v, spread)]
    unnamed x16, local copies, waits for them, and re-layouts: 1.48 us -> 0.2 us
where the time goes in v15:
time: 105 us; the launch traced here: 104 us
  waiting for transfers between devices  43 us (41%)
  matrix products  27.8 us (26%)
  starting transfers between devices  20.5 us (20%)
  other arithmetic  7.89 us (8%)
  between operations  3.7 us (4%)
  local copies, waits for them, and re-layouts  1.44 us (1%)
    ppermute x14, waiting for transfers between devices, exchange(): return lax.ppermute(value, 'user', [(i, i ^ distance) for i in range(n)])  30.1 us
    dot_general x22, matrix products, product(): jnp.dot(left, right, precision=precision, preferred_element_type=jnp.floa...  27.8 us
    all_to_all x2, waiting for transfers between devices, sum_rows(): spread = lax.all_to_all(spread, 'user', 0, 0, tiled=False)  12.9 us
    ppermute x14, starting transfers between devices, exchange(): return lax.ppermute(value, 'user', [(i, i ^ distance) for i in range(n)])  11.3 us
    all_to_all x2, starting transfers between devices, sum_rows(): spread = lax.all_to_all(spread, 'user', 0, 0, tiled=False)  9.21 us
  transfers between devices with their start and end apart: 16, of which 12 were waited for; matrix products, arithmetic and copies ran while one was open for 12% of the time, Pallas kernels for 0%

profile of v15, /device:TPU:0, one launch (start us, length us, event | category | flops | bytes accessed | tf_op | source)
XLA Modules:
  0.0 104.4 jit_solution(4027115040208483677)
XLA Ops:
  0.7 6.2 %multiply_select_fusion.3 = (f32[1024,512]{1,0:T(8,128)}, f32[1024,512]{1,0:T(8,128)S(1)}) fusion(s32[512]{0:T(512)} %param.6, f32[512]{0:T(512)} %param.9, s32[1024,512]{1,0:T(8,128)} %param.5, f32[1024,128]{1,0:T(8,128)} %param.7, f32[512,128]{1,0:T(8,128)} %param.8), kind=kOutput, calls=%fused_computation.6 | convolution fusion | flops 413138944 | bytes 7081984 | tf_op jit(solution)/shard_map/dot_general | solution.py:14
  6.9 1.8 %fusion.31 = f32[1024,128]{1,0:T(8,128)} fusion(f32[1024,512]{1,0:T(8,128)S(1)} %get-tuple-element.9, f32[512,128]{1,0:T(8,128)S(1)} %copy-done), kind=kOutput, calls=%fused_computation.94 | convolution fusion | flops 402653184 | bytes 2883584 | tf_op jit(solution)/shard_map/dot_general | solution.py:14
  8.7 1.0 constant_dynamic-slice_fusion.3
  9.6 0.5 collective-permute-start
  10.2 2.4 %multiply_reduce_fusion.1 = (f32[]{:T(128)}, f32[512,128]{1,0:T(8,128)S(1)}) fusion(f32[1024,512]{1,0:T(8,128)S(1)} %get-tuple-element.9, f32[1024,128]{1,0:T(8,128)S(1)} %copy-done.1), kind=kOutput, calls=%fused_computation.40 | convolution fusion | flops 402784256 | bytes 2883588 | tf_op jit(solution)/shard_map/dot_general | solution.py:14
  12.6 0.4 fusion.17
  13.0 1.1 %dynamic-slice_add_fusion.1 = f32[512,128]{1,0:T(8,128)S(1)} fusion(f32[512,128]{1,0:T(8,128)} %collective-permute-done, f32[1024,128]{1,0:T(8,128)} %fusion.31, s32[]{:T(128)S(6)} %select_n.135), kind=kLoop, calls=%fused_computation.41 | loop fusion | flops 65536 | bytes 786436 | tf_op jit(solution)/shard_map/add | solution.py:54
  14.1 2.6 %collective-permute-start.1 = (f32[256,128]{1,0:T(8,128)S(1)}, f32[256,128]{1,0:T(8,128)S(1)}, u32[]{:S(2)}, u32[]{:S(2)}) collective-permute-start(f32[256,128]{1,0:T(8,128)S(1)} %constant_dynamic-slice_fusion.2), channel_id=1, source_target_pairs={{0,2},{1,3},{2,0},{3,1},{4,6},{5,7},{6,4},{7,5},{8,10},{9,11},{10,... | collective-permute-start | bytes 393224 | tf_op jit(solution)/shard_map/ppermute | solution.py:31
  16.6 0.4 fusion.19
  17.0 3.8 %collective-permute-done.1 = f32[256,128]{1,0:T(8,128)S(1)} collective-permute-done((f32[256,128]{1,0:T(8,128)S(1)}, f32[256,128]{1,0:T(8,128)S(1)}, u32[]{:S(2)}, u32[]{:S(2)}) %collective-permute-start.1) | collective-permute-done | bytes 131104 | tf_op jit(solution)/shard_map/ppermute | solution.py:31
  20.8 1.9 %collective-permute-start.2 = (f32[256,128]{1,0:T(8,128)S(1)}, f32[256,128]{1,0:T(8,128)S(1)}, u32[]{:S(2)}, u32[]{:S(2)}) collective-permute-start(f32[256,128]{1,0:T(8,128)S(1)} %dynamic-slice_add_fusion.3), channel_id=1, source_target_pairs={{0,4},{1,5},{2,6},{3,7},{4,0},{5,1},{6,2},{7,3},{8,12},{9,13},{10,... | collective-permute-start | bytes 393224 | tf_op jit(solution)/shard_map/ppermute | solution.py:31
  22.7 0.4 fusion.15
  23.1 3.1 %collective-permute-done.2 = f32[256,128]{1,0:T(8,128)S(1)} collective-permute-done((f32[256,128]{1,0:T(8,128)S(1)}, f32[256,128]{1,0:T(8,128)S(1)}, u32[]{:S(2)}, u32[]{:S(2)}) %collective-permute-start.2) | collective-permute-done | bytes 131104 | tf_op jit(solution)/shard_map/ppermute | solution.py:31
  26.2 2.7 %collective-permute-start.3 = (f32[256,128]{1,0:T(8,128)S(1)}, f32[256,128]{1,0:T(8,128)S(1)}, u32[]{:S(2)}, u32[]{:S(2)}) collective-permute-start(f32[256,128]{1,0:T(8,128)S(1)} %add.233), channel_id=1, source_target_pairs={{0,8},{1,9},{2,10},{3,11},{4,12},{5,13},{6,14},{7,15},{8,0},{9,1},... | collective-permute-start | bytes 393224 | tf_op jit(solution)/shard_map/ppermute | solution.py:31
  28.9 0.4 fusion.13
  29.3 5.1 %collective-permute-done.3 = f32[256,128]{1,0:T(8,128)S(1)} collective-permute-done((f32[256,128]{1,0:T(8,128)S(1)}, f32[256,128]{1,0:T(8,128)S(1)}, u32[]{:S(2)}, u32[]{:S(2)}) %collective-permute-start.3) | collective-permute-done | bytes 131104 | tf_op jit(solution)/shard_map/ppermute | solution.py:31
  34.4 0.6 multiply_reduce_fusion.3
  35.1 1.3 %collective-permute-start.4 = (f32[256,128]{1,0:T(8,128)S(1)}, f32[256,128]{1,0:T(8,128)S(1)}, u32[]{:S(2)}, u32[]{:S(2)}) collective-permute-start(f32[256,128]{1,0:T(8,128)S(1)} %get-tuple-element.5), channel_id=1, source_target_pairs={{0,2},{1,3},{2,0},{3,1},{4,6},{5,7},{6,4},{7,5},{8,10},{9,11},{10,... | collective-permute-start | bytes 393224 | tf_op jit(solution)/shard_map/ppermute | solution.py:31
  36.4 1.5 %fusion.7 = f32[512]{0:T(512)S(1)} fusion(f32[256,512]{1,0:T(8,128)S(1)} %fusion.19, f32[256,128]{1,0:T(8,128)S(1)} %get-tuple-element.5, f32[512,128]{1,0:T(8,128)S(1)} %copy-done, f32[1024,512]{1,0:T(8,128)} %get-tuple-element.8, s32[]{:T(128)S(6)} %select_n.133), kind=kOutput, calls=%fused_computation.34 | convolution fusion | flops 101187072 | bytes 1443844 | tf_op jit(solution)/shard_map/dot_general | solution.py:14
  39.2 0.8 collective-permute-done.4
  40.0 1.5 %fusion.6 = f32[512]{0:T(512)S(1)} fusion(f32[256,512]{1,0:T(8,128)S(1)} %fusion.17, f32[256,128]{1,0:T(8,128)S(1)} %collective-permute-done.4, f32[512,128]{1,0:T(8,128)S(1)} %copy-done, f32[1024,512]{1,0:T(8,128)} %get-tuple-element.8, s32[]{:T(128)S(6)} %select_n.139), kind=kOutput, calls=%fused_computation.32 | convolution fusion | flops 101187072 | bytes 1443844 | tf_op jit(solution)/shard_map/dot_general | solution.py:14
  41.5 0.0 copy-start.2
  41.5 0.4 fusion.5
  42.0 0.0 copy-start.6
  42.0 0.4 fusion.4
  42.5 0.7 broadcast_select_fusion.1
  43.2 5.7 %all-to-all-start = ((f32[16,2,128]{2,1,0:T(2,128)}), f32[16,2,128]{2,1,0:T(2,128)S(1)}, u32[]{:S(2)}, u32[]{:S(2)}) async-start(f32[16,2,128]{2,1,0:T(2,128)} %broadcast_select_fusion.1), calls=%async_computation | async-start | bytes 32768 | tf_op jit(solution)/shard_map/all_to_all | solution.py:75
  48.9 6.5 %all-to-all-done = f32[16,2,128]{2,1,0:T(2,128)S(1)} async-done(((f32[16,2,128]{2,1,0:T(2,128)}), f32[16,2,128]{2,1,0:T(2,128)S(1)}, u32[]{:S(2)}, u32[]{:S(2)}) %all-to-all-start) | async-done | bytes 16416 | tf_op jit(solution)/shard_map/all_to_all | solution.py:75
  55.4 0.6 slice_reduce_fusion.1
  56.0 0.7 fusion.30
  56.8 0.1 multiply_subtract_fusion
  56.9 0.2 copy-done.5
  57.0 4.3 %multiply_select_fusion.1 = (f32[1024,512]{1,0:T(8,128)}, f32[1024,512]{1,0:T(8,128)S(1)}) fusion(s32[512]{0:T(512)S(1)} %copy-done.6, f32[512]{0:T(512)S(1)} %copy-done.7, s32[1024,512]{1,0:T(8,128)S(1)} %copy-done.5, f32[1024,128]{1,0:T(8,128)S(1)} %multiply_subtract_fusion, f32[512,128]{1,0:T(8,128)S(1)} %multiply_subtract_fusion.2), kind=kOutput, calls=%fused_computation.1 | convolution fusion | flops 413138944 | bytes 7081984 | tf_op jit(solution)/shard_map/dot_general | solution.py:14
  61.4 1.0 fusion.32
  62.4 0.1 collective-permute-start.7
  62.5 1.5 %collective-permute-done.7 = f32[512,128]{1,0:T(8,128)S(1)} collective-permute-done((f32[512,128]{1,0:T(8,128)S(1)}, f32[512,128]{1,0:T(8,128)S(1)}, u32[]{:S(2)}, u32[]{:S(2)}) %collective-permute-start.7) | collective-permute-done | bytes 262176 | tf_op jit(solution)/shard_map/ppermute | solution.py:31
  64.0 0.5 collective-permute-start.8
  64.6 5.1 %collective-permute-done.8 = f32[256,128]{1,0:T(8,128)S(1)} collective-permute-done((f32[256,128]{1,0:T(8,128)S(1)}, f32[256,128]{1,0:T(8,128)S(1)}, u32[]{:S(2)}, u32[]{:S(2)}) %collective-permute-start.8) | collective-permute-done | bytes 131104 | tf_op jit(solution)/shard_map/ppermute | solution.py:31
  69.7 0.5 collective-permute-start.9
  70.2 2.4 %multiply_reduce_fusion = (f32[]{:T(128)}, f32[512,128]{1,0:T(8,128)S(1)}) fusion(f32[1024,512]{1,0:T(8,128)S(1)} %get-tuple-element.7, f32[1024,128]{1,0:T(8,128)S(1)} %multiply_subtract_fusion), kind=kOutput, calls=%fused_computation.37 | convolution fusion | flops 402784256 | bytes 2883588 | tf_op jit(solution)/shard_map/dot_general | solution.py:14
  72.6 2.1 %collective-permute-done.9 = f32[256,128]{1,0:T(8,128)S(1)} collective-permute-done((f32[256,128]{1,0:T(8,128)S(1)}, f32[256,128]{1,0:T(8,128)S(1)}, u32[]{:S(2)}, u32[]{:S(2)}) %collective-permute-start.9) | collective-permute-done | bytes 131104 | tf_op jit(solution)/shard_map/ppermute | solution.py:31
  74.7 0.5 collective-permute-start.10
  75.3 0.4 fusion.8
  75.7 6.3 %collective-permute-done.10 = f32[256,128]{1,0:T(8,128)S(1)} collective-permute-done((f32[256,128]{1,0:T(8,128)S(1)}, f32[256,128]{1,0:T(8,128)S(1)}, u32[]{:S(2)}, u32[]{:S(2)}) %collective-permute-start.10) | collective-permute-done | bytes 131104 | tf_op jit(solution)/shard_map/ppermute | solution.py:31
  81.9 0.6 multiply_reduce_fusion.2
  82.6 0.6 collective-permute-start.11
  83.1 0.4 fusion.33
  83.5 0.1 collective-permute-start.12
  84.9 1.6 %fusion.3 = f32[512]{0:T(512)S(1)} fusion(f32[256,512]{1,0:T(8,128)S(1)} %fusion.33, f32[512,128]{1,0:T(8,128)S(1)} %get-tuple-element.13, f32[1024,512]{1,0:T(8,128)} %get-tuple-element.6, s32[]{:T(128)S(6)} %select_n.133, f32[1024,128]{1,0:T(8,128)S(1)} %multiply_subtract_fusion), kind=kOutput, calls=%fused_computation.26 | convolution fusion | flops 101187072 | bytes 1444864 | tf_op jit(solution)/shard_map/dot_general | solution.py:14
  86.6 0.9 collective-permute-done.11
  87.5 0.4 fusion.34
  87.9 0.4 fusion.2
  88.4 0.4 fusion.35
  88.8 0.4 fusion.1
  89.2 0.1 collective-permute-start.13
  89.3 1.3 %collective-permute-done.13 = f32[256,128]{1,0:T(8,128)S(1)} collective-permute-done((f32[256,128]{1,0:T(8,128)S(1)}, f32[256,128]{1,0:T(8,128)S(1)}, u32[]{:S(2)}, u32[]{:S(2)}) %collective-permute-start.13) | collective-permute-done | bytes 131104 | tf_op jit(solution)/shard_map/ppermute | solution.py:31
  90.6 0.4 fusion
  91.1 0.7 broadcast_select_fusion
  91.8 3.5 %all-to-all-start.1 = ((f32[16,2,128]{2,1,0:T(2,128)}), f32[16,2,128]{2,1,0:T(2,128)S(1)}, u32[]{:S(2)}, u32[]{:S(2)}) async-start(f32[16,2,128]{2,1,0:T(2,128)} %broadcast_select_fusion), calls=%async_computation.1 | async-start | bytes 32768 | tf_op jit(solution)/shard_map/all_to_all | solution.py:75
  95.3 6.4 %all-to-all-done.1 = f32[16,2,128]{2,1,0:T(2,128)S(1)} async-done(((f32[16,2,128]{2,1,0:T(2,128)}), f32[16,2,128]{2,1,0:T(2,128)S(1)}, u32[]{:S(2)}, u32[]{:S(2)}) %all-to-all-start.1) | async-done | bytes 16416 | tf_op jit(solution)/shard_map/all_to_all | solution.py:75
  101.8 0.6 slice_reduce_fusion
  102.4 0.7 fusion.29
  103.0 0.7 multiply_subtract_fusion.1
  103.7 0.6 dynamic-slice_subtract_fusion
  (45 shorter events, 0.6 us)
Async XLA Ops:
  0.6 6.2 %copy-start = (f32[512,128]{1,0:T(8,128)S(1)}, f32[512,128]{1,0:T(8,128)}, u32[]{:S(2)}) copy-start(f32[512,128]{1,0:T(8,128)} %param.8) | copy-start | bytes 786436
  6.9 3.3 %copy-start.1 = (f32[1024,128]{1,0:T(8,128)S(1)}, f32[1024,128]{1,0:T(8,128)}, u32[]{:S(2)}) copy-start(f32[1024,128]{1,0:T(8,128)} %param.7) | copy-start | bytes 1572868
  9.6 3.3 %collective-permute-start = (f32[512,128]{1,0:T(8,128)S(1)}, f32[512,128]{1,0:T(8,128)}, u32[]{:S(2)}, u32[]{:S(2)}) collective-permute-start(f32[512,128]{1,0:T(8,128)S(1)} %constant_dynamic-slice_fusion.3), channel_id=1, source_target_pairs={{0,1},{1,0},{2,3},{3,2},{4,5},{5,4},{6,7},{7,6},{8,9},{9,8},{10,11... | collective-permute-start | bytes 786440 | tf_op jit(solution)/shard_map/ppermute | solution.py:31
  14.1 6.7 %collective-permute-start.1 = (f32[256,128]{1,0:T(8,128)S(1)}, f32[256,128]{1,0:T(8,128)S(1)}, u32[]{:S(2)}, u32[]{:S(2)}) collective-permute-start(f32[256,128]{1,0:T(8,128)S(1)} %constant_dynamic-slice_fusion.2), channel_id=1, source_target_pairs={{0,2},{1,3},{2,0},{3,1},{4,6},{5,7},{6,4},{7,5},{8,10},{9,11},{10,... | collective-permute-start | bytes 393224 | tf_op jit(solution)/shard_map/ppermute | solution.py:31
  20.8 5.4 %collective-permute-start.2 = (f32[256,128]{1,0:T(8,128)S(1)}, f32[256,128]{1,0:T(8,128)S(1)}, u32[]{:S(2)}, u32[]{:S(2)}) collective-permute-start(f32[256,128]{1,0:T(8,128)S(1)} %dynamic-slice_add_fusion.3), channel_id=1, source_target_pairs={{0,4},{1,5},{2,6},{3,7},{4,0},{5,1},{6,2},{7,3},{8,12},{9,13},{10,... | collective-permute-start | bytes 393224 | tf_op jit(solution)/shard_map/ppermute | solution.py:31
  26.2 8.2 %collective-permute-start.3 = (f32[256,128]{1,0:T(8,128)S(1)}, f32[256,128]{1,0:T(8,128)S(1)}, u32[]{:S(2)}, u32[]{:S(2)}) collective-permute-start(f32[256,128]{1,0:T(8,128)S(1)} %add.233), channel_id=1, source_target_pairs={{0,8},{1,9},{2,10},{3,11},{4,12},{5,13},{6,14},{7,15},{8,0},{9,1},... | collective-permute-start | bytes 393224 | tf_op jit(solution)/shard_map/ppermute | solution.py:31
  35.1 5.0 %collective-permute-start.4 = (f32[256,128]{1,0:T(8,128)S(1)}, f32[256,128]{1,0:T(8,128)S(1)}, u32[]{:S(2)}, u32[]{:S(2)}) collective-permute-start(f32[256,128]{1,0:T(8,128)S(1)} %get-tuple-element.5), channel_id=1, source_target_pairs={{0,2},{1,3},{2,0},{3,1},{4,6},{5,7},{6,4},{7,5},{8,10},{9,11},{10,... | collective-permute-start | bytes 393224 | tf_op jit(solution)/shard_map/ppermute | solution.py:31
  36.4 5.1 %collective-permute-start.5 = (f32[256,128]{1,0:T(8,128)S(1)}, f32[256,128]{1,0:T(8,128)S(1)}, u32[]{:S(2)}, u32[]{:S(2)}) collective-permute-start(f32[256,128]{1,0:T(8,128)S(1)} %get-tuple-element.5), channel_id=1, source_target_pairs={{0,1},{1,0},{2,3},{3,2},{4,5},{5,4},{6,7},{7,6},{8,9},{9,8},{10,11... | collective-permute-start | bytes 393224 | tf_op jit(solution)/shard_map/ppermute | solution.py:31
  39.1 2.4 %copy-start.4 = (f32[1024,512]{1,0:T(8,128)S(1)}, f32[1024,512]{1,0:T(8,128)}, u32[]{:S(2)}) copy-start(f32[1024,512]{1,0:T(8,128)} %get-tuple-element.8) | copy-start | bytes 6291460
  40.0 2.0 %collective-permute-start.6 = (f32[256,128]{1,0:T(8,128)S(1)}, f32[256,128]{1,0:T(8,128)S(1)}, u32[]{:S(2)}, u32[]{:S(2)}) collective-permute-start(f32[256,128]{1,0:T(8,128)S(1)} %collective-permute-done.4), channel_id=1, source_target_pairs={{0,1},{1,0},{2,3},{3,2},{4,5},{5,4},{6,7},{7,6},{8,9},{9,8},{10,11... | collective-permute-start | bytes 393224 | tf_op jit(solution)/shard_map/ppermute | solution.py:31
  41.5 15.3 %copy-start.2 = (f32[1024,128]{1,0:T(8,128)S(1)}, f32[1024,128]{1,0:T(8,128)}, u32[]{:S(2)}) copy-start(f32[1024,128]{1,0:T(8,128)} %param.7) | copy-start | bytes 1572868
  42.0 14.8 %copy-start.6 = (s32[512]{0:T(512)S(1)}, s32[512]{0:T(512)}, u32[]{:S(2)}) copy-start(s32[512]{0:T(512)} %param.6) | copy-start | bytes 6148
  42.0 14.8 %copy-start.7 = (f32[512]{0:T(512)S(1)}, f32[512]{0:T(512)}, u32[]{:S(2)}) copy-start(f32[512]{0:T(512)} %param.9) | copy-start | bytes 6148
  43.2 12.2 %all-to-all-start = ((f32[16,2,128]{2,1,0:T(2,128)}), f32[16,2,128]{2,1,0:T(2,128)S(1)}, u32[]{:S(2)}, u32[]{:S(2)}) async-start(f32[16,2,128]{2,1,0:T(2,128)} %broadcast_select_fusion.1), calls=%async_computation | async-start | bytes 32768 | tf_op jit(solution)/shard_map/all_to_all | solution.py:75
  55.4 1.6 %copy-start.5 = (s32[1024,512]{1,0:T(8,128)S(1)}, s32[1024,512]{1,0:T(8,128)}, u32[]{:S(2)}) copy-start(s32[1024,512]{1,0:T(8,128)} %param.5) | copy-start | bytes 6291460
  62.4 1.6 %collective-permute-start.7 = (f32[512,128]{1,0:T(8,128)S(1)}, f32[512,128]{1,0:T(8,128)S(1)}, u32[]{:S(2)}, u32[]{:S(2)}) collective-permute-start(f32[512,128]{1,0:T(8,128)S(1)} %constant_dynamic-slice_fusion.1), channel_id=1, source_target_pairs={{0,1},{1,0},{2,3},{3,2},{4,5},{5,4},{6,7},{7,6},{8,9},{9,8},{10,11... | collective-permute-start | bytes 786440 | tf_op jit(solution)/shard_map/ppermute | solution.py:31
  64.0 5.6 %collective-permute-start.8 = (f32[256,128]{1,0:T(8,128)S(1)}, f32[256,128]{1,0:T(8,128)S(1)}, u32[]{:S(2)}, u32[]{:S(2)}) collective-permute-start(f32[256,128]{1,0:T(8,128)S(1)} %constant_dynamic-slice_fusion), channel_id=1, source_target_pairs={{0,2},{1,3},{2,0},{3,1},{4,6},{5,7},{6,4},{7,5},{8,10},{9,11},{10,... | collective-permute-start | bytes 393224 | tf_op jit(solution)/shard_map/ppermute | solution.py:31
  69.7 5.0 %collective-permute-start.9 = (f32[256,128]{1,0:T(8,128)S(1)}, f32[256,128]{1,0:T(8,128)S(1)}, u32[]{:S(2)}, u32[]{:S(2)}) collective-permute-start(f32[256,128]{1,0:T(8,128)S(1)} %dynamic-slice_add_fusion.2), channel_id=1, source_target_pairs={{0,4},{1,5},{2,6},{3,7},{4,0},{5,1},{6,2},{7,3},{8,12},{9,13},{10,... | collective-permute-start | bytes 393224 | tf_op jit(solution)/shard_map/ppermute | solution.py:31
  74.7 7.2 %collective-permute-start.10 = (f32[256,128]{1,0:T(8,128)S(1)}, f32[256,128]{1,0:T(8,128)S(1)}, u32[]{:S(2)}, u32[]{:S(2)}) collective-permute-start(f32[256,128]{1,0:T(8,128)S(1)} %add.258), channel_id=1, source_target_pairs={{0,8},{1,9},{2,10},{3,11},{4,12},{5,13},{6,14},{7,15},{8,0},{9,1},... | collective-permute-start | bytes 393224 | tf_op jit(solution)/shard_map/ppermute | solution.py:31
  82.6 5.0 %collective-permute-start.11 = (f32[256,128]{1,0:T(8,128)S(1)}, f32[256,128]{1,0:T(8,128)S(1)}, u32[]{:S(2)}, u32[]{:S(2)}) collective-permute-start(f32[256,128]{1,0:T(8,128)S(1)} %get-tuple-element.3), channel_id=1, source_target_pairs={{0,2},{1,3},{2,0},{3,1},{4,6},{5,7},{6,4},{7,5},{8,10},{9,11},{10,... | collective-permute-start | bytes 393224 | tf_op jit(solution)/shard_map/ppermute | solution.py:31
  83.5 4.8 %collective-permute-start.12 = (f32[256,128]{1,0:T(8,128)S(1)}, f32[256,128]{1,0:T(8,128)S(1)}, u32[]{:S(2)}, u32[]{:S(2)}) collective-permute-start(f32[256,128]{1,0:T(8,128)S(1)} %get-tuple-element.3), channel_id=1, source_target_pairs={{0,1},{1,0},{2,3},{3,2},{4,5},{5,4},{6,7},{7,6},{8,9},{9,8},{10,11... | collective-permute-start | bytes 393224 | tf_op jit(solution)/shard_map/ppermute | solution.py:31
  84.9 3.0 %copy-start.3 = (f32[1024,512]{1,0:T(8,128)S(1)}, f32[1024,512]{1,0:T(8,128)}, u32[]{:S(2)}) copy-start(f32[1024,512]{1,0:T(8,128)} %get-tuple-element.6) | copy-start | bytes 6291460
  89.2 1.4 %collective-permute-start.13 = (f32[256,128]{1,0:T(8,128)S(1)}, f32[256,128]{1,0:T(8,128)S(1)}, u32[]{:S(2)}, u32[]{:S(2)}) collective-permute-start(f32[256,128]{1,0:T(8,128)S(1)} %collective-permute-done.11), channel_id=1, source_target_pairs={{0,1},{1,0},{2,3},{3,2},{4,5},{5,4},{6,7},{7,6},{8,9},{9,8},{10,11... | collective-permute-start | bytes 393224 | tf_op jit(solution)/shard_map/ppermute | solution.py:31
  91.8 10.0 %all-to-all-start.1 = ((f32[16,2,128]{2,1,0:T(2,128)}), f32[16,2,128]{2,1,0:T(2,128)S(1)}, u32[]{:S(2)}, u32[]{:S(2)}) async-start(f32[16,2,128]{2,1,0:T(2,128)} %broadcast_select_fusion), calls=%async_computation.1 | async-start | bytes 32768 | tf_op jit(solution)/shard_map/all_to_all | solution.py:75

commit v16 on v15

--- a/solution.py
+++ b/solution.py
@@ -56,10 +56,13 @@
         block = block + exchange(block, n, d)
     share = jnp.where(me < 4, jnp.sum(block * block), 0.0)
     pieces = [(block, offset)]
+    rows = block.shape[0]
     for level in reversed(range(len(halving))):
         d = halving[level]
         shift = (1 - 2 * ((me // d) % 2)) * (partial.shape[0] >> (level + 1))
-        pieces = pieces + [(exchange(piece, n, d), first + shift) for piece, first in pieces]
+        held = jnp.concatenate([piece for piece, _ in pieces]) if len(pieces) > 1 else pieces[0][0]
+        got = exchange(held, n, d)
+        pieces = pieces + [(got[k * rows:(k + 1) * rows], first + shift) for k, (_, first) in enumerate(pieces)]
     block = jnp.zeros_like(partial)
     for piece, first in pieces:
         block = lax.dynamic_update_slice_in_dim(block, piece, first, 0)

time: 105 us -> 107 us (1.019)
  local copies, waits for them, and re-layouts: 1.44 us -> 4.81 us
  waiting for transfers between devices: 43 us -> 40.6 us
    dynamic_update_slice x8, local copies, waits for them, and re-layouts: 0.13 us -> 2.7 us  [sum_over_users(): block = lax.dynamic_update_slice_in_dim(block, piece, first, 0)]
    all_to_all x2, waiting for transfers between devices: 12.9 us -> 11.6 us  [sum_rows(): spread = lax.all_to_all(spread, 'user', 0, 0, tiled=False)]
    ppermute x14 -> x12, waiting for transfers between devices: 30.1 us -> 29 us  [exchange(): return lax.ppermute(value, 'user', [(i, i ^ distance) for i in range(n)])]
    ppermute x14 -> x12, starting transfers between devices: 11.3 us -> 11.4 us  [exchange(): return lax.ppermute(value, 'user', [(i, i ^ distance) for i in range(n)])]
  transfers between devices with their start and end apart: 16 -> 14, of which waited for: 12 -> 10; matrix products, arithmetic and copies ran while one was open for 12% -> 15% of each run, Pallas kernels for 0% -> 0%
where the time goes in v16:
time: 107 us; the launch traced here: 106 us
  waiting for transfers between devices  40.6 us (38%)
  matrix products  27.8 us (26%)
  starting transfers between devices  20.6 us (19%)
  other arithmetic  8.68 us (8%)
  local copies, waits for them, and re-layouts  4.81 us (4%)
  between operations  3.64 us (3%)
    ppermute x12, waiting for transfers between devices, exchange(): return lax.ppermute(value, 'user', [(i, i ^ distance) for i in range(n)])  29 us
    dot_general x22, matrix products, product(): jnp.dot(left, right, precision=precision, preferred_element_type=jnp.floa...  27.8 us
    all_to_all x2, waiting for transfers between devices, sum_rows(): spread = lax.all_to_all(spread, 'user', 0, 0, tiled=False)  11.6 us
    ppermute x12, starting transfers between devices, exchange(): return lax.ppermute(value, 'user', [(i, i ^ distance) for i in range(n)])  11.4 us
    all_to_all x2, starting transfers between devices, sum_rows(): spread = lax.all_to_all(spread, 'user', 0, 0, tiled=False)  9.18 us
    dynamic_update_slice x8, local copies, waits for them, and re-layouts, sum_over_users(): block = lax.dynamic_update_slice_in_dim(block, piece, first, 0)  2.7 us
  transfers between devices with their start and end apart: 14, of which 10 were waited for; matrix products, arithmetic and copies ran while one was open for 15% of the time, Pallas kernels for 0%

profile of v16, /device:TPU:0, one launch (start us, length us, event | category | flops | bytes accessed | tf_op | source)
XLA Modules:
  0.0 106.1 jit_solution(11842735879485780468)
XLA Ops:
  0.7 6.2 %multiply_select_fusion.3 = (f32[1024,512]{1,0:T(8,128)}, f32[1024,512]{1,0:T(8,128)S(1)}) fusion(s32[512]{0:T(512)} %param.6, f32[512]{0:T(512)} %param.9, s32[1024,512]{1,0:T(8,128)} %param.5, f32[1024,128]{1,0:T(8,128)} %param.7, f32[512,128]{1,0:T(8,128)} %param.8), kind=kOutput, calls=%fused_computation.6 | convolution fusion | flops 413138944 | bytes 7081984 | tf_op jit(solution)/shard_map/dot_general | solution.py:14
  6.9 1.8 %fusion.38 = f32[1024,128]{1,0:T(8,128)} fusion(f32[1024,512]{1,0:T(8,128)S(1)} %get-tuple-element.9, f32[512,128]{1,0:T(8,128)S(1)} %copy-done), kind=kOutput, calls=%fused_computation.103 | convolution fusion | flops 402653184 | bytes 2883584 | tf_op jit(solution)/shard_map/dot_general | solution.py:14
  8.7 1.0 constant_dynamic-slice_fusion.3
  9.6 0.5 collective-permute-start
  10.2 2.4 %multiply_reduce_fusion.1 = (f32[]{:T(128)}, f32[512,128]{1,0:T(8,128)S(1)}) fusion(f32[1024,512]{1,0:T(8,128)S(1)} %get-tuple-element.9, f32[1024,128]{1,0:T(8,128)S(1)} %copy-done.1), kind=kOutput, calls=%fused_computation.42 | convolution fusion | flops 402784256 | bytes 2883588 | tf_op jit(solution)/shard_map/dot_general | solution.py:14
  12.6 0.4 fusion.20
  13.0 1.1 %dynamic-slice_add_fusion.1 = f32[512,128]{1,0:T(8,128)S(1)} fusion(f32[512,128]{1,0:T(8,128)} %collective-permute-done, f32[1024,128]{1,0:T(8,128)} %fusion.38, s32[]{:T(128)S(6)} %select_n.135), kind=kLoop, calls=%fused_computation.43 | loop fusion | flops 65536 | bytes 786436 | tf_op jit(solution)/shard_map/add | solution.py:54
  14.1 2.6 %collective-permute-start.1 = (f32[256,128]{1,0:T(8,128)S(1)}, f32[256,128]{1,0:T(8,128)S(1)}, u32[]{:S(2)}, u32[]{:S(2)}) collective-permute-start(f32[256,128]{1,0:T(8,128)S(1)} %constant_dynamic-slice_fusion.2), channel_id=1, source_target_pairs={{0,2},{1,3},{2,0},{3,1},{4,6},{5,7},{6,4},{7,5},{8,10},{9,11},{10,... | collective-permute-start | bytes 393224 | tf_op jit(solution)/shard_map/ppermute | solution.py:31
  16.6 0.4 fusion.22
  17.0 3.8 %collective-permute-done.1 = f32[256,128]{1,0:T(8,128)S(1)} collective-permute-done((f32[256,128]{1,0:T(8,128)S(1)}, f32[256,128]{1,0:T(8,128)S(1)}, u32[]{:S(2)}, u32[]{:S(2)}) %collective-permute-start.1) | collective-permute-done | bytes 131104 | tf_op jit(solution)/shard_map/ppermute | solution.py:31
  20.8 1.9 %collective-permute-start.2 = (f32[256,128]{1,0:T(8,128)S(1)}, f32[256,128]{1,0:T(8,128)S(1)}, u32[]{:S(2)}, u32[]{:S(2)}) collective-permute-start(f32[256,128]{1,0:T(8,128)S(1)} %dynamic-slice_add_fusion.3), channel_id=1, source_target_pairs={{0,4},{1,5},{2,6},{3,7},{4,0},{5,1},{6,2},{7,3},{8,12},{9,13},{10,... | collective-permute-start | bytes 393224 | tf_op jit(solution)/shard_map/ppermute | solution.py:31
  22.7 0.4 fusion.18
  23.1 3.1 %collective-permute-done.2 = f32[256,128]{1,0:T(8,128)S(1)} collective-permute-done((f32[256,128]{1,0:T(8,128)S(1)}, f32[256,128]{1,0:T(8,128)S(1)}, u32[]{:S(2)}, u32[]{:S(2)}) %collective-permute-start.2) | collective-permute-done | bytes 131104 | tf_op jit(solution)/shard_map/ppermute | solution.py:31
  26.2 2.7 %collective-permute-start.3 = (f32[256,128]{1,0:T(8,128)S(1)}, f32[256,128]{1,0:T(8,128)S(1)}, u32[]{:S(2)}, u32[]{:S(2)}) collective-permute-start(f32[256,128]{1,0:T(8,128)S(1)} %add.233), channel_id=1, source_target_pairs={{0,8},{1,9},{2,10},{3,11},{4,12},{5,13},{6,14},{7,15},{8,0},{9,1},... | collective-permute-start | bytes 393224 | tf_op jit(solution)/shard_map/ppermute | solution.py:31
  28.9 0.4 fusion.16
  29.3 5.1 %collective-permute-done.3 = f32[256,128]{1,0:T(8,128)S(1)} collective-permute-done((f32[256,128]{1,0:T(8,128)S(1)}, f32[256,128]{1,0:T(8,128)S(1)}, u32[]{:S(2)}, u32[]{:S(2)}) %collective-permute-start.3) | collective-permute-done | bytes 131104 | tf_op jit(solution)/shard_map/ppermute | solution.py:31
  34.4 0.6 multiply_reduce_fusion.3
  35.1 1.3 %collective-permute-start.4 = (f32[256,128]{1,0:T(8,128)S(1)}, f32[256,128]{1,0:T(8,128)S(1)}, u32[]{:S(2)}, u32[]{:S(2)}) collective-permute-start(f32[256,128]{1,0:T(8,128)S(1)} %get-tuple-element.5), channel_id=1, source_target_pairs={{0,2},{1,3},{2,0},{3,1},{4,6},{5,7},{6,4},{7,5},{8,10},{9,11},{10,... | collective-permute-start | bytes 393224 | tf_op jit(solution)/shard_map/ppermute | solution.py:31
  36.4 1.4 %fusion.7 = f32[512]{0:T(512)S(1)} fusion(f32[256,512]{1,0:T(8,128)S(1)} %fusion.22, f32[256,128]{1,0:T(8,128)S(1)} %get-tuple-element.5, f32[512,128]{1,0:T(8,128)S(1)} %copy-done, f32[1024,512]{1,0:T(8,128)} %get-tuple-element.8, s32[]{:T(128)S(6)} %select_n.133), kind=kOutput, calls=%fused_computation.34 | convolution fusion | flops 101187072 | bytes 1443844 | tf_op jit(solution)/shard_map/dot_general | solution.py:14
  39.2 0.8 collective-permute-done.4
  40.1 0.1 collective-permute-start.5
  40.2 1.5 %fusion.6 = f32[512]{0:T(512)S(1)} fusion(f32[256,512]{1,0:T(8,128)S(1)} %fusion.20, f32[256,128]{1,0:T(8,128)S(1)} %collective-permute-done.4, f32[512,128]{1,0:T(8,128)S(1)} %copy-done, f32[1024,512]{1,0:T(8,128)} %get-tuple-element.8, s32[]{:T(128)S(6)} %select_n.139), kind=kOutput, calls=%fused_computation.32 | convolution fusion | flops 101187072 | bytes 1443844 | tf_op jit(solution)/shard_map/dot_general | solution.py:14
  41.7 0.4 fusion.5
  42.1 0.4 fusion.4
  42.6 0.7 broadcast_select_fusion.1
  43.3 5.7 %all-to-all-start = ((f32[16,2,128]{2,1,0:T(2,128)}), f32[16,2,128]{2,1,0:T(2,128)S(1)}, u32[]{:S(2)}, u32[]{:S(2)}) async-start(f32[16,2,128]{2,1,0:T(2,128)} %broadcast_select_fusion.1), calls=%async_computation | async-start | bytes 32768 | tf_op jit(solution)/shard_map/all_to_all | solution.py:78
  49.0 6.4 %all-to-all-done = f32[16,2,128]{2,1,0:T(2,128)S(1)} async-done(((f32[16,2,128]{2,1,0:T(2,128)}), f32[16,2,128]{2,1,0:T(2,128)S(1)}, u32[]{:S(2)}, u32[]{:S(2)}) %all-to-all-start) | async-done | bytes 16416 | tf_op jit(solution)/shard_map/all_to_all | solution.py:78
  55.5 0.6 slice_reduce_fusion.1
  56.1 0.7 fusion.37
  56.9 0.2 copy-done.4
  57.1 4.3 %multiply_select_fusion.1 = (f32[1024,512]{1,0:T(8,128)}, f32[1024,512]{1,0:T(8,128)S(1)}) fusion(s32[512]{0:T(512)S(1)} %copy-done.5, f32[512]{0:T(512)S(1)} %copy-done.6, s32[1024,512]{1,0:T(8,128)S(1)} %copy-done.4, f32[1024,128]{1,0:T(8,128)S(1)} %multiply_subtract_fusion, f32[512,128]{1,0:T(8,128)S(1)} %multiply_subtract_fusion.2), kind=kOutput, calls=%fused_computation.1 | convolution fusion | flops 413138944 | bytes 7081984 | tf_op jit(solution)/shard_map/dot_general | solution.py:14
  61.4 1.0 fusion.39
  62.4 0.1 collective-permute-start.6
  62.5 2.4 %multiply_reduce_fusion = (f32[]{:T(128)}, f32[512,128]{1,0:T(8,128)S(1)}) fusion(f32[1024,512]{1,0:T(8,128)S(1)} %get-tuple-element.7, f32[1024,128]{1,0:T(8,128)S(1)} %multiply_subtract_fusion), kind=kOutput, calls=%fused_computation.39 | convolution fusion | flops 402784256 | bytes 2883588 | tf_op jit(solution)/shard_map/dot_general | solution.py:14
  64.9 0.4 fusion.12
  65.4 0.6 collective-permute-start.7
  66.0 0.4 fusion.14
  66.4 5.0 %collective-permute-done.7 = f32[256,128]{1,0:T(8,128)S(1)} collective-permute-done((f32[256,128]{1,0:T(8,128)S(1)}, f32[256,128]{1,0:T(8,128)S(1)}, u32[]{:S(2)}, u32[]{:S(2)}) %collective-permute-start.7) | collective-permute-done | bytes 131104 | tf_op jit(solution)/shard_map/ppermute | solution.py:31
  71.4 0.5 collective-permute-start.8
  71.9 0.4 fusion.10
  72.3 4.3 %collective-permute-done.8 = f32[256,128]{1,0:T(8,128)S(1)} collective-permute-done((f32[256,128]{1,0:T(8,128)S(1)}, f32[256,128]{1,0:T(8,128)S(1)}, u32[]{:S(2)}, u32[]{:S(2)}) %collective-permute-start.8) | collective-permute-done | bytes 131104 | tf_op jit(solution)/shard_map/ppermute | solution.py:31
  76.6 0.5 collective-permute-start.9
  77.1 0.4 fusion.8
  77.5 6.5 %collective-permute-done.9 = f32[256,128]{1,0:T(8,128)S(1)} collective-permute-done((f32[256,128]{1,0:T(8,128)S(1)}, f32[256,128]{1,0:T(8,128)S(1)}, u32[]{:S(2)}, u32[]{:S(2)}) %collective-permute-start.9) | collective-permute-done | bytes 131104 | tf_op jit(solution)/shard_map/ppermute | solution.py:31
  83.9 0.6 multiply_reduce_fusion.2
  84.6 0.6 collective-permute-start.10
  86.4 1.6 %fusion.3 = f32[512]{0:T(512)S(1)} fusion(f32[256,512]{1,0:T(8,128)S(1)} %fusion.14, f32[256,128]{1,0:T(8,128)S(1)} %get-tuple-element.3, f32[512,128]{1,0:T(8,128)S(1)} %multiply_subtract_fusion.2, f32[1024,512]{1,0:T(8,128)} %get-tuple-element.6, s32[]{:T(128)S(6)} %select_n.133), kind=kOutput, calls=%fused_computation.26 | convolution fusion | flops 101187072 | bytes 1443844 | tf_op jit(solution)/shard_map/dot_general | solution.py:14
  88.1 0.8 broadcast.48
  88.9 0.7 constant_dynamic-update-slice_fusion.1
  89.6 0.1 collective-permute-start.11
  89.7 0.7 constant_dynamic-update-slice_fusion
  90.3 0.4 fusion.2
  90.8 0.4 collective-permute-done.11
  91.2 0.4 fusion.1
  91.6 0.4 fusion
  92.1 0.7 broadcast_select_fusion
  92.8 3.5 %all-to-all-start.1 = ((f32[16,2,128]{2,1,0:T(2,128)}), f32[16,2,128]{2,1,0:T(2,128)S(1)}, u32[]{:S(2)}, u32[]{:S(2)}) async-start(f32[16,2,128]{2,1,0:T(2,128)} %broadcast_select_fusion), calls=%async_computation.1 | async-start | bytes 32768 | tf_op jit(solution)/shard_map/all_to_all | solution.py:78
  96.3 0.7 slice_dynamic-update-slice_fusion.1
  96.9 0.7 slice_dynamic-update-slice_fusion
  97.6 5.1 %all-to-all-done.1 = f32[16,2,128]{2,1,0:T(2,128)S(1)} async-done(((f32[16,2,128]{2,1,0:T(2,128)}), f32[16,2,128]{2,1,0:T(2,128)S(1)}, u32[]{:S(2)}, u32[]{:S(2)}) %all-to-all-start.1) | async-done | bytes 16416 | tf_op jit(solution)/shard_map/all_to_all | solution.py:78
  102.8 0.6 slice_reduce_fusion
  103.4 0.7 fusion.36
  104.0 0.7 multiply_subtract_fusion.1
  104.8 1.4 %dynamic-slice_subtract_fusion = f32[64,128]{1,0:T(8,128)} fusion(f32[1024,128]{1,0:T(8,128)S(1)} %multiply_subtract_fusion, s32[]{:T(128)S(6)} %select_n.151, f32[1024,128]{1,0:T(8,128)} %slice_dynamic-update-slice_fusion, f32[128]{0:T(128)S(1)} %fusion.36), kind=kLoop, calls=%fused_computation.72 | loop fusion | flops 16384 | bytes 98820 | tf_op jit(solution)/shard_map/sub | solution.py:109
  (41 shorter events, 0.6 us)
Async XLA Ops:
  0.6 6.2 %copy-start = (f32[512,128]{1,0:T(8,128)S(1)}, f32[512,128]{1,0:T(8,128)}, u32[]{:S(2)}) copy-start(f32[512,128]{1,0:T(8,128)} %param.8) | copy-start | bytes 786436
  6.9 3.3 %copy-start.1 = (f32[1024,128]{1,0:T(8,128)S(1)}, f32[1024,128]{1,0:T(8,128)}, u32[]{:S(2)}) copy-start(f32[1024,128]{1,0:T(8,128)} %param.7) | copy-start | bytes 1572868
  9.6 3.3 %collective-permute-start = (f32[512,128]{1,0:T(8,128)S(1)}, f32[512,128]{1,0:T(8,128)}, u32[]{:S(2)}, u32[]{:S(2)}) collective-permute-start(f32[512,128]{1,0:T(8,128)S(1)} %constant_dynamic-slice_fusion.3), channel_id=1, source_target_pairs={{0,1},{1,0},{2,3},{3,2},{4,5},{5,4},{6,7},{7,6},{8,9},{9,8},{10,11... | collective-permute-start | bytes 786440 | tf_op jit(solution)/shard_map/ppermute | solution.py:31
  14.1 6.7 %collective-permute-start.1 = (f32[256,128]{1,0:T(8,128)S(1)}, f32[256,128]{1,0:T(8,128)S(1)}, u32[]{:S(2)}, u32[]{:S(2)}) collective-permute-start(f32[256,128]{1,0:T(8,128)S(1)} %constant_dynamic-slice_fusion.2), channel_id=1, source_target_pairs={{0,2},{1,3},{2,0},{3,1},{4,6},{5,7},{6,4},{7,5},{8,10},{9,11},{10,... | collective-permute-start | bytes 393224 | tf_op jit(solution)/shard_map/ppermute | solution.py:31
  20.8 5.4 %collective-permute-start.2 = (f32[256,128]{1,0:T(8,128)S(1)}, f32[256,128]{1,0:T(8,128)S(1)}, u32[]{:S(2)}, u32[]{:S(2)}) collective-permute-start(f32[256,128]{1,0:T(8,128)S(1)} %dynamic-slice_add_fusion.3), channel_id=1, source_target_pairs={{0,4},{1,5},{2,6},{3,7},{4,0},{5,1},{6,2},{7,3},{8,12},{9,13},{10,... | collective-permute-start | bytes 393224 | tf_op jit(solution)/shard_map/ppermute | solution.py:31
  26.2 8.2 %collective-permute-start.3 = (f32[256,128]{1,0:T(8,128)S(1)}, f32[256,128]{1,0:T(8,128)S(1)}, u32[]{:S(2)}, u32[]{:S(2)}) collective-permute-start(f32[256,128]{1,0:T(8,128)S(1)} %add.233), channel_id=1, source_target_pairs={{0,8},{1,9},{2,10},{3,11},{4,12},{5,13},{6,14},{7,15},{8,0},{9,1},... | collective-permute-start | bytes 393224 | tf_op jit(solution)/shard_map/ppermute | solution.py:31
  35.1 5.0 %collective-permute-start.4 = (f32[256,128]{1,0:T(8,128)S(1)}, f32[256,128]{1,0:T(8,128)S(1)}, u32[]{:S(2)}, u32[]{:S(2)}) collective-permute-start(f32[256,128]{1,0:T(8,128)S(1)} %get-tuple-element.5), channel_id=1, source_target_pairs={{0,2},{1,3},{2,0},{3,1},{4,6},{5,7},{6,4},{7,5},{8,10},{9,11},{10,... | collective-permute-start | bytes 393224 | tf_op jit(solution)/shard_map/ppermute | solution.py:31
  39.1 2.5 %copy-start.2 = (f32[1024,512]{1,0:T(8,128)S(1)}, f32[1024,512]{1,0:T(8,128)}, u32[]{:S(2)}) copy-start(f32[1024,512]{1,0:T(8,128)} %get-tuple-element.8) | copy-start | bytes 6291460
  40.1 1.6 %collective-permute-start.5 = (f32[512,128]{1,0:T(8,128)S(1)}, f32[512,128]{1,0:T(8,128)S(1)}, u32[]{:S(2)}, u32[]{:S(2)}) collective-permute-start(f32[512,128]{1,0:T(8,128)S(1)} %pad_maximum_fusion), channel_id=1, source_target_pairs={{0,1},{1,0},{2,3},{3,2},{4,5},{5,4},{6,7},{7,6},{8,9},{9,8},{10,11... | collective-permute-start | bytes 786440 | tf_op jit(solution)/shard_map/ppermute | solution.py:31
  42.1 14.8 %copy-start.5 = (s32[512]{0:T(512)S(1)}, s32[512]{0:T(512)}, u32[]{:S(2)}) copy-start(s32[512]{0:T(512)} %param.6) | copy-start | bytes 6148
  42.1 14.8 %copy-start.6 = (f32[512]{0:T(512)S(1)}, f32[512]{0:T(512)}, u32[]{:S(2)}) copy-start(f32[512]{0:T(512)} %param.9) | copy-start | bytes 6148
  43.3 12.2 %all-to-all-start = ((f32[16,2,128]{2,1,0:T(2,128)}), f32[16,2,128]{2,1,0:T(2,128)S(1)}, u32[]{:S(2)}, u32[]{:S(2)}) async-start(f32[16,2,128]{2,1,0:T(2,128)} %broadcast_select_fusion.1), calls=%async_computation | async-start | bytes 32768 | tf_op jit(solution)/shard_map/all_to_all | solution.py:78
  55.5 1.6 %copy-start.4 = (s32[1024,512]{1,0:T(8,128)S(1)}, s32[1024,512]{1,0:T(8,128)}, u32[]{:S(2)}) copy-start(s32[1024,512]{1,0:T(8,128)} %param.5) | copy-start | bytes 6291460
  62.4 2.9 %collective-permute-start.6 = (f32[512,128]{1,0:T(8,128)S(1)}, f32[512,128]{1,0:T(8,128)S(1)}, u32[]{:S(2)}, u32[]{:S(2)}) collective-permute-start(f32[512,128]{1,0:T(8,128)S(1)} %constant_dynamic-slice_fusion.1), channel_id=1, source_target_pairs={{0,1},{1,0},{2,3},{3,2},{4,5},{5,4},{6,7},{7,6},{8,9},{9,8},{10,11... | collective-permute-start | bytes 786440 | tf_op jit(solution)/shard_map/ppermute | solution.py:31
  65.4 6.0 %collective-permute-start.7 = (f32[256,128]{1,0:T(8,128)S(1)}, f32[256,128]{1,0:T(8,128)S(1)}, u32[]{:S(2)}, u32[]{:S(2)}) collective-permute-start(f32[256,128]{1,0:T(8,128)S(1)} %constant_dynamic-slice_fusion), channel_id=1, source_target_pairs={{0,2},{1,3},{2,0},{3,1},{4,6},{5,7},{6,4},{7,5},{8,10},{9,11},{10,... | collective-permute-start | bytes 393224 | tf_op jit(solution)/shard_map/ppermute | solution.py:31
  71.4 5.2 %collective-permute-start.8 = (f32[256,128]{1,0:T(8,128)S(1)}, f32[256,128]{1,0:T(8,128)S(1)}, u32[]{:S(2)}, u32[]{:S(2)}) collective-permute-start(f32[256,128]{1,0:T(8,128)S(1)} %dynamic-slice_add_fusion.2), channel_id=1, source_target_pairs={{0,4},{1,5},{2,6},{3,7},{4,0},{5,1},{6,2},{7,3},{8,12},{9,13},{10,... | collective-permute-start | bytes 393224 | tf_op jit(solution)/shard_map/ppermute | solution.py:31
  76.6 7.3 %collective-permute-start.9 = (f32[256,128]{1,0:T(8,128)S(1)}, f32[256,128]{1,0:T(8,128)S(1)}, u32[]{:S(2)}, u32[]{:S(2)}) collective-permute-start(f32[256,128]{1,0:T(8,128)S(1)} %add.258), channel_id=1, source_target_pairs={{0,8},{1,9},{2,10},{3,11},{4,12},{5,13},{6,14},{7,15},{8,0},{9,1},... | collective-permute-start | bytes 393224 | tf_op jit(solution)/shard_map/ppermute | solution.py:31
  84.6 5.0 %collective-permute-start.10 = (f32[256,128]{1,0:T(8,128)S(1)}, f32[256,128]{1,0:T(8,128)S(1)}, u32[]{:S(2)}, u32[]{:S(2)}) collective-permute-start(f32[256,128]{1,0:T(8,128)S(1)} %get-tuple-element.3), channel_id=1, source_target_pairs={{0,2},{1,3},{2,0},{3,1},{4,6},{5,7},{6,4},{7,5},{8,10},{9,11},{10,... | collective-permute-start | bytes 393224 | tf_op jit(solution)/shard_map/ppermute | solution.py:31
  86.4 3.9 %copy-start.3 = (f32[1024,512]{1,0:T(8,128)S(1)}, f32[1024,512]{1,0:T(8,128)}, u32[]{:S(2)}) copy-start(f32[1024,512]{1,0:T(8,128)} %get-tuple-element.6) | copy-start | bytes 6291460
  89.6 1.6 %collective-permute-start.11 = (f32[512,128]{1,0:T(8,128)S(1)}, f32[512,128]{1,0:T(8,128)S(1)}, u32[]{:S(2)}, u32[]{:S(2)}) collective-permute-start(f32[512,128]{1,0:T(8,128)S(1)} %pad_maximum_fusion.1), channel_id=1, source_target_pairs={{0,1},{1,0},{2,3},{3,2},{4,5},{5,4},{6,7},{7,6},{8,9},{9,8},{10,11... | collective-permute-start | bytes 786440 | tf_op jit(solution)/shard_map/ppermute | solution.py:31
  92.8 10.0 %all-to-all-start.1 = ((f32[16,2,128]{2,1,0:T(2,128)}), f32[16,2,128]{2,1,0:T(2,128)S(1)}, u32[]{:S(2)}, u32[]{:S(2)}) async-start(f32[16,2,128]{2,1,0:T(2,128)} %broadcast_select_fusion), calls=%async_computation.1 | async-start | bytes 32768 | tf_op jit(solution)/shard_map/all_to_all | solution.py:78

commit v17 on v15

--- a/solution.py
+++ b/solution.py
@@ -34,10 +34,10 @@
 def sum_over_users(partial, n):
     me = lax.axis_index("user")
     if n == 1:
-        return partial, [(partial, 0)], jnp.sum(partial * partial)
+        return partial, [(partial, 0)], jnp.sum(partial * partial, axis=0)
     if n & (n - 1) or partial.shape[0] % n:
         total = lax.psum(partial, "user")
-        return total, [(total, 0)], jnp.where(me == 0, jnp.sum(total * total), 0.0)
+        return total, [(total, 0)], jnp.where(me == 0, jnp.sum(total * total, axis=0), 0.0)
     distances = []
     d = 1
     while d < n:
@@ -54,7 +54,7 @@
         block = keep + exchange(send, n, d)
     for d in butterfly:
         block = block + exchange(block, n, d)
-    share = jnp.where(me < 4, jnp.sum(block * block), 0.0)
+    share = jnp.where(me < 4, jnp.sum(block * block, axis=0), 0.0)
     pieces = [(block, offset)]
     for level in reversed(range(len(halving))):
         d = halving[level]
@@ -85,7 +85,7 @@
         residual, curvature = local_terms(time_factor, user_factor, user_base, counts, first_bin)
         grad_user = product(residual.T, time_factor)
         grad_whole, pieces, time_norm = sum_over_users(product(residual, user_factor), n)
-        user_norm = jnp.sum(grad_user * grad_user)
+        user_norm = jnp.sum(grad_user * grad_user, axis=0)
         bending = jnp.zeros((user_factor.shape[0],), jnp.float32)
         for piece, first in pieces:
             rows = piece.shape[0]
@@ -95,9 +95,10 @@
             weight = lax.dynamic_slice_in_dim(curvature, first, rows, 0)
             bending = bending + jnp.sum(weight * tangent_image * tangent_image, axis=0)
         lanes = jnp.sum(bending.reshape(-1, 128), axis=0)
-        norm_total, bend_lanes = sum_rows([user_norm + time_norm, lanes], n)
+        norm_lanes, bend_lanes = sum_rows([user_norm + time_norm, lanes], n)
+        norm_total = jnp.sum(norm_lanes, axis=1, keepdims=True)
         bend_total = jnp.sum(bend_lanes, axis=1, keepdims=True)
-        relax_step = norm_total / (bend_total + damping * norm_total)
+        relax_step = jnp.broadcast_to(norm_total / (bend_total + damping * norm_total), (1, 128))
         user_factor = user_factor - relax_step * grad_user
         if sweep + 1 < SWEEPS:
             time_factor = time_factor - relax_step * grad_whole

time: 105 us -> 105 us (level)
  waiting for transfers between devices: 43 us -> 47.7 us
  matrix products: 27.8 us -> 24.5 us
  other arithmetic: 7.89 us -> 5.4 us
  between operations: 3.7 us -> 5.08 us
    ppermute x14, waiting for transfers between devices: 30.1 us -> 34.8 us  [exchange(): return lax.ppermute(value, 'user', [(i, i ^ distance) for i in range(n)])]
    dot_general x22, matrix products: 27.8 us -> 24.5 us  [product(): jnp.dot(left, right, precision=precision, preferred_element_type=jnp.floa...]
    mul x2 -> x0, other arithmetic: 1.33 us -> none  [the longest x1 0.68 us: body(): time_factor = time_factor - relax_step * grad_whole]
    reduce_sum x2, other arithmetic: 1.27 us -> 0.1 us  [sum_over_users(): share = jnp.where(me < 4, jnp.sum(block * block, axis=0), 0.0)]
  transfers between devices with their start and end apart: 16 -> 16, of which waited for: 12 -> 13; matrix products, arithmetic and copies ran while one was open for 12% -> 9% of each run, Pallas kernels for 0% -> 0%
where the time goes in v17:
time: 105 us; the launch traced here: 104 us
  waiting for transfers between devices  47.7 us (45%)
  matrix products  24.5 us (23%)
  starting transfers between devices  20.6 us (20%)
  other arithmetic  5.4 us (5%)
  between operations  5.08 us (5%)
  local copies, waits for them, and re-layouts  1.27 us (1%)
    ppermute x14, waiting for transfers between devices, exchange(): return lax.ppermute(value, 'user', [(i, i ^ distance) for i in range(n)])  34.8 us
    dot_general x22, matrix products, product(): jnp.dot(left, right, precision=precision, preferred_element_type=jnp.floa...  24.5 us
    all_to_all x2, waiting for transfers between devices, sum_rows(): spread = lax.all_to_all(spread, 'user', 0, 0, tiled=False)  12.9 us
    ppermute x14, starting transfers between devices, exchange(): return lax.ppermute(value, 'user', [(i, i ^ distance) for i in range(n)])  11.4 us
    all_to_all x2, starting transfers between devices, sum_rows(): spread = lax.all_to_all(spread, 'user', 0, 0, tiled=False)  9.11 us
  transfers between devices with their start and end apart: 16, of which 13 were waited for; matrix products, arithmetic and copies ran while one was open for 9% of the time, Pallas kernels for 0%

profile of v17, /device:TPU:0, one launch (start us, length us, event | category | flops | bytes accessed | tf_op | source)
XLA Modules:
  0.0 104.5 jit_solution(1163013268071677517)
XLA Ops:
  0.7 6.2 %multiply_select_fusion.3 = (f32[1024,512]{1,0:T(8,128)}, f32[1024,512]{1,0:T(8,128)S(1)}) fusion(s32[512]{0:T(512)} %param.6, f32[512]{0:T(512)} %param.9, s32[1024,512]{1,0:T(8,128)} %param.5, f32[1024,128]{1,0:T(8,128)} %param.7, f32[512,128]{1,0:T(8,128)} %param.8), kind=kOutput, calls=%fused_computation.6 | convolution fusion | flops 413138944 | bytes 7081984 | tf_op jit(solution)/shard_map/dot_general | solution.py:14
  6.9 1.8 %fusion.31 = f32[1024,128]{1,0:T(8,128)} fusion(f32[1024,512]{1,0:T(8,128)S(1)} %get-tuple-element.13, f32[512,128]{1,0:T(8,128)S(1)} %copy-done), kind=kOutput, calls=%fused_computation.95 | convolution fusion | flops 402653184 | bytes 2883584 | tf_op jit(solution)/shard_map/dot_general | solution.py:14
  8.7 1.0 constant_dynamic-slice_fusion.3
  9.7 0.5 collective-permute-start
  10.2 1.8 %multiply_reduce_fusion.1 = (f32[128]{0:T(128)S(1)}, f32[512,128]{1,0:T(8,128)S(1)}) fusion(f32[1024,512]{1,0:T(8,128)S(1)} %get-tuple-element.13, f32[1024,128]{1,0:T(8,128)S(1)} %copy-done.1), kind=kOutput, calls=%fused_computation.40 | convolution fusion | flops 402784128 | bytes 2884096 | tf_op jit(solution)/shard_map/dot_general | solution.py:14
  12.1 0.4 fusion.17
  12.5 0.0 collective-permute-done
  12.5 1.1 %dynamic-slice_add_fusion.1 = f32[512,128]{1,0:T(8,128)S(1)} fusion(f32[512,128]{1,0:T(8,128)} %collective-permute-done, f32[1024,128]{1,0:T(8,128)} %fusion.31, s32[]{:T(128)S(6)} %select_n.137), kind=kLoop, calls=%fused_computation.41 | loop fusion | flops 65536 | bytes 786436 | tf_op jit(solution)/shard_map/add | solution.py:54
  13.6 2.6 %collective-permute-start.1 = (f32[256,128]{1,0:T(8,128)S(1)}, f32[256,128]{1,0:T(8,128)S(1)}, u32[]{:S(2)}, u32[]{:S(2)}) collective-permute-start(f32[256,128]{1,0:T(8,128)S(1)} %constant_dynamic-slice_fusion.2), channel_id=1, source_target_pairs={{0,2},{1,3},{2,0},{3,1},{4,6},{5,7},{6,4},{7,5},{8,10},{9,11},{10,... | collective-permute-start | bytes 393224 | tf_op jit(solution)/shard_map/ppermute | solution.py:31
  16.1 0.4 fusion.19
  16.5 3.8 %collective-permute-done.1 = f32[256,128]{1,0:T(8,128)S(1)} collective-permute-done((f32[256,128]{1,0:T(8,128)S(1)}, f32[256,128]{1,0:T(8,128)S(1)}, u32[]{:S(2)}, u32[]{:S(2)}) %collective-permute-start.1) | collective-permute-done | bytes 131104 | tf_op jit(solution)/shard_map/ppermute | solution.py:31
  20.3 1.9 %collective-permute-start.2 = (f32[256,128]{1,0:T(8,128)S(1)}, f32[256,128]{1,0:T(8,128)S(1)}, u32[]{:S(2)}, u32[]{:S(2)}) collective-permute-start(f32[256,128]{1,0:T(8,128)S(1)} %dynamic-slice_add_fusion.3), channel_id=1, source_target_pairs={{0,4},{1,5},{2,6},{3,7},{4,0},{5,1},{6,2},{7,3},{8,12},{9,13},{10,... | collective-permute-start | bytes 393224 | tf_op jit(solution)/shard_map/ppermute | solution.py:31
  22.2 0.4 fusion.15
  22.6 3.1 %collective-permute-done.2 = f32[256,128]{1,0:T(8,128)S(1)} collective-permute-done((f32[256,128]{1,0:T(8,128)S(1)}, f32[256,128]{1,0:T(8,128)S(1)}, u32[]{:S(2)}, u32[]{:S(2)}) %collective-permute-start.2) | collective-permute-done | bytes 131104 | tf_op jit(solution)/shard_map/ppermute | solution.py:31
  25.7 2.7 %collective-permute-start.3 = (f32[256,128]{1,0:T(8,128)S(1)}, f32[256,128]{1,0:T(8,128)S(1)}, u32[]{:S(2)}, u32[]{:S(2)}) collective-permute-start(f32[256,128]{1,0:T(8,128)S(1)} %add.223), channel_id=1, source_target_pairs={{0,8},{1,9},{2,10},{3,11},{4,12},{5,13},{6,14},{7,15},{8,0},{9,1},... | collective-permute-start | bytes 393224 | tf_op jit(solution)/shard_map/ppermute | solution.py:31
  28.4 0.4 fusion.13
  28.8 5.1 %collective-permute-done.3 = f32[256,128]{1,0:T(8,128)S(1)} collective-permute-done((f32[256,128]{1,0:T(8,128)S(1)}, f32[256,128]{1,0:T(8,128)S(1)}, u32[]{:S(2)}, u32[]{:S(2)}) %collective-permute-start.3) | collective-permute-done | bytes 131104 | tf_op jit(solution)/shard_map/ppermute | solution.py:31
  33.9 0.1 multiply_reduce_fusion.3
  34.0 1.4 %collective-permute-start.4 = (f32[256,128]{1,0:T(8,128)S(1)}, f32[256,128]{1,0:T(8,128)S(1)}, u32[]{:S(2)}, u32[]{:S(2)}) collective-permute-start(f32[256,128]{1,0:T(8,128)S(1)} %get-tuple-element.9), channel_id=1, source_target_pairs={{0,2},{1,3},{2,0},{3,1},{4,6},{5,7},{6,4},{7,5},{8,10},{9,11},{10,... | collective-permute-start | bytes 393224 | tf_op jit(solution)/shard_map/ppermute | solution.py:31
  35.4 1.5 %fusion.7 = f32[512]{0:T(512)S(1)} fusion(f32[256,512]{1,0:T(8,128)S(1)} %fusion.19, f32[256,128]{1,0:T(8,128)S(1)} %get-tuple-element.9, f32[512,128]{1,0:T(8,128)S(1)} %copy-done, f32[1024,512]{1,0:T(8,128)} %get-tuple-element.12, s32[]{:T(128)S(6)} %select_n.135), kind=kOutput, calls=%fused_computation.34 | convolution fusion | flops 101187072 | bytes 1443844 | tf_op jit(solution)/shard_map/dot_general | solution.py:14
  36.9 2.1 %collective-permute-done.4 = f32[256,128]{1,0:T(8,128)S(1)} collective-permute-done((f32[256,128]{1,0:T(8,128)S(1)}, f32[256,128]{1,0:T(8,128)S(1)}, u32[]{:S(2)}, u32[]{:S(2)}) %collective-permute-start.4) | collective-permute-done | bytes 131104 | tf_op jit(solution)/shard_map/ppermute | solution.py:31
  39.0 0.4 fusion.6
  39.5 0.0 copy-start.2
  39.5 0.4 fusion.5
  40.0 0.0 copy-start.6
  40.0 0.0 copy-start.7
  40.0 0.4 collective-permute-done.6
  40.4 0.4 fusion.4
  40.8 0.7 select_select_fusion.1
  41.5 5.6 %all-to-all-start = ((f32[16,2,128]{2,1,0:T(2,128)}), f32[16,2,128]{2,1,0:T(2,128)S(1)}, u32[]{:S(2)}, u32[]{:S(2)}) async-start(f32[16,2,128]{2,1,0:T(2,128)} %select_select_fusion.1), calls=%async_computation | async-start | bytes 32768 | tf_op jit(solution)/shard_map/all_to_all | solution.py:75
  47.2 6.5 %all-to-all-done = f32[16,2,128]{2,1,0:T(2,128)S(1)} async-done(((f32[16,2,128]{2,1,0:T(2,128)}), f32[16,2,128]{2,1,0:T(2,128)S(1)}, u32[]{:S(2)}, u32[]{:S(2)}) %all-to-all-start) | async-done | bytes 16416 | tf_op jit(solution)/shard_map/all_to_all | solution.py:75
  53.7 0.6 slice_reduce_fusion.2
  56.3 0.1 multiply_subtract_fusion
  56.4 4.3 %multiply_select_fusion.1 = (f32[1024,512]{1,0:T(8,128)}, f32[1024,512]{1,0:T(8,128)S(1)}) fusion(s32[512]{0:T(512)S(1)} %copy-done.6, f32[512]{0:T(512)S(1)} %copy-done.7, s32[1024,512]{1,0:T(8,128)S(1)} %copy-done.5, f32[1024,128]{1,0:T(8,128)S(1)} %multiply_subtract_fusion, f32[512,128]{1,0:T(8,128)S(1)} %multiply_subtract_fusion.2), kind=kOutput, calls=%fused_computation.1 | convolution fusion | flops 413138944 | bytes 7081984 | tf_op jit(solution)/shard_map/dot_general | solution.py:14
  60.7 1.0 fusion.32
  61.7 0.1 collective-permute-start.7
  61.8 1.5 %collective-permute-done.7 = f32[512,128]{1,0:T(8,128)S(1)} collective-permute-done((f32[512,128]{1,0:T(8,128)S(1)}, f32[512,128]{1,0:T(8,128)S(1)}, u32[]{:S(2)}, u32[]{:S(2)}) %collective-permute-start.7) | collective-permute-done | bytes 262176 | tf_op jit(solution)/shard_map/ppermute | solution.py:31
  63.4 0.5 collective-permute-start.8
  63.9 5.1 %collective-permute-done.8 = f32[256,128]{1,0:T(8,128)S(1)} collective-permute-done((f32[256,128]{1,0:T(8,128)S(1)}, f32[256,128]{1,0:T(8,128)S(1)}, u32[]{:S(2)}, u32[]{:S(2)}) %collective-permute-start.8) | collective-permute-done | bytes 131104 | tf_op jit(solution)/shard_map/ppermute | solution.py:31
  69.0 0.5 collective-permute-start.9
  69.6 1.8 %multiply_reduce_fusion = (f32[128]{0:T(128)S(1)}, f32[512,128]{1,0:T(8,128)S(1)}) fusion(f32[1024,512]{1,0:T(8,128)S(1)} %get-tuple-element.11, f32[1024,128]{1,0:T(8,128)S(1)} %multiply_subtract_fusion), kind=kOutput, calls=%fused_computation.37 | convolution fusion | flops 402784128 | bytes 2884096 | tf_op jit(solution)/shard_map/dot_general | solution.py:14
  71.4 2.7 %collective-permute-done.9 = f32[256,128]{1,0:T(8,128)S(1)} collective-permute-done((f32[256,128]{1,0:T(8,128)S(1)}, f32[256,128]{1,0:T(8,128)S(1)}, u32[]{:S(2)}, u32[]{:S(2)}) %collective-permute-start.9) | collective-permute-done | bytes 131104 | tf_op jit(solution)/shard_map/ppermute | solution.py:31
  74.1 0.5 collective-permute-start.10
  74.6 0.4 fusion.8
  75.0 6.3 %collective-permute-done.10 = f32[256,128]{1,0:T(8,128)S(1)} collective-permute-done((f32[256,128]{1,0:T(8,128)S(1)}, f32[256,128]{1,0:T(8,128)S(1)}, u32[]{:S(2)}, u32[]{:S(2)}) %collective-permute-start.10) | collective-permute-done | bytes 131104 | tf_op jit(solution)/shard_map/ppermute | solution.py:31
  81.3 0.1 multiply_reduce_fusion.2
  81.4 0.6 collective-permute-start.11
  82.0 0.4 fusion.33
  82.4 0.1 collective-permute-start.12
  82.5 0.4 fusion.3
  83.0 3.4 %collective-permute-done.11 = f32[256,128]{1,0:T(8,128)S(1)} collective-permute-done((f32[256,128]{1,0:T(8,128)S(1)}, f32[256,128]{1,0:T(8,128)S(1)}, u32[]{:S(2)}, u32[]{:S(2)}) %collective-permute-start.11) | collective-permute-done | bytes 131104 | tf_op jit(solution)/shard_map/ppermute | solution.py:31
  86.4 0.4 fusion.34
  86.8 0.4 fusion.2
  87.2 0.4 fusion.35
  87.6 0.4 fusion.1
  88.0 0.1 collective-permute-start.13
  88.1 1.3 %collective-permute-done.13 = f32[256,128]{1,0:T(8,128)S(1)} collective-permute-done((f32[256,128]{1,0:T(8,128)S(1)}, f32[256,128]{1,0:T(8,128)S(1)}, u32[]{:S(2)}, u32[]{:S(2)}) %collective-permute-start.13) | collective-permute-done | bytes 131104 | tf_op jit(solution)/shard_map/ppermute | solution.py:31
  89.4 0.4 fusion
  89.9 0.7 select_select_fusion
  90.6 3.5 %all-to-all-start.1 = ((f32[16,2,128]{2,1,0:T(2,128)}), f32[16,2,128]{2,1,0:T(2,128)S(1)}, u32[]{:S(2)}, u32[]{:S(2)}) async-start(f32[16,2,128]{2,1,0:T(2,128)} %select_select_fusion), calls=%async_computation.1 | async-start | bytes 32768 | tf_op jit(solution)/shard_map/all_to_all | solution.py:75
  94.1 6.4 %all-to-all-done.1 = f32[16,2,128]{2,1,0:T(2,128)S(1)} async-done(((f32[16,2,128]{2,1,0:T(2,128)}), f32[16,2,128]{2,1,0:T(2,128)S(1)}, u32[]{:S(2)}, u32[]{:S(2)}) %all-to-all-start.1) | async-done | bytes 16416 | tf_op jit(solution)/shard_map/all_to_all | solution.py:75
  100.6 0.6 slice_reduce_fusion
  103.1 0.7 multiply_subtract_fusion.1
  103.8 0.6 dynamic-slice_subtract_fusion
  (43 shorter events, 0.5 us)
Async XLA Ops:
  0.6 6.2 %copy-start = (f32[512,128]{1,0:T(8,128)S(1)}, f32[512,128]{1,0:T(8,128)}, u32[]{:S(2)}) copy-start(f32[512,128]{1,0:T(8,128)} %param.8) | copy-start | bytes 786436
  6.9 3.3 %copy-start.1 = (f32[1024,128]{1,0:T(8,128)S(1)}, f32[1024,128]{1,0:T(8,128)}, u32[]{:S(2)}) copy-start(f32[1024,128]{1,0:T(8,128)} %param.7) | copy-start | bytes 1572868
  9.7 2.8 %collective-permute-start = (f32[512,128]{1,0:T(8,128)S(1)}, f32[512,128]{1,0:T(8,128)}, u32[]{:S(2)}, u32[]{:S(2)}) collective-permute-start(f32[512,128]{1,0:T(8,128)S(1)} %constant_dynamic-slice_fusion.3), channel_id=1, source_target_pairs={{0,1},{1,0},{2,3},{3,2},{4,5},{5,4},{6,7},{7,6},{8,9},{9,8},{10,11... | collective-permute-start | bytes 786440 | tf_op jit(solution)/shard_map/ppermute | solution.py:31
  13.6 6.7 %collective-permute-start.1 = (f32[256,128]{1,0:T(8,128)S(1)}, f32[256,128]{1,0:T(8,128)S(1)}, u32[]{:S(2)}, u32[]{:S(2)}) collective-permute-start(f32[256,128]{1,0:T(8,128)S(1)} %constant_dynamic-slice_fusion.2), channel_id=1, source_target_pairs={{0,2},{1,3},{2,0},{3,1},{4,6},{5,7},{6,4},{7,5},{8,10},{9,11},{10,... | collective-permute-start | bytes 393224 | tf_op jit(solution)/shard_map/ppermute | solution.py:31
  20.3 5.4 %collective-permute-start.2 = (f32[256,128]{1,0:T(8,128)S(1)}, f32[256,128]{1,0:T(8,128)S(1)}, u32[]{:S(2)}, u32[]{:S(2)}) collective-permute-start(f32[256,128]{1,0:T(8,128)S(1)} %dynamic-slice_add_fusion.3), channel_id=1, source_target_pairs={{0,4},{1,5},{2,6},{3,7},{4,0},{5,1},{6,2},{7,3},{8,12},{9,13},{10,... | collective-permute-start | bytes 393224 | tf_op jit(solution)/shard_map/ppermute | solution.py:31
  25.7 8.2 %collective-permute-start.3 = (f32[256,128]{1,0:T(8,128)S(1)}, f32[256,128]{1,0:T(8,128)S(1)}, u32[]{:S(2)}, u32[]{:S(2)}) collective-permute-start(f32[256,128]{1,0:T(8,128)S(1)} %add.223), channel_id=1, source_target_pairs={{0,8},{1,9},{2,10},{3,11},{4,12},{5,13},{6,14},{7,15},{8,0},{9,1},... | collective-permute-start | bytes 393224 | tf_op jit(solution)/shard_map/ppermute | solution.py:31
  28.8 10.2 %copy-start.4 = (f32[1024,512]{1,0:T(8,128)S(1)}, f32[1024,512]{1,0:T(8,128)}, u32[]{:S(2)}) copy-start(f32[1024,512]{1,0:T(8,128)} %get-tuple-element.12) | copy-start | bytes 6291460
  34.0 5.0 %collective-permute-start.4 = (f32[256,128]{1,0:T(8,128)S(1)}, f32[256,128]{1,0:T(8,128)S(1)}, u32[]{:S(2)}, u32[]{:S(2)}) collective-permute-start(f32[256,128]{1,0:T(8,128)S(1)} %get-tuple-element.9), channel_id=1, source_target_pairs={{0,2},{1,3},{2,0},{3,1},{4,6},{5,7},{6,4},{7,5},{8,10},{9,11},{10,... | collective-permute-start | bytes 393224 | tf_op jit(solution)/shard_map/ppermute | solution.py:31
  35.4 4.1 %collective-permute-start.5 = (f32[256,128]{1,0:T(8,128)S(1)}, f32[256,128]{1,0:T(8,128)S(1)}, u32[]{:S(2)}, u32[]{:S(2)}) collective-permute-start(f32[256,128]{1,0:T(8,128)S(1)} %get-tuple-element.9), channel_id=1, source_target_pairs={{0,1},{1,0},{2,3},{3,2},{4,5},{5,4},{6,7},{7,6},{8,9},{9,8},{10,11... | collective-permute-start | bytes 393224 | tf_op jit(solution)/shard_map/ppermute | solution.py:31
  39.0 1.3 %collective-permute-start.6 = (f32[256,128]{1,0:T(8,128)S(1)}, f32[256,128]{1,0:T(8,128)S(1)}, u32[]{:S(2)}, u32[]{:S(2)}) collective-permute-start(f32[256,128]{1,0:T(8,128)S(1)} %collective-permute-done.4), channel_id=1, source_target_pairs={{0,1},{1,0},{2,3},{3,2},{4,5},{5,4},{6,7},{7,6},{8,9},{9,8},{10,11... | collective-permute-start | bytes 393224 | tf_op jit(solution)/shard_map/ppermute | solution.py:31
  39.5 16.8 %copy-start.2 = (f32[1024,128]{1,0:T(8,128)S(1)}, f32[1024,128]{1,0:T(8,128)}, u32[]{:S(2)}) copy-start(f32[1024,128]{1,0:T(8,128)} %param.7) | copy-start | bytes 1572868
  40.0 16.4 %copy-start.6 = (s32[512]{0:T(512)S(1)}, s32[512]{0:T(512)}, u32[]{:S(2)}) copy-start(s32[512]{0:T(512)} %param.6) | copy-start | bytes 6148
  40.0 16.4 %copy-start.7 = (f32[512]{0:T(512)S(1)}, f32[512]{0:T(512)}, u32[]{:S(2)}) copy-start(f32[512]{0:T(512)} %param.9) | copy-start | bytes 6148
  41.5 12.1 %all-to-all-start = ((f32[16,2,128]{2,1,0:T(2,128)}), f32[16,2,128]{2,1,0:T(2,128)S(1)}, u32[]{:S(2)}, u32[]{:S(2)}) async-start(f32[16,2,128]{2,1,0:T(2,128)} %select_select_fusion.1), calls=%async_computation | async-start | bytes 32768 | tf_op jit(solution)/shard_map/all_to_all | solution.py:75
  53.7 2.7 %copy-start.5 = (s32[1024,512]{1,0:T(8,128)S(1)}, s32[1024,512]{1,0:T(8,128)}, u32[]{:S(2)}) copy-start(s32[1024,512]{1,0:T(8,128)} %param.5) | copy-start | bytes 6291460
  61.7 1.6 %collective-permute-start.7 = (f32[512,128]{1,0:T(8,128)S(1)}, f32[512,128]{1,0:T(8,128)S(1)}, u32[]{:S(2)}, u32[]{:S(2)}) collective-permute-start(f32[512,128]{1,0:T(8,128)S(1)} %constant_dynamic-slice_fusion.1), channel_id=1, source_target_pairs={{0,1},{1,0},{2,3},{3,2},{4,5},{5,4},{6,7},{7,6},{8,9},{9,8},{10,11... | collective-permute-start | bytes 786440 | tf_op jit(solution)/shard_map/ppermute | solution.py:31
  63.4 5.6 %collective-permute-start.8 = (f32[256,128]{1,0:T(8,128)S(1)}, f32[256,128]{1,0:T(8,128)S(1)}, u32[]{:S(2)}, u32[]{:S(2)}) collective-permute-start(f32[256,128]{1,0:T(8,128)S(1)} %constant_dynamic-slice_fusion), channel_id=1, source_target_pairs={{0,2},{1,3},{2,0},{3,1},{4,6},{5,7},{6,4},{7,5},{8,10},{9,11},{10,... | collective-permute-start | bytes 393224 | tf_op jit(solution)/shard_map/ppermute | solution.py:31
  69.0 13.4 %copy-start.3 = (f32[1024,512]{1,0:T(8,128)S(1)}, f32[1024,512]{1,0:T(8,128)}, u32[]{:S(2)}) copy-start(f32[1024,512]{1,0:T(8,128)} %get-tuple-element.10) | copy-start | bytes 6291460
  69.0 5.0 %collective-permute-start.9 = (f32[256,128]{1,0:T(8,128)S(1)}, f32[256,128]{1,0:T(8,128)S(1)}, u32[]{:S(2)}, u32[]{:S(2)}) collective-permute-start(f32[256,128]{1,0:T(8,128)S(1)} %dynamic-slice_add_fusion.2), channel_id=1, source_target_pairs={{0,4},{1,5},{2,6},{3,7},{4,0},{5,1},{6,2},{7,3},{8,12},{9,13},{10,... | collective-permute-start | bytes 393224 | tf_op jit(solution)/shard_map/ppermute | solution.py:31
  74.1 7.2 %collective-permute-start.10 = (f32[256,128]{1,0:T(8,128)S(1)}, f32[256,128]{1,0:T(8,128)S(1)}, u32[]{:S(2)}, u32[]{:S(2)}) collective-permute-start(f32[256,128]{1,0:T(8,128)S(1)} %add.247), channel_id=1, source_target_pairs={{0,8},{1,9},{2,10},{3,11},{4,12},{5,13},{6,14},{7,15},{8,0},{9,1},... | collective-permute-start | bytes 393224 | tf_op jit(solution)/shard_map/ppermute | solution.py:31
  81.4 5.0 %collective-permute-start.11 = (f32[256,128]{1,0:T(8,128)S(1)}, f32[256,128]{1,0:T(8,128)S(1)}, u32[]{:S(2)}, u32[]{:S(2)}) collective-permute-start(f32[256,128]{1,0:T(8,128)S(1)} %get-tuple-element.7), channel_id=1, source_target_pairs={{0,2},{1,3},{2,0},{3,1},{4,6},{5,7},{6,4},{7,5},{8,10},{9,11},{10,... | collective-permute-start | bytes 393224 | tf_op jit(solution)/shard_map/ppermute | solution.py:31
  82.4 4.8 %collective-permute-start.12 = (f32[256,128]{1,0:T(8,128)S(1)}, f32[256,128]{1,0:T(8,128)S(1)}, u32[]{:S(2)}, u32[]{:S(2)}) collective-permute-start(f32[256,128]{1,0:T(8,128)S(1)} %get-tuple-element.7), channel_id=1, source_target_pairs={{0,1},{1,0},{2,3},{3,2},{4,5},{5,4},{6,7},{7,6},{8,9},{9,8},{10,11... | collective-permute-start | bytes 393224 | tf_op jit(solution)/shard_map/ppermute | solution.py:31
  88.0 1.4 %collective-permute-start.13 = (f32[256,128]{1,0:T(8,128)S(1)}, f32[256,128]{1,0:T(8,128)S(1)}, u32[]{:S(2)}, u32[]{:S(2)}) collective-permute-start(f32[256,128]{1,0:T(8,128)S(1)} %collective-permute-done.11), channel_id=1, source_target_pairs={{0,1},{1,0},{2,3},{3,2},{4,5},{5,4},{6,7},{7,6},{8,9},{9,8},{10,11... | collective-permute-start | bytes 393224 | tf_op jit(solution)/shard_map/ppermute | solution.py:31
  90.6 10.0 %all-to-all-start.1 = ((f32[16,2,128]{2,1,0:T(2,128)}), f32[16,2,128]{2,1,0:T(2,128)S(1)}, u32[]{:S(2)}, u32[]{:S(2)}) async-start(f32[16,2,128]{2,1,0:T(2,128)} %select_select_fusion), calls=%async_computation.1 | async-start | bytes 32768 | tf_op jit(solution)/shard_map/all_to_all | solution.py:75

commit v18 on v15

--- a/solution.py
+++ b/solution.py
@@ -31,7 +31,9 @@
     return lax.ppermute(value, "user", [(i, i ^ distance) for i in range(n)])
 
 
-def sum_over_users(partial, n):
+def sum_over_users(partial, n, halves=None):
+    if halves is not None:
+        partial = jnp.zeros((2 * halves[0].shape[0], halves[0].shape[1]), halves[0].dtype)
     me = lax.axis_index("user")
     if n == 1:
         return partial, [(partial, 0)], jnp.sum(partial * partial)
@@ -45,7 +47,17 @@
         d *= 2
     halving, butterfly = distances[:2], distances[2:]
     block, offset = partial, 0
-    for d in halving:
+    if halves is not None:
+        lower, upper_half = halves
+        upper = me % 2
+        from_even = lax.ppermute(upper_half, "user", [(i, i ^ 1) for i in range(0, n, 2)])
+        from_odd = lax.ppermute(lower, "user", [(i, i ^ 1) for i in range(1, n, 2)])
+        block = jnp.where(upper == 0, lower, upper_half) + from_even + from_odd
+        offset = upper * lower.shape[0]
+        halving_rest = halving[1:]
+    else:
+        halving_rest = halving
+    for d in halving_rest:
         half = block.shape[0] // 2
         upper = (me // d) % 2
         keep = lax.dynamic_slice_in_dim(block, upper * half, half, 0)
@@ -84,7 +96,12 @@
     for sweep in range(SWEEPS):
         residual, curvature = local_terms(time_factor, user_factor, user_base, counts, first_bin)
         grad_user = product(residual.T, time_factor)
-        grad_whole, pieces, time_norm = sum_over_users(product(residual, user_factor), n)
+        half = residual.shape[0] // 2
+        grad_whole, pieces, time_norm = sum_over_users(
+            None, n, (product(residual[:half], user_factor), product(residual[half:], user_factor))
+        ) if n >= 4 and not n & (n - 1) and residual.shape[0] % n == 0 else sum_over_users(
+            product(residual, user_factor), n
+        )
         user_norm = jnp.sum(grad_user * grad_user)
         bending = jnp.zeros((user_factor.shape[0],), jnp.float32)
         for piece, first in pieces:

time: 105 us -> 112 us (1.067)
  starting transfers between devices: 20.5 us -> 28.7 us
    ppermute x0 -> x4, starting transfers between devices: none -> 6.63 us  [the longest x2 4.05 us: sum_over_users(): lax.ppermute(upper_half, 'user', [(i, i ^ 1) for i in range(0, n, 2)])]
    ppermute x14 -> x12, waiting for transfers between devices: 30.1 us -> 27.8 us  [exchange(): return lax.ppermute(value, 'user', [(i, i ^ distance) for i in range(n)])]
    ppermute x0 -> x4, waiting for transfers between devices: none -> 2.13 us  [the longest x2 2.12 us: sum_over_users(): from_odd = lax.ppermute(lower, 'user', [(i, i ^ 1) for i in range(1, n, 2)])]
    ppermute x14 -> x12, starting transfers between devices: 11.3 us -> 12.5 us  [exchange(): return lax.ppermute(value, 'user', [(i, i ^ distance) for i in range(n)])]
    dot_general x22 -> x24, matrix products: 27.8 us -> 28.4 us  [product(): jnp.dot(left, right, precision=precision, preferred_element_type=jnp.floa...]
  transfers between devices with their start and end apart: 16 -> 18, of which waited for: 12 -> 12; matrix products, arithmetic and copies ran while one was open for 12% -> 14% of each run, Pallas kernels for 0% -> 0%
where the time goes in v18:
time: 112 us
  waiting for transfers between devices  42.9 us (38%)
  starting transfers between devices  28.7 us (26%)
  matrix products  28.4 us (25%)
  other arithmetic  6.88 us (6%)
  between operations  3.72 us (3%)
  local copies, waits for them, and re-layouts  1.35 us (1%)
    dot_general x24, matrix products, product(): jnp.dot(left, right, precision=precision, preferred_element_type=jnp.floa...  28.4 us
    ppermute x12, waiting for transfers between devices, exchange(): return lax.ppermute(value, 'user', [(i, i ^ distance) for i in range(n)])  27.8 us
    all_to_all x2, waiting for transfers between devices, sum_rows(): spread = lax.all_to_all(spread, 'user', 0, 0, tiled=False)  12.9 us
    ppermute x12, starting transfers between devices, exchange(): return lax.ppermute(value, 'user', [(i, i ^ distance) for i in range(n)])  12.5 us
    all_to_all x2, starting transfers between devices, sum_rows(): spread = lax.all_to_all(spread, 'user', 0, 0, tiled=False)  9.53 us
    ppermute x2, starting transfers between devices, sum_over_users(): lax.ppermute(upper_half, 'user', [(i, i ^ 1) for i in range(0, n, 2)])  4.05 us
    ppermute x2, starting transfers between devices, sum_over_users(): from_odd = lax.ppermute(lower, 'user', [(i, i ^ 1) for i in range(1, n, 2)])  2.58 us
  transfers between devices with their start and end apart: 18, of which 12 were waited for; matrix products, arithmetic and copies ran while one was open for 14% of the time, Pallas kernels for 0%

profile of v18, /device:TPU:0, one launch (start us, length us, event | category | flops | bytes accessed | tf_op | source)
XLA Modules:
  0.0 111.9 jit_solution(13374399136035680850)
XLA Ops:
  0.6 6.2 %multiply_select_fusion.3 = (f32[1024,512]{1,0:T(8,128)}, f32[1024,512]{1,0:T(8,128)S(1)}) fusion(s32[512]{0:T(512)} %param.6, f32[512]{0:T(512)} %param.9, s32[1024,512]{1,0:T(8,128)} %param.5, f32[1024,128]{1,0:T(8,128)} %param.7, f32[512,128]{1,0:T(8,128)} %param.8), kind=kOutput, calls=%fused_computation.6 | convolution fusion | flops 413138944 | bytes 7081984 | tf_op jit(solution)/shard_map/dot_general | solution.py:14
  6.9 0.6 fusion.4
  7.5 2.4 %collective-permute-start = (f32[512,128]{1,0:T(8,128)S(1)}, f32[512,128]{1,0:T(8,128)S(1)}, u32[]{:S(2)}, u32[]{:S(2)}) collective-permute-start(f32[512,128]{1,0:T(8,128)S(1)} %fusion.4), channel_id=1, source_target_pairs={{0,1},{2,3},{4,5},{6,7},{8,9},{10,11},{12,13},{14,15},{16,17},{18,... | collective-permute-start | bytes 786440 | tf_op jit(solution)/shard_map/ppermute | solution.py:53
  9.8 0.6 fusion.6
  10.4 1.3 %collective-permute-start.1 = (f32[512,128]{1,0:T(8,128)S(1)}, f32[512,128]{1,0:T(8,128)S(1)}, u32[]{:S(2)}, u32[]{:S(2)}) collective-permute-start(f32[512,128]{1,0:T(8,128)S(1)} %fusion.6), channel_id=1, source_target_pairs={{1,0},{3,2},{5,4},{7,6},{9,8},{11,10},{13,12},{15,14},{17,16},{19,... | collective-permute-start | bytes 786440 | tf_op jit(solution)/shard_map/ppermute | solution.py:54
  11.8 2.4 %multiply_reduce_fusion.1 = (f32[]{:T(128)}, f32[512,128]{1,0:T(8,128)S(1)}) fusion(f32[1024,512]{1,0:T(8,128)S(1)} %get-tuple-element.9, f32[1024,128]{1,0:T(8,128)S(1)} %copy-done.1), kind=kOutput, calls=%fused_computation.48 | convolution fusion | flops 402784256 | bytes 2883588 | tf_op jit(solution)/shard_map/dot_general | solution.py:14
  14.2 0.4 fusion.25
  14.7 2.4 %collective-permute-start.2 = (f32[256,128]{1,0:T(8,128)S(1)}, f32[256,128]{1,0:T(8,128)S(1)}, u32[]{:S(2)}, u32[]{:S(2)}) collective-permute-start(f32[256,128]{1,0:T(8,128)S(1)} %constant_dynamic-slice_fusion.1), channel_id=1, source_target_pairs={{0,2},{1,3},{2,0},{3,1},{4,6},{5,7},{6,4},{7,5},{8,10},{9,11},{10,... | collective-permute-start | bytes 393224 | tf_op jit(solution)/shard_map/ppermute | solution.py:31
  17.1 0.4 fusion.27
  17.4 3.6 %collective-permute-done.2 = f32[256,128]{1,0:T(8,128)S(1)} collective-permute-done((f32[256,128]{1,0:T(8,128)S(1)}, f32[256,128]{1,0:T(8,128)S(1)}, u32[]{:S(2)}, u32[]{:S(2)}) %collective-permute-start.2) | collective-permute-done | bytes 131104 | tf_op jit(solution)/shard_map/ppermute | solution.py:31
  21.1 2.4 %collective-permute-start.3 = (f32[256,128]{1,0:T(8,128)S(1)}, f32[256,128]{1,0:T(8,128)S(1)}, u32[]{:S(2)}, u32[]{:S(2)}) collective-permute-start(f32[256,128]{1,0:T(8,128)S(1)} %dynamic-slice_add_fusion.1), channel_id=1, source_target_pairs={{0,4},{1,5},{2,6},{3,7},{4,0},{5,1},{6,2},{7,3},{8,12},{9,13},{10,... | collective-permute-start | bytes 393224 | tf_op jit(solution)/shard_map/ppermute | solution.py:31
  23.4 0.4 fusion.23
  23.8 3.4 %collective-permute-done.3 = f32[256,128]{1,0:T(8,128)S(1)} collective-permute-done((f32[256,128]{1,0:T(8,128)S(1)}, f32[256,128]{1,0:T(8,128)S(1)}, u32[]{:S(2)}, u32[]{:S(2)}) %collective-permute-start.3) | collective-permute-done | bytes 131104 | tf_op jit(solution)/shard_map/ppermute | solution.py:31
  27.2 2.8 %collective-permute-start.4 = (f32[256,128]{1,0:T(8,128)S(1)}, f32[256,128]{1,0:T(8,128)S(1)}, u32[]{:S(2)}, u32[]{:S(2)}) collective-permute-start(f32[256,128]{1,0:T(8,128)S(1)} %add.230), channel_id=1, source_target_pairs={{0,8},{1,9},{2,10},{3,11},{4,12},{5,13},{6,14},{7,15},{8,0},{9,1},... | collective-permute-start | bytes 393224 | tf_op jit(solution)/shard_map/ppermute | solution.py:31
  30.1 0.4 fusion.21
  30.5 5.5 %collective-permute-done.4 = f32[256,128]{1,0:T(8,128)S(1)} collective-permute-done((f32[256,128]{1,0:T(8,128)S(1)}, f32[256,128]{1,0:T(8,128)S(1)}, u32[]{:S(2)}, u32[]{:S(2)}) %collective-permute-start.4) | collective-permute-done | bytes 131104 | tf_op jit(solution)/shard_map/ppermute | solution.py:31
  36.0 0.6 multiply_reduce_fusion.3
  36.6 1.4 %collective-permute-start.5 = (f32[256,128]{1,0:T(8,128)S(1)}, f32[256,128]{1,0:T(8,128)S(1)}, u32[]{:S(2)}, u32[]{:S(2)}) collective-permute-start(f32[256,128]{1,0:T(8,128)S(1)} %get-tuple-element.5), channel_id=1, source_target_pairs={{0,2},{1,3},{2,0},{3,1},{4,6},{5,7},{6,4},{7,5},{8,10},{9,11},{10,... | collective-permute-start | bytes 393224 | tf_op jit(solution)/shard_map/ppermute | solution.py:31
  38.0 1.5 %fusion.15 = f32[512]{0:T(512)S(1)} fusion(f32[256,512]{1,0:T(8,128)S(1)} %fusion.27, f32[256,128]{1,0:T(8,128)S(1)} %get-tuple-element.5, f32[512,128]{1,0:T(8,128)S(1)} %copy-done, f32[1024,512]{1,0:T(8,128)} %get-tuple-element.8, s32[]{:T(128)S(6)} %select_n.135), kind=kOutput, calls=%fused_computation.42 | convolution fusion | flops 101187072 | bytes 1443844 | tf_op jit(solution)/shard_map/dot_general | solution.py:14
  40.8 0.8 collective-permute-done.5
  41.6 1.4 %fusion.14 = f32[512]{0:T(512)S(1)} fusion(f32[256,512]{1,0:T(8,128)S(1)} %fusion.25, f32[256,128]{1,0:T(8,128)S(1)} %collective-permute-done.5, f32[512,128]{1,0:T(8,128)S(1)} %copy-done, f32[1024,512]{1,0:T(8,128)} %get-tuple-element.8, s32[]{:T(128)S(6)} %select_n.141), kind=kOutput, calls=%fused_computation.40 | convolution fusion | flops 101187072 | bytes 1443844 | tf_op jit(solution)/shard_map/dot_general | solution.py:14
  43.1 1.3 %fusion.13 = f32[512]{0:T(512)S(1)} fusion(f32[256,512]{1,0:T(8,128)S(1)} %fusion.23, f32[256,128]{1,0:T(8,128)} %collective-permute-done.6, f32[512,128]{1,0:T(8,128)S(1)} %copy-done, f32[1024,512]{1,0:T(8,128)S(1)} %copy-done.3, s32[]{:T(128)S(6)} %select_n.142), kind=kOutput, calls=%fused_computation.38 | convolution fusion | flops 101187072 | bytes 1443844 | tf_op jit(solution)/shard_map/dot_general | solution.py:14
  44.4 0.9 constant_dynamic-update-slice_fusion.5
  45.4 0.4 fusion.12
  45.9 0.7 broadcast_select_fusion.1
  46.6 6.0 %all-to-all-start = ((f32[16,2,128]{2,1,0:T(2,128)}), f32[16,2,128]{2,1,0:T(2,128)S(1)}, u32[]{:S(2)}, u32[]{:S(2)}) async-start(f32[16,2,128]{2,1,0:T(2,128)} %broadcast_select_fusion.1), calls=%async_computation | async-start | bytes 32768 | tf_op jit(solution)/shard_map/all_to_all | solution.py:87
  52.6 6.5 %all-to-all-done = f32[16,2,128]{2,1,0:T(2,128)S(1)} async-done(((f32[16,2,128]{2,1,0:T(2,128)}), f32[16,2,128]{2,1,0:T(2,128)S(1)}, u32[]{:S(2)}, u32[]{:S(2)}) %all-to-all-start) | async-done | bytes 16416 | tf_op jit(solution)/shard_map/all_to_all | solution.py:87
  59.1 0.6 slice_reduce_fusion.1
  59.7 0.7 fusion.38
  60.5 0.2 copy-done.4
  60.7 4.3 %multiply_select_fusion.1 = (f32[1024,512]{1,0:T(8,128)}, f32[1024,512]{1,0:T(8,128)S(1)}) fusion(s32[512]{0:T(512)S(1)} %copy-done.5, f32[512]{0:T(512)S(1)} %copy-done.6, s32[1024,512]{1,0:T(8,128)S(1)} %copy-done.4, f32[1024,128]{1,0:T(8,128)S(1)} %multiply_subtract_fusion, f32[512,128]{1,0:T(8,128)S(1)} %multiply_subtract_fusion.2), kind=kOutput, calls=%fused_computation.1 | convolution fusion | flops 413138944 | bytes 7081984 | tf_op jit(solution)/shard_map/dot_general | solution.py:14
  65.0 0.6 fusion
  65.6 0.6 fusion.2
  66.2 1.7 %collective-permute-start.8 = (f32[512,128]{1,0:T(8,128)S(1)}, f32[512,128]{1,0:T(8,128)S(1)}, u32[]{:S(2)}, u32[]{:S(2)}) collective-permute-start(f32[512,128]{1,0:T(8,128)S(1)} %fusion), channel_id=1, source_target_pairs={{0,1},{2,3},{4,5},{6,7},{8,9},{10,11},{12,13},{14,15},{16,17},{18,... | collective-permute-start | bytes 786440 | tf_op jit(solution)/shard_map/ppermute | solution.py:53
  67.9 1.3 %collective-permute-start.9 = (f32[512,128]{1,0:T(8,128)S(1)}, f32[512,128]{1,0:T(8,128)S(1)}, u32[]{:S(2)}, u32[]{:S(2)}) collective-permute-start(f32[512,128]{1,0:T(8,128)S(1)} %fusion.2), channel_id=1, source_target_pairs={{1,0},{3,2},{5,4},{7,6},{9,8},{11,10},{13,12},{15,14},{17,16},{19,... | collective-permute-start | bytes 786440 | tf_op jit(solution)/shard_map/ppermute | solution.py:54
  69.2 2.1 %collective-permute-done.9 = f32[512,128]{1,0:T(8,128)S(1)} collective-permute-done((f32[512,128]{1,0:T(8,128)S(1)}, f32[512,128]{1,0:T(8,128)S(1)}, u32[]{:S(2)}, u32[]{:S(2)}) %collective-permute-start.9) | collective-permute-done | bytes 262176 | tf_op jit(solution)/shard_map/ppermute | solution.py:54
  71.4 0.9 collective-permute-start.10
  72.3 4.7 %collective-permute-done.10 = f32[256,128]{1,0:T(8,128)S(1)} collective-permute-done((f32[256,128]{1,0:T(8,128)S(1)}, f32[256,128]{1,0:T(8,128)S(1)}, u32[]{:S(2)}, u32[]{:S(2)}) %collective-permute-start.10) | collective-permute-done | bytes 131104 | tf_op jit(solution)/shard_map/ppermute | solution.py:31
  77.1 0.9 collective-permute-start.11
  77.9 2.4 %multiply_reduce_fusion = (f32[]{:T(128)}, f32[512,128]{1,0:T(8,128)S(1)}) fusion(f32[1024,512]{1,0:T(8,128)S(1)} %get-tuple-element.7, f32[1024,128]{1,0:T(8,128)S(1)} %multiply_subtract_fusion), kind=kOutput, calls=%fused_computation.45 | convolution fusion | flops 402784256 | bytes 2883588 | tf_op jit(solution)/shard_map/dot_general | solution.py:14
  80.3 1.8 %collective-permute-done.11 = f32[256,128]{1,0:T(8,128)S(1)} collective-permute-done((f32[256,128]{1,0:T(8,128)S(1)}, f32[256,128]{1,0:T(8,128)S(1)}, u32[]{:S(2)}, u32[]{:S(2)}) %collective-permute-start.11) | collective-permute-done | bytes 131104 | tf_op jit(solution)/shard_map/ppermute | solution.py:31
  82.1 0.9 collective-permute-start.12
  83.0 0.4 fusion.16
  83.4 6.1 %collective-permute-done.12 = f32[256,128]{1,0:T(8,128)S(1)} collective-permute-done((f32[256,128]{1,0:T(8,128)S(1)}, f32[256,128]{1,0:T(8,128)S(1)}, u32[]{:S(2)}, u32[]{:S(2)}) %collective-permute-start.12) | collective-permute-done | bytes 131104 | tf_op jit(solution)/shard_map/ppermute | solution.py:31
  89.4 0.6 multiply_reduce_fusion.2
  90.1 0.8 collective-permute-start.13
  90.9 0.4 fusion.39
  91.3 0.1 collective-permute-start.14
  92.7 1.6 %fusion.11 = f32[512]{0:T(512)S(1)} fusion(f32[256,512]{1,0:T(8,128)S(1)} %fusion.39, f32[512,128]{1,0:T(8,128)S(1)} %get-tuple-element.13, f32[1024,512]{1,0:T(8,128)} %get-tuple-element.6, s32[]{:T(128)S(6)} %select_n.135, f32[1024,128]{1,0:T(8,128)S(1)} %multiply_subtract_fusion), kind=kOutput, calls=%fused_computation.34 | convolution fusion | flops 101187072 | bytes 1444864 | tf_op jit(solution)/shard_map/dot_general | solution.py:14
  94.3 0.7 collective-permute-done.13
  95.0 0.4 fusion.40
  95.4 0.4 fusion.10
  95.9 0.4 fusion.41
  96.3 0.4 fusion.9
  96.7 0.1 collective-permute-start.15
  96.8 1.3 %collective-permute-done.15 = f32[256,128]{1,0:T(8,128)S(1)} collective-permute-done((f32[256,128]{1,0:T(8,128)S(1)}, f32[256,128]{1,0:T(8,128)S(1)}, u32[]{:S(2)}, u32[]{:S(2)}) %collective-permute-start.15) | collective-permute-done | bytes 131104 | tf_op jit(solution)/shard_map/ppermute | solution.py:31
  98.1 0.4 fusion.8
  98.6 0.7 broadcast_select_fusion
  99.3 3.5 %all-to-all-start.1 = ((f32[16,2,128]{2,1,0:T(2,128)}), f32[16,2,128]{2,1,0:T(2,128)S(1)}, u32[]{:S(2)}, u32[]{:S(2)}) async-start(f32[16,2,128]{2,1,0:T(2,128)} %broadcast_select_fusion), calls=%async_computation.1 | async-start | bytes 32768 | tf_op jit(solution)/shard_map/all_to_all | solution.py:87
  102.8 6.4 %all-to-all-done.1 = f32[16,2,128]{2,1,0:T(2,128)S(1)} async-done(((f32[16,2,128]{2,1,0:T(2,128)}), f32[16,2,128]{2,1,0:T(2,128)S(1)}, u32[]{:S(2)}, u32[]{:S(2)}) %all-to-all-start.1) | async-done | bytes 16416 | tf_op jit(solution)/shard_map/all_to_all | solution.py:87
  109.3 0.6 slice_reduce_fusion
  109.9 0.7 fusion.37
  110.5 0.7 multiply_subtract_fusion.1
  111.3 0.6 dynamic-slice_subtract_fusion
  (47 shorter events, 0.6 us)
Async XLA Ops:
  0.6 6.2 %copy-start = (f32[512,128]{1,0:T(8,128)S(1)}, f32[512,128]{1,0:T(8,128)}, u32[]{:S(2)}) copy-start(f32[512,128]{1,0:T(8,128)} %param.8) | copy-start | bytes 786436
  6.9 4.9 %copy-start.1 = (f32[1024,128]{1,0:T(8,128)S(1)}, f32[1024,128]{1,0:T(8,128)}, u32[]{:S(2)}) copy-start(f32[1024,128]{1,0:T(8,128)} %param.7) | copy-start | bytes 1572868
  7.5 7.1 %collective-permute-start = (f32[512,128]{1,0:T(8,128)S(1)}, f32[512,128]{1,0:T(8,128)S(1)}, u32[]{:S(2)}, u32[]{:S(2)}) collective-permute-start(f32[512,128]{1,0:T(8,128)S(1)} %fusion.4), channel_id=1, source_target_pairs={{0,1},{2,3},{4,5},{6,7},{8,9},{10,11},{12,13},{14,15},{16,17},{18,... | collective-permute-start | bytes 786440 | tf_op jit(solution)/shard_map/ppermute | solution.py:53
  10.4 4.1 %collective-permute-start.1 = (f32[512,128]{1,0:T(8,128)S(1)}, f32[512,128]{1,0:T(8,128)S(1)}, u32[]{:S(2)}, u32[]{:S(2)}) collective-permute-start(f32[512,128]{1,0:T(8,128)S(1)} %fusion.6), channel_id=1, source_target_pairs={{1,0},{3,2},{5,4},{7,6},{9,8},{11,10},{13,12},{15,14},{17,16},{19,... | collective-permute-start | bytes 786440 | tf_op jit(solution)/shard_map/ppermute | solution.py:54
  14.7 6.4 %collective-permute-start.2 = (f32[256,128]{1,0:T(8,128)S(1)}, f32[256,128]{1,0:T(8,128)S(1)}, u32[]{:S(2)}, u32[]{:S(2)}) collective-permute-start(f32[256,128]{1,0:T(8,128)S(1)} %constant_dynamic-slice_fusion.1), channel_id=1, source_target_pairs={{0,2},{1,3},{2,0},{3,1},{4,6},{5,7},{6,4},{7,5},{8,10},{9,11},{10,... | collective-permute-start | bytes 393224 | tf_op jit(solution)/shard_map/ppermute | solution.py:31
  21.1 6.1 %collective-permute-start.3 = (f32[256,128]{1,0:T(8,128)S(1)}, f32[256,128]{1,0:T(8,128)S(1)}, u32[]{:S(2)}, u32[]{:S(2)}) collective-permute-start(f32[256,128]{1,0:T(8,128)S(1)} %dynamic-slice_add_fusion.1), channel_id=1, source_target_pairs={{0,4},{1,5},{2,6},{3,7},{4,0},{5,1},{6,2},{7,3},{8,12},{9,13},{10,... | collective-permute-start | bytes 393224 | tf_op jit(solution)/shard_map/ppermute | solution.py:31
  27.2 8.8 %collective-permute-start.4 = (f32[256,128]{1,0:T(8,128)S(1)}, f32[256,128]{1,0:T(8,128)S(1)}, u32[]{:S(2)}, u32[]{:S(2)}) collective-permute-start(f32[256,128]{1,0:T(8,128)S(1)} %add.230), channel_id=1, source_target_pairs={{0,8},{1,9},{2,10},{3,11},{4,12},{5,13},{6,14},{7,15},{8,0},{9,1},... | collective-permute-start | bytes 393224 | tf_op jit(solution)/shard_map/ppermute | solution.py:31
  36.6 5.0 %collective-permute-start.5 = (f32[256,128]{1,0:T(8,128)S(1)}, f32[256,128]{1,0:T(8,128)S(1)}, u32[]{:S(2)}, u32[]{:S(2)}) collective-permute-start(f32[256,128]{1,0:T(8,128)S(1)} %get-tuple-element.5), channel_id=1, source_target_pairs={{0,2},{1,3},{2,0},{3,1},{4,6},{5,7},{6,4},{7,5},{8,10},{9,11},{10,... | collective-permute-start | bytes 393224 | tf_op jit(solution)/shard_map/ppermute | solution.py:31
  38.0 5.1 %collective-permute-start.6 = (f32[256,128]{1,0:T(8,128)S(1)}, f32[256,128]{1,0:T(8,128)}, u32[]{:S(2)}, u32[]{:S(2)}) collective-permute-start(f32[256,128]{1,0:T(8,128)S(1)} %get-tuple-element.5), channel_id=1, source_target_pairs={{0,1},{1,0},{2,3},{3,2},{4,5},{5,4},{6,7},{7,6},{8,9},{9,8},{10,11... | collective-permute-start | bytes 393224 | tf_op jit(solution)/shard_map/ppermute | solution.py:31
  40.7 2.3 %copy-start.3 = (f32[1024,512]{1,0:T(8,128)S(1)}, f32[1024,512]{1,0:T(8,128)}, u32[]{:S(2)}) copy-start(f32[1024,512]{1,0:T(8,128)} %get-tuple-element.8) | copy-start | bytes 6291460
  41.6 3.8 %collective-permute-start.7 = (f32[256,128]{1,0:T(8,128)S(1)}, f32[256,128]{1,0:T(8,128)S(1)}, u32[]{:S(2)}, u32[]{:S(2)}) collective-permute-start(f32[256,128]{1,0:T(8,128)S(1)} %collective-permute-done.5), channel_id=1, source_target_pairs={{0,1},{1,0},{2,3},{3,2},{4,5},{5,4},{6,7},{7,6},{8,9},{9,8},{10,11... | collective-permute-start | bytes 393224 | tf_op jit(solution)/shard_map/ppermute | solution.py:31
  45.4 15.1 %copy-start.5 = (s32[512]{0:T(512)S(1)}, s32[512]{0:T(512)}, u32[]{:S(2)}) copy-start(s32[512]{0:T(512)} %param.6) | copy-start | bytes 6148
  45.4 15.1 %copy-start.6 = (f32[512]{0:T(512)S(1)}, f32[512]{0:T(512)}, u32[]{:S(2)}) copy-start(f32[512]{0:T(512)} %param.9) | copy-start | bytes 6148
  46.6 12.5 %all-to-all-start = ((f32[16,2,128]{2,1,0:T(2,128)}), f32[16,2,128]{2,1,0:T(2,128)S(1)}, u32[]{:S(2)}, u32[]{:S(2)}) async-start(f32[16,2,128]{2,1,0:T(2,128)} %broadcast_select_fusion.1), calls=%async_computation | async-start | bytes 32768 | tf_op jit(solution)/shard_map/all_to_all | solution.py:87
  59.1 1.6 %copy-start.4 = (s32[1024,512]{1,0:T(8,128)S(1)}, s32[1024,512]{1,0:T(8,128)}, u32[]{:S(2)}) copy-start(s32[1024,512]{1,0:T(8,128)} %param.5) | copy-start | bytes 6291460
  66.2 3.0 %collective-permute-start.8 = (f32[512,128]{1,0:T(8,128)S(1)}, f32[512,128]{1,0:T(8,128)S(1)}, u32[]{:S(2)}, u32[]{:S(2)}) collective-permute-start(f32[512,128]{1,0:T(8,128)S(1)} %fusion), channel_id=1, source_target_pairs={{0,1},{2,3},{4,5},{6,7},{8,9},{10,11},{12,13},{14,15},{16,17},{18,... | collective-permute-start | bytes 786440 | tf_op jit(solution)/shard_map/ppermute | solution.py:53
  67.9 3.4 %collective-permute-start.9 = (f32[512,128]{1,0:T(8,128)S(1)}, f32[512,128]{1,0:T(8,128)S(1)}, u32[]{:S(2)}, u32[]{:S(2)}) collective-permute-start(f32[512,128]{1,0:T(8,128)S(1)} %fusion.2), channel_id=1, source_target_pairs={{1,0},{3,2},{5,4},{7,6},{9,8},{11,10},{13,12},{15,14},{17,16},{19,... | collective-permute-start | bytes 786440 | tf_op jit(solution)/shard_map/ppermute | solution.py:54
  71.4 5.6 %collective-permute-start.10 = (f32[256,128]{1,0:T(8,128)S(1)}, f32[256,128]{1,0:T(8,128)S(1)}, u32[]{:S(2)}, u32[]{:S(2)}) collective-permute-start(f32[256,128]{1,0:T(8,128)S(1)} %constant_dynamic-slice_fusion), channel_id=1, source_target_pairs={{0,2},{1,3},{2,0},{3,1},{4,6},{5,7},{6,4},{7,5},{8,10},{9,11},{10,... | collective-permute-start | bytes 393224 | tf_op jit(solution)/shard_map/ppermute | solution.py:31
  77.1 5.0 %collective-permute-start.11 = (f32[256,128]{1,0:T(8,128)S(1)}, f32[256,128]{1,0:T(8,128)S(1)}, u32[]{:S(2)}, u32[]{:S(2)}) collective-permute-start(f32[256,128]{1,0:T(8,128)S(1)} %dynamic-slice_add_fusion), channel_id=1, source_target_pairs={{0,4},{1,5},{2,6},{3,7},{4,0},{5,1},{6,2},{7,3},{8,12},{9,13},{10,... | collective-permute-start | bytes 393224 | tf_op jit(solution)/shard_map/ppermute | solution.py:31
  82.1 7.3 %collective-permute-start.12 = (f32[256,128]{1,0:T(8,128)S(1)}, f32[256,128]{1,0:T(8,128)S(1)}, u32[]{:S(2)}, u32[]{:S(2)}) collective-permute-start(f32[256,128]{1,0:T(8,128)S(1)} %add.256), channel_id=1, source_target_pairs={{0,8},{1,9},{2,10},{3,11},{4,12},{5,13},{6,14},{7,15},{8,0},{9,1},... | collective-permute-start | bytes 393224 | tf_op jit(solution)/shard_map/ppermute | solution.py:31
  90.1 5.0 %collective-permute-start.13 = (f32[256,128]{1,0:T(8,128)S(1)}, f32[256,128]{1,0:T(8,128)S(1)}, u32[]{:S(2)}, u32[]{:S(2)}) collective-permute-start(f32[256,128]{1,0:T(8,128)S(1)} %get-tuple-element.3), channel_id=1, source_target_pairs={{0,2},{1,3},{2,0},{3,1},{4,6},{5,7},{6,4},{7,5},{8,10},{9,11},{10,... | collective-permute-start | bytes 393224 | tf_op jit(solution)/shard_map/ppermute | solution.py:31
  91.3 4.6 %collective-permute-start.14 = (f32[256,128]{1,0:T(8,128)S(1)}, f32[256,128]{1,0:T(8,128)S(1)}, u32[]{:S(2)}, u32[]{:S(2)}) collective-permute-start(f32[256,128]{1,0:T(8,128)S(1)} %get-tuple-element.3), channel_id=1, source_target_pairs={{0,1},{1,0},{2,3},{3,2},{4,5},{5,4},{6,7},{7,6},{8,9},{9,8},{10,11... | collective-permute-start | bytes 393224 | tf_op jit(solution)/shard_map/ppermute | solution.py:31
  92.6 2.8 %copy-start.2 = (f32[1024,512]{1,0:T(8,128)S(1)}, f32[1024,512]{1,0:T(8,128)}, u32[]{:S(2)}) copy-start(f32[1024,512]{1,0:T(8,128)} %get-tuple-element.6) | copy-start | bytes 6291460
  96.7 1.4 %collective-permute-start.15 = (f32[256,128]{1,0:T(8,128)S(1)}, f32[256,128]{1,0:T(8,128)S(1)}, u32[]{:S(2)}, u32[]{:S(2)}) collective-permute-start(f32[256,128]{1,0:T(8,128)S(1)} %collective-permute-done.13), channel_id=1, source_target_pairs={{0,1},{1,0},{2,3},{3,2},{4,5},{5,4},{6,7},{7,6},{8,9},{9,8},{10,11... | collective-permute-start | bytes 393224 | tf_op jit(solution)/shard_map/ppermute | solution.py:31
  99.3 10.0 %all-to-all-start.1 = ((f32[16,2,128]{2,1,0:T(2,128)}), f32[16,2,128]{2,1,0:T(2,128)S(1)}, u32[]{:S(2)}, u32[]{:S(2)}) async-start(f32[16,2,128]{2,1,0:T(2,128)} %broadcast_select_fusion), calls=%async_computation.1 | async-start | bytes 32768 | tf_op jit(solution)/shard_map/all_to_all | solution.py:87

commit v19 on v15

--- a/solution.py
+++ b/solution.py
@@ -96,7 +96,7 @@
             bending = bending + jnp.sum(weight * tangent_image * tangent_image, axis=0)
         lanes = jnp.sum(bending.reshape(-1, 128), axis=0)
         norm_total, bend_lanes = sum_rows([user_norm + time_norm, lanes], n)
-        bend_total = jnp.sum(bend_lanes, axis=1, keepdims=True)
+        bend_total = jnp.dot(bend_lanes, jnp.ones((128, 128), jnp.float32), precision=lax.Precision.HIGHEST)
         relax_step = norm_total / (bend_total + damping * norm_total)
         user_factor = user_factor - relax_step * grad_user
         if sweep + 1 < SWEEPS:

time: 105 us -> 104 us (level)
  other arithmetic: 7.89 us -> 5.4 us
  local copies, waits for them, and re-layouts: 1.44 us -> 2.57 us
    mul x2 -> x0, other arithmetic: 1.33 us -> none  [the longest x1 0.68 us: body(): time_factor = time_factor - relax_step * grad_whole]
    reduce_sum x2 -> x0, other arithmetic: 1.2 us -> none  [body(): bend_total = jnp.sum(bend_lanes, axis=1, keepdims=True)]
    unnamed x16, local copies, waits for them, and re-layouts: 0.2 us -> 1.34 us
  transfers between devices with their start and end apart: 16 -> 16, of which waited for: 12 -> 12; matrix products, arithmetic and copies ran while one was open for 12% -> 13% of each run, Pallas kernels for 0% -> 0%
where the time goes in v19:
time: 104 us; the launch traced here: 103 us
  waiting for transfers between devices  43 us (41%)
  matrix products  28.1 us (27%)
  starting transfers between devices  20.5 us (20%)
  other arithmetic  5.4 us (5%)
  between operations  3.69 us (4%)
  local copies, waits for them, and re-layouts  2.57 us (2%)
    ppermute x14, waiting for transfers between devices, exchange(): return lax.ppermute(value, 'user', [(i, i ^ distance) for i in range(n)])  30.1 us
    dot_general x22, matrix products, product(): jnp.dot(left, right, precision=precision, preferred_element_type=jnp.floa...  27.8 us
    all_to_all x2, waiting for transfers between devices, sum_rows(): spread = lax.all_to_all(spread, 'user', 0, 0, tiled=False)  12.9 us
    ppermute x14, starting transfers between devices, exchange(): return lax.ppermute(value, 'user', [(i, i ^ distance) for i in range(n)])  11.3 us
    all_to_all x2, starting transfers between devices, sum_rows(): spread = lax.all_to_all(spread, 'user', 0, 0, tiled=False)  9.21 us
  transfers between devices with their start and end apart: 16, of which 12 were waited for; matrix products, arithmetic and copies ran while one was open for 13% of the time, Pallas kernels for 0%

profile of v19, /device:TPU:0, one launch (start us, length us, event | category | flops | bytes accessed | tf_op | source)
XLA Modules:
  0.0 103.3 jit_solution(3537101948167456689)
XLA Ops:
  0.7 6.2 %multiply_select_fusion.3 = (f32[1024,512]{1,0:T(8,128)}, f32[1024,512]{1,0:T(8,128)S(1)}) fusion(s32[512]{0:T(512)} %param.6, f32[512]{0:T(512)} %param.9, s32[1024,512]{1,0:T(8,128)} %param.5, f32[1024,128]{1,0:T(8,128)} %param.7, f32[512,128]{1,0:T(8,128)} %param.8), kind=kOutput, calls=%fused_computation.6 | convolution fusion | flops 413138944 | bytes 7081984 | tf_op jit(solution)/shard_map/dot_general | solution.py:14
  6.9 1.8 %fusion.37 = f32[1024,128]{1,0:T(8,128)} fusion(f32[1024,512]{1,0:T(8,128)S(1)} %get-tuple-element.9, f32[512,128]{1,0:T(8,128)S(1)} %copy-done), kind=kOutput, calls=%fused_computation.100 | convolution fusion | flops 402653184 | bytes 2883584 | tf_op jit(solution)/shard_map/dot_general | solution.py:14
  8.7 1.0 constant_dynamic-slice_fusion.3
  9.6 0.5 collective-permute-start
  10.2 2.4 %multiply_reduce_fusion.1 = (f32[]{:T(128)}, f32[512,128]{1,0:T(8,128)S(1)}) fusion(f32[1024,512]{1,0:T(8,128)S(1)} %get-tuple-element.9, f32[1024,128]{1,0:T(8,128)S(1)} %copy-done.1), kind=kOutput, calls=%fused_computation.46 | convolution fusion | flops 402784256 | bytes 2883588 | tf_op jit(solution)/shard_map/dot_general | solution.py:14
  12.6 0.4 fusion.21
  13.0 1.1 %dynamic-slice_add_fusion.1 = f32[512,128]{1,0:T(8,128)S(1)} fusion(f32[512,128]{1,0:T(8,128)} %collective-permute-done, f32[1024,128]{1,0:T(8,128)} %fusion.37, s32[]{:T(128)S(6)} %select_n.135), kind=kLoop, calls=%fused_computation.47 | loop fusion | flops 65536 | bytes 786436 | tf_op jit(solution)/shard_map/add | solution.py:54
  14.1 2.6 %collective-permute-start.1 = (f32[256,128]{1,0:T(8,128)S(1)}, f32[256,128]{1,0:T(8,128)S(1)}, u32[]{:S(2)}, u32[]{:S(2)}) collective-permute-start(f32[256,128]{1,0:T(8,128)S(1)} %constant_dynamic-slice_fusion.2), channel_id=1, source_target_pairs={{0,2},{1,3},{2,0},{3,1},{4,6},{5,7},{6,4},{7,5},{8,10},{9,11},{10,... | collective-permute-start | bytes 393224 | tf_op jit(solution)/shard_map/ppermute | solution.py:31
  16.6 0.4 fusion.23
  17.0 3.8 %collective-permute-done.1 = f32[256,128]{1,0:T(8,128)S(1)} collective-permute-done((f32[256,128]{1,0:T(8,128)S(1)}, f32[256,128]{1,0:T(8,128)S(1)}, u32[]{:S(2)}, u32[]{:S(2)}) %collective-permute-start.1) | collective-permute-done | bytes 131104 | tf_op jit(solution)/shard_map/ppermute | solution.py:31
  20.8 1.9 %collective-permute-start.2 = (f32[256,128]{1,0:T(8,128)S(1)}, f32[256,128]{1,0:T(8,128)S(1)}, u32[]{:S(2)}, u32[]{:S(2)}) collective-permute-start(f32[256,128]{1,0:T(8,128)S(1)} %dynamic-slice_add_fusion.3), channel_id=1, source_target_pairs={{0,4},{1,5},{2,6},{3,7},{4,0},{5,1},{6,2},{7,3},{8,12},{9,13},{10,... | collective-permute-start | bytes 393224 | tf_op jit(solution)/shard_map/ppermute | solution.py:31
  22.7 0.4 fusion.19
  23.1 3.1 %collective-permute-done.2 = f32[256,128]{1,0:T(8,128)S(1)} collective-permute-done((f32[256,128]{1,0:T(8,128)S(1)}, f32[256,128]{1,0:T(8,128)S(1)}, u32[]{:S(2)}, u32[]{:S(2)}) %collective-permute-start.2) | collective-permute-done | bytes 131104 | tf_op jit(solution)/shard_map/ppermute | solution.py:31
  26.2 2.7 %collective-permute-start.3 = (f32[256,128]{1,0:T(8,128)S(1)}, f32[256,128]{1,0:T(8,128)S(1)}, u32[]{:S(2)}, u32[]{:S(2)}) collective-permute-start(f32[256,128]{1,0:T(8,128)S(1)} %add.223), channel_id=1, source_target_pairs={{0,8},{1,9},{2,10},{3,11},{4,12},{5,13},{6,14},{7,15},{8,0},{9,1},... | collective-permute-start | bytes 393224 | tf_op jit(solution)/shard_map/ppermute | solution.py:31
  28.9 0.4 fusion.17
  29.3 5.1 %collective-permute-done.3 = f32[256,128]{1,0:T(8,128)S(1)} collective-permute-done((f32[256,128]{1,0:T(8,128)S(1)}, f32[256,128]{1,0:T(8,128)S(1)}, u32[]{:S(2)}, u32[]{:S(2)}) %collective-permute-start.3) | collective-permute-done | bytes 131104 | tf_op jit(solution)/shard_map/ppermute | solution.py:31
  34.4 0.6 multiply_reduce_fusion.3
  35.1 1.3 %collective-permute-start.4 = (f32[256,128]{1,0:T(8,128)S(1)}, f32[256,128]{1,0:T(8,128)S(1)}, u32[]{:S(2)}, u32[]{:S(2)}) collective-permute-start(f32[256,128]{1,0:T(8,128)S(1)} %get-tuple-element.5), channel_id=1, source_target_pairs={{0,2},{1,3},{2,0},{3,1},{4,6},{5,7},{6,4},{7,5},{8,10},{9,11},{10,... | collective-permute-start | bytes 393224 | tf_op jit(solution)/shard_map/ppermute | solution.py:31
  36.4 1.5 %fusion.11 = f32[512]{0:T(512)S(1)} fusion(f32[256,512]{1,0:T(8,128)S(1)} %fusion.23, f32[256,128]{1,0:T(8,128)S(1)} %get-tuple-element.5, f32[512,128]{1,0:T(8,128)S(1)} %copy-done, f32[1024,512]{1,0:T(8,128)} %get-tuple-element.8, s32[]{:T(128)S(6)} %select_n.133), kind=kOutput, calls=%fused_computation.40 | convolution fusion | flops 101187072 | bytes 1443844 | tf_op jit(solution)/shard_map/dot_general | solution.py:14
  39.2 0.8 collective-permute-done.4
  40.0 1.5 %fusion.10 = f32[512]{0:T(512)S(1)} fusion(f32[256,512]{1,0:T(8,128)S(1)} %fusion.21, f32[256,128]{1,0:T(8,128)S(1)} %collective-permute-done.4, f32[512,128]{1,0:T(8,128)S(1)} %copy-done, f32[1024,512]{1,0:T(8,128)} %get-tuple-element.8, s32[]{:T(128)S(6)} %select_n.139), kind=kOutput, calls=%fused_computation.38 | convolution fusion | flops 101187072 | bytes 1443844 | tf_op jit(solution)/shard_map/dot_general | solution.py:14
  41.5 0.0 copy-start.2
  41.5 0.4 fusion.9
  42.0 0.0 copy-start.6
  42.0 0.0 copy-start.7
  42.0 0.4 fusion.8
  42.5 0.7 broadcast_select_fusion.1
  43.2 5.7 %all-to-all-start = ((f32[16,2,128]{2,1,0:T(2,128)}), f32[16,2,128]{2,1,0:T(2,128)S(1)}, u32[]{:S(2)}, u32[]{:S(2)}) async-start(f32[16,2,128]{2,1,0:T(2,128)} %broadcast_select_fusion.1), calls=%async_computation | async-start | bytes 32768 | tf_op jit(solution)/shard_map/all_to_all | solution.py:75
  48.9 6.5 %all-to-all-done = f32[16,2,128]{2,1,0:T(2,128)S(1)} async-done(((f32[16,2,128]{2,1,0:T(2,128)}), f32[16,2,128]{2,1,0:T(2,128)S(1)}, u32[]{:S(2)}, u32[]{:S(2)}) %all-to-all-start) | async-done | bytes 16416 | tf_op jit(solution)/shard_map/all_to_all | solution.py:75
  55.4 0.1 fusion.1
  55.6 0.1 multiply_subtract_fusion.2
  55.6 0.1 multiply_subtract_fusion
  55.7 1.3 %copy-done.5 = s32[1024,512]{1,0:T(8,128)S(1)} copy-done((s32[1024,512]{1,0:T(8,128)S(1)}, s32[1024,512]{1,0:T(8,128)}, u32[]{:S(2)}) %copy-start.5) | copy-done | bytes 2097176
  57.0 4.3 %multiply_select_fusion.1 = (f32[1024,512]{1,0:T(8,128)}, f32[1024,512]{1,0:T(8,128)S(1)}) fusion(s32[512]{0:T(512)S(1)} %copy-done.6, f32[512]{0:T(512)S(1)} %copy-done.7, s32[1024,512]{1,0:T(8,128)S(1)} %copy-done.5, f32[1024,128]{1,0:T(8,128)S(1)} %multiply_subtract_fusion, f32[512,128]{1,0:T(8,128)S(1)} %multiply_subtract_fusion.2), kind=kOutput, calls=%fused_computation.1 | convolution fusion | flops 413138944 | bytes 7081984 | tf_op jit(solution)/shard_map/dot_general | solution.py:14
  61.4 1.0 fusion.38
  62.4 0.1 collective-permute-start.7
  62.5 1.5 %collective-permute-done.7 = f32[512,128]{1,0:T(8,128)S(1)} collective-permute-done((f32[512,128]{1,0:T(8,128)S(1)}, f32[512,128]{1,0:T(8,128)S(1)}, u32[]{:S(2)}, u32[]{:S(2)}) %collective-permute-start.7) | collective-permute-done | bytes 262176 | tf_op jit(solution)/shard_map/ppermute | solution.py:31
  64.0 0.5 collective-permute-start.8
  64.6 5.1 %collective-permute-done.8 = f32[256,128]{1,0:T(8,128)S(1)} collective-permute-done((f32[256,128]{1,0:T(8,128)S(1)}, f32[256,128]{1,0:T(8,128)S(1)}, u32[]{:S(2)}, u32[]{:S(2)}) %collective-permute-start.8) | collective-permute-done | bytes 131104 | tf_op jit(solution)/shard_map/ppermute | solution.py:31
  69.7 0.5 collective-permute-start.9
  70.2 2.4 %multiply_reduce_fusion = (f32[]{:T(128)}, f32[512,128]{1,0:T(8,128)S(1)}) fusion(f32[1024,512]{1,0:T(8,128)S(1)} %get-tuple-element.7, f32[1024,128]{1,0:T(8,128)S(1)} %multiply_subtract_fusion), kind=kOutput, calls=%fused_computation.43 | convolution fusion | flops 402784256 | bytes 2883588 | tf_op jit(solution)/shard_map/dot_general | solution.py:14
  72.6 2.1 %collective-permute-done.9 = f32[256,128]{1,0:T(8,128)S(1)} collective-permute-done((f32[256,128]{1,0:T(8,128)S(1)}, f32[256,128]{1,0:T(8,128)S(1)}, u32[]{:S(2)}, u32[]{:S(2)}) %collective-permute-start.9) | collective-permute-done | bytes 131104 | tf_op jit(solution)/shard_map/ppermute | solution.py:31
  74.7 0.5 collective-permute-start.10
  75.3 0.4 fusion.12
  75.6 6.3 %collective-permute-done.10 = f32[256,128]{1,0:T(8,128)S(1)} collective-permute-done((f32[256,128]{1,0:T(8,128)S(1)}, f32[256,128]{1,0:T(8,128)S(1)}, u32[]{:S(2)}, u32[]{:S(2)}) %collective-permute-start.10) | collective-permute-done | bytes 131104 | tf_op jit(solution)/shard_map/ppermute | solution.py:31
  81.9 0.6 multiply_reduce_fusion.2
  82.6 0.6 collective-permute-start.11
  83.1 0.4 fusion.39
  83.5 0.1 collective-permute-start.12
  84.9 1.6 %fusion.7 = f32[512]{0:T(512)S(1)} fusion(f32[256,512]{1,0:T(8,128)S(1)} %fusion.39, f32[512,128]{1,0:T(8,128)S(1)} %get-tuple-element.13, f32[1024,512]{1,0:T(8,128)} %get-tuple-element.6, s32[]{:T(128)S(6)} %select_n.133, f32[1024,128]{1,0:T(8,128)S(1)} %multiply_subtract_fusion), kind=kOutput, calls=%fused_computation.32 | convolution fusion | flops 101187072 | bytes 1444864 | tf_op jit(solution)/shard_map/dot_general | solution.py:14
  86.6 0.9 collective-permute-done.11
  87.5 0.4 fusion.40
  87.9 0.4 fusion.6
  88.4 0.4 fusion.41
  88.8 0.4 fusion.5
  89.2 0.1 collective-permute-start.13
  89.3 1.3 %collective-permute-done.13 = f32[256,128]{1,0:T(8,128)S(1)} collective-permute-done((f32[256,128]{1,0:T(8,128)S(1)}, f32[256,128]{1,0:T(8,128)S(1)}, u32[]{:S(2)}, u32[]{:S(2)}) %collective-permute-start.13) | collective-permute-done | bytes 131104 | tf_op jit(solution)/shard_map/ppermute | solution.py:31
  90.6 0.4 fusion.4
  91.1 0.7 broadcast_select_fusion
  91.8 3.5 %all-to-all-start.1 = ((f32[16,2,128]{2,1,0:T(2,128)}), f32[16,2,128]{2,1,0:T(2,128)S(1)}, u32[]{:S(2)}, u32[]{:S(2)}) async-start(f32[16,2,128]{2,1,0:T(2,128)} %broadcast_select_fusion), calls=%async_computation.1 | async-start | bytes 32768 | tf_op jit(solution)/shard_map/all_to_all | solution.py:75
  95.3 6.4 %all-to-all-done.1 = f32[16,2,128]{2,1,0:T(2,128)S(1)} async-done(((f32[16,2,128]{2,1,0:T(2,128)}), f32[16,2,128]{2,1,0:T(2,128)S(1)}, u32[]{:S(2)}, u32[]{:S(2)}) %all-to-all-start.1) | async-done | bytes 16416 | tf_op jit(solution)/shard_map/all_to_all | solution.py:75
  101.7 0.1 fusion.3
  101.9 0.8 multiply_subtract_fusion.1
  102.6 0.6 dynamic-slice_subtract_fusion
  (43 shorter events, 0.5 us)
Async XLA Ops:
  0.6 6.2 %copy-start = (f32[512,128]{1,0:T(8,128)S(1)}, f32[512,128]{1,0:T(8,128)}, u32[]{:S(2)}) copy-start(f32[512,128]{1,0:T(8,128)} %param.8) | copy-start | bytes 786436
  6.9 3.3 %copy-start.1 = (f32[1024,128]{1,0:T(8,128)S(1)}, f32[1024,128]{1,0:T(8,128)}, u32[]{:S(2)}) copy-start(f32[1024,128]{1,0:T(8,128)} %param.7) | copy-start | bytes 1572868
  9.6 3.3 %collective-permute-start = (f32[512,128]{1,0:T(8,128)S(1)}, f32[512,128]{1,0:T(8,128)}, u32[]{:S(2)}, u32[]{:S(2)}) collective-permute-start(f32[512,128]{1,0:T(8,128)S(1)} %constant_dynamic-slice_fusion.3), channel_id=1, source_target_pairs={{0,1},{1,0},{2,3},{3,2},{4,5},{5,4},{6,7},{7,6},{8,9},{9,8},{10,11... | collective-permute-start | bytes 786440 | tf_op jit(solution)/shard_map/ppermute | solution.py:31
  14.1 6.7 %collective-permute-start.1 = (f32[256,128]{1,0:T(8,128)S(1)}, f32[256,128]{1,0:T(8,128)S(1)}, u32[]{:S(2)}, u32[]{:S(2)}) collective-permute-start(f32[256,128]{1,0:T(8,128)S(1)} %constant_dynamic-slice_fusion.2), channel_id=1, source_target_pairs={{0,2},{1,3},{2,0},{3,1},{4,6},{5,7},{6,4},{7,5},{8,10},{9,11},{10,... | collective-permute-start | bytes 393224 | tf_op jit(solution)/shard_map/ppermute | solution.py:31
  20.8 5.4 %collective-permute-start.2 = (f32[256,128]{1,0:T(8,128)S(1)}, f32[256,128]{1,0:T(8,128)S(1)}, u32[]{:S(2)}, u32[]{:S(2)}) collective-permute-start(f32[256,128]{1,0:T(8,128)S(1)} %dynamic-slice_add_fusion.3), channel_id=1, source_target_pairs={{0,4},{1,5},{2,6},{3,7},{4,0},{5,1},{6,2},{7,3},{8,12},{9,13},{10,... | collective-permute-start | bytes 393224 | tf_op jit(solution)/shard_map/ppermute | solution.py:31
  26.2 8.2 %collective-permute-start.3 = (f32[256,128]{1,0:T(8,128)S(1)}, f32[256,128]{1,0:T(8,128)S(1)}, u32[]{:S(2)}, u32[]{:S(2)}) collective-permute-start(f32[256,128]{1,0:T(8,128)S(1)} %add.223), channel_id=1, source_target_pairs={{0,8},{1,9},{2,10},{3,11},{4,12},{5,13},{6,14},{7,15},{8,0},{9,1},... | collective-permute-start | bytes 393224 | tf_op jit(solution)/shard_map/ppermute | solution.py:31
  35.1 5.0 %collective-permute-start.4 = (f32[256,128]{1,0:T(8,128)S(1)}, f32[256,128]{1,0:T(8,128)S(1)}, u32[]{:S(2)}, u32[]{:S(2)}) collective-permute-start(f32[256,128]{1,0:T(8,128)S(1)} %get-tuple-element.5), channel_id=1, source_target_pairs={{0,2},{1,3},{2,0},{3,1},{4,6},{5,7},{6,4},{7,5},{8,10},{9,11},{10,... | collective-permute-start | bytes 393224 | tf_op jit(solution)/shard_map/ppermute | solution.py:31
  36.4 5.1 %collective-permute-start.5 = (f32[256,128]{1,0:T(8,128)S(1)}, f32[256,128]{1,0:T(8,128)S(1)}, u32[]{:S(2)}, u32[]{:S(2)}) collective-permute-start(f32[256,128]{1,0:T(8,128)S(1)} %get-tuple-element.5), channel_id=1, source_target_pairs={{0,1},{1,0},{2,3},{3,2},{4,5},{5,4},{6,7},{7,6},{8,9},{9,8},{10,11... | collective-permute-start | bytes 393224 | tf_op jit(solution)/shard_map/ppermute | solution.py:31
  39.1 2.4 %copy-start.4 = (f32[1024,512]{1,0:T(8,128)S(1)}, f32[1024,512]{1,0:T(8,128)}, u32[]{:S(2)}) copy-start(f32[1024,512]{1,0:T(8,128)} %get-tuple-element.8) | copy-start | bytes 6291460
  40.0 2.0 %collective-permute-start.6 = (f32[256,128]{1,0:T(8,128)S(1)}, f32[256,128]{1,0:T(8,128)S(1)}, u32[]{:S(2)}, u32[]{:S(2)}) collective-permute-start(f32[256,128]{1,0:T(8,128)S(1)} %collective-permute-done.4), channel_id=1, source_target_pairs={{0,1},{1,0},{2,3},{3,2},{4,5},{5,4},{6,7},{7,6},{8,9},{9,8},{10,11... | collective-permute-start | bytes 393224 | tf_op jit(solution)/shard_map/ppermute | solution.py:31
  41.5 14.1 %copy-start.2 = (f32[1024,128]{1,0:T(8,128)S(1)}, f32[1024,128]{1,0:T(8,128)}, u32[]{:S(2)}) copy-start(f32[1024,128]{1,0:T(8,128)} %param.7) | copy-start | bytes 1572868
  42.0 13.7 %copy-start.6 = (s32[512]{0:T(512)S(1)}, s32[512]{0:T(512)}, u32[]{:S(2)}) copy-start(s32[512]{0:T(512)} %param.6) | copy-start | bytes 6148
  42.0 13.7 %copy-start.7 = (f32[512]{0:T(512)S(1)}, f32[512]{0:T(512)}, u32[]{:S(2)}) copy-start(f32[512]{0:T(512)} %param.9) | copy-start | bytes 6148
  43.2 12.2 %all-to-all-start = ((f32[16,2,128]{2,1,0:T(2,128)}), f32[16,2,128]{2,1,0:T(2,128)S(1)}, u32[]{:S(2)}, u32[]{:S(2)}) async-start(f32[16,2,128]{2,1,0:T(2,128)} %broadcast_select_fusion.1), calls=%async_computation | async-start | bytes 32768 | tf_op jit(solution)/shard_map/all_to_all | solution.py:75
  55.4 1.6 %copy-start.5 = (s32[1024,512]{1,0:T(8,128)S(1)}, s32[1024,512]{1,0:T(8,128)}, u32[]{:S(2)}) copy-start(s32[1024,512]{1,0:T(8,128)} %param.5) | copy-start | bytes 6291460
  62.4 1.6 %collective-permute-start.7 = (f32[512,128]{1,0:T(8,128)S(1)}, f32[512,128]{1,0:T(8,128)S(1)}, u32[]{:S(2)}, u32[]{:S(2)}) collective-permute-start(f32[512,128]{1,0:T(8,128)S(1)} %constant_dynamic-slice_fusion.1), channel_id=1, source_target_pairs={{0,1},{1,0},{2,3},{3,2},{4,5},{5,4},{6,7},{7,6},{8,9},{9,8},{10,11... | collective-permute-start | bytes 786440 | tf_op jit(solution)/shard_map/ppermute | solution.py:31
  64.0 5.6 %collective-permute-start.8 = (f32[256,128]{1,0:T(8,128)S(1)}, f32[256,128]{1,0:T(8,128)S(1)}, u32[]{:S(2)}, u32[]{:S(2)}) collective-permute-start(f32[256,128]{1,0:T(8,128)S(1)} %constant_dynamic-slice_fusion), channel_id=1, source_target_pairs={{0,2},{1,3},{2,0},{3,1},{4,6},{5,7},{6,4},{7,5},{8,10},{9,11},{10,... | collective-permute-start | bytes 393224 | tf_op jit(solution)/shard_map/ppermute | solution.py:31
  69.7 5.0 %collective-permute-start.9 = (f32[256,128]{1,0:T(8,128)S(1)}, f32[256,128]{1,0:T(8,128)S(1)}, u32[]{:S(2)}, u32[]{:S(2)}) collective-permute-start(f32[256,128]{1,0:T(8,128)S(1)} %dynamic-slice_add_fusion.2), channel_id=1, source_target_pairs={{0,4},{1,5},{2,6},{3,7},{4,0},{5,1},{6,2},{7,3},{8,12},{9,13},{10,... | collective-permute-start | bytes 393224 | tf_op jit(solution)/shard_map/ppermute | solution.py:31
  74.7 7.2 %collective-permute-start.10 = (f32[256,128]{1,0:T(8,128)S(1)}, f32[256,128]{1,0:T(8,128)S(1)}, u32[]{:S(2)}, u32[]{:S(2)}) collective-permute-start(f32[256,128]{1,0:T(8,128)S(1)} %add.247), channel_id=1, source_target_pairs={{0,8},{1,9},{2,10},{3,11},{4,12},{5,13},{6,14},{7,15},{8,0},{9,1},... | collective-permute-start | bytes 393224 | tf_op jit(solution)/shard_map/ppermute | solution.py:31
  82.6 5.0 %collective-permute-start.11 = (f32[256,128]{1,0:T(8,128)S(1)}, f32[256,128]{1,0:T(8,128)S(1)}, u32[]{:S(2)}, u32[]{:S(2)}) collective-permute-start(f32[256,128]{1,0:T(8,128)S(1)} %get-tuple-element.3), channel_id=1, source_target_pairs={{0,2},{1,3},{2,0},{3,1},{4,6},{5,7},{6,4},{7,5},{8,10},{9,11},{10,... | collective-permute-start | bytes 393224 | tf_op jit(solution)/shard_map/ppermute | solution.py:31
  83.5 4.8 %collective-permute-start.12 = (f32[256,128]{1,0:T(8,128)S(1)}, f32[256,128]{1,0:T(8,128)S(1)}, u32[]{:S(2)}, u32[]{:S(2)}) collective-permute-start(f32[256,128]{1,0:T(8,128)S(1)} %get-tuple-element.3), channel_id=1, source_target_pairs={{0,1},{1,0},{2,3},{3,2},{4,5},{5,4},{6,7},{7,6},{8,9},{9,8},{10,11... | collective-permute-start | bytes 393224 | tf_op jit(solution)/shard_map/ppermute | solution.py:31
  84.9 3.0 %copy-start.3 = (f32[1024,512]{1,0:T(8,128)S(1)}, f32[1024,512]{1,0:T(8,128)}, u32[]{:S(2)}) copy-start(f32[1024,512]{1,0:T(8,128)} %get-tuple-element.6) | copy-start | bytes 6291460
  89.2 1.4 %collective-permute-start.13 = (f32[256,128]{1,0:T(8,128)S(1)}, f32[256,128]{1,0:T(8,128)S(1)}, u32[]{:S(2)}, u32[]{:S(2)}) collective-permute-start(f32[256,128]{1,0:T(8,128)S(1)} %collective-permute-done.11), channel_id=1, source_target_pairs={{0,1},{1,0},{2,3},{3,2},{4,5},{5,4},{6,7},{7,6},{8,9},{9,8},{10,11... | collective-permute-start | bytes 393224 | tf_op jit(solution)/shard_map/ppermute | solution.py:31
  91.8 10.0 %all-to-all-start.1 = ((f32[16,2,128]{2,1,0:T(2,128)}), f32[16,2,128]{2,1,0:T(2,128)S(1)}, u32[]{:S(2)}, u32[]{:S(2)}) async-start(f32[16,2,128]{2,1,0:T(2,128)} %broadcast_select_fusion), calls=%async_computation.1 | async-start | bytes 32768 | tf_op jit(solution)/shard_map/all_to_all | solution.py:75
